TPU v7x, 32 devices: a whole 2x2x4 slice. The times are simulated.
32 devices in a mesh: inv: 2 (over y), tracer: 4 (over z), band: 4 (over x, core).
Axes of the slice: x: 2, y: 2, z: 4, core: 2. Of those that a mesh axis runs over, the one named last changes fastest.
Arguments:
- tracer_state: float32 [32, 32, 48, 512], P(('inv', 'tracer'), 'band'), parts along dimension 0, may hold values from -6 to 6
- control: float32 [32, 32, 512], P(('inv', 'tracer'), 'band'), parts along dimension 0, may hold values from -6 to 6
- prior_tiles: float32 [8, 8, 8], replicated, may hold values from -1 to 1
- tile_index: int32 [4, 4], replicated, may hold values from 0 to 7, as said below
- region_map: int32 [32, 512], P('band'), may hold values from 0 to 21
- region_sigma: float32 [16, 22], P('tracer'), may hold values from 0.3 to 3
- zonal_courant: float32 [64, 48, 512], P(('inv', 'band'), None, 'tracer'), parts along dimension 0, may hold values from -0.3 to 0.3
- meridional_courant: float32 [64, 48, 512], P(('inv', 'band'), None, 'tracer'), parts along dimension 0, may hold values from -0.3 to 0.3
- vertical_diffusion: float32 [64, 48, 512], P(('inv', 'band'), None, 'tracer'), parts along dimension 0, may hold values from 0.02 to 0.2
Outputs:
- final_state: float32 [32, 32, 48, 512], P(('inv', 'tracer'), 'band'), parts along dimension 0
- emission: float32 [32, 32, 512], P(('inv', 'tracer'), 'band'), parts along dimension 0
There are 2 independent parts, one for each index of `inv`. A program takes and returns all parts, laid end to end along the dimension named above; an argument that names none is the same for every part. Nothing has to cross between parts.
Inputs may be any that keep to these rules, and one draw needn't show every extreme that they name: `tile_index`: each entry names one of the 8 tiles; 0 and 7 both occur.
All inputs are finite; a program needn't handle non-finite values.
Results may differ from a plain program's by a relative error of at most 0.000071.
Values sent between devices are 32-bit elements; how exact they have to be, the bound alone decides.
No kernel may reach another device: no remote copies, remote signals or barrier semaphores. Data moves between devices by JAX's collectives and lax.ppermute only.
A program may use at most 128 MiB of HBM per device.

v0:
```python
import jax
import jax.numpy as jnp
from jax import lax
from jax.sharding import PartitionSpec as P

STEPS = 2


exact_dot = lax.Precision.HIGHEST


def padded_2(block, sides, width):
    for axis, dim in sides:
        count = lax.axis_size(axis)
        forward = [(i, i + 1) for i in range(count - 1)]
        backward = [(target, source) for source, target in forward]
        low = lax.ppermute(
            lax.slice_in_dim(block, block.shape[dim] - width, None, axis=dim), axis, forward
        )
        high = lax.ppermute(lax.slice_in_dim(block, 0, width, axis=dim), axis, backward)
        block = jnp.concatenate([low, block, high], axis=dim)
    return block


def passed_along(value, axis, by):
    count = lax.axis_size(axis)
    pairs = [(i, i + by) for i in range(count) if 0 <= i + by < count]
    return lax.ppermute(value, axis, pairs)


def vertical_mixing(tracer_now, mixing):
    levels = tracer_now.shape[2]
    upper_level = jnp.concatenate(
        [tracer_now[:, :, 1:], jnp.zeros_like(tracer_now[:, :, :1])], axis=2
    )
    open_top = (lax.broadcasted_iota(jnp.int32, (levels, 1), 0) < levels - 1).astype(jnp.float32)
    flux_up = mixing * (tracer_now - upper_level) * open_top
    flux_down = jnp.concatenate([jnp.zeros_like(flux_up[:, :, :1]), flux_up[:, :, :-1]], axis=2)
    return flux_up - flux_down


def advance(tracer_now, weather, sideways, north_open, source):
    zonal, zonal_west, meridional, meridional_south, mixing = weather
    west_side, east_side = sideways(tracer_now)
    flux_east = jnp.maximum(zonal, 0.0) * tracer_now + jnp.minimum(zonal, 0.0) * east_side
    flux_west = jnp.maximum(zonal_west, 0.0) * west_side + jnp.minimum(zonal_west, 0.0) * tracer_now
    padded = padded_2(tracer_now, (("band", 1),), 1)
    north_side = padded[:, 2:]
    south_side = padded[:, :-2]
    flux_north = (
        jnp.maximum(meridional, 0.0) * tracer_now + jnp.minimum(meridional, 0.0) * north_side
    ) * north_open
    flux_south = (
        jnp.maximum(meridional_south, 0.0) * south_side
        + jnp.minimum(meridional_south, 0.0) * tracer_now
    )
    result = (
        tracer_now
        - (flux_east - flux_west)
        - (flux_north - flux_south)
        - vertical_mixing(tracer_now, mixing)
    )
    return result.at[:, :, 0, :].add(source)


def on_device(
    tracer_state,
    control,
    prior_tiles,
    tile_index,
    region_map,
    region_sigma,
    zonal_courant,
    meridional_courant,
    vertical_diffusion,
):
    band_count = lax.axis_size("band")
    band_index = lax.axis_index("band")
    tiles_count = prior_tiles.shape[0]
    lat_rows = control.shape[1]
    choose = (
        tile_index[:, :, None] == lax.broadcasted_iota(jnp.int32, (1, 1, tiles_count), 2)
    ).astype(jnp.float32)
    own_row = lax.dynamic_slice_in_dim(choose, band_index, 1, 0)[0]
    blocks = jnp.einsum("bt,tmn->bmn", own_row, prior_tiles, precision=exact_dot)
    row_block = jnp.transpose(blocks, (1, 0, 2)).reshape(lat_rows, band_count * lat_rows)
    prior_field = jnp.einsum(
        "jm,kmn->kjn",
        row_block,
        lax.all_gather(control, "band", axis=1, tiled=True),
        precision=exact_dot,
    )
    regions = region_sigma.shape[1]
    onehot = (region_map[:, :, None] == lax.broadcasted_iota(jnp.int32, (1, 1, regions), 2)).astype(
        jnp.float32
    )
    cell_sigma = jnp.einsum("kr,jnr->kjn", region_sigma, onehot, precision=exact_dot)
    emission = cell_sigma * prior_field
    latitude = band_index * lat_rows + lax.broadcasted_iota(jnp.int32, (lat_rows, 1, 1), 0)
    north_open = (latitude < band_count * lat_rows - 1).astype(jnp.float32)
    south_row = passed_along(meridional_courant[-1:], "band", 1)
    zonal, meridional, mixing, south_edge = (
        lax.all_gather(zonal_courant, "tracer", axis=2, tiled=True),
        lax.all_gather(meridional_courant, "tracer", axis=2, tiled=True),
        lax.all_gather(vertical_diffusion, "tracer", axis=2, tiled=True),
        lax.all_gather(south_row, "tracer", axis=2, tiled=True),
    )
    weather = (
        zonal,
        jnp.roll(zonal, 1, axis=2),
        meridional,
        jnp.concatenate([south_edge, meridional[:-1]], axis=0),
        mixing,
    )

    def sideways(tracer_now):
        return (jnp.roll(tracer_now, 1, axis=3), jnp.roll(tracer_now, -1, axis=3))

    tracer_field = tracer_state
    for substep in range(STEPS):
        tracer_field = advance(tracer_field, weather, sideways, north_open, emission)
    return (tracer_field, emission)


def solution(mesh):
    in_specs = (
        P(("inv", "tracer"), "band", None, None),
        P(("inv", "tracer"), "band", None),
        P(),
        P(),
        P("band", None),
        P("tracer", None),
        P(("inv", "band"), None, "tracer"),
        P(("inv", "band"), None, "tracer"),
        P(("inv", "band"), None, "tracer"),
    )
    out_specs = (P(("inv", "tracer"), "band", None, None), P(("inv", "tracer"), "band", None))
    return jax.shard_map(
        on_device, mesh=mesh, in_specs=in_specs, out_specs=out_specs, check_vma=False
    )
```

profile of v0, /device:TPU:1, one launch (start us, length us, event | category | flops | bytes accessed | tf_op | source)
XLA Modules:
  0.0 151.5 jit_solution(13097804177532343057)
XLA Ops:
  0.7 4.0 %copy.21 = f32[4,8,48,512]{3,0,1,2:T(4,128)S(1)} copy(f32[4,8,48,512]{3,2,1,0:T(8,128)} %param.13) | data formatting | bytes 6291456 | tf_op args[0]
  4.6 1.1 fusion.42
  5.7 2.0 %collective-permute-start = (f32[4,1,48,512]{3,0,1,2:T(4,128)}, f32[4,1,48,512]{3,0,1,2:T(4,128)}, u32[]{:S(2)}, u32[]{:S(2)}) collective-permute-start(f32[4,1,48,512]{3,0,1,2:T(4,128)} %get-tuple-element.38), channel_id=1, source_target_pairs={{1,0},{2,1},{3,2},{5,4},{6,5},{7,6},{9,8},{10,9},{11,10},{13,12},{... | collective-permute-start | bytes 1179656 | tf_op jit(solution)/shard_map/ppermute | solution.py:20
  7.7 4.5 %collective-permute-start.2 = (f32[4,1,48,512]{3,0,1,2:T(4,128)}, f32[4,1,48,512]{3,0,1,2:T(4,128)}, u32[]{:S(2)}, u32[]{:S(2)}) collective-permute-start(f32[4,1,48,512]{3,0,1,2:T(4,128)} %get-tuple-element.39), channel_id=1, source_target_pairs={{0,1},{1,2},{2,3},{4,5},{5,6},{6,7},{8,9},{9,10},{10,11},{12,13},{... | collective-permute-start | bytes 1179656 | tf_op jit(solution)/shard_map/ppermute | solution.py:17
  12.2 3.1 %collective-permute-start.1 = (f32[1,48,128]{2,1,0:T(8,128)S(1)}, f32[1,48,128]{2,1,0:T(8,128)S(1)}, u32[]{:S(2)}, u32[]{:S(2)}) collective-permute-start(f32[1,48,128]{2,1,0:T(8,128)S(1)} %slice.144), channel_id=1, source_target_pairs={{0,1},{1,2},{2,3},{4,5},{5,6},{6,7},{8,9},{9,10},{10,11},{12,13},{... | collective-permute-start | bytes 73736 | tf_op jit(solution)/shard_map/ppermute | solution.py:28
  15.3 4.8 %fusion.41 = (f32[4,8,48,511]{3,0,1,2:T(4,128)}, f32[4,8,48,511]{3,0,1,2:T(4,128)}) fusion(f32[4,8,48,512]{3,0,1,2:T(4,128)S(1)} %copy.21), kind=kLoop, calls=%fused_computation.65 | loop fusion | bytes 12558336 | tf_op jit(solution)/shard_map/jit(_roll_static)/slice | solution.py:117
  20.2 1.7 %fusion.40 = (f32[4,8,48,1]{3,0,1,2:T(4,128)}, f32[4,8,48,1]{3,0,1,2:T(4,128)}) fusion(f32[4,8,48,512]{3,0,1,2:T(4,128)S(1)} %copy.21), kind=kLoop, calls=%fused_computation.64 | loop fusion | bytes 24576 | tf_op jit(solution)/shard_map/jit(_roll_static)/slice | solution.py:117
  21.9 18.7 %all_gather.15 = f32[8,48,512]{2,1,0:T(8,128)S(1)} all-gather(f32[8,48,128]{2,1,0:T(8,128)S(1)} %copy-done.18), channel_id=1, replica_groups=mesh['inv'=2,'tracer'=4,'band'=4] {'tracer'}, dimensions={2}, use_global_device_ids=true | all-gather | bytes 983040 | tf_op jit(solution)/shard_map/all_gather | solution.py:103
  40.7 1.4 broadcast_maximum_fusion.1
  42.1 16.4 %all_gather.16 = f32[8,48,512]{2,1,0:T(8,128)} all-gather(f32[8,48,128]{2,1,0:T(8,128)S(1)} %copy-done.17), channel_id=1, replica_groups=mesh['inv'=2,'tracer'=4,'band'=4] {'tracer'}, dimensions={2}, use_global_device_ids=true | all-gather | bytes 983040 | tf_op jit(solution)/shard_map/all_gather | solution.py:104
  58.5 15.9 %all_gather.18 = f32[8,48,512]{2,1,0:T(8,128)S(1)} all-gather(f32[8,48,128]{2,1,0:T(8,128)S(1)} %copy-done.19), channel_id=1, replica_groups=mesh['inv'=2,'tracer'=4,'band'=4] {'tracer'}, dimensions={2}, use_global_device_ids=true | all-gather | bytes 983040 | tf_op jit(solution)/shard_map/all_gather | solution.py:105
  74.5 1.3 copy.32
  75.8 2.5 %broadcast_maximum_fusion = (f32[8,48,512]{2,1,0:T(8,128)}, f32[8,48,512]{2,1,0:T(8,128)}) fusion(f32[8,48,512]{2,1,0:T(8,128)} %all_gather.16), kind=kLoop, calls=%fused_computation.45 | loop fusion | flops 393216 | bytes 2359296 | tf_op jit(solution)/shard_map/max | solution.py:51
  78.3 0.7 constant_dynamic-slice_fusion
  79.3 10.5 %all_gather.19 = f32[4,32,512]{2,1,0:T(8,128)S(1)} all-gather(f32[4,8,512]{2,1,0:T(8,128)S(1)} %copy-done.20), channel_id=1, replica_groups=mesh['inv'=2,'tracer'=4,'band'=4] {'band'}, dimensions={1}, use_global_device_ids=true | all-gather | bytes 327680 | tf_op jit(solution)/shard_map/all_gather | solution.py:90
  90.0 6.1 %multiply_multiply_fusion.1 = f32[4,8,48,512]{3,0,1,2:T(4,128)S(1)} fusion(f32[4,8,47,512]{3,0,1,2:T(4,128)S(1)} %slice-done, f32[48]{0:T(128)S(1)} %compare_convert_fusion, f32[8,48,512]{2,0,1:T(8,128)} %copy.32, f32[4,8,48,512]{3,2,1,0:T(8,128)} %param.13), kind=kLoop, calls=%fused_computation.33 | loop fusion | flops 2359296 | bytes 10158272 | tf_op jit(solution)/shard_map/mul | solution.py:37
  96.5 1.3 copy-done.4
  100.7 10.5 %all_gather.17 = f32[1,48,512]{2,1,0:T(8,128)S(1)} all-gather(f32[1,48,128]{2,1,0:T(8,128)S(1)} %collective-permute-done.1), channel_id=1, replica_groups=mesh['inv'=2,'tracer'=4,'band'=4] {'tracer'}, dimensions={2}, use_global_device_ids=true | all-gather | bytes 122880 | tf_op jit(solution)/shard_map/all_gather | solution.py:106
  111.4 0.5 copy.27
  112.5 10.2 %fusion.12 = f32[4,8,48,512]{3,0,1,2:T(4,128)S(1)} fusion(f32[4,8,48,512]{3,0,1,2:T(4,128)S(1)} %copy-done.3, f32[4,1,48,512]{3,0,1,2:T(4,128)} %collective-permute-done.2, f32[4,1,48,512]{3,0,1,2:T(4,128)} %collective-permute-done, f32[4,8,48,1]{3,0,1,2:T(4,128)S(1)} %copy-done.12, f32[4,8,48,511]{3,0,1,2:T(4,128)S(1)} %copy-done.7, ...), kind=kLoop, calls=%fused_computation.15 | loop fusion | flops 18087936 | bytes 25886752 | tf_op jit(solution)/shard_map/sub | solution.py:58
  123.0 0.5 slice.180
  123.6 0.5 fusion.37
  124.2 0.5 copy-done.10
  124.7 1.5 %multiply_multiply_fusion = f32[4,8,48,512]{3,0,1,2:T(4,128)S(1)} fusion(f32[4,8,48,512]{3,0,1,2:T(4,128)S(1)} %get-tuple-element.48, f32[4,8,47,512]{3,0,1,2:T(4,128)S(1)} %slice.180, f32[48]{0:T(128)S(1)} %compare_convert_fusion, f32[8,48,512]{2,0,1:T(8,128)S(1)} %copy-done.10), kind=kLoop, calls=%fused_computation.32 | loop fusion | flops 2359296 | bytes 10158272 | tf_op jit(solution)/shard_map/mul | solution.py:37
  126.2 0.9 slice.181
  127.2 5.0 %collective-permute-start.3 = (f32[4,1,48,512]{3,0,1,2:T(4,128)S(1)}, f32[4,1,48,512]{3,0,1,2:T(4,128)S(1)}, u32[]{:S(2)}, u32[]{:S(2)}) collective-permute-start(f32[4,1,48,512]{3,0,1,2:T(4,128)S(1)} %get-tuple-element.32), channel_id=1, source_target_pairs={{1,0},{2,1},{3,2},{5,4},{6,5},{7,6},{9,8},{10,9},{11,10},{13,12},{... | collective-permute-start | bytes 1179656 | tf_op jit(solution)/shard_map/ppermute | solution.py:20
  132.1 2.2 %collective-permute-start.4 = (f32[4,1,48,512]{3,0,1,2:T(4,128)S(1)}, f32[4,1,48,512]{3,0,1,2:T(4,128)S(1)}, u32[]{:S(2)}, u32[]{:S(2)}) collective-permute-start(f32[4,1,48,512]{3,0,1,2:T(4,128)S(1)} %get-tuple-element.33), channel_id=1, source_target_pairs={{0,1},{1,2},{2,3},{4,5},{5,6},{6,7},{8,9},{9,10},{10,11},{12,13},{... | collective-permute-start | bytes 1179656 | tf_op jit(solution)/shard_map/ppermute | solution.py:17
  134.4 0.7 copy.38
  135.0 2.5 %fusion.38 = (f32[4,8,48,511]{3,0,1,2:T(4,128)S(1)}, f32[4,8,48,511]{3,0,1,2:T(4,128)S(1)}) fusion(f32[4,8,48,512]{3,0,1,2:T(4,128)S(1)} %get-tuple-element.48), kind=kLoop, calls=%fused_computation.62 | loop fusion | bytes 12558336 | tf_op jit(solution)/shard_map/jit(_roll_static)/slice | solution.py:117
  137.7 1.2 collective-permute-done.4
  138.9 9.1 %fusion.4 = f32[4,8,48,512]{3,0,1,2:T(4,128)S(1)} fusion(f32[4,8,48,512]{3,0,1,2:T(4,128)S(1)} %get-tuple-element.48, f32[4,1,48,512]{3,0,1,2:T(4,128)S(1)} %collective-permute-done.4, f32[4,1,48,512]{3,0,1,2:T(4,128)S(1)} %collective-permute-done.3, f32[4,8,48,1]{3,0,1,2:T(4,128)S(1)} %get-tuple-element.29, f32[4,8,48,511]{3,0,1,2:T(4,128)S(1)} %get-tuple-element.31, ...), kind=kLoop, calls=%fused_computation.5 | loop fusion | flops 18087936 | bytes 25886752 | tf_op jit(solution)/shard_map/sub | solution.py:58
  148.0 3.5 %copy.37 = f32[4,8,48,512]{3,2,1,0:T(8,128)} copy(f32[4,8,48,512]{3,0,1,2:T(4,128)S(1)} %fusion.30) | data formatting | bytes 6291456
  (73 shorter events, 5.0 us)
Async XLA Ops:
  0.6 78.4 %copy-start = (f32[8,8,8]{2,1,0:T(8,128)S(1)}, f32[8,8,8]{2,1,0:T(8,128)}, u32[]{:S(2)}) copy-start(f32[8,8,8]{2,1,0:T(8,128)} %param.15) | copy-start | bytes 6148
  0.6 11.5 %copy-start.17 = (f32[8,48,128]{2,1,0:T(8,128)S(1)}, f32[8,48,128]{2,1,0:T(8,128)}, u32[]{:S(2)}) copy-start(f32[8,48,128]{2,1,0:T(8,128)} %param.20) | copy-start | bytes 589828
  4.6 15.6 %copy-start.2 = (f32[4,8,48,512]{3,0,1,2:T(4,128)}, f32[4,8,48,512]{3,0,1,2:T(4,128)S(1)}, u32[]{:S(2)}) copy-start(f32[4,8,48,512]{3,0,1,2:T(4,128)S(1)} %copy.21) | copy-start | bytes 9437188
  5.7 106.7 %collective-permute-start = (f32[4,1,48,512]{3,0,1,2:T(4,128)}, f32[4,1,48,512]{3,0,1,2:T(4,128)}, u32[]{:S(2)}, u32[]{:S(2)}) collective-permute-start(f32[4,1,48,512]{3,0,1,2:T(4,128)} %get-tuple-element.38), channel_id=1, source_target_pairs={{1,0},{2,1},{3,2},{5,4},{6,5},{7,6},{9,8},{10,9},{11,10},{13,12},{... | collective-permute-start | bytes 1179656 | tf_op jit(solution)/shard_map/ppermute | solution.py:20
  7.7 104.7 %collective-permute-start.2 = (f32[4,1,48,512]{3,0,1,2:T(4,128)}, f32[4,1,48,512]{3,0,1,2:T(4,128)}, u32[]{:S(2)}, u32[]{:S(2)}) collective-permute-start(f32[4,1,48,512]{3,0,1,2:T(4,128)} %get-tuple-element.39), channel_id=1, source_target_pairs={{0,1},{1,2},{2,3},{4,5},{5,6},{6,7},{8,9},{9,10},{10,11},{12,13},{... | collective-permute-start | bytes 1179656 | tf_op jit(solution)/shard_map/ppermute | solution.py:17
  12.2 88.5 %collective-permute-start.1 = (f32[1,48,128]{2,1,0:T(8,128)S(1)}, f32[1,48,128]{2,1,0:T(8,128)S(1)}, u32[]{:S(2)}, u32[]{:S(2)}) collective-permute-start(f32[1,48,128]{2,1,0:T(8,128)S(1)} %slice.144), channel_id=1, source_target_pairs={{0,1},{1,2},{2,3},{4,5},{5,6},{6,7},{8,9},{9,10},{10,11},{12,13},{... | collective-permute-start | bytes 73736 | tf_op jit(solution)/shard_map/ppermute | solution.py:28
  20.2 1.7 %copy-start.18 = (f32[8,48,128]{2,1,0:T(8,128)S(1)}, f32[8,48,128]{2,1,0:T(8,128)}, u32[]{:S(2)}) copy-start(f32[8,48,128]{2,1,0:T(8,128)} %param.19) | copy-start | bytes 589828
  21.9 36.6 %copy-start.19 = (f32[8,48,128]{2,1,0:T(8,128)S(1)}, f32[8,48,128]{2,1,0:T(8,128)}, u32[]{:S(2)}) copy-start(f32[8,48,128]{2,1,0:T(8,128)} %param.21) | copy-start | bytes 589828
  40.6 1.5 copy-start.8
  42.1 37.2 %copy-start.20 = (f32[4,8,512]{2,1,0:T(8,128)S(1)}, f32[4,8,512]{2,1,0:T(8,128)}, u32[]{:S(2)}) copy-start(f32[4,8,512]{2,1,0:T(8,128)} %param.14) | copy-start | bytes 196612
  42.1 47.9 %slice-start = ((f32[4,8,48,512]{3,0,1,2:T(4,128)}), f32[4,8,47,512]{3,0,1,2:T(4,128)S(1)}, s32[]{:S(2)}) async-start(f32[4,8,48,512]{3,0,1,2:T(4,128)} %copy-done.2), calls=%async_computation | async-start | bytes 6160384 | tf_op jit(solution)/shard_map/slice | solution.py:34
  90.0 6.1 %copy-start.9 = (f32[8,48,512]{2,1,0:T(8,128)S(1)}, f32[8,48,512]{2,1,0:T(8,128)}, u32[]{:S(2)}) copy-start(f32[8,48,512]{2,1,0:T(8,128)} %copy-done.8) | copy-start | bytes 2359300
  96.1 1.7 %copy-start.4 = (f32[4,8,48,512]{3,0,1,2:T(4,128)}, f32[4,8,48,512]{3,0,1,2:T(4,128)S(1)}, u32[]{:S(2)}) copy-start(f32[4,8,48,512]{3,0,1,2:T(4,128)S(1)} %multiply_multiply_fusion.1) | copy-start | bytes 9437188
  96.5 2.3 %copy-start.14 = (f32[8,48,512]{2,1,0:T(8,128)S(1)}, f32[8,48,512]{2,1,0:T(8,128)}, u32[]{:S(2)}) copy-start(f32[8,48,512]{2,1,0:T(8,128)} %get-tuple-element.42) | copy-start | bytes 2359300
  96.5 2.8 %copy-start.13 = (f32[8,48,512]{2,1,0:T(8,128)S(1)}, f32[8,48,512]{2,1,0:T(8,128)}, u32[]{:S(2)}) copy-start(f32[8,48,512]{2,1,0:T(8,128)} %get-tuple-element.43) | copy-start | bytes 2359300
  96.5 3.2 %copy-start.16 = (f32[8,48,512]{2,1,0:T(8,128)S(1)}, f32[8,48,512]{2,1,0:T(8,128)}, u32[]{:S(2)}) copy-start(f32[8,48,512]{2,1,0:T(8,128)} %get-tuple-element.44) | copy-start | bytes 2359300
  96.5 3.7 %copy-start.15 = (f32[8,48,512]{2,1,0:T(8,128)S(1)}, f32[8,48,512]{2,1,0:T(8,128)}, u32[]{:S(2)}) copy-start(f32[8,48,512]{2,1,0:T(8,128)} %get-tuple-element.45) | copy-start | bytes 2359300
  96.5 15.9 %copy-start.7 = (f32[4,8,48,511]{3,0,1,2:T(4,128)S(1)}, f32[4,8,48,511]{3,0,1,2:T(4,128)}, u32[]{:S(2)}) copy-start(f32[4,8,48,511]{3,0,1,2:T(4,128)} %get-tuple-element.37) | copy-start | bytes 9418756
  97.8 14.6 %copy-start.11 = (f32[4,8,48,1]{3,0,1,2:T(4,128)S(1)}, f32[4,8,48,1]{3,0,1,2:T(4,128)}, u32[]{:S(2)}) copy-start(f32[4,8,48,1]{3,0,1,2:T(4,128)} %get-tuple-element.34) | copy-start | bytes 18436
  97.8 14.6 %copy-start.12 = (f32[4,8,48,1]{3,0,1,2:T(4,128)S(1)}, f32[4,8,48,1]{3,0,1,2:T(4,128)}, u32[]{:S(2)}) copy-start(f32[4,8,48,1]{3,0,1,2:T(4,128)} %get-tuple-element.35) | copy-start | bytes 18436
  98.3 14.1 %copy-start.6 = (f32[4,8,48,511]{3,0,1,2:T(4,128)S(1)}, f32[4,8,48,511]{3,0,1,2:T(4,128)}, u32[]{:S(2)}) copy-start(f32[4,8,48,511]{3,0,1,2:T(4,128)} %get-tuple-element.36) | copy-start | bytes 9418756
  98.8 12.4 %slice-start.2 = ((f32[8,48,512]{2,1,0:T(8,128)}), f32[7,48,512]{2,1,0:T(8,128)S(1)}, s32[]{:S(2)}) async-start(f32[8,48,512]{2,1,0:T(8,128)} %all_gather.16), calls=%async_computation.2 | async-start | bytes 1376256 | tf_op jit(solution)/shard_map/slice | solution.py:112
  99.3 13.2 %copy-start.5 = (f32[4,8,48,512]{3,0,1,2:T(4,128)S(1)}, f32[4,8,48,512]{3,0,1,2:T(4,128)}, u32[]{:S(2)}) copy-start(f32[4,8,48,512]{3,0,1,2:T(4,128)} %copy-done.4) | copy-start | bytes 9437188
  100.2 12.2 %slice-start.1 = ((f32[4,8,48,512]{3,0,1,2:T(4,128)}), f32[4,8,47,512]{3,0,1,2:T(4,128)S(1)}, s32[]{:S(2)}) async-start(f32[4,8,48,512]{3,0,1,2:T(4,128)} %copy-done.4), calls=%async_computation.1 | async-start | bytes 6160384 | tf_op jit(solution)/shard_map/slice | solution.py:38
  100.7 11.7 %copy-start.3 = (f32[4,8,48,512]{3,0,1,2:T(4,128)S(1)}, f32[4,8,48,512]{3,0,1,2:T(4,128)}, u32[]{:S(2)}) copy-start(f32[4,8,48,512]{3,0,1,2:T(4,128)} %copy-done.2) | copy-start | bytes 9437188
  112.5 10.3 %copy-start.21 = (s32[8,512]{1,0:T(8,128)S(1)}, s32[8,512]{1,0:T(8,128)}, u32[]{:S(2)}) copy-start(s32[8,512]{1,0:T(8,128)} %param.17) | copy-start | bytes 49156
  112.5 10.3 %copy-start.22 = (f32[4,22]{1,0:T(4,128)S(1)}, f32[4,22]{1,0:T(4,128)}, u32[]{:S(2)}) copy-start(f32[4,22]{1,0:T(4,128)} %param.18) | copy-start | bytes 1060
  123.6 1.1 copy-start.10
  127.2 10.5 %collective-permute-start.3 = (f32[4,1,48,512]{3,0,1,2:T(4,128)S(1)}, f32[4,1,48,512]{3,0,1,2:T(4,128)S(1)}, u32[]{:S(2)}, u32[]{:S(2)}) collective-permute-start(f32[4,1,48,512]{3,0,1,2:T(4,128)S(1)} %get-tuple-element.32), channel_id=1, source_target_pairs={{1,0},{2,1},{3,2},{5,4},{6,5},{7,6},{9,8},{10,9},{11,10},{13,12},{... | collective-permute-start | bytes 1179656 | tf_op jit(solution)/shard_map/ppermute | solution.py:20
  132.1 6.7 %collective-permute-start.4 = (f32[4,1,48,512]{3,0,1,2:T(4,128)S(1)}, f32[4,1,48,512]{3,0,1,2:T(4,128)S(1)}, u32[]{:S(2)}, u32[]{:S(2)}) collective-permute-start(f32[4,1,48,512]{3,0,1,2:T(4,128)S(1)} %get-tuple-element.33), channel_id=1, source_target_pairs={{0,1},{1,2},{2,3},{4,5},{5,6},{6,7},{8,9},{9,10},{10,11},{12,13},{... | collective-permute-start | bytes 1179656 | tf_op jit(solution)/shard_map/ppermute | solution.py:17
  148.0 3.5 %copy-start.1 = (f32[8,8,8]{2,1,0:T(8,128)S(1)}, f32[8,8,8]{2,1,0:T(8,128)}, u32[]{:S(2)}) copy-start(f32[8,8,8]{2,1,0:T(8,128)} %param.15) | copy-start | bytes 6148
where the time goes:
time: 152 us
  blocking collectives  72.1 us (47%)
  other arithmetic  31.4 us (21%)
  local copies, waits for them, and re-layouts  28.1 us (18%)
  starting transfers between devices  16.8 us (11%)
    sub x2, other arithmetic, advance(): tracer_now - (flux_east - flux_west) - (flux_north - flux_south)  19.4 us
    all_gather x1, blocking collectives, on_device(): lax.all_gather(zonal_courant, 'tracer', axis=2, tiled=True)  18.7 us
    all_gather x1, blocking collectives, on_device(): lax.all_gather(meridional_courant, 'tracer', axis=2, tiled=True)  16.4 us
    all_gather x1, blocking collectives, on_device(): lax.all_gather(vertical_diffusion, 'tracer', axis=2, tiled=True)  15.9 us
    all_gather x1, blocking collectives, on_device(): lax.all_gather(control, 'band', axis=1, tiled=True)  10.5 us
    all_gather x1, blocking collectives, on_device(): lax.all_gather(south_row, 'tracer', axis=2, tiled=True)  10.5 us
    unnamed x49, local copies, waits for them, and re-layouts  9.99 us
    slice x4, local copies, waits for them, and re-layouts, sideways(): return (jnp.roll(tracer_now, 1, axis=3), jnp.roll(tracer_now, -1, axis=3))  9.62 us
  transfers between devices with their start and end apart: 5, of which 2 were waited for; matrix products, arithmetic and copies ran while one was open for 18% of the time, Pallas kernels for 0%

commit v1 on v0

v1 whole, which is shorter than its diff:
```python
import functools

import jax
import jax.numpy as jnp
from jax import lax
from jax.experimental import pallas as pl
from jax.experimental.pallas import tpu as pltpu
from jax.sharding import PartitionSpec as P

STEPS = 2

exact_dot = lax.Precision.HIGHEST


def passed_along(value, axis, by):
    count = lax.axis_size(axis)
    pairs = [(i, i + by) for i in range(count) if 0 <= i + by < count]
    return lax.ppermute(value, axis, pairs)


def step_kernel(north_ref, q_ref, qs_ref, qn_ref, u_ref, v_ref, vs_ref, w_ref, src_ref, o_ref):
    lat_rows = q_ref.shape[1]
    levels, lon = q_ref.shape[2], q_ref.shape[3]
    level = lax.broadcasted_iota(jnp.int32, (levels, lon), 0)
    not_top = level < levels - 1
    not_bottom = level > 0
    bottom = level == 0
    for a in range(lat_rows):
        qa = q_ref[0, a]
        qm = qs_ref[0] if a == 0 else q_ref[0, a - 1]
        qp = qn_ref[0] if a == lat_rows - 1 else q_ref[0, a + 1]
        u = u_ref[a]
        v = v_ref[a]
        vm = vs_ref[...] if a == 0 else v_ref[a - 1]
        w = w_ref[a]
        east = pltpu.roll(qa, lon - 1, 1)
        west = pltpu.roll(qa, 1, 1)
        uw = pltpu.roll(u, 1, 1)
        flux_east = jnp.maximum(u, 0.0) * qa + jnp.minimum(u, 0.0) * east
        flux_west = jnp.maximum(uw, 0.0) * west + jnp.minimum(uw, 0.0) * qa
        flux_north = (jnp.maximum(v, 0.0) * qa + jnp.minimum(v, 0.0) * qp) * north_ref[a]
        flux_south = jnp.maximum(vm, 0.0) * qm + jnp.minimum(vm, 0.0) * qa
        upper = jnp.where(not_top, pltpu.roll(qa, levels - 1, 0), 0.0)
        flux_up = jnp.where(not_top, w * (qa - upper), 0.0)
        flux_down = jnp.where(not_bottom, pltpu.roll(flux_up, 1, 0), 0.0)
        result = qa - (flux_east - flux_west) - (flux_north - flux_south) - (flux_up - flux_down)
        source = jnp.broadcast_to(src_ref[0, a : a + 1, :], (levels, lon))
        o_ref[0, a] = result + jnp.where(bottom, source, 0.0)


def advance(state, south, north, zonal, merid, merid_south, mixing, emission, north_open):
    tracers, lat_rows, levels, lon = state.shape
    row = pl.BlockSpec((1, lat_rows, levels, lon), lambda k: (k, 0, 0, 0))
    edge = pl.BlockSpec((1, levels, lon), lambda k: (k, 0, 0))
    weather = pl.BlockSpec((lat_rows, levels, lon), lambda k: (0, 0, 0))
    return pl.pallas_call(
        step_kernel,
        grid=(tracers,),
        in_specs=[
            pl.BlockSpec(memory_space=pltpu.SMEM),
            row,
            edge,
            edge,
            weather,
            weather,
            pl.BlockSpec((levels, lon), lambda k: (0, 0)),
            weather,
            pl.BlockSpec((1, lat_rows, lon), lambda k: (k, 0, 0)),
        ],
        out_specs=row,
        out_shape=jax.ShapeDtypeStruct(state.shape, state.dtype),
    )(north_open, state, south, north, zonal, merid, merid_south, mixing, emission)


def on_device(
    tracer_state,
    control,
    prior_tiles,
    tile_index,
    region_map,
    region_sigma,
    zonal_courant,
    meridional_courant,
    vertical_diffusion,
):
    band_count = lax.axis_size("band")
    band_index = lax.axis_index("band")
    tiles_count = prior_tiles.shape[0]
    lat_rows = control.shape[1]

    south_v = passed_along(meridional_courant[-1:], "band", 1)
    q_south = passed_along(tracer_state[:, -1], "band", 1)
    q_north = passed_along(tracer_state[:, 0], "band", -1)
    shifted = [control]
    for s in range(1, band_count):
        pairs = [(i, (i + s) % band_count) for i in range(band_count)]
        shifted.append(lax.ppermute(control, "band", pairs))

    pack = jnp.concatenate([zonal_courant, meridional_courant, vertical_diffusion, south_v], axis=0)
    weather = lax.all_gather(pack, "tracer", axis=2, tiled=True)
    zonal = weather[:lat_rows]
    merid = weather[lat_rows : 2 * lat_rows]
    mixing = weather[2 * lat_rows : 3 * lat_rows]
    merid_south = weather[3 * lat_rows]

    choose = (
        tile_index[:, :, None] == lax.broadcasted_iota(jnp.int32, (1, 1, tiles_count), 2)
    ).astype(jnp.float32)
    own_row = lax.dynamic_slice_in_dim(choose, band_index, 1, 0)[0]
    row_tiles = jnp.einsum("bt,tmn->bmn", own_row, prior_tiles, precision=exact_dot)
    prior_field = None
    for s, part in enumerate(shifted):
        source_band = (band_index - s) % band_count
        tile = lax.dynamic_index_in_dim(row_tiles, source_band, 0, keepdims=False)
        term = jnp.einsum("jm,kmn->kjn", tile, part, precision=exact_dot)
        prior_field = term if prior_field is None else prior_field + term
    regions = region_sigma.shape[1]
    onehot = (region_map[:, :, None] == lax.broadcasted_iota(jnp.int32, (1, 1, regions), 2)).astype(
        jnp.float32
    )
    cell_sigma = jnp.einsum("kr,jnr->kjn", region_sigma, onehot, precision=exact_dot)
    emission = cell_sigma * prior_field

    latitude = band_index * lat_rows + jnp.arange(lat_rows, dtype=jnp.int32)
    north_open = (latitude < band_count * lat_rows - 1).astype(jnp.float32)

    tracer_field = tracer_state
    south, north = q_south, q_north
    for substep in range(STEPS):
        if substep > 0:
            south = passed_along(tracer_field[:, -1], "band", 1)
            north = passed_along(tracer_field[:, 0], "band", -1)
        tracer_field = advance(
            tracer_field, south, north, zonal, merid, merid_south, mixing, emission, north_open
        )
    return (tracer_field, emission)


def solution(mesh):
    in_specs = (
        P(("inv", "tracer"), "band", None, None),
        P(("inv", "tracer"), "band", None),
        P(),
        P(),
        P("band", None),
        P("tracer", None),
        P(("inv", "band"), None, "tracer"),
        P(("inv", "band"), None, "tracer"),
        P(("inv", "band"), None, "tracer"),
    )
    out_specs = (P(("inv", "tracer"), "band", None, None), P(("inv", "tracer"), "band", None))
    return jax.shard_map(
        on_device, mesh=mesh, in_specs=in_specs, out_specs=out_specs, check_vma=False
    )
```

time: 152 us -> 110 us (0.72)
  blocking collectives: 72.1 us -> 0 us
  waiting for transfers between devices: 1.29 us -> 46.7 us
  other arithmetic: 31.4 us -> 2.56 us
  local copies, waits for them, and re-layouts: 28.1 us -> 10.1 us
  Pallas kernels: 0 us -> 15.3 us
  between operations: 1.17 us -> 14.3 us
  starting transfers between devices: 16.8 us -> 18.7 us
    all_gather x5 -> x0, blocking collectives: 72.1 us -> none  [the longest x1 18.7 us: on_device(): lax.all_gather(zonal_courant, 'tracer', axis=2, tiled=True)]
    all_gather x0 -> x1, waiting for transfers between devices: none -> 41 us  [on_device(): weather = lax.all_gather(pack, 'tracer', axis=2, tiled=True)]
    sub x2 -> x0, other arithmetic: 19.4 us -> none  [advance(): tracer_now - (flux_east - flux_west) - (flux_north - flux_south)]
    pallas_call x0 -> x2, Pallas kernels: none -> 15.3 us  [advance(): pl.pallas_call(step_kernel, grid=(tracers,), in_specs=[pl.BlockSpec(memor...]
    ppermute x1 -> x5, starting transfers between devices: 3.15 us -> 16.1 us  [passed_along(): return lax.ppermute(value, axis, pairs)]
    ppermute x4 -> x3, starting transfers between devices: 13.6 us -> 2.54 us  [on_device(): shifted.append(lax.ppermute(control, 'band', pairs))]
    slice x16 -> x2, local copies, waits for them, and re-layouts: 12.4 us -> 3.86 us  [the longest x1 3.12 us: on_device(): mixing = weather[2 * lat_rows:3 * lat_rows]]
    unnamed x49 -> x16, local copies, waits for them, and re-layouts: 9.99 us -> 1.64 us
  transfers between devices with their start and end apart: 5 -> 9, of which waited for: 2 -> 4; matrix products, arithmetic and copies ran while one was open for 18% -> 8% of each run, Pallas kernels for 0% -> 0%
where the time goes in v1:
time: 110 us; the launch traced here: 109 us
  waiting for transfers between devices  46.7 us (42%)
  starting transfers between devices  18.7 us (17%)
  Pallas kernels  15.3 us (14%)
  between operations  14.3 us (13%)
  local copies, waits for them, and re-layouts  10.1 us (9%)
  other arithmetic  2.56 us (2%)
  matrix products  1.85 us (2%)
    all_gather x1, waiting for transfers between devices, on_device(): weather = lax.all_gather(pack, 'tracer', axis=2, tiled=True)  41 us
    ppermute x5, starting transfers between devices, passed_along(): return lax.ppermute(value, axis, pairs)  16.1 us
    pallas_call x2, Pallas kernels, advance(): pl.pallas_call(step_kernel, grid=(tracers,), in_specs=[pl.BlockSpec(memor...  15.3 us
    ppermute x5, waiting for transfers between devices, passed_along(): return lax.ppermute(value, axis, pairs)  5.63 us
    slice x1, local copies, waits for them, and re-layouts, on_device(): mixing = weather[2 * lat_rows:3 * lat_rows]  3.12 us
    ppermute x3, starting transfers between devices, on_device(): shifted.append(lax.ppermute(control, 'band', pairs))  2.54 us
  transfers between devices with their start and end apart: 9, of which 4 were waited for; matrix products, arithmetic and copies ran while one was open for 8% of the time, Pallas kernels for 0%

profile of v1, /device:TPU:1, one launch (start us, length us, event | category | flops | bytes accessed | tf_op | source)
XLA Modules:
  0.0 109.5 jit_solution(13985903292132523101)
XLA Ops:
  7.2 0.0 all-gather.2.cloned.1.call-start
  7.3 0.7 slice.29
  8.0 4.5 %collective-permute-start.2 = (f32[1,48,128]{2,1,0:T(8,128)S(1)}, f32[1,48,128]{2,1,0:T(8,128)S(1)}, u32[]{:S(2)}, u32[]{:S(2)}) collective-permute-start(f32[1,48,128]{2,1,0:T(8,128)S(1)} %slice.29), channel_id=1, source_target_pairs={{0,1},{1,2},{2,3},{4,5},{5,6},{6,7},{8,9},{9,10},{10,11},{12,13},{... | collective-permute-start | bytes 73736 | tf_op jit(solution)/shard_map/ppermute | solution.py:18
  12.5 0.9 collective-permute-done.2
  13.4 2.0 %pad_maximum_fusion = f32[25,48,128]{2,1,0:T(8,128)} fusion(f32[1,48,128]{2,1,0:T(8,128)S(1)} %collective-permute-done.2, f32[8,48,128]{2,1,0:T(8,128)} %param.17, f32[8,48,128]{2,1,0:T(8,128)} %param.16, f32[8,48,128]{2,1,0:T(8,128)} %param.15), kind=kLoop, calls=%fused_computation.5 | loop fusion | flops 460800 | bytes 1228800 | tf_op jit(solution)/shard_map/concatenate | solution.py:99
  15.4 0.0 all-gather.2.cloned.1.call-update
  15.4 2.4 %collective-permute-start.3 = (f32[4,8,512]{2,1,0:T(8,128)}, f32[4,8,512]{2,1,0:T(8,128)S(1)}, u32[]{:S(2)}, u32[]{:S(2)}) collective-permute-start(f32[4,8,512]{2,1,0:T(8,128)} %param.10), channel_id=1, source_target_pairs={{0,1},{1,2},{2,3},{3,0},{4,5},{5,6},{6,7},{7,4},{8,9},{9,10},{10,1... | collective-permute-start | bytes 196616 | tf_op jit(solution)/shard_map/ppermute | solution.py:97
  17.8 0.2 collective-permute-start.4
  18.0 1.2 %slice_bitcast_fusion.2 = (f32[4,48,512]{2,1,0:T(8,128)S(1)}, f32[4,48,512]{2,1,0:T(8,128)S(1)}) fusion(f32[4,8,48,512]{3,2,1,0:T(8,128)} %q_ref.1), kind=kLoop, calls=%fused_computation.9 | loop fusion | bytes 1572864 | tf_op jit(solution)/shard_map/squeeze | solution.py:93
  19.2 3.9 %collective-permute-start.1 = (f32[4,48,512]{2,1,0:T(8,128)S(1)}, f32[4,48,512]{2,1,0:T(8,128)S(1)}, u32[]{:S(2)}, u32[]{:S(2)}) collective-permute-start(f32[4,48,512]{2,1,0:T(8,128)S(1)} %get-tuple-element.4), channel_id=1, source_target_pairs={{1,0},{2,1},{3,2},{5,4},{6,5},{7,6},{9,8},{10,9},{11,10},{13,12},{... | collective-permute-start | bytes 1179656 | tf_op jit(solution)/shard_map/ppermute | solution.py:18
  23.0 1.9 %collective-permute-start = (f32[4,48,512]{2,1,0:T(8,128)S(1)}, f32[4,48,512]{2,1,0:T(8,128)S(1)}, u32[]{:S(2)}, u32[]{:S(2)}) collective-permute-start(f32[4,48,512]{2,1,0:T(8,128)S(1)} %get-tuple-element.5), channel_id=1, source_target_pairs={{0,1},{1,2},{2,3},{4,5},{5,6},{6,7},{8,9},{9,10},{10,11},{12,13},{... | collective-permute-start | bytes 1179656 | tf_op jit(solution)/shard_map/ppermute | solution.py:18
  25.1 0.7 constant_dynamic-slice_fusion.4
  25.8 0.2 fusion.5
  26.0 0.3 fusion.3
  26.3 0.2 fusion.12
  26.5 0.6 compare_convert_fusion.north_ref
  27.1 0.2 convolution_add_fusion.1
  27.3 0.2 fusion.13
  27.5 0.8 fusion.2.src_ref
  28.3 41.0 %all-gather.2.cloned.1.call-done = f32[25,48,512]{2,1,0:T(8,128)} async-done(((f32[25,48,128]{2,1,0:T(8,128)}), f32[25,48,512]{2,1,0:T(8,128)}) %all-gather.2.cloned.1.call-update) | async-done | bytes 2457616 | tf_op jit(solution)/shard_map/all_gather | solution.py:100
  69.3 1.5 %slice_bitcast_fusion.4.vs_ref = f32[48,512]{1,0:T(8,128)} fusion(f32[25,48,512]{2,1,0:T(8,128)} %all-gather.2.cloned.1.call-done), kind=kLoop, calls=%fused_computation.13 | loop fusion | bytes 196608 | tf_op jit(solution)/shard_map/squeeze | solution.py:104
  70.9 3.1 %fusion.11 = (f32[8,48,512]{2,1,0:T(8,128)}, f32[8,48,512]{2,1,0:T(8,128)}, f32[8,48,512]{2,1,0:T(8,128)}) fusion(f32[25,48,512]{2,1,0:T(8,128)} %all-gather.2.cloned.1.call-done), kind=kLoop, calls=%fused_computation.26 | loop fusion | bytes 4718592 | tf_op jit(solution)/shard_map/slice | solution.py:103
  74.0 0.7 copy-done.1
  74.8 0.1 copy-done.2
  74.9 7.7 %shard_map.104.q_ref = f32[4,8,48,512]{3,2,1,0:T(8,128)} custom-call(f32[8]{0:T(128)} %compare_convert_fusion.north_ref, f32[4,8,48,512]{3,2,1,0:T(8,128)} %q_ref.1, f32[4,48,512]{2,1,0:T(8,128)} %copy-done.2, f32[4,48,512]{2,1,0:T(8,128)} %copy-done.1, f32[8,48,512]{2,1,0:T(8,128)} %get-tuple-element.8.u_ref, f32[8,48,512]{2,1,0:T(8,128)} %get-tuple-element.7.v_ref, ...), custom_call_target="tpu_custom_call" | custom-call | tf_op jit(solution)/shard_map/pallas_call | solution.py:56
  82.5 1.2 %slice_bitcast_fusion = (f32[4,48,512]{2,1,0:T(8,128)S(1)}, f32[4,48,512]{2,1,0:T(8,128)S(1)}) fusion(f32[4,8,48,512]{3,2,1,0:T(8,128)} %shard_map.104.q_ref), kind=kLoop, calls=%fused_computation.6 | loop fusion | bytes 1572864 | tf_op jit(solution)/shard_map/squeeze | solution.py:132
  83.7 2.8 %collective-permute-start.7 = (f32[4,48,512]{2,1,0:T(8,128)S(1)}, f32[4,48,512]{2,1,0:T(8,128)S(1)}, u32[]{:S(2)}, u32[]{:S(2)}) collective-permute-start(f32[4,48,512]{2,1,0:T(8,128)S(1)} %get-tuple-element.2), channel_id=1, source_target_pairs={{1,0},{2,1},{3,2},{5,4},{6,5},{7,6},{9,8},{10,9},{11,10},{13,12},{... | collective-permute-start | bytes 1179656 | tf_op jit(solution)/shard_map/ppermute | solution.py:18
  86.5 3.0 %collective-permute-start.6 = (f32[4,48,512]{2,1,0:T(8,128)S(1)}, f32[4,48,512]{2,1,0:T(8,128)S(1)}, u32[]{:S(2)}, u32[]{:S(2)}) collective-permute-start(f32[4,48,512]{2,1,0:T(8,128)S(1)} %get-tuple-element.3), channel_id=1, source_target_pairs={{0,1},{1,2},{2,3},{4,5},{5,6},{6,7},{8,9},{9,10},{10,11},{12,13},{... | collective-permute-start | bytes 1179656 | tf_op jit(solution)/shard_map/ppermute | solution.py:18
  89.5 3.5 %collective-permute-done.7.qn_ref = f32[4,48,512]{2,1,0:T(8,128)S(1)} collective-permute-done((f32[4,48,512]{2,1,0:T(8,128)S(1)}, f32[4,48,512]{2,1,0:T(8,128)S(1)}, u32[]{:S(2)}, u32[]{:S(2)}) %collective-permute-start.7) | collective-permute-done | bytes 393248 | tf_op jit(solution)/shard_map/ppermute | solution.py:18
  93.1 1.2 %collective-permute-done.6.qs_ref = f32[4,48,512]{2,1,0:T(8,128)S(1)} collective-permute-done((f32[4,48,512]{2,1,0:T(8,128)S(1)}, f32[4,48,512]{2,1,0:T(8,128)S(1)}, u32[]{:S(2)}, u32[]{:S(2)}) %collective-permute-start.6) | collective-permute-done | bytes 393248 | tf_op jit(solution)/shard_map/ppermute | solution.py:18
  94.2 0.8 copy-done.4
  95.0 7.6 %shard_map.105 = f32[4,8,48,512]{3,2,1,0:T(8,128)} custom-call(f32[8]{0:T(128)} %compare_convert_fusion.north_ref, f32[4,8,48,512]{3,2,1,0:T(8,128)} %shard_map.104.q_ref, f32[4,48,512]{2,1,0:T(8,128)} %copy-done.4, f32[4,48,512]{2,1,0:T(8,128)} %copy-done.3, f32[8,48,512]{2,1,0:T(8,128)} %get-tuple-element.8.u_ref, f32[8,48,512]{2,1,0:T(8,128)} %get-tuple-element.7.v_ref, ...), custom_call_target="tpu_custom_call" | custom-call | tf_op jit(solution)/shard_map/pallas_call | solution.py:56
  (20 shorter events, 0.1 us)
Async XLA Ops:
  7.2 18.6 %copy-start = (f32[8,8,8]{2,1,0:T(8,128)S(1)}, f32[8,8,8]{2,1,0:T(8,128)}, u32[]{:S(2)}) copy-start(f32[8,8,8]{2,1,0:T(8,128)} %param.11) | copy-start | bytes 6148
  7.2 19.1 %copy-start.5 = (f32[4,8,512]{2,1,0:T(8,128)S(1)}, f32[4,8,512]{2,1,0:T(8,128)}, u32[]{:S(2)}) copy-start(f32[4,8,512]{2,1,0:T(8,128)} %param.10) | copy-start | bytes 196612
  7.2 18.8 %copy-start.7 = (f32[4,22]{1,0:T(4,128)S(1)}, f32[4,22]{1,0:T(4,128)}, u32[]{:S(2)}) copy-start(f32[4,22]{1,0:T(4,128)} %param.14) | copy-start | bytes 1060
  7.2 18.8 %copy-start.6 = (s32[8,512]{1,0:T(8,128)S(1)}, s32[8,512]{1,0:T(8,128)}, u32[]{:S(2)}) copy-start(s32[8,512]{1,0:T(8,128)} %param.13) | copy-start | bytes 49156
  7.2 62.1 %all-gather.2.cloned.1.call-start = ((), (), s32[]{:S(2)}) async-start(), calls=%async_computation | async-start | bytes 3072000 | tf_op jit(solution)/shard_map/all_gather | solution.py:100
  8.0 5.4 %collective-permute-start.2 = (f32[1,48,128]{2,1,0:T(8,128)S(1)}, f32[1,48,128]{2,1,0:T(8,128)S(1)}, u32[]{:S(2)}, u32[]{:S(2)}) collective-permute-start(f32[1,48,128]{2,1,0:T(8,128)S(1)} %slice.29), channel_id=1, source_target_pairs={{0,1},{1,2},{2,3},{4,5},{5,6},{6,7},{8,9},{9,10},{10,11},{12,13},{... | collective-permute-start | bytes 73736 | tf_op jit(solution)/shard_map/ppermute | solution.py:18
  15.4 11.6 %collective-permute-start.3 = (f32[4,8,512]{2,1,0:T(8,128)}, f32[4,8,512]{2,1,0:T(8,128)S(1)}, u32[]{:S(2)}, u32[]{:S(2)}) collective-permute-start(f32[4,8,512]{2,1,0:T(8,128)} %param.10), channel_id=1, source_target_pairs={{0,1},{1,2},{2,3},{3,0},{4,5},{5,6},{6,7},{7,4},{8,9},{9,10},{10,1... | collective-permute-start | bytes 196616 | tf_op jit(solution)/shard_map/ppermute | solution.py:97
  17.8 9.5 %collective-permute-start.5 = (f32[4,8,512]{2,1,0:T(8,128)}, f32[4,8,512]{2,1,0:T(8,128)S(1)}, u32[]{:S(2)}, u32[]{:S(2)}) collective-permute-start(f32[4,8,512]{2,1,0:T(8,128)} %param.10), channel_id=1, source_target_pairs={{0,3},{1,0},{2,1},{3,2},{4,7},{5,4},{6,5},{7,6},{8,11},{9,8},{10,9... | collective-permute-start | bytes 196616 | tf_op jit(solution)/shard_map/ppermute | solution.py:97
  17.8 9.7 %collective-permute-start.4 = (f32[4,8,512]{2,1,0:T(8,128)}, f32[4,8,512]{2,1,0:T(8,128)S(1)}, u32[]{:S(2)}, u32[]{:S(2)}) collective-permute-start(f32[4,8,512]{2,1,0:T(8,128)} %param.10), channel_id=1, source_target_pairs={{0,2},{1,3},{2,0},{3,1},{4,6},{5,7},{6,4},{7,5},{8,10},{9,11},{10,... | collective-permute-start | bytes 196616 | tf_op jit(solution)/shard_map/ppermute | solution.py:97
  19.2 54.8 %collective-permute-start.1 = (f32[4,48,512]{2,1,0:T(8,128)S(1)}, f32[4,48,512]{2,1,0:T(8,128)S(1)}, u32[]{:S(2)}, u32[]{:S(2)}) collective-permute-start(f32[4,48,512]{2,1,0:T(8,128)S(1)} %get-tuple-element.4), channel_id=1, source_target_pairs={{1,0},{2,1},{3,2},{5,4},{6,5},{7,6},{9,8},{10,9},{11,10},{13,12},{... | collective-permute-start | bytes 1179656 | tf_op jit(solution)/shard_map/ppermute | solution.py:18
  23.0 51.0 %collective-permute-start = (f32[4,48,512]{2,1,0:T(8,128)S(1)}, f32[4,48,512]{2,1,0:T(8,128)S(1)}, u32[]{:S(2)}, u32[]{:S(2)}) collective-permute-start(f32[4,48,512]{2,1,0:T(8,128)S(1)} %get-tuple-element.5), channel_id=1, source_target_pairs={{0,1},{1,2},{2,3},{4,5},{5,6},{6,7},{8,9},{9,10},{10,11},{12,13},{... | collective-permute-start | bytes 1179656 | tf_op jit(solution)/shard_map/ppermute | solution.py:18
  74.0 0.8 copy-start.1
  74.0 0.9 copy-start.2
  83.7 9.3 %collective-permute-start.7 = (f32[4,48,512]{2,1,0:T(8,128)S(1)}, f32[4,48,512]{2,1,0:T(8,128)S(1)}, u32[]{:S(2)}, u32[]{:S(2)}) collective-permute-start(f32[4,48,512]{2,1,0:T(8,128)S(1)} %get-tuple-element.2), channel_id=1, source_target_pairs={{1,0},{2,1},{3,2},{5,4},{6,5},{7,6},{9,8},{10,9},{11,10},{13,12},{... | collective-permute-start | bytes 1179656 | tf_op jit(solution)/shard_map/ppermute | solution.py:18
  86.5 7.7 %collective-permute-start.6 = (f32[4,48,512]{2,1,0:T(8,128)S(1)}, f32[4,48,512]{2,1,0:T(8,128)S(1)}, u32[]{:S(2)}, u32[]{:S(2)}) collective-permute-start(f32[4,48,512]{2,1,0:T(8,128)S(1)} %get-tuple-element.3), channel_id=1, source_target_pairs={{0,1},{1,2},{2,3},{4,5},{5,6},{6,7},{8,9},{9,10},{10,11},{12,13},{... | collective-permute-start | bytes 1179656 | tf_op jit(solution)/shard_map/ppermute | solution.py:18
  93.1 1.2 %copy-start.3 = (f32[4,48,512]{2,1,0:T(8,128)}, f32[4,48,512]{2,1,0:T(8,128)S(1)}, u32[]{:S(2)}) copy-start(f32[4,48,512]{2,1,0:T(8,128)S(1)} %collective-permute-done.7.qn_ref) | copy-start | bytes 1179652
  94.2 0.8 copy-start.4
Sparse Core Ops, SparseCore 0:
  15.6 53.7 all-gather.1

commit v2 on v1

v2 whole, which is shorter than its diff:
```python
import jax
import jax.numpy as jnp
from jax import lax
from jax.experimental import pallas as pl
from jax.experimental.pallas import tpu as pltpu
from jax.sharding import PartitionSpec as P

exact_dot = lax.Precision.HIGHEST


def passed_along(value, axis, by):
    count = lax.axis_size(axis)
    pairs = [(i, i + by) for i in range(count) if 0 <= i + by < count]
    return lax.ppermute(value, axis, pairs)


def row_blocks(lat_rows):
    edge = max(1, lat_rows // 4)
    outer = sorted(set(range(edge)) | set(range(lat_rows - edge, lat_rows)))
    inner = [r for r in range(lat_rows) if r not in outer]
    return [outer, inner] if inner else [outer]


def merid_schedule(blocks):
    seen = set()
    plan = []
    for rows in blocks:
        fresh = []
        for r in rows:
            for need in (r - 1, r):
                if need not in seen:
                    seen.add(need)
                    fresh.append(need)
        plan.append(sorted(fresh))
    return plan


def step_rows(rows, state_loc, n_state, zonal_loc, merid_loc, mixing_loc, n_met):
    def kernel(*refs):
        north_ref = refs[0]
        state = refs[1 : 1 + n_state]
        met = refs[1 + n_state : 1 + n_state + n_met]
        src_ref = refs[1 + n_state + n_met]
        o_ref = refs[2 + n_state + n_met]

        def q_row(r):
            i, p = state_loc[r]
            return state[i][0, p]

        def met_row(loc, r):
            i, p = loc[r]
            return met[i][p]

        levels, lon = o_ref.shape[2], o_ref.shape[3]
        level = lax.broadcasted_iota(jnp.int32, (levels, lon), 0)
        not_top = level < levels - 1
        not_bottom = level > 0
        bottom = level == 0
        for out_index, a in enumerate(rows):
            qa = q_row(a)
            qm = q_row(a - 1)
            qp = q_row(a + 1)
            u = met_row(zonal_loc, a)
            v = met_row(merid_loc, a)
            vm = met_row(merid_loc, a - 1)
            w = met_row(mixing_loc, a)
            east = pltpu.roll(qa, lon - 1, 1)
            west = pltpu.roll(qa, 1, 1)
            uw = pltpu.roll(u, 1, 1)
            flux_east = jnp.maximum(u, 0.0) * qa + jnp.minimum(u, 0.0) * east
            flux_west = jnp.maximum(uw, 0.0) * west + jnp.minimum(uw, 0.0) * qa
            flux_north = (jnp.maximum(v, 0.0) * qa + jnp.minimum(v, 0.0) * qp) * north_ref[a]
            flux_south = jnp.maximum(vm, 0.0) * qm + jnp.minimum(vm, 0.0) * qa
            upper = jnp.where(not_top, pltpu.roll(qa, levels - 1, 0), 0.0)
            flux_up = jnp.where(not_top, w * (qa - upper), 0.0)
            flux_down = jnp.where(not_bottom, pltpu.roll(flux_up, 1, 0), 0.0)
            result = qa - (flux_east - flux_west) - (flux_north - flux_south) - (flux_up - flux_down)
            source = jnp.broadcast_to(src_ref[0, a : a + 1, :], (levels, lon))
            o_ref[0, out_index] = result + jnp.where(bottom, source, 0.0)

    return kernel


def advance_rows(rows, states, state_loc, mets, zonal_loc, merid_loc, mixing_loc, emission, north_open):
    tracers, lat_rows, lon = emission.shape
    levels = states[0].shape[2]
    kernel = step_rows(rows, state_loc, len(states), zonal_loc, merid_loc, mixing_loc, len(mets))
    in_specs = [pl.BlockSpec(memory_space=pltpu.SMEM)]
    in_specs += [pl.BlockSpec((1,) + s.shape[1:], lambda k: (k, 0, 0, 0)) for s in states]
    in_specs += [pl.BlockSpec(m.shape, lambda k: (0, 0, 0)) for m in mets]
    in_specs += [pl.BlockSpec((1, lat_rows, lon), lambda k: (k, 0, 0))]
    out_shape = (tracers, len(rows), levels, lon)
    return pl.pallas_call(
        kernel,
        grid=(tracers,),
        in_specs=in_specs,
        out_specs=pl.BlockSpec((1,) + out_shape[1:], lambda k: (k, 0, 0, 0)),
        out_shape=jax.ShapeDtypeStruct(out_shape, jnp.float32),
    )(north_open, *states, *mets, emission)


def on_device(
    tracer_state,
    control,
    prior_tiles,
    tile_index,
    region_map,
    region_sigma,
    zonal_courant,
    meridional_courant,
    vertical_diffusion,
):
    band_count = lax.axis_size("band")
    band_index = lax.axis_index("band")
    tiles_count = prior_tiles.shape[0]
    lat_rows = control.shape[1]

    blocks = row_blocks(lat_rows)
    v_plan = merid_schedule(blocks)

    south_v = passed_along(meridional_courant[-1:], "band", 1)
    q_south = passed_along(tracer_state[:, -1:], "band", 1)
    q_north = passed_along(tracer_state[:, :1], "band", -1)
    shifted = [control]
    for s in range(1, band_count):
        pairs = [(i, (i + s) % band_count) for i in range(band_count)]
        shifted.append(lax.ppermute(control, "band", pairs))

    mets = []
    zonal_loc, merid_loc, mixing_loc = {}, {}, {}
    for j, rows in enumerate(blocks):
        parts = []
        for r in rows:
            zonal_loc[r] = (j, len(parts))
            parts.append(zonal_courant[r : r + 1])
        for r in rows:
            mixing_loc[r] = (j, len(parts))
            parts.append(vertical_diffusion[r : r + 1])
        for r in v_plan[j]:
            merid_loc[r] = (j, len(parts))
            parts.append(south_v if r < 0 else meridional_courant[r : r + 1])
        pack = jnp.concatenate(parts, axis=0)
        mets.append(lax.all_gather(pack, "tracer", axis=2, tiled=True))

    choose = (
        tile_index[:, :, None] == lax.broadcasted_iota(jnp.int32, (1, 1, tiles_count), 2)
    ).astype(jnp.float32)
    own_row = lax.dynamic_slice_in_dim(choose, band_index, 1, 0)[0]
    row_tiles = jnp.einsum("bt,tmn->bmn", own_row, prior_tiles, precision=exact_dot)
    prior_field = None
    for s, part in enumerate(shifted):
        source_band = (band_index - s) % band_count
        tile = lax.dynamic_index_in_dim(row_tiles, source_band, 0, keepdims=False)
        term = jnp.einsum("jm,kmn->kjn", tile, part, precision=exact_dot)
        prior_field = term if prior_field is None else prior_field + term
    regions = region_sigma.shape[1]
    onehot = (region_map[:, :, None] == lax.broadcasted_iota(jnp.int32, (1, 1, regions), 2)).astype(
        jnp.float32
    )
    cell_sigma = jnp.einsum("kr,jnr->kjn", region_sigma, onehot, precision=exact_dot)
    emission = cell_sigma * prior_field

    latitude = band_index * lat_rows + jnp.arange(lat_rows, dtype=jnp.int32)
    north_open = (latitude < band_count * lat_rows - 1).astype(jnp.float32)

    first_loc = {r: (0, r) for r in range(lat_rows)}
    first_loc[-1] = (1, 0)
    first_loc[lat_rows] = (2, 0)
    first_states = [tracer_state, q_south, q_north]

    s1_blocks = []
    s1_loc = {}
    halo = None
    finals = []
    final_loc = {}

    def second(rows, pieces):
        need = set()
        for r in rows:
            need |= {r - 1, r, r + 1}
        used = sorted({s1_loc[r][0] for r in need if 0 <= r < lat_rows})
        states = [s1_blocks[i] for i in used] + list(halo)
        loc = {}
        for r in need:
            if r < 0:
                loc[r] = (len(used), 0)
            elif r >= lat_rows:
                loc[r] = (len(used) + 1, 0)
            else:
                i, p = s1_loc[r]
                loc[r] = (used.index(i), p)
        out = advance_rows(rows, states, loc, pieces, zonal_loc, merid_loc, mixing_loc, emission, north_open)
        for p, r in enumerate(rows):
            final_loc[r] = (len(finals), p)
        finals.append(out)

    done = set()
    for j, rows in enumerate(blocks):
        out = advance_rows(
            rows, first_states, first_loc, mets[: j + 1], zonal_loc, merid_loc, mixing_loc, emission, north_open
        )
        for p, r in enumerate(rows):
            s1_loc[r] = (j, p)
        s1_blocks.append(out)
        if j == 0:
            i_top, p_top = s1_loc[lat_rows - 1]
            i_bot, p_bot = s1_loc[0]
            halo = (
                passed_along(out[:, p_top : p_top + 1], "band", 1),
                passed_along(out[:, p_bot : p_bot + 1], "band", -1),
            )
        ready = [
            r
            for r in range(lat_rows)
            if r not in done and all(n < 0 or n >= lat_rows or n in s1_loc for n in (r - 1, r, r + 1))
        ]
        if ready:
            second(ready, mets[: j + 1])
            done |= set(ready)

    final_state = jnp.concatenate(
        [finals[final_loc[r][0]][:, final_loc[r][1] : final_loc[r][1] + 1] for r in range(lat_rows)], axis=1
    )
    return (final_state, emission)


def solution(mesh):
    in_specs = (
        P(("inv", "tracer"), "band", None, None),
        P(("inv", "tracer"), "band", None),
        P(),
        P(),
        P("band", None),
        P("tracer", None),
        P(("inv", "band"), None, "tracer"),
        P(("inv", "band"), None, "tracer"),
        P(("inv", "band"), None, "tracer"),
    )
    out_specs = (P(("inv", "tracer"), "band", None, None), P(("inv", "tracer"), "band", None))
    return jax.shard_map(
        on_device, mesh=mesh, in_specs=in_specs, out_specs=out_specs, check_vma=False
    )
```

time: 110 us -> 116 us (1.055)
  the two profiles are of different devices: /device:TPU:1 before, /device:TPU:0 now
where the time goes in v2:
time: 116 us; the launch traced here: 115 us
  waiting for transfers between devices  42.7 us (37%)
  Pallas kernels  23.1 us (20%)
  starting transfers between devices  15.5 us (13%)
  between operations  14.4 us (12%)
  local copies, waits for them, and re-layouts  12.3 us (11%)
  other arithmetic  5.15 us (4%)
  matrix products  1.85 us (2%)
    all_gather x2, waiting for transfers between devices, on_device(): mets.append(lax.all_gather(pack, 'tracer', axis=2, tiled=True))  42.6 us
    pallas_call x4, Pallas kernels, advance_rows(): pl.pallas_call(kernel, grid=(tracers,), in_specs=in_specs, out_specs=pl.B...  23.1 us
    ppermute x5, starting transfers between devices, passed_along(): return lax.ppermute(value, axis, pairs)  11 us
    unnamed x24, local copies, waits for them, and re-layouts  6.27 us
    ppermute x3, starting transfers between devices, on_device(): shifted.append(lax.ppermute(control, 'band', pairs))  4.35 us
    concatenate x1, other arithmetic, on_device(): jnp.concatenate([finals[final_loc[r][0]][:, final_loc[r][1]:final_loc[r][...  3.91 us
  transfers between devices with their start and end apart: 10, of which 2 were waited for; matrix products, arithmetic and copies ran while one was open for 8% of the time, Pallas kernels for 10%

profile of v2, /device:TPU:0, one launch (start us, length us, event | category | flops | bytes accessed | tf_op | source)
XLA Modules:
  0.0 114.9 jit_solution(16573014860965517044)
XLA Ops:
  7.3 0.8 slice.85
  8.1 2.3 %collective-permute-start.2 = (f32[1,48,128]{2,1,0:T(8,128)S(1)}, f32[1,48,128]{2,1,0:T(8,128)S(1)}, u32[]{:S(2)}, u32[]{:S(2)}) collective-permute-start(f32[1,48,128]{2,1,0:T(8,128)S(1)} %slice.85), channel_id=1, source_target_pairs={{0,1},{1,2},{2,3},{4,5},{5,6},{6,7},{8,9},{9,10},{10,11},{12,13},{... | collective-permute-start | bytes 73736 | tf_op jit(solution)/shard_map/ppermute | solution.py:14
  10.4 0.8 slice_dynamic-update-slice_fusion.5
  11.2 0.8 slice_dynamic-update-slice_fusion.4
  12.0 0.8 slice_dynamic-update-slice_fusion.3
  12.8 0.8 slice_dynamic-update-slice_fusion.2
  13.6 0.8 slice_dynamic-update-slice_fusion.1
  14.4 0.9 fusion.14
  15.4 0.7 copy-done.5
  16.2 2.7 %collective-permute-start.3 = (f32[4,8,512]{2,1,0:T(8,128)}, f32[4,8,512]{2,1,0:T(8,128)S(1)}, u32[]{:S(2)}, u32[]{:S(2)}) collective-permute-start(f32[4,8,512]{2,1,0:T(8,128)} %param.10), channel_id=1, source_target_pairs={{0,1},{1,2},{2,3},{3,0},{4,5},{5,6},{6,7},{7,4},{8,9},{9,10},{10,1... | collective-permute-start | bytes 196616 | tf_op jit(solution)/shard_map/ppermute | solution.py:127
  18.8 1.7 %collective-permute-start.4 = (f32[4,8,512]{2,1,0:T(8,128)}, f32[4,8,512]{2,1,0:T(8,128)S(1)}, u32[]{:S(2)}, u32[]{:S(2)}) collective-permute-start(f32[4,8,512]{2,1,0:T(8,128)} %param.10), channel_id=1, source_target_pairs={{0,2},{1,3},{2,0},{3,1},{4,6},{5,7},{6,4},{7,5},{8,10},{9,11},{10,... | collective-permute-start | bytes 196616 | tf_op jit(solution)/shard_map/ppermute | solution.py:127
  20.5 1.2 %fusion.11 = (f32[4,1,48,512]{3,2,1,0:T(8,128)S(1)}, f32[4,1,48,512]{3,2,1,0:T(8,128)S(1)}) fusion(f32[4,8,48,512]{3,2,1,0:T(8,128)} %refs_1_.3), kind=kLoop, calls=%fused_computation.29 | loop fusion | bytes 1572864 | tf_op jit(solution)/shard_map/slice | solution.py:123
  21.7 1.3 %collective-permute-start.1 = (f32[4,1,48,512]{3,2,1,0:T(8,128)S(1)}, f32[4,1,48,512]{3,2,1,0:T(8,128)S(1)}, u32[]{:S(2)}, u32[]{:S(2)}) collective-permute-start(f32[4,1,48,512]{3,2,1,0:T(8,128)S(1)} %get-tuple-element.2), channel_id=1, source_target_pairs={{1,0},{2,1},{3,2},{5,4},{6,5},{7,6},{9,8},{10,9},{11,10},{13,12},{... | collective-permute-start | bytes 1179656 | tf_op jit(solution)/shard_map/ppermute | solution.py:14
  23.0 3.1 %collective-permute-start = (f32[4,1,48,512]{3,2,1,0:T(8,128)S(1)}, f32[4,1,48,512]{3,2,1,0:T(8,128)S(1)}, u32[]{:S(2)}, u32[]{:S(2)}) collective-permute-start(f32[4,1,48,512]{3,2,1,0:T(8,128)S(1)} %get-tuple-element.3), channel_id=1, source_target_pairs={{0,1},{1,2},{2,3},{4,5},{5,6},{6,7},{8,9},{9,10},{10,11},{12,13},{... | collective-permute-start | bytes 1179656 | tf_op jit(solution)/shard_map/ppermute | solution.py:14
  26.2 0.7 constant_dynamic-slice_fusion.4
  27.3 0.7 pad_maximum_fusion.1
  28.1 0.3 fusion.3
  28.4 0.5 compare_convert_fusion.refs_0_
  29.3 0.8 fusion.2.refs_5_.refs_6_.refs_7_
  30.1 23.2 %all-gather.3.cloned.1.call-done.refs_4_.refs_5_ = f32[14,48,512]{2,1,0:T(8,128)} async-done(((f32[14,48,128]{2,1,0:T(8,128)}), f32[14,48,512]{2,1,0:T(8,128)}) %all-gather.3.cloned.1.call-update) | async-done | bytes 1376272 | tf_op jit(solution)/shard_map/all_gather | solution.py:143
  53.4 5.6 %shard_map.104.refs_1_ = f32[4,4,48,512]{3,2,1,0:T(8,128)} custom-call(f32[8]{0:T(128)} %compare_convert_fusion.refs_0_, f32[4,8,48,512]{3,2,1,0:T(8,128)} %refs_1_.3, f32[4,1,48,512]{3,2,1,0:T(8,128)} %copy-done.2, f32[4,1,48,512]{3,2,1,0:T(8,128)} %copy-done.1, f32[14,48,512]{2,1,0:T(8,128)} %all-gather.3.cloned.1.call-done.refs_4_.refs_5_, ...), custom_call_target="tpu_custom_call" | custom-call | tf_op jit(solution)/shard_map/pallas_call | solution.py:93
  59.0 1.2 %fusion.12 = (f32[4,1,48,512]{3,2,1,0:T(8,128)S(1)}, f32[4,1,48,512]{3,2,1,0:T(8,128)S(1)}) fusion(f32[4,4,48,512]{3,2,1,0:T(8,128)} %shard_map.104.refs_1_), kind=kLoop, calls=%fused_computation.30 | loop fusion | bytes 1572864 | tf_op jit(solution)/shard_map/slice | solution.py:210
  60.2 1.3 %collective-permute-start.7 = (f32[4,1,48,512]{3,2,1,0:T(8,128)S(1)}, f32[4,1,48,512]{3,2,1,0:T(8,128)S(1)}, u32[]{:S(2)}, u32[]{:S(2)}) collective-permute-start(f32[4,1,48,512]{3,2,1,0:T(8,128)S(1)} %get-tuple-element.4), channel_id=1, source_target_pairs={{1,0},{2,1},{3,2},{5,4},{6,5},{7,6},{9,8},{10,9},{11,10},{13,12},{... | collective-permute-start | bytes 1179656 | tf_op jit(solution)/shard_map/ppermute | solution.py:14
  61.5 3.1 %collective-permute-start.6 = (f32[4,1,48,512]{3,2,1,0:T(8,128)S(1)}, f32[4,1,48,512]{3,2,1,0:T(8,128)S(1)}, u32[]{:S(2)}, u32[]{:S(2)}) collective-permute-start(f32[4,1,48,512]{3,2,1,0:T(8,128)S(1)} %get-tuple-element.5), channel_id=1, source_target_pairs={{0,1},{1,2},{2,3},{4,5},{5,6},{6,7},{8,9},{9,10},{10,11},{12,13},{... | collective-permute-start | bytes 1179656 | tf_op jit(solution)/shard_map/ppermute | solution.py:14
  64.5 19.4 %all-gather.5.cloned.1.call-done.refs_5_.refs_6_ = f32[11,48,512]{2,1,0:T(8,128)} async-done(((f32[11,48,128]{2,1,0:T(8,128)}), f32[11,48,512]{2,1,0:T(8,128)}) %all-gather.5.cloned.1.call-update) | async-done | bytes 1081360 | tf_op jit(solution)/shard_map/all_gather | solution.py:143
  84.0 5.9 %shard_map.106.refs_2_ = f32[4,4,48,512]{3,2,1,0:T(8,128)} custom-call(f32[8]{0:T(128)} %compare_convert_fusion.refs_0_, f32[4,8,48,512]{3,2,1,0:T(8,128)} %refs_1_.3, f32[4,1,48,512]{3,2,1,0:T(8,128)} %copy-done.2, f32[4,1,48,512]{3,2,1,0:T(8,128)} %copy-done.1, f32[14,48,512]{2,1,0:T(8,128)} %all-gather.3.cloned.1.call-done.refs_4_.refs_5_, ...), custom_call_target="tpu_custom_call" | custom-call | tf_op jit(solution)/shard_map/pallas_call | solution.py:93
  89.9 0.7 copy-done.3
  90.6 0.8 copy-done.4
  91.4 4.7 %shard_map.105 = f32[4,2,48,512]{3,2,1,0:T(8,128)} custom-call(f32[8]{0:T(128)} %compare_convert_fusion.refs_0_, f32[4,4,48,512]{3,2,1,0:T(8,128)} %shard_map.104.refs_1_, f32[4,1,48,512]{3,2,1,0:T(8,128)} %copy-done.4, f32[4,1,48,512]{3,2,1,0:T(8,128)} %copy-done.3, f32[14,48,512]{2,1,0:T(8,128)} %all-gather.3.cloned.1.call-done.refs_4_.refs_5_, ...), custom_call_target="tpu_custom_call" | custom-call | tf_op jit(solution)/shard_map/pallas_call | solution.py:93
  96.0 1.2 %fusion.13 = (f32[4,1,48,512]{3,2,1,0:T(8,128)S(1)}, f32[4,1,48,512]{3,2,1,0:T(8,128)S(1)}) fusion(f32[4,2,48,512]{3,2,1,0:T(8,128)} %shard_map.105), kind=kLoop, calls=%fused_computation.31 | loop fusion | bytes 1572864 | tf_op jit(solution)/shard_map/slice | solution.py:222
  97.2 6.9 %shard_map.107 = f32[4,6,48,512]{3,2,1,0:T(8,128)} custom-call(f32[8]{0:T(128)} %compare_convert_fusion.refs_0_, f32[4,4,48,512]{3,2,1,0:T(8,128)} %shard_map.104.refs_1_, f32[4,4,48,512]{3,2,1,0:T(8,128)} %shard_map.106.refs_2_, f32[4,1,48,512]{3,2,1,0:T(8,128)} %copy-done.4, f32[4,1,48,512]{3,2,1,0:T(8,128)} %copy-done.3, ...), custom_call_target="tpu_custom_call" | custom-call | tf_op jit(solution)/shard_map/pallas_call | solution.py:93
  104.2 3.9 %pad_maximum_fusion = f32[4,8,48,512]{3,2,1,0:T(8,128)} fusion(f32[4,1,48,512]{3,2,1,0:T(8,128)S(1)} %get-tuple-element.7, f32[4,6,48,512]{3,2,1,0:T(8,128)} %shard_map.107, f32[4,1,48,512]{3,2,1,0:T(8,128)S(1)} %get-tuple-element.6), kind=kLoop, calls=%fused_computation | loop fusion | flops 1572864 | bytes 6291456 | tf_op jit(solution)/shard_map/concatenate | solution.py:221
  (38 shorter events, 1.0 us)
Async XLA Ops:
  7.2 19.7 %copy-start = (f32[8,8,8]{2,1,0:T(8,128)S(1)}, f32[8,8,8]{2,1,0:T(8,128)}, u32[]{:S(2)}) copy-start(f32[8,8,8]{2,1,0:T(8,128)} %param.11) | copy-start | bytes 6148
  7.2 20.1 %slice-start = ((f32[8,48,128]{2,1,0:T(8,128)}), f32[4,48,128]{2,1,0:T(8,128)S(1)}, s32[]{:S(2)}) async-start(f32[8,48,128]{2,1,0:T(8,128)} %param.15), calls=%async_computation.2 | async-start | bytes 196608 | tf_op jit(solution)/shard_map/slice | solution.py:135
  7.2 20.1 %slice-start.1 = ((f32[8,48,128]{2,1,0:T(8,128)}), f32[4,48,128]{2,1,0:T(8,128)S(1)}, s32[]{:S(2)}) async-start(f32[8,48,128]{2,1,0:T(8,128)} %param.17), calls=%async_computation.3 | async-start | bytes 196608 | tf_op jit(solution)/shard_map/slice | solution.py:138
  7.2 19.9 %copy-start.6 = (f32[4,8,512]{2,1,0:T(8,128)S(1)}, f32[4,8,512]{2,1,0:T(8,128)}, u32[]{:S(2)}) copy-start(f32[4,8,512]{2,1,0:T(8,128)} %param.10) | copy-start | bytes 196612
  7.2 20.9 %copy-start.8 = (f32[4,22]{1,0:T(4,128)S(1)}, f32[4,22]{1,0:T(4,128)}, u32[]{:S(2)}) copy-start(f32[4,22]{1,0:T(4,128)} %param.14) | copy-start | bytes 1060
  7.2 20.9 %copy-start.7 = (s32[8,512]{1,0:T(8,128)S(1)}, s32[8,512]{1,0:T(8,128)}, u32[]{:S(2)}) copy-start(s32[8,512]{1,0:T(8,128)} %param.13) | copy-start | bytes 49156
  7.2 46.1 %all-gather.3.cloned.1.call-start = ((), (), s32[]{:S(2)}) async-start(), calls=%async_computation | async-start | bytes 1720320 | tf_op jit(solution)/shard_map/all_gather | solution.py:143
  8.1 5.6 %collective-permute-start.2 = (f32[1,48,128]{2,1,0:T(8,128)S(1)}, f32[1,48,128]{2,1,0:T(8,128)S(1)}, u32[]{:S(2)}, u32[]{:S(2)}) collective-permute-start(f32[1,48,128]{2,1,0:T(8,128)S(1)} %slice.85), channel_id=1, source_target_pairs={{0,1},{1,2},{2,3},{4,5},{5,6},{6,7},{8,9},{9,10},{10,11},{12,13},{... | collective-permute-start | bytes 73736 | tf_op jit(solution)/shard_map/ppermute | solution.py:14
  15.4 0.7 copy-start.5
  16.1 67.8 %all-gather.5.cloned.1.call-start = ((), (), s32[]{:S(2)}) async-start(), calls=%async_computation.1 | async-start | bytes 1351680 | tf_op jit(solution)/shard_map/all_gather | solution.py:143
  16.2 12.7 %collective-permute-start.3 = (f32[4,8,512]{2,1,0:T(8,128)}, f32[4,8,512]{2,1,0:T(8,128)S(1)}, u32[]{:S(2)}, u32[]{:S(2)}) collective-permute-start(f32[4,8,512]{2,1,0:T(8,128)} %param.10), channel_id=1, source_target_pairs={{0,1},{1,2},{2,3},{3,0},{4,5},{5,6},{6,7},{7,4},{8,9},{9,10},{10,1... | collective-permute-start | bytes 196616 | tf_op jit(solution)/shard_map/ppermute | solution.py:127
  18.8 10.2 %collective-permute-start.5 = (f32[4,8,512]{2,1,0:T(8,128)}, f32[4,8,512]{2,1,0:T(8,128)S(1)}, u32[]{:S(2)}, u32[]{:S(2)}) collective-permute-start(f32[4,8,512]{2,1,0:T(8,128)} %param.10), channel_id=1, source_target_pairs={{0,3},{1,0},{2,1},{3,2},{4,7},{5,4},{6,5},{7,6},{8,11},{9,8},{10,9... | collective-permute-start | bytes 196616 | tf_op jit(solution)/shard_map/ppermute | solution.py:127
  18.8 10.4 %collective-permute-start.4 = (f32[4,8,512]{2,1,0:T(8,128)}, f32[4,8,512]{2,1,0:T(8,128)S(1)}, u32[]{:S(2)}, u32[]{:S(2)}) collective-permute-start(f32[4,8,512]{2,1,0:T(8,128)} %param.10), channel_id=1, source_target_pairs={{0,2},{1,3},{2,0},{3,1},{4,6},{5,7},{6,4},{7,5},{8,10},{9,11},{10,... | collective-permute-start | bytes 196616 | tf_op jit(solution)/shard_map/ppermute | solution.py:127
  21.7 8.4 %collective-permute-start.1 = (f32[4,1,48,512]{3,2,1,0:T(8,128)S(1)}, f32[4,1,48,512]{3,2,1,0:T(8,128)S(1)}, u32[]{:S(2)}, u32[]{:S(2)}) collective-permute-start(f32[4,1,48,512]{3,2,1,0:T(8,128)S(1)} %get-tuple-element.2), channel_id=1, source_target_pairs={{1,0},{2,1},{3,2},{5,4},{6,5},{7,6},{9,8},{10,9},{11,10},{13,12},{... | collective-permute-start | bytes 1179656 | tf_op jit(solution)/shard_map/ppermute | solution.py:14
  23.0 7.1 %collective-permute-start = (f32[4,1,48,512]{3,2,1,0:T(8,128)S(1)}, f32[4,1,48,512]{3,2,1,0:T(8,128)S(1)}, u32[]{:S(2)}, u32[]{:S(2)}) collective-permute-start(f32[4,1,48,512]{3,2,1,0:T(8,128)S(1)} %get-tuple-element.3), channel_id=1, source_target_pairs={{0,1},{1,2},{2,3},{4,5},{5,6},{6,7},{8,9},{9,10},{10,11},{12,13},{... | collective-permute-start | bytes 1179656 | tf_op jit(solution)/shard_map/ppermute | solution.py:14
  30.1 23.2 %copy-start.1 = (f32[4,1,48,512]{3,2,1,0:T(8,128)}, f32[4,1,48,512]{3,2,1,0:T(8,128)S(1)}, u32[]{:S(2)}) copy-start(f32[4,1,48,512]{3,2,1,0:T(8,128)S(1)} %collective-permute-done.1.refs_3_) | copy-start | bytes 1179652
  30.1 23.2 %copy-start.2 = (f32[4,1,48,512]{3,2,1,0:T(8,128)}, f32[4,1,48,512]{3,2,1,0:T(8,128)S(1)}, u32[]{:S(2)}) copy-start(f32[4,1,48,512]{3,2,1,0:T(8,128)S(1)} %collective-permute-done.refs_2_) | copy-start | bytes 1179652
  60.2 29.7 %collective-permute-start.7 = (f32[4,1,48,512]{3,2,1,0:T(8,128)S(1)}, f32[4,1,48,512]{3,2,1,0:T(8,128)S(1)}, u32[]{:S(2)}, u32[]{:S(2)}) collective-permute-start(f32[4,1,48,512]{3,2,1,0:T(8,128)S(1)} %get-tuple-element.4), channel_id=1, source_target_pairs={{1,0},{2,1},{3,2},{5,4},{6,5},{7,6},{9,8},{10,9},{11,10},{13,12},{... | collective-permute-start | bytes 1179656 | tf_op jit(solution)/shard_map/ppermute | solution.py:14
  61.5 28.4 %collective-permute-start.6 = (f32[4,1,48,512]{3,2,1,0:T(8,128)S(1)}, f32[4,1,48,512]{3,2,1,0:T(8,128)S(1)}, u32[]{:S(2)}, u32[]{:S(2)}) collective-permute-start(f32[4,1,48,512]{3,2,1,0:T(8,128)S(1)} %get-tuple-element.5), channel_id=1, source_target_pairs={{0,1},{1,2},{2,3},{4,5},{5,6},{6,7},{8,9},{9,10},{10,11},{12,13},{... | collective-permute-start | bytes 1179656 | tf_op jit(solution)/shard_map/ppermute | solution.py:14
  89.8 0.8 copy-start.3
  90.6 0.8 copy-start.4
Sparse Core Ops, SparseCore 0:
  16.3 37.0 all-gather.2
  54.9 28.9 all-gather.4

commit v3 on v1

v3 whole, which is shorter than its diff:
```python
import jax
import jax.numpy as jnp
from jax import lax
from jax.experimental import pallas as pl
from jax.experimental.pallas import tpu as pltpu
from jax.sharding import PartitionSpec as P

exact_dot = lax.Precision.HIGHEST


def passed_along(value, axis, by):
    count = lax.axis_size(axis)
    pairs = [(i, i + by) for i in range(count) if 0 <= i + by < count]
    return lax.ppermute(value, axis, pairs)


def step_kernel(north_ref, q_ref, qs_ref, qn_ref, wx_ref, src_ref, *rest):
    o_ref = rest[0]
    edges = rest[1:-1]
    coef_ref = rest[-1]
    lat_rows = q_ref.shape[1]
    levels, lon = q_ref.shape[2], q_ref.shape[3]
    level = lax.broadcasted_iota(jnp.int32, (levels, lon), 0)
    not_top = level < levels - 1
    not_bottom = level > 0
    bottom = level == 0

    @pl.when(pl.program_id(0) == 0)
    def _():
        for a in range(lat_rows):
            u = wx_ref[a]
            uw = pltpu.roll(u, 1, 1)
            v = wx_ref[lat_rows + a] * north_ref[a]
            vm = wx_ref[3 * lat_rows] if a == 0 else wx_ref[lat_rows + a - 1]
            w = wx_ref[2 * lat_rows + a]
            w_up = jnp.where(not_top, w, 0.0)
            w_down = jnp.where(not_bottom, pltpu.roll(w, 1, 0), 0.0)
            coef_ref[0, a] = (
                1.0
                - jnp.maximum(u, 0.0)
                + jnp.minimum(uw, 0.0)
                - jnp.maximum(v, 0.0)
                + jnp.minimum(vm, 0.0)
                - w_up
                - w_down
            )
            coef_ref[1, a] = -jnp.minimum(u, 0.0)
            coef_ref[2, a] = jnp.maximum(uw, 0.0)
            coef_ref[3, a] = -jnp.minimum(v, 0.0)
            coef_ref[4, a] = jnp.maximum(vm, 0.0)
            coef_ref[5, a] = w_up
            coef_ref[6, a] = w_down

    for a in range(lat_rows):
        qa = q_ref[0, a]
        qm = qs_ref[0] if a == 0 else q_ref[0, a - 1]
        qp = qn_ref[0] if a == lat_rows - 1 else q_ref[0, a + 1]
        result = (
            coef_ref[0, a] * qa
            + coef_ref[1, a] * pltpu.roll(qa, lon - 1, 1)
            + coef_ref[2, a] * pltpu.roll(qa, 1, 1)
            + coef_ref[3, a] * qp
            + coef_ref[4, a] * qm
            + coef_ref[5, a] * pltpu.roll(qa, levels - 1, 0)
            + coef_ref[6, a] * pltpu.roll(qa, 1, 0)
        )
        source = jnp.broadcast_to(src_ref[0, a : a + 1, :], (levels, lon))
        result = result + jnp.where(bottom, source, 0.0)
        o_ref[0, a] = result
        if edges and a == 0:
            edges[0][0] = result
        if edges and a == lat_rows - 1:
            edges[1][0] = result


def advance(state, south, north, weather, emission, north_open, with_edges):
    tracers, lat_rows, levels, lon = state.shape
    row = pl.BlockSpec((1, lat_rows, levels, lon), lambda k: (k, 0, 0, 0))
    edge = pl.BlockSpec((1, levels, lon), lambda k: (k, 0, 0))
    out_specs = [row]
    out_shape = [jax.ShapeDtypeStruct(state.shape, state.dtype)]
    if with_edges:
        out_specs += [edge, edge]
        out_shape += [jax.ShapeDtypeStruct((tracers, levels, lon), state.dtype)] * 2
    grid_spec = pltpu.PrefetchScalarGridSpec(
        num_scalar_prefetch=0,
        grid=(tracers,),
        in_specs=[
            pl.BlockSpec(memory_space=pltpu.SMEM),
            row,
            edge,
            edge,
            pl.BlockSpec(weather.shape, lambda k: (0, 0, 0)),
            pl.BlockSpec((1, lat_rows, lon), lambda k: (k, 0, 0)),
        ],
        out_specs=out_specs,
        scratch_shapes=[pltpu.VMEM((7, lat_rows, levels, lon), jnp.float32)],
    )
    return pl.pallas_call(
        step_kernel,
        grid_spec=grid_spec,
        out_shape=out_shape,
        compiler_params=pltpu.CompilerParams(dimension_semantics=("arbitrary",)),
    )(north_open, state, south, north, weather, emission)


def on_device(
    tracer_state,
    control,
    prior_tiles,
    tile_index,
    region_map,
    region_sigma,
    zonal_courant,
    meridional_courant,
    vertical_diffusion,
):
    band_count = lax.axis_size("band")
    band_index = lax.axis_index("band")
    tiles_count = prior_tiles.shape[0]
    lat_rows = control.shape[1]

    south_v = passed_along(meridional_courant[-1:], "band", 1)
    q_south = passed_along(tracer_state[:, -1], "band", 1)
    q_north = passed_along(tracer_state[:, 0], "band", -1)
    shifted = [control]
    for s in range(1, band_count):
        pairs = [(i, (i + s) % band_count) for i in range(band_count)]
        shifted.append(lax.ppermute(control, "band", pairs))

    pack = jnp.concatenate([zonal_courant, meridional_courant, vertical_diffusion, south_v], axis=0)
    weather = lax.all_gather(pack, "tracer", axis=2, tiled=True)

    choose = (
        tile_index[:, :, None] == lax.broadcasted_iota(jnp.int32, (1, 1, tiles_count), 2)
    ).astype(jnp.float32)
    own_row = lax.dynamic_slice_in_dim(choose, band_index, 1, 0)[0]
    row_tiles = jnp.einsum("bt,tmn->bmn", own_row, prior_tiles, precision=exact_dot)
    prior_field = None
    for s, part in enumerate(shifted):
        source_band = (band_index - s) % band_count
        tile = lax.dynamic_index_in_dim(row_tiles, source_band, 0, keepdims=False)
        term = jnp.einsum("jm,kmn->kjn", tile, part, precision=exact_dot)
        prior_field = term if prior_field is None else prior_field + term
    regions = region_sigma.shape[1]
    onehot = (region_map[:, :, None] == lax.broadcasted_iota(jnp.int32, (1, 1, regions), 2)).astype(
        jnp.float32
    )
    cell_sigma = jnp.einsum("kr,jnr->kjn", region_sigma, onehot, precision=exact_dot)
    emission = cell_sigma * prior_field

    latitude = band_index * lat_rows + jnp.arange(lat_rows, dtype=jnp.int32)
    north_open = (latitude < band_count * lat_rows - 1).astype(jnp.float32)

    first, bottom_row, top_row = advance(
        tracer_state, q_south, q_north, weather, emission, north_open, True
    )
    s1_south = passed_along(top_row, "band", 1)
    s1_north = passed_along(bottom_row, "band", -1)
    (tracer_field,) = advance(first, s1_south, s1_north, weather, emission, north_open, False)
    return (tracer_field, emission)


def solution(mesh):
    in_specs = (
        P(("inv", "tracer"), "band", None, None),
        P(("inv", "tracer"), "band", None),
        P(),
        P(),
        P("band", None),
        P("tracer", None),
        P(("inv", "band"), None, "tracer"),
        P(("inv", "band"), None, "tracer"),
        P(("inv", "band"), None, "tracer"),
    )
    out_specs = (P(("inv", "tracer"), "band", None, None), P(("inv", "tracer"), "band", None))
    return jax.shard_map(
        on_device, mesh=mesh, in_specs=in_specs, out_specs=out_specs, check_vma=False
    )
```

time: 110 us -> 106 us (0.964)
  local copies, waits for them, and re-layouts: 10.1 us -> 3.42 us
  waiting for transfers between devices: 46.7 us -> 49.3 us
    ppermute x5, waiting for transfers between devices: 5.63 us -> 9.65 us  [passed_along(): return lax.ppermute(value, axis, pairs)]
    slice x1 -> x0, local copies, waits for them, and re-layouts: 3.12 us -> none  [on_device(): mixing = weather[2 * lat_rows:3 * lat_rows]]
    squeeze x2 -> x0, local copies, waits for them, and re-layouts: 2.72 us -> none  [the longest x1 1.54 us: on_device(): merid_south = weather[3 * lat_rows]]
    all_gather x1, waiting for transfers between devices: 41 us -> 39.7 us  [on_device(): weather = lax.all_gather(pack, 'tracer', axis=2, tiled=True)]
  transfers between devices with their start and end apart: 9 -> 9, of which waited for: 4 -> 5; matrix products, arithmetic and copies ran while one was open for 8% -> 4% of each run, Pallas kernels for 0% -> 0%
where the time goes in v3:
time: 106 us; the launch traced here: 105 us
  waiting for transfers between devices  49.3 us (47%)
  starting transfers between devices  18.6 us (18%)
  Pallas kernels  15.1 us (14%)
  between operations  14.3 us (13%)
  local copies, waits for them, and re-layouts  3.42 us (3%)
  other arithmetic  2.58 us (2%)
  matrix products  1.85 us (2%)
    all_gather x1, waiting for transfers between devices, on_device(): weather = lax.all_gather(pack, 'tracer', axis=2, tiled=True)  39.7 us
    ppermute x5, starting transfers between devices, passed_along(): return lax.ppermute(value, axis, pairs)  16.1 us
    pallas_call x2, Pallas kernels, advance(): pl.pallas_call(step_kernel, grid_spec=grid_spec, out_shape=out_shape, com...  15.1 us
    ppermute x5, waiting for transfers between devices, passed_along(): return lax.ppermute(value, axis, pairs)  9.65 us
    ppermute x3, starting transfers between devices, on_device(): shifted.append(lax.ppermute(control, 'band', pairs))  2.54 us
  transfers between devices with their start and end apart: 9, of which 5 were waited for; matrix products, arithmetic and copies ran while one was open for 4% of the time, Pallas kernels for 0%

profile of v3, /device:TPU:1, one launch (start us, length us, event | category | flops | bytes accessed | tf_op | source)
XLA Modules:
  0.0 105.3 jit_solution(4471818833376649596)
XLA Ops:
  7.2 0.0 copy-start
  7.2 0.0 copy-start.5
  7.2 0.0 all-gather.2.cloned.1.call-start
  7.3 0.7 slice.11
  8.0 4.5 %collective-permute-start.2 = (f32[1,48,128]{2,1,0:T(8,128)S(1)}, f32[1,48,128]{2,1,0:T(8,128)S(1)}, u32[]{:S(2)}, u32[]{:S(2)}) collective-permute-start(f32[1,48,128]{2,1,0:T(8,128)S(1)} %slice.11), channel_id=1, source_target_pairs={{0,1},{1,2},{2,3},{4,5},{5,6},{6,7},{8,9},{9,10},{10,11},{12,13},{... | collective-permute-start | bytes 73736 | tf_op jit(solution)/shard_map/ppermute | solution.py:14
  12.5 0.9 collective-permute-done.2
  13.4 2.0 %pad_maximum_fusion = f32[25,48,128]{2,1,0:T(8,128)} fusion(f32[1,48,128]{2,1,0:T(8,128)S(1)} %collective-permute-done.2, f32[8,48,128]{2,1,0:T(8,128)} %param.17, f32[8,48,128]{2,1,0:T(8,128)} %param.16, f32[8,48,128]{2,1,0:T(8,128)} %param.15), kind=kLoop, calls=%fused_computation.5 | loop fusion | flops 460800 | bytes 1228800 | tf_op jit(solution)/shard_map/concatenate | solution.py:131
  15.4 0.0 all-gather.2.cloned.1.call-update
  15.4 2.4 %collective-permute-start.3 = (f32[4,8,512]{2,1,0:T(8,128)}, f32[4,8,512]{2,1,0:T(8,128)S(1)}, u32[]{:S(2)}, u32[]{:S(2)}) collective-permute-start(f32[4,8,512]{2,1,0:T(8,128)} %param.10), channel_id=1, source_target_pairs={{0,1},{1,2},{2,3},{3,0},{4,5},{5,6},{6,7},{7,4},{8,9},{9,10},{10,1... | collective-permute-start | bytes 196616 | tf_op jit(solution)/shard_map/ppermute | solution.py:129
  17.8 0.0 collective-permute-start.5
  17.8 0.2 collective-permute-start.4
  18.0 1.2 %slice_bitcast_fusion = (f32[4,48,512]{2,1,0:T(8,128)S(1)}, f32[4,48,512]{2,1,0:T(8,128)S(1)}) fusion(f32[4,8,48,512]{3,2,1,0:T(8,128)} %q_ref.1), kind=kLoop, calls=%fused_computation.7 | loop fusion | bytes 1572864 | tf_op jit(solution)/shard_map/squeeze | solution.py:125
  19.2 3.9 %collective-permute-start.1 = (f32[4,48,512]{2,1,0:T(8,128)S(1)}, f32[4,48,512]{2,1,0:T(8,128)S(1)}, u32[]{:S(2)}, u32[]{:S(2)}) collective-permute-start(f32[4,48,512]{2,1,0:T(8,128)S(1)} %get-tuple-element.8), channel_id=1, source_target_pairs={{1,0},{2,1},{3,2},{5,4},{6,5},{7,6},{9,8},{10,9},{11,10},{13,12},{... | collective-permute-start | bytes 1179656 | tf_op jit(solution)/shard_map/ppermute | solution.py:14
  23.0 1.9 %collective-permute-start = (f32[4,48,512]{2,1,0:T(8,128)S(1)}, f32[4,48,512]{2,1,0:T(8,128)S(1)}, u32[]{:S(2)}, u32[]{:S(2)}) collective-permute-start(f32[4,48,512]{2,1,0:T(8,128)S(1)} %get-tuple-element.9), channel_id=1, source_target_pairs={{0,1},{1,2},{2,3},{4,5},{5,6},{6,7},{8,9},{9,10},{10,11},{12,13},{... | collective-permute-start | bytes 1179656 | tf_op jit(solution)/shard_map/ppermute | solution.py:14
  25.1 0.7 constant_dynamic-slice_fusion.4
  25.8 0.2 fusion.5
  26.0 0.3 fusion.3
  26.3 0.2 fusion.11
  26.5 0.6 compare_convert_fusion.north_ref
  27.1 0.0 collective-permute-done.3
  27.1 0.2 convolution_add_fusion.1
  27.3 0.2 fusion.12
  27.5 0.8 fusion.2.src_ref
  28.3 1.3 %collective-permute-done.qs_ref = f32[4,48,512]{2,1,0:T(8,128)S(1)} collective-permute-done((f32[4,48,512]{2,1,0:T(8,128)S(1)}, f32[4,48,512]{2,1,0:T(8,128)S(1)}, u32[]{:S(2)}, u32[]{:S(2)}) %collective-permute-start) | collective-permute-done | bytes 393248 | tf_op jit(solution)/shard_map/ppermute | solution.py:14
  29.7 39.7 %all-gather.2.cloned.1.call-done.wx_ref = f32[25,48,512]{2,1,0:T(8,128)} async-done(((f32[25,48,128]{2,1,0:T(8,128)}), f32[25,48,512]{2,1,0:T(8,128)}) %all-gather.2.cloned.1.call-update) | async-done | bytes 2457616 | tf_op jit(solution)/shard_map/all_gather | solution.py:132
  69.3 7.6 %shard_map.104 = (f32[4,8,48,512]{3,2,1,0:T(8,128)}, f32[4,48,512]{2,1,0:T(8,128)}, f32[4,48,512]{2,1,0:T(8,128)}) custom-call(f32[8]{0:T(128)} %compare_convert_fusion.north_ref, f32[4,8,48,512]{3,2,1,0:T(8,128)} %q_ref.1, f32[4,48,512]{2,1,0:T(8,128)} %copy-done.4, f32[4,48,512]{2,1,0:T(8,128)} %copy-done.3, ...), custom_call_target="tpu_custom_call" | custom-call | tf_op jit(solution)/shard_map/pallas_call | solution.py:99
  77.0 3.9 %collective-permute-start.6 = (f32[4,48,512]{2,1,0:T(8,128)}, f32[4,48,512]{2,1,0:T(8,128)S(1)}, u32[]{:S(2)}, u32[]{:S(2)}) collective-permute-start(f32[4,48,512]{2,1,0:T(8,128)} %get-tuple-element.6), channel_id=1, source_target_pairs={{0,1},{1,2},{2,3},{4,5},{5,6},{6,7},{8,9},{9,10},{10,11},{12,13},{... | collective-permute-start | bytes 1179656 | tf_op jit(solution)/shard_map/ppermute | solution.py:14
  80.8 1.9 %collective-permute-start.7 = (f32[4,48,512]{2,1,0:T(8,128)}, f32[4,48,512]{2,1,0:T(8,128)S(1)}, u32[]{:S(2)}, u32[]{:S(2)}) collective-permute-start(f32[4,48,512]{2,1,0:T(8,128)} %get-tuple-element.7), channel_id=1, source_target_pairs={{1,0},{2,1},{3,2},{5,4},{6,5},{7,6},{9,8},{10,9},{11,10},{13,12},{... | collective-permute-start | bytes 1179656 | tf_op jit(solution)/shard_map/ppermute | solution.py:14
  82.7 3.1 %collective-permute-done.6.qs_ref = f32[4,48,512]{2,1,0:T(8,128)S(1)} collective-permute-done((f32[4,48,512]{2,1,0:T(8,128)}, f32[4,48,512]{2,1,0:T(8,128)S(1)}, u32[]{:S(2)}, u32[]{:S(2)}) %collective-permute-start.6) | collective-permute-done | bytes 393248 | tf_op jit(solution)/shard_map/ppermute | solution.py:14
  85.8 4.3 %collective-permute-done.7.qn_ref = f32[4,48,512]{2,1,0:T(8,128)S(1)} collective-permute-done((f32[4,48,512]{2,1,0:T(8,128)}, f32[4,48,512]{2,1,0:T(8,128)S(1)}, u32[]{:S(2)}, u32[]{:S(2)}) %collective-permute-start.7) | collective-permute-done | bytes 393248 | tf_op jit(solution)/shard_map/ppermute | solution.py:14
  90.1 0.7 copy-done.2
  90.9 7.5 %shard_map.105 = f32[4,8,48,512]{3,2,1,0:T(8,128)} custom-call(f32[8]{0:T(128)} %compare_convert_fusion.north_ref, f32[4,8,48,512]{3,2,1,0:T(8,128)} %get-tuple-element.5.q_ref, f32[4,48,512]{2,1,0:T(8,128)} %copy-done.1, f32[4,48,512]{2,1,0:T(8,128)} %copy-done.2, f32[25,48,512]{2,1,0:T(8,128)} %all-gather.2.cloned.1.call-done.wx_ref, ...), custom_call_target="tpu_custom_call" | custom-call | tf_op jit(solution)/shard_map/pallas_call | solution.py:99
  (17 shorter events, 0.1 us)
Async XLA Ops:
  7.2 18.6 %copy-start = (f32[8,8,8]{2,1,0:T(8,128)S(1)}, f32[8,8,8]{2,1,0:T(8,128)}, u32[]{:S(2)}) copy-start(f32[8,8,8]{2,1,0:T(8,128)} %param.11) | copy-start | bytes 6148
  7.2 19.1 %copy-start.5 = (f32[4,8,512]{2,1,0:T(8,128)S(1)}, f32[4,8,512]{2,1,0:T(8,128)}, u32[]{:S(2)}) copy-start(f32[4,8,512]{2,1,0:T(8,128)} %param.10) | copy-start | bytes 196612
  7.2 18.8 %copy-start.7 = (f32[4,22]{1,0:T(4,128)S(1)}, f32[4,22]{1,0:T(4,128)}, u32[]{:S(2)}) copy-start(f32[4,22]{1,0:T(4,128)} %param.14) | copy-start | bytes 1060
  7.2 18.8 %copy-start.6 = (s32[8,512]{1,0:T(8,128)S(1)}, s32[8,512]{1,0:T(8,128)}, u32[]{:S(2)}) copy-start(s32[8,512]{1,0:T(8,128)} %param.13) | copy-start | bytes 49156
  7.2 62.1 %all-gather.2.cloned.1.call-start = ((), (), s32[]{:S(2)}) async-start(), calls=%async_computation | async-start | bytes 3072000 | tf_op jit(solution)/shard_map/all_gather | solution.py:132
  8.0 5.4 %collective-permute-start.2 = (f32[1,48,128]{2,1,0:T(8,128)S(1)}, f32[1,48,128]{2,1,0:T(8,128)S(1)}, u32[]{:S(2)}, u32[]{:S(2)}) collective-permute-start(f32[1,48,128]{2,1,0:T(8,128)S(1)} %slice.11), channel_id=1, source_target_pairs={{0,1},{1,2},{2,3},{4,5},{5,6},{6,7},{8,9},{9,10},{10,11},{12,13},{... | collective-permute-start | bytes 73736 | tf_op jit(solution)/shard_map/ppermute | solution.py:14
  15.4 11.6 %collective-permute-start.3 = (f32[4,8,512]{2,1,0:T(8,128)}, f32[4,8,512]{2,1,0:T(8,128)S(1)}, u32[]{:S(2)}, u32[]{:S(2)}) collective-permute-start(f32[4,8,512]{2,1,0:T(8,128)} %param.10), channel_id=1, source_target_pairs={{0,1},{1,2},{2,3},{3,0},{4,5},{5,6},{6,7},{7,4},{8,9},{9,10},{10,1... | collective-permute-start | bytes 196616 | tf_op jit(solution)/shard_map/ppermute | solution.py:129
  17.8 9.5 %collective-permute-start.5 = (f32[4,8,512]{2,1,0:T(8,128)}, f32[4,8,512]{2,1,0:T(8,128)S(1)}, u32[]{:S(2)}, u32[]{:S(2)}) collective-permute-start(f32[4,8,512]{2,1,0:T(8,128)} %param.10), channel_id=1, source_target_pairs={{0,3},{1,0},{2,1},{3,2},{4,7},{5,4},{6,5},{7,6},{8,11},{9,8},{10,9... | collective-permute-start | bytes 196616 | tf_op jit(solution)/shard_map/ppermute | solution.py:129
  17.8 9.7 %collective-permute-start.4 = (f32[4,8,512]{2,1,0:T(8,128)}, f32[4,8,512]{2,1,0:T(8,128)S(1)}, u32[]{:S(2)}, u32[]{:S(2)}) collective-permute-start(f32[4,8,512]{2,1,0:T(8,128)} %param.10), channel_id=1, source_target_pairs={{0,2},{1,3},{2,0},{3,1},{4,6},{5,7},{6,4},{7,5},{8,10},{9,11},{10,... | collective-permute-start | bytes 196616 | tf_op jit(solution)/shard_map/ppermute | solution.py:129
  19.2 9.2 %collective-permute-start.1 = (f32[4,48,512]{2,1,0:T(8,128)S(1)}, f32[4,48,512]{2,1,0:T(8,128)S(1)}, u32[]{:S(2)}, u32[]{:S(2)}) collective-permute-start(f32[4,48,512]{2,1,0:T(8,128)S(1)} %get-tuple-element.8), channel_id=1, source_target_pairs={{1,0},{2,1},{3,2},{5,4},{6,5},{7,6},{9,8},{10,9},{11,10},{13,12},{... | collective-permute-start | bytes 1179656 | tf_op jit(solution)/shard_map/ppermute | solution.py:14
  23.0 6.6 %collective-permute-start = (f32[4,48,512]{2,1,0:T(8,128)S(1)}, f32[4,48,512]{2,1,0:T(8,128)S(1)}, u32[]{:S(2)}, u32[]{:S(2)}) collective-permute-start(f32[4,48,512]{2,1,0:T(8,128)S(1)} %get-tuple-element.9), channel_id=1, source_target_pairs={{0,1},{1,2},{2,3},{4,5},{5,6},{6,7},{8,9},{9,10},{10,11},{12,13},{... | collective-permute-start | bytes 1179656 | tf_op jit(solution)/shard_map/ppermute | solution.py:14
  28.3 41.0 %copy-start.3 = (f32[4,48,512]{2,1,0:T(8,128)}, f32[4,48,512]{2,1,0:T(8,128)S(1)}, u32[]{:S(2)}) copy-start(f32[4,48,512]{2,1,0:T(8,128)S(1)} %collective-permute-done.1.qn_ref) | copy-start | bytes 1179652
  29.7 39.7 %copy-start.4 = (f32[4,48,512]{2,1,0:T(8,128)}, f32[4,48,512]{2,1,0:T(8,128)S(1)}, u32[]{:S(2)}) copy-start(f32[4,48,512]{2,1,0:T(8,128)S(1)} %collective-permute-done.qs_ref) | copy-start | bytes 1179652
  77.0 8.9 %collective-permute-start.6 = (f32[4,48,512]{2,1,0:T(8,128)}, f32[4,48,512]{2,1,0:T(8,128)S(1)}, u32[]{:S(2)}, u32[]{:S(2)}) collective-permute-start(f32[4,48,512]{2,1,0:T(8,128)} %get-tuple-element.6), channel_id=1, source_target_pairs={{0,1},{1,2},{2,3},{4,5},{5,6},{6,7},{8,9},{9,10},{10,11},{12,13},{... | collective-permute-start | bytes 1179656 | tf_op jit(solution)/shard_map/ppermute | solution.py:14
  80.8 9.3 %collective-permute-start.7 = (f32[4,48,512]{2,1,0:T(8,128)}, f32[4,48,512]{2,1,0:T(8,128)S(1)}, u32[]{:S(2)}, u32[]{:S(2)}) collective-permute-start(f32[4,48,512]{2,1,0:T(8,128)} %get-tuple-element.7), channel_id=1, source_target_pairs={{1,0},{2,1},{3,2},{5,4},{6,5},{7,6},{9,8},{10,9},{11,10},{13,12},{... | collective-permute-start | bytes 1179656 | tf_op jit(solution)/shard_map/ppermute | solution.py:14
  85.8 4.3 %copy-start.1 = (f32[4,48,512]{2,1,0:T(8,128)}, f32[4,48,512]{2,1,0:T(8,128)S(1)}, u32[]{:S(2)}) copy-start(f32[4,48,512]{2,1,0:T(8,128)S(1)} %collective-permute-done.6.qs_ref) | copy-start | bytes 1179652
  90.1 0.7 copy-start.2
Sparse Core Ops, SparseCore 0:
  15.6 53.7 all-gather.1

commit v4 on v3

--- a/solution.py
+++ b/solution.py
@@ -12,6 +12,23 @@
     count = lax.axis_size(axis)
     pairs = [(i, i + by) for i in range(count) if 0 <= i + by < count]
     return lax.ppermute(value, axis, pairs)
+
+
+def relay_gather(x, axis):
+    count = lax.axis_size(axis)
+    me = lax.axis_index(axis)
+    rows, levels, width = x.shape
+    buf = jnp.zeros((rows, levels, (count + 1) * width), x.dtype)
+    buf = lax.dynamic_update_slice(buf, x, (0, 0, me * width))
+    right = left = x
+    for r in range(1, count):
+        right = lax.ppermute(right, axis, [(i, i + 1) for i in range(r - 1, count - 1)])
+        left = lax.ppermute(left, axis, [(j, j - 1) for j in range(1, count - r + 1)])
+        slot = jnp.where(me - r >= 0, me - r, count)
+        buf = lax.dynamic_update_slice(buf, right, (0, 0, slot * width))
+        slot = jnp.where(me + r < count, me + r, count)
+        buf = lax.dynamic_update_slice(buf, left, (0, 0, slot * width))
+    return buf
 
 
 def step_kernel(north_ref, q_ref, qs_ref, qn_ref, wx_ref, src_ref, *rest):
@@ -90,7 +107,7 @@
             row,
             edge,
             edge,
-            pl.BlockSpec(weather.shape, lambda k: (0, 0, 0)),
+            pl.BlockSpec(weather.shape[:2] + (lon,), lambda k: (0, 0, 0)),
             pl.BlockSpec((1, lat_rows, lon), lambda k: (k, 0, 0)),
         ],
         out_specs=out_specs,
@@ -129,7 +146,7 @@
         shifted.append(lax.ppermute(control, "band", pairs))
 
     pack = jnp.concatenate([zonal_courant, meridional_courant, vertical_diffusion, south_v], axis=0)
-    weather = lax.all_gather(pack, "tracer", axis=2, tiled=True)
+    weather = relay_gather(pack, "tracer")
 
     choose = (
         tile_index[:, :, None] == lax.broadcasted_iota(jnp.int32, (1, 1, tiles_count), 2)

time: 106 us -> 104 us (0.981)
  local copies, waits for them, and re-layouts: 3.42 us -> 17 us
  between operations: 14.3 us -> 0.98 us
  waiting for transfers between devices: 49.3 us -> 36.2 us
  starting transfers between devices: 18.6 us -> 26.3 us
  matrix products: 1.85 us -> 7.19 us
  other arithmetic: 2.58 us -> 0.54 us
    all_gather x1 -> x0, waiting for transfers between devices: 39.7 us -> none  [on_device(): weather = lax.all_gather(pack, 'tracer', axis=2, tiled=True)]
    ppermute x0 -> x6, waiting for transfers between devices: none -> 30.1 us  [the longest x3 23.9 us: relay_gather(): lax.ppermute(left, axis, [(j, j - 1) for j in range(1, count - r + 1)])]
    ppermute x0 -> x6, starting transfers between devices: none -> 10.6 us  [the longest x3 6.76 us: relay_gather(): lax.ppermute(right, axis, [(i, i + 1) for i in range(r - 1, count - 1)])]
    unnamed x16 -> x23, local copies, waits for them, and re-layouts: 0.77 us -> 7.97 us
    dynamic_update_slice x0 -> x7, local copies, waits for them, and re-layouts: none -> 4.68 us  [the longest x3 2.29 us: relay_gather(): buf = lax.dynamic_update_slice(buf, right, (0, 0, slot * width))]
    dot_general x4, matrix products: 1.4 us -> 5.38 us  [on_device(): term = jnp.einsum('jm,kmn->kjn', tile, part, precision=exact_dot)]
    ppermute x5, waiting for transfers between devices: 9.65 us -> 6.03 us  [passed_along(): return lax.ppermute(value, axis, pairs)]
    ppermute x5, starting transfers between devices: 16.1 us -> 12.9 us  [passed_along(): return lax.ppermute(value, axis, pairs)]
  transfers between devices with their start and end apart: 9 -> 14, of which waited for: 5 -> 6; matrix products, arithmetic and copies ran while one was open for 4% -> 21% of each run, Pallas kernels for 0% -> 0%
where the time goes in v4:
time: 104 us; the launch traced here: 103 us
  waiting for transfers between devices  36.2 us (35%)
  starting transfers between devices  26.3 us (25%)
  local copies, waits for them, and re-layouts  17 us (16%)
  Pallas kernels  15.2 us (15%)
  matrix products  7.19 us (7%)
    ppermute x3, waiting for transfers between devices, relay_gather(): lax.ppermute(left, axis, [(j, j - 1) for j in range(1, count - r + 1)])  23.9 us
    pallas_call x2, Pallas kernels, advance(): pl.pallas_call(step_kernel, grid_spec=grid_spec, out_shape=out_shape, com...  15.2 us
    ppermute x5, starting transfers between devices, passed_along(): return lax.ppermute(value, axis, pairs)  12.9 us
    unnamed x23, local copies, waits for them, and re-layouts  7.97 us
    ppermute x3, starting transfers between devices, relay_gather(): lax.ppermute(right, axis, [(i, i + 1) for i in range(r - 1, count - 1)])  6.76 us
    ppermute x3, waiting for transfers between devices, relay_gather(): lax.ppermute(right, axis, [(i, i + 1) for i in range(r - 1, count - 1)])  6.22 us
    ppermute x5, waiting for transfers between devices, passed_along(): return lax.ppermute(value, axis, pairs)  6.03 us
    dot_general x4, matrix products, on_device(): term = jnp.einsum('jm,kmn->kjn', tile, part, precision=exact_dot)  5.38 us
  transfers between devices with their start and end apart: 14, of which 6 were waited for; matrix products, arithmetic and copies ran while one was open for 21% of the time, Pallas kernels for 0%

profile of v4, /device:TPU:1, one launch (start us, length us, event | category | flops | bytes accessed | tf_op | source)
XLA Modules:
  0.0 103.3 jit_solution(6378846587611580709)
XLA Ops:
  0.6 2.7 %collective-permute-start.9 = (f32[4,8,512]{2,1,0:T(8,128)}, f32[4,8,512]{2,1,0:T(8,128)S(1)}, u32[]{:S(2)}, u32[]{:S(2)}) collective-permute-start(f32[4,8,512]{2,1,0:T(8,128)} %param.10), channel_id=1, source_target_pairs={{0,1},{1,2},{2,3},{3,0},{4,5},{5,6},{6,7},{7,4},{8,9},{9,10},{10,1... | collective-permute-start | bytes 196616 | tf_op jit(solution)/shard_map/ppermute | solution.py:146
  4.2 3.5 %collective-permute-start.2 = (f32[1,48,128]{2,1,0:T(8,128)S(1)}, f32[1,48,128]{2,1,0:T(8,128)S(1)}, u32[]{:S(2)}, u32[]{:S(2)}) collective-permute-start(f32[1,48,128]{2,1,0:T(8,128)S(1)} %slice.11), channel_id=1, source_target_pairs={{0,1},{1,2},{2,3},{4,5},{5,6},{6,7},{8,9},{9,10},{10,11},{12,13},{... | collective-permute-start | bytes 73736 | tf_op jit(solution)/shard_map/ppermute | solution.py:14
  7.8 1.6 %constant_dynamic-update-slice_fusion.3 = f32[25,48,128]{2,1,0:T(8,128)} fusion(f32[8,48,128]{2,1,0:T(8,128)} %param.15), kind=kLoop, calls=%fused_computation.15 | loop fusion | bytes 393216
  9.4 1.6 %constant_dynamic-update-slice_fusion.2 = f32[25,48,128]{2,1,0:T(8,128)} fusion(f32[25,48,128]{2,1,0:T(8,128)} %constant_dynamic-update-slice_fusion.3, f32[8,48,128]{2,1,0:T(8,128)} %param.16), kind=kLoop, calls=%fused_computation.14 | loop fusion | bytes 393216
  11.0 1.6 %constant_dynamic-update-slice_fusion.1 = f32[25,48,128]{2,1,0:T(8,128)} fusion(f32[25,48,128]{2,1,0:T(8,128)} %constant_dynamic-update-slice_fusion.2, f32[8,48,128]{2,1,0:T(8,128)} %param.17), kind=kLoop, calls=%fused_computation.13 | loop fusion | bytes 393216
  14.2 4.6 %collective-permute-start.3 = (f32[25,48,128]{2,1,0:T(8,128)}, f32[25,48,128]{2,1,0:T(8,128)}, u32[]{:S(2)}, u32[]{:S(2)}) collective-permute-start(f32[25,48,128]{2,1,0:T(8,128)} %constant_dynamic-update-slice_fusion), channel_id=1, source_target_pairs={{0,4},{4,8},{8,12},{1,5},{5,9},{9,13},{2,6},{6,10},{10,14},{3,7},{... | collective-permute-start | bytes 1843208 | tf_op jit(solution)/shard_map/ppermute | solution.py:25
  18.7 1.7 %fusion.11 = f32[8,4,512]{2,0,1:T(8,128)} fusion(f32[8,8,1]{1,0,2:T(8,128)S(1)} %bitcast.39, f32[4,8,512]{2,1,0:T(8,128)} %param.10), kind=kOutput, calls=%fused_computation.33 | convolution fusion | flops 1572864 | bytes 131328 | tf_op jit(solution)/shard_map/jm,kmn->kjn/dot_general | solution.py:160
  20.4 1.3 %collective-permute-start.4 = (f32[25,48,128]{2,1,0:T(8,128)}, f32[25,48,128]{2,1,0:T(8,128)}, u32[]{:S(2)}, u32[]{:S(2)}) collective-permute-start(f32[25,48,128]{2,1,0:T(8,128)} %constant_dynamic-update-slice_fusion), channel_id=1, source_target_pairs={{4,0},{8,4},{12,8},{5,1},{9,5},{13,9},{6,2},{10,6},{14,10},{7,3},{... | collective-permute-start | bytes 1843208 | tf_op jit(solution)/shard_map/ppermute | solution.py:26
  21.7 1.6 %fusion.3 = f32[8,512,4]{1,2,0:T(4,128)} fusion(s32[8,512]{1,0:T(8,128)} %param.13, f32[4,22]{1,0:T(4,128)} %param.14), kind=kOutput, calls=%fused_computation.8 | convolution fusion | flops 4415488 | bytes 82272 | tf_op jit(solution)/shard_map/kr,jnr->kjn/dot_general | solution.py:166
  23.3 2.1 %slice_bitcast_fusion = (f32[4,48,512]{2,1,0:T(8,128)}, f32[4,48,512]{2,1,0:T(8,128)}) fusion(f32[4,8,48,512]{3,2,1,0:T(8,128)} %q_ref.1), kind=kLoop, calls=%fused_computation.6 | loop fusion | bytes 1572864 | tf_op jit(solution)/shard_map/squeeze | solution.py:142
  25.3 6.2 %collective-permute-done.3 = f32[25,48,128]{2,1,0:T(8,128)} collective-permute-done((f32[25,48,128]{2,1,0:T(8,128)}, f32[25,48,128]{2,1,0:T(8,128)}, u32[]{:S(2)}, u32[]{:S(2)}) %collective-permute-start.3) | collective-permute-done | bytes 614432 | tf_op jit(solution)/shard_map/ppermute | solution.py:25
  31.6 1.5 %collective-permute-start.5 = (f32[25,48,128]{2,1,0:T(8,128)}, f32[25,48,128]{2,1,0:T(8,128)}, u32[]{:S(2)}, u32[]{:S(2)}) collective-permute-start(f32[25,48,128]{2,1,0:T(8,128)} %collective-permute-done.3), channel_id=1, source_target_pairs={{4,8},{8,12},{5,9},{9,13},{6,10},{10,14},{7,11},{11,15},{20,24},{2... | collective-permute-start | bytes 1843208 | tf_op jit(solution)/shard_map/ppermute | solution.py:25
  33.8 1.2 %constant_dynamic-update-slice_fusion.10 = f32[25,48,640]{2,1,0:T(8,128)S(1)} fusion(f32[25,48,640]{2,1,0:T(8,128)S(1)} %broadcast_in_dim.2, f32[25,48,128]{2,1,0:T(8,128)} %constant_dynamic-update-slice_fusion, s32[]{:T(128)S(6)} %select_n.75), kind=kLoop, calls=%fused_computation.27 | loop fusion | bytes 1228804 | tf_op jit(solution)/shard_map/dynamic_update_slice | solution.py:22
  35.6 1.9 %collective-permute-start = (f32[4,48,512]{2,1,0:T(8,128)S(1)}, f32[4,48,512]{2,1,0:T(8,128)S(1)}, u32[]{:S(2)}, u32[]{:S(2)}) collective-permute-start(f32[4,48,512]{2,1,0:T(8,128)S(1)} %copy-done.6), channel_id=1, source_target_pairs={{0,1},{1,2},{2,3},{4,5},{5,6},{6,7},{8,9},{9,10},{10,11},{12,13},{... | collective-permute-start | bytes 1179656 | tf_op jit(solution)/shard_map/ppermute | solution.py:14
  38.4 1.3 %collective-permute-start.6 = (f32[25,48,128]{2,1,0:T(8,128)}, f32[25,48,128]{2,1,0:T(8,128)S(1)}, u32[]{:S(2)}, u32[]{:S(2)}) collective-permute-start(f32[25,48,128]{2,1,0:T(8,128)} %collective-permute-done.4), channel_id=1, source_target_pairs={{4,0},{8,4},{5,1},{9,5},{6,2},{10,6},{7,3},{11,7},{20,16},{24,20},... | collective-permute-start | bytes 1843208 | tf_op jit(solution)/shard_map/ppermute | solution.py:26
  39.7 1.0 convolution_add_fusion.1
  40.8 2.3 %collective-permute-start.1 = (f32[4,48,512]{2,1,0:T(8,128)S(1)}, f32[4,48,512]{2,1,0:T(8,128)}, u32[]{:S(2)}, u32[]{:S(2)}) collective-permute-start(f32[4,48,512]{2,1,0:T(8,128)S(1)} %copy-done.5), channel_id=1, source_target_pairs={{1,0},{2,1},{3,2},{5,4},{6,5},{7,6},{9,8},{10,9},{11,10},{13,12},{... | collective-permute-start | bytes 1179656 | tf_op jit(solution)/shard_map/ppermute | solution.py:14
  43.1 1.0 fusion.12
  44.9 1.7 %fusion.2.src_ref = f32[4,8,512]{2,1,0:T(8,128)} fusion(f32[8,4,512]{2,0,1:T(8,128)S(1)} %fusion.12, f32[8,4,512]{2,0,1:T(8,128)S(1)} %convolution_add_fusion.1, f32[8,8,1]{1,0,2:T(8,128)S(1)} %bitcast.40, f32[4,8,512]{2,1,0:T(8,128)} %collective-permute-done.10, f32[8,512,4]{1,2,0:T(4,128)S(1)} %copy-done.9), kind=kOutput, calls=%fused_computation.3 | convolution fusion | flops 1622016 | bytes 327936 | tf_op jit(solution)/shard_map/jm,kmn->kjn/dot_general | solution.py:160
  46.5 11.6 %collective-permute-done.6 = f32[25,48,128]{2,1,0:T(8,128)S(1)} collective-permute-done((f32[25,48,128]{2,1,0:T(8,128)}, f32[25,48,128]{2,1,0:T(8,128)S(1)}, u32[]{:S(2)}, u32[]{:S(2)}) %collective-permute-start.6) | collective-permute-done | bytes 614432 | tf_op jit(solution)/shard_map/ppermute | solution.py:26
  58.2 1.3 %collective-permute-start.8 = (f32[25,48,128]{2,1,0:T(8,128)S(1)}, f32[25,48,128]{2,1,0:T(8,128)S(1)}, u32[]{:S(2)}, u32[]{:S(2)}) collective-permute-start(f32[25,48,128]{2,1,0:T(8,128)S(1)} %collective-permute-done.6), channel_id=1, source_target_pairs={{4,0},{5,1},{6,2},{7,3},{20,16},{21,17},{22,18},{23,19}} | collective-permute-start | bytes 1843208 | tf_op jit(solution)/shard_map/ppermute | solution.py:26
  59.5 1.1 %constant_dynamic-update-slice_fusion.9 = f32[25,48,640]{2,1,0:T(8,128)S(1)} fusion(f32[25,48,640]{2,1,0:T(8,128)S(1)} %constant_dynamic-update-slice_fusion.10, f32[25,48,128]{2,1,0:T(8,128)} %collective-permute-done.3, s32[]{:T(128)S(6)} %select_n.77), kind=kLoop, calls=%fused_computation.26 | loop fusion | bytes 1228804 | tf_op jit(solution)/shard_map/dynamic_update_slice | solution.py:28
  60.6 1.1 %constant_dynamic-update-slice_fusion.8 = f32[25,48,640]{2,1,0:T(8,128)S(1)} fusion(f32[25,48,640]{2,1,0:T(8,128)S(1)} %constant_dynamic-update-slice_fusion.9, f32[25,48,128]{2,1,0:T(8,128)} %collective-permute-done.4, s32[]{:T(128)S(6)} %select_n.79), kind=kLoop, calls=%fused_computation.25 | loop fusion | bytes 1228804 | tf_op jit(solution)/shard_map/dynamic_update_slice | solution.py:30
  61.7 1.1 %constant_dynamic-update-slice_fusion.7 = f32[25,48,640]{2,1,0:T(8,128)S(1)} fusion(f32[25,48,640]{2,1,0:T(8,128)S(1)} %constant_dynamic-update-slice_fusion.8, f32[25,48,128]{2,1,0:T(8,128)} %collective-permute-done.5, s32[]{:T(128)S(6)} %select_n.81), kind=kLoop, calls=%fused_computation.24 | loop fusion | bytes 1228804 | tf_op jit(solution)/shard_map/dynamic_update_slice | solution.py:28
  63.0 11.4 %collective-permute-done.8 = f32[25,48,128]{2,1,0:T(8,128)S(1)} collective-permute-done((f32[25,48,128]{2,1,0:T(8,128)S(1)}, f32[25,48,128]{2,1,0:T(8,128)S(1)}, u32[]{:S(2)}, u32[]{:S(2)}) %collective-permute-start.8) | collective-permute-done | bytes 614432 | tf_op jit(solution)/shard_map/ppermute | solution.py:26
  74.4 1.6 %copy-done.1 = f32[25,48,640]{2,1,0:T(8,128)} copy-done((f32[25,48,640]{2,1,0:T(8,128)}, f32[25,48,640]{2,1,0:T(8,128)S(1)}, u32[]{:S(2)}) %copy-start.1) | copy-done | bytes 3072024
  76.2 7.7 %shard_map.104 = (f32[4,8,48,512]{3,2,1,0:T(8,128)}, f32[4,48,512]{2,1,0:T(8,128)}, f32[4,48,512]{2,1,0:T(8,128)}) custom-call(f32[8]{0:T(128)} %compare_convert_fusion.north_ref, f32[4,8,48,512]{3,2,1,0:T(8,128)} %q_ref.1, f32[4,48,512]{2,1,0:T(8,128)} %copy-done.4, f32[4,48,512]{2,1,0:T(8,128)} %collective-permute-done.1.qn_ref, f32[25,48,640]{2,1,0:T(8,128)} %copy-done.1, ...), custom_call_target="tpu_custom_call" | custom-call | tf_op jit(solution)/shard_map/pallas_call | solution.py:116
  83.8 1.9 %collective-permute-start.12 = (f32[4,48,512]{2,1,0:T(8,128)}, f32[4,48,512]{2,1,0:T(8,128)S(1)}, u32[]{:S(2)}, u32[]{:S(2)}) collective-permute-start(f32[4,48,512]{2,1,0:T(8,128)} %get-tuple-element.6), channel_id=1, source_target_pairs={{0,1},{1,2},{2,3},{4,5},{5,6},{6,7},{8,9},{9,10},{10,11},{12,13},{... | collective-permute-start | bytes 1179656 | tf_op jit(solution)/shard_map/ppermute | solution.py:14
  85.7 3.3 %collective-permute-start.13 = (f32[4,48,512]{2,1,0:T(8,128)}, f32[4,48,512]{2,1,0:T(8,128)S(1)}, u32[]{:S(2)}, u32[]{:S(2)}) collective-permute-start(f32[4,48,512]{2,1,0:T(8,128)} %get-tuple-element.7), channel_id=1, source_target_pairs={{1,0},{2,1},{3,2},{5,4},{6,5},{7,6},{9,8},{10,9},{11,10},{13,12},{... | collective-permute-start | bytes 1179656 | tf_op jit(solution)/shard_map/ppermute | solution.py:14
  89.0 1.7 %collective-permute-done.12.qs_ref = f32[4,48,512]{2,1,0:T(8,128)S(1)} collective-permute-done((f32[4,48,512]{2,1,0:T(8,128)}, f32[4,48,512]{2,1,0:T(8,128)S(1)}, u32[]{:S(2)}, u32[]{:S(2)}) %collective-permute-start.12) | collective-permute-done | bytes 393248 | tf_op jit(solution)/shard_map/ppermute | solution.py:14
  90.7 4.3 %collective-permute-done.13.qn_ref = f32[4,48,512]{2,1,0:T(8,128)S(1)} collective-permute-done((f32[4,48,512]{2,1,0:T(8,128)}, f32[4,48,512]{2,1,0:T(8,128)S(1)}, u32[]{:S(2)}, u32[]{:S(2)}) %collective-permute-start.13) | collective-permute-done | bytes 393248 | tf_op jit(solution)/shard_map/ppermute | solution.py:14
  95.8 7.5 %shard_map.105 = f32[4,8,48,512]{3,2,1,0:T(8,128)} custom-call(f32[8]{0:T(128)} %compare_convert_fusion.north_ref, f32[4,8,48,512]{3,2,1,0:T(8,128)} %get-tuple-element.5.q_ref, f32[4,48,512]{2,1,0:T(8,128)} %copy-done.2, f32[4,48,512]{2,1,0:T(8,128)} %copy-done.3, f32[25,48,640]{2,1,0:T(8,128)} %copy-done.1, f32[4,8,512]{2,1,0:T(8,128)} %fusion.2.src_ref), custom_call_target="tpu_custom_call" | custom-call | tf_op jit(solution)/shard_map/pallas_call | solution.py:116
  (41 shorter events, 6.4 us)
Async XLA Ops:
  0.6 12.7 %copy-start = (f32[8,8,8]{2,1,0:T(8,128)S(1)}, f32[8,8,8]{2,1,0:T(8,128)}, u32[]{:S(2)}) copy-start(f32[8,8,8]{2,1,0:T(8,128)} %param.11) | copy-start | bytes 6148
  0.6 34.3 %collective-permute-start.9 = (f32[4,8,512]{2,1,0:T(8,128)}, f32[4,8,512]{2,1,0:T(8,128)S(1)}, u32[]{:S(2)}, u32[]{:S(2)}) collective-permute-start(f32[4,8,512]{2,1,0:T(8,128)} %param.10), channel_id=1, source_target_pairs={{0,1},{1,2},{2,3},{3,0},{4,5},{5,6},{6,7},{7,4},{8,9},{9,10},{10,1... | collective-permute-start | bytes 196616 | tf_op jit(solution)/shard_map/ppermute | solution.py:146
  3.3 37.5 %collective-permute-start.11 = (f32[4,8,512]{2,1,0:T(8,128)}, f32[4,8,512]{2,1,0:T(8,128)}, u32[]{:S(2)}, u32[]{:S(2)}) collective-permute-start(f32[4,8,512]{2,1,0:T(8,128)} %param.10), channel_id=1, source_target_pairs={{0,3},{1,0},{2,1},{3,2},{4,7},{5,4},{6,5},{7,6},{8,11},{9,8},{10,9... | collective-permute-start | bytes 196616 | tf_op jit(solution)/shard_map/ppermute | solution.py:146
  3.3 41.6 %collective-permute-start.10 = (f32[4,8,512]{2,1,0:T(8,128)}, f32[4,8,512]{2,1,0:T(8,128)}, u32[]{:S(2)}, u32[]{:S(2)}) collective-permute-start(f32[4,8,512]{2,1,0:T(8,128)} %param.10), channel_id=1, source_target_pairs={{0,2},{1,3},{2,0},{3,1},{4,6},{5,7},{6,4},{7,5},{8,10},{9,11},{10,... | collective-permute-start | bytes 196616 | tf_op jit(solution)/shard_map/ppermute | solution.py:146
  4.2 9.3 %collective-permute-start.2 = (f32[1,48,128]{2,1,0:T(8,128)S(1)}, f32[1,48,128]{2,1,0:T(8,128)S(1)}, u32[]{:S(2)}, u32[]{:S(2)}) collective-permute-start(f32[1,48,128]{2,1,0:T(8,128)S(1)} %slice.11), channel_id=1, source_target_pairs={{0,1},{1,2},{2,3},{4,5},{5,6},{6,7},{8,9},{9,10},{10,11},{12,13},{... | collective-permute-start | bytes 73736 | tf_op jit(solution)/shard_map/ppermute | solution.py:14
  14.2 17.4 %collective-permute-start.3 = (f32[25,48,128]{2,1,0:T(8,128)}, f32[25,48,128]{2,1,0:T(8,128)}, u32[]{:S(2)}, u32[]{:S(2)}) collective-permute-start(f32[25,48,128]{2,1,0:T(8,128)} %constant_dynamic-update-slice_fusion), channel_id=1, source_target_pairs={{0,4},{4,8},{8,12},{1,5},{5,9},{9,13},{2,6},{6,10},{10,14},{3,7},{... | collective-permute-start | bytes 1843208 | tf_op jit(solution)/shard_map/ppermute | solution.py:25
  20.4 18.0 %collective-permute-start.4 = (f32[25,48,128]{2,1,0:T(8,128)}, f32[25,48,128]{2,1,0:T(8,128)}, u32[]{:S(2)}, u32[]{:S(2)}) collective-permute-start(f32[25,48,128]{2,1,0:T(8,128)} %constant_dynamic-update-slice_fusion), channel_id=1, source_target_pairs={{4,0},{8,4},{12,8},{5,1},{9,5},{13,9},{6,2},{10,6},{14,10},{7,3},{... | collective-permute-start | bytes 1843208 | tf_op jit(solution)/shard_map/ppermute | solution.py:26
  31.6 12.6 %collective-permute-start.5 = (f32[25,48,128]{2,1,0:T(8,128)}, f32[25,48,128]{2,1,0:T(8,128)}, u32[]{:S(2)}, u32[]{:S(2)}) collective-permute-start(f32[25,48,128]{2,1,0:T(8,128)} %collective-permute-done.3), channel_id=1, source_target_pairs={{4,8},{8,12},{5,9},{9,13},{6,10},{10,14},{7,11},{11,15},{20,24},{2... | collective-permute-start | bytes 1843208 | tf_op jit(solution)/shard_map/ppermute | solution.py:25
  33.6 2.0 %copy-start.6 = (f32[4,48,512]{2,1,0:T(8,128)S(1)}, f32[4,48,512]{2,1,0:T(8,128)}, u32[]{:S(2)}) copy-start(f32[4,48,512]{2,1,0:T(8,128)} %get-tuple-element.9) | copy-start | bytes 1179652
  33.6 6.1 %copy-start.7 = (f32[8,4,512]{2,0,1:T(8,128)S(1)}, f32[8,4,512]{2,0,1:T(8,128)}, u32[]{:S(2)}) copy-start(f32[8,4,512]{2,0,1:T(8,128)} %fusion.11) | copy-start | bytes 196612
  33.6 7.2 %copy-start.5 = (f32[4,48,512]{2,1,0:T(8,128)S(1)}, f32[4,48,512]{2,1,0:T(8,128)}, u32[]{:S(2)}) copy-start(f32[4,48,512]{2,1,0:T(8,128)} %get-tuple-element.8) | copy-start | bytes 1179652
  33.6 11.3 %copy-start.9 = (f32[8,512,4]{1,2,0:T(4,128)S(1)}, f32[8,512,4]{1,2,0:T(4,128)}, u32[]{:S(2)}) copy-start(f32[8,512,4]{1,2,0:T(4,128)} %fusion.3) | copy-start | bytes 196612
  35.0 0.6 copy-start.8
  35.6 38.8 %collective-permute-start = (f32[4,48,512]{2,1,0:T(8,128)S(1)}, f32[4,48,512]{2,1,0:T(8,128)S(1)}, u32[]{:S(2)}, u32[]{:S(2)}) collective-permute-start(f32[4,48,512]{2,1,0:T(8,128)S(1)} %copy-done.6), channel_id=1, source_target_pairs={{0,1},{1,2},{2,3},{4,5},{5,6},{6,7},{8,9},{9,10},{10,11},{12,13},{... | collective-permute-start | bytes 1179656 | tf_op jit(solution)/shard_map/ppermute | solution.py:14
  38.4 19.7 %collective-permute-start.6 = (f32[25,48,128]{2,1,0:T(8,128)}, f32[25,48,128]{2,1,0:T(8,128)S(1)}, u32[]{:S(2)}, u32[]{:S(2)}) collective-permute-start(f32[25,48,128]{2,1,0:T(8,128)} %collective-permute-done.4), channel_id=1, source_target_pairs={{4,0},{8,4},{5,1},{9,5},{6,2},{10,6},{7,3},{11,7},{20,16},{24,20},... | collective-permute-start | bytes 1843208 | tf_op jit(solution)/shard_map/ppermute | solution.py:26
  40.8 33.6 %collective-permute-start.1 = (f32[4,48,512]{2,1,0:T(8,128)S(1)}, f32[4,48,512]{2,1,0:T(8,128)}, u32[]{:S(2)}, u32[]{:S(2)}) collective-permute-start(f32[4,48,512]{2,1,0:T(8,128)S(1)} %copy-done.5), channel_id=1, source_target_pairs={{1,0},{2,1},{3,2},{5,4},{6,5},{7,6},{9,8},{10,9},{11,10},{13,12},{... | collective-permute-start | bytes 1179656 | tf_op jit(solution)/shard_map/ppermute | solution.py:14
  44.2 18.7 %collective-permute-start.7 = (f32[25,48,128]{2,1,0:T(8,128)}, f32[25,48,128]{2,1,0:T(8,128)S(1)}, u32[]{:S(2)}, u32[]{:S(2)}) collective-permute-start(f32[25,48,128]{2,1,0:T(8,128)} %collective-permute-done.5), channel_id=1, source_target_pairs={{8,12},{9,13},{10,14},{11,15},{24,28},{25,29},{26,30},{27,31}} | collective-permute-start | bytes 1843208 | tf_op jit(solution)/shard_map/ppermute | solution.py:25
  58.2 16.2 %collective-permute-start.8 = (f32[25,48,128]{2,1,0:T(8,128)S(1)}, f32[25,48,128]{2,1,0:T(8,128)S(1)}, u32[]{:S(2)}, u32[]{:S(2)}) collective-permute-start(f32[25,48,128]{2,1,0:T(8,128)S(1)} %collective-permute-done.6), channel_id=1, source_target_pairs={{4,0},{5,1},{6,2},{7,3},{20,16},{21,17},{22,18},{23,19}} | collective-permute-start | bytes 1843208 | tf_op jit(solution)/shard_map/ppermute | solution.py:26
  74.4 1.6 %copy-start.1 = (f32[25,48,640]{2,1,0:T(8,128)}, f32[25,48,640]{2,1,0:T(8,128)S(1)}, u32[]{:S(2)}) copy-start(f32[25,48,640]{2,1,0:T(8,128)S(1)} %constant_dynamic-update-slice_fusion.4.wx_ref) | copy-start | bytes 9216004
  74.4 1.7 %copy-start.4 = (f32[4,48,512]{2,1,0:T(8,128)}, f32[4,48,512]{2,1,0:T(8,128)S(1)}, u32[]{:S(2)}) copy-start(f32[4,48,512]{2,1,0:T(8,128)S(1)} %collective-permute-done.qs_ref) | copy-start | bytes 1179652
  83.8 6.9 %collective-permute-start.12 = (f32[4,48,512]{2,1,0:T(8,128)}, f32[4,48,512]{2,1,0:T(8,128)S(1)}, u32[]{:S(2)}, u32[]{:S(2)}) collective-permute-start(f32[4,48,512]{2,1,0:T(8,128)} %get-tuple-element.6), channel_id=1, source_target_pairs={{0,1},{1,2},{2,3},{4,5},{5,6},{6,7},{8,9},{9,10},{10,11},{12,13},{... | collective-permute-start | bytes 1179656 | tf_op jit(solution)/shard_map/ppermute | solution.py:14
  85.7 9.3 %collective-permute-start.13 = (f32[4,48,512]{2,1,0:T(8,128)}, f32[4,48,512]{2,1,0:T(8,128)S(1)}, u32[]{:S(2)}, u32[]{:S(2)}) collective-permute-start(f32[4,48,512]{2,1,0:T(8,128)} %get-tuple-element.7), channel_id=1, source_target_pairs={{1,0},{2,1},{3,2},{5,4},{6,5},{7,6},{9,8},{10,9},{11,10},{13,12},{... | collective-permute-start | bytes 1179656 | tf_op jit(solution)/shard_map/ppermute | solution.py:14
  90.7 4.3 %copy-start.2 = (f32[4,48,512]{2,1,0:T(8,128)}, f32[4,48,512]{2,1,0:T(8,128)S(1)}, u32[]{:S(2)}) copy-start(f32[4,48,512]{2,1,0:T(8,128)S(1)} %collective-permute-done.12.qs_ref) | copy-start | bytes 1179652
  95.0 0.8 copy-start.3

commit v5 on v4

--- a/solution.py
+++ b/solution.py
@@ -40,7 +40,6 @@
     level = lax.broadcasted_iota(jnp.int32, (levels, lon), 0)
     not_top = level < levels - 1
     not_bottom = level > 0
-    bottom = level == 0
 
     @pl.when(pl.program_id(0) == 0)
     def _():
@@ -81,13 +80,15 @@
             + coef_ref[5, a] * pltpu.roll(qa, levels - 1, 0)
             + coef_ref[6, a] * pltpu.roll(qa, 1, 0)
         )
-        source = jnp.broadcast_to(src_ref[0, a : a + 1, :], (levels, lon))
-        result = result + jnp.where(bottom, source, 0.0)
-        o_ref[0, a] = result
+        surface = result[0:1] + src_ref[0, a : a + 1, :]
+        targets = [o_ref.at[0, a]]
         if edges and a == 0:
-            edges[0][0] = result
+            targets.append(edges[0].at[0])
         if edges and a == lat_rows - 1:
-            edges[1][0] = result
+            targets.append(edges[1].at[0])
+        for target in targets:
+            target[...] = result
+            target[0:1, :] = surface
 
 
 def advance(state, south, north, weather, emission, north_open, with_edges):
@@ -138,15 +139,15 @@
     lat_rows = control.shape[1]
 
     south_v = passed_along(meridional_courant[-1:], "band", 1)
-    q_south = passed_along(tracer_state[:, -1], "band", 1)
-    q_north = passed_along(tracer_state[:, 0], "band", -1)
+    pack = jnp.concatenate([zonal_courant, meridional_courant, vertical_diffusion, south_v], axis=0)
+    weather = relay_gather(pack, "tracer")
+    held_state, held_control, _ = lax.optimization_barrier((tracer_state, control, pack))
+    q_south = passed_along(held_state[:, -1], "band", 1)
+    q_north = passed_along(held_state[:, 0], "band", -1)
     shifted = [control]
     for s in range(1, band_count):
         pairs = [(i, (i + s) % band_count) for i in range(band_count)]
-        shifted.append(lax.ppermute(control, "band", pairs))
-
-    pack = jnp.concatenate([zonal_courant, meridional_courant, vertical_diffusion, south_v], axis=0)
-    weather = relay_gather(pack, "tracer")
+        shifted.append(lax.ppermute(held_control, "band", pairs))
 
     choose = (
         tile_index[:, :, None] == lax.broadcasted_iota(jnp.int32, (1, 1, tiles_count), 2)

time: 104 us -> 101 us (0.971)
  waiting for transfers between devices: 36.2 us -> 43.7 us
  matrix products: 7.19 us -> 3.4 us
  local copies, waits for them, and re-layouts: 17 us -> 13.3 us
  starting transfers between devices: 26.3 us -> 23.2 us
    ppermute x3, waiting for transfers between devices: 23.9 us -> 29.4 us  [relay_gather(): lax.ppermute(left, axis, [(j, j - 1) for j in range(1, count - r + 1)])]
    dot_general x4, matrix products: 5.38 us -> 2.24 us  [on_device(): term = jnp.einsum('jm,kmn->kjn', tile, part, precision=exact_dot)]
    ppermute x3, starting transfers between devices: 2.83 us -> 0.56 us  [on_device(): shifted.append(lax.ppermute(held_control, 'band', pairs))]
    ppermute x3, waiting for transfers between devices: 6.22 us -> 7.89 us  [relay_gather(): lax.ppermute(right, axis, [(i, i + 1) for i in range(r - 1, count - 1)])]
    ppermute x3, starting transfers between devices: 6.76 us -> 5.43 us  [relay_gather(): lax.ppermute(right, axis, [(i, i + 1) for i in range(r - 1, count - 1)])]
    dynamic_update_slice x3, local copies, waits for them, and re-layouts: 1.21 us -> 0.14 us  [relay_gather(): buf = lax.dynamic_update_slice(buf, left, (0, 0, slot * width))]
    dynamic_update_slice x3, local copies, waits for them, and re-layouts: 2.29 us -> 1.22 us  [relay_gather(): buf = lax.dynamic_update_slice(buf, right, (0, 0, slot * width))]
    unnamed x23 -> x13, local copies, waits for them, and re-layouts: 7.97 us -> 7.35 us
  transfers between devices with their start and end apart: 14 -> 14, of which waited for: 6 -> 6; matrix products, arithmetic and copies ran while one was open for 21% -> 13% of each run, Pallas kernels for 0% -> 0%
where the time goes in v5:
time: 101 us; the launch traced here: 100 us
  waiting for transfers between devices  43.7 us (43%)
  starting transfers between devices  23.2 us (23%)
  Pallas kernels  15.1 us (15%)
  local copies, waits for them, and re-layouts  13.3 us (13%)
  matrix products  3.4 us (3%)
    ppermute x3, waiting for transfers between devices, relay_gather(): lax.ppermute(left, axis, [(j, j - 1) for j in range(1, count - r + 1)])  29.4 us
    pallas_call x2, Pallas kernels, advance(): pl.pallas_call(step_kernel, grid_spec=grid_spec, out_shape=out_shape, com...  15.1 us
    ppermute x5, starting transfers between devices, passed_along(): return lax.ppermute(value, axis, pairs)  13.4 us
    ppermute x3, waiting for transfers between devices, relay_gather(): lax.ppermute(right, axis, [(i, i + 1) for i in range(r - 1, count - 1)])  7.89 us
    unnamed x13, local copies, waits for them, and re-layouts  7.35 us
    ppermute x5, waiting for transfers between devices, passed_along(): return lax.ppermute(value, axis, pairs)  6.39 us
    ppermute x3, starting transfers between devices, relay_gather(): lax.ppermute(right, axis, [(i, i + 1) for i in range(r - 1, count - 1)])  5.43 us
    ppermute x3, starting transfers between devices, relay_gather(): lax.ppermute(left, axis, [(j, j - 1) for j in range(1, count - r + 1)])  3.85 us
  transfers between devices with their start and end apart: 14, of which 6 were waited for; matrix products, arithmetic and copies ran while one was open for 13% of the time, Pallas kernels for 0%

profile of v5, /device:TPU:1, one launch (start us, length us, event | category | flops | bytes accessed | tf_op | source)
XLA Modules:
  0.0 100.1 jit_solution(6076482699394782754)
XLA Ops:
  0.6 0.7 slice.9
  1.4 4.5 %collective-permute-start = (f32[1,48,128]{2,1,0:T(8,128)S(1)}, f32[1,48,128]{2,1,0:T(8,128)S(1)}, u32[]{:S(2)}, u32[]{:S(2)}) collective-permute-start(f32[1,48,128]{2,1,0:T(8,128)S(1)} %slice.9), channel_id=1, source_target_pairs={{0,1},{1,2},{2,3},{4,5},{5,6},{6,7},{8,9},{9,10},{10,11},{12,13},{... | collective-permute-start | bytes 73736 | tf_op jit(solution)/shard_map/ppermute | solution.py:14
  5.9 1.6 %constant_dynamic-update-slice_fusion.3 = f32[25,48,128]{2,1,0:T(8,128)} fusion(f32[8,48,128]{2,1,0:T(8,128)} %param.15), kind=kLoop, calls=%fused_computation.18 | loop fusion | bytes 393216
  7.5 1.6 %constant_dynamic-update-slice_fusion.2 = f32[25,48,128]{2,1,0:T(8,128)} fusion(f32[25,48,128]{2,1,0:T(8,128)} %constant_dynamic-update-slice_fusion.3, f32[8,48,128]{2,1,0:T(8,128)} %param.16), kind=kLoop, calls=%fused_computation.17 | loop fusion | bytes 393216
  9.1 0.7 constant_dynamic-slice_fusion.4
  10.0 1.6 %constant_dynamic-update-slice_fusion.1 = f32[25,48,128]{2,1,0:T(8,128)} fusion(f32[25,48,128]{2,1,0:T(8,128)} %constant_dynamic-update-slice_fusion.2, f32[8,48,128]{2,1,0:T(8,128)} %param.17), kind=kLoop, calls=%fused_computation.16 | loop fusion | bytes 393216
  12.3 4.0 %collective-permute-start.3 = (f32[25,48,128]{2,1,0:T(8,128)}, f32[25,48,128]{2,1,0:T(8,128)}, u32[]{:S(2)}, u32[]{:S(2)}) collective-permute-start(f32[25,48,128]{2,1,0:T(8,128)} %constant_dynamic-update-slice_fusion), channel_id=1, source_target_pairs={{0,4},{4,8},{8,12},{1,5},{5,9},{9,13},{2,6},{6,10},{10,14},{3,7},{... | collective-permute-start | bytes 1843208 | tf_op jit(solution)/shard_map/ppermute | solution.py:25
  16.9 1.0 %convolution_bitcast_fusion.3 = f32[4,8,512]{2,1,0:T(8,128)S(1)} fusion(f32[8,8,1]{1,0,2:T(8,128)S(1)} %bitcast.47, f32[4,8,512]{2,1,0:T(8,128)} %param.10), kind=kOutput, calls=%fused_computation.7 | convolution fusion | flops 1572864 | bytes 131328 | tf_op jit(solution)/shard_map/jm,kmn->kjn/dot_general | solution.py:161
  17.9 1.3 %collective-permute-start.4 = (f32[25,48,128]{2,1,0:T(8,128)}, f32[25,48,128]{2,1,0:T(8,128)S(1)}, u32[]{:S(2)}, u32[]{:S(2)}) collective-permute-start(f32[25,48,128]{2,1,0:T(8,128)} %constant_dynamic-update-slice_fusion), channel_id=1, source_target_pairs={{4,0},{8,4},{12,8},{5,1},{9,5},{13,9},{6,2},{10,6},{14,10},{7,3},{... | collective-permute-start | bytes 1843208 | tf_op jit(solution)/shard_map/ppermute | solution.py:26
  19.2 1.0 fusion.4
  20.7 7.9 %collective-permute-done.3 = f32[25,48,128]{2,1,0:T(8,128)} collective-permute-done((f32[25,48,128]{2,1,0:T(8,128)}, f32[25,48,128]{2,1,0:T(8,128)}, u32[]{:S(2)}, u32[]{:S(2)}) %collective-permute-start.3) | collective-permute-done | bytes 614432 | tf_op jit(solution)/shard_map/ppermute | solution.py:25
  28.6 0.7 collective-permute-start.5
  29.3 1.2 %slice_bitcast_fusion = (f32[4,48,512]{2,1,0:T(8,128)S(1)}, f32[4,48,512]{2,1,0:T(8,128)S(1)}) fusion(f32[4,8,48,512]{3,2,1,0:T(8,128)} %q_ref.1), kind=kLoop, calls=%fused_computation.8 | loop fusion | bytes 1572864 | tf_op jit(solution)/shard_map/squeeze | solution.py:146
  30.7 1.1 %constant_dynamic-update-slice_fusion.10 = f32[25,48,640]{2,1,0:T(8,128)S(1)} fusion(f32[25,48,640]{2,1,0:T(8,128)S(1)} %broadcast_in_dim.2, f32[25,48,128]{2,1,0:T(8,128)} %constant_dynamic-update-slice_fusion, s32[]{:T(128)S(6)} %select_n.75), kind=kLoop, calls=%fused_computation.30 | loop fusion | bytes 1228804 | tf_op jit(solution)/shard_map/dynamic_update_slice | solution.py:22
  31.8 1.9 %collective-permute-start.1 = (f32[4,48,512]{2,1,0:T(8,128)S(1)}, f32[4,48,512]{2,1,0:T(8,128)S(1)}, u32[]{:S(2)}, u32[]{:S(2)}) collective-permute-start(f32[4,48,512]{2,1,0:T(8,128)S(1)} %get-tuple-element.13), channel_id=1, source_target_pairs={{0,1},{1,2},{2,3},{4,5},{5,6},{6,7},{8,9},{9,10},{10,11},{12,13},{... | collective-permute-start | bytes 1179656 | tf_op jit(solution)/shard_map/ppermute | solution.py:14
  33.8 1.3 %collective-permute-done.4 = f32[25,48,128]{2,1,0:T(8,128)S(1)} collective-permute-done((f32[25,48,128]{2,1,0:T(8,128)}, f32[25,48,128]{2,1,0:T(8,128)S(1)}, u32[]{:S(2)}, u32[]{:S(2)}) %collective-permute-start.4) | collective-permute-done | bytes 614432 | tf_op jit(solution)/shard_map/ppermute | solution.py:26
  35.1 1.3 %collective-permute-start.6 = (f32[25,48,128]{2,1,0:T(8,128)S(1)}, f32[25,48,128]{2,1,0:T(8,128)S(1)}, u32[]{:S(2)}, u32[]{:S(2)}) collective-permute-start(f32[25,48,128]{2,1,0:T(8,128)S(1)} %collective-permute-done.4), channel_id=1, source_target_pairs={{4,0},{8,4},{5,1},{9,5},{6,2},{10,6},{7,3},{11,7},{20,16},{24,20},... | collective-permute-start | bytes 1843208 | tf_op jit(solution)/shard_map/ppermute | solution.py:26
  36.6 2.1 %collective-permute-start.2 = (f32[4,48,512]{2,1,0:T(8,128)S(1)}, f32[4,48,512]{2,1,0:T(8,128)}, u32[]{:S(2)}, u32[]{:S(2)}) collective-permute-start(f32[4,48,512]{2,1,0:T(8,128)S(1)} %get-tuple-element.12), channel_id=1, source_target_pairs={{1,0},{2,1},{3,2},{5,4},{6,5},{7,6},{9,8},{10,9},{11,10},{13,12},{... | collective-permute-start | bytes 1179656 | tf_op jit(solution)/shard_map/ppermute | solution.py:14
  38.9 0.7 collective-permute-start.7
  39.6 0.8 fusion.2.src_ref
  40.5 14.2 %collective-permute-done.6 = f32[25,48,128]{2,1,0:T(8,128)S(1)} collective-permute-done((f32[25,48,128]{2,1,0:T(8,128)S(1)}, f32[25,48,128]{2,1,0:T(8,128)S(1)}, u32[]{:S(2)}, u32[]{:S(2)}) %collective-permute-start.6) | collective-permute-done | bytes 614432 | tf_op jit(solution)/shard_map/ppermute | solution.py:26
  54.7 1.3 %collective-permute-start.8 = (f32[25,48,128]{2,1,0:T(8,128)S(1)}, f32[25,48,128]{2,1,0:T(8,128)S(1)}, u32[]{:S(2)}, u32[]{:S(2)}) collective-permute-start(f32[25,48,128]{2,1,0:T(8,128)S(1)} %collective-permute-done.6), channel_id=1, source_target_pairs={{4,0},{5,1},{6,2},{7,3},{20,16},{21,17},{22,18},{23,19}} | collective-permute-start | bytes 1843208 | tf_op jit(solution)/shard_map/ppermute | solution.py:26
  56.0 1.1 %constant_dynamic-update-slice_fusion.9 = f32[25,48,640]{2,1,0:T(8,128)S(1)} fusion(f32[25,48,640]{2,1,0:T(8,128)S(1)} %constant_dynamic-update-slice_fusion.10, f32[25,48,128]{2,1,0:T(8,128)} %collective-permute-done.3, s32[]{:T(128)S(6)} %select_n.77), kind=kLoop, calls=%fused_computation.29 | loop fusion | bytes 1228804 | tf_op jit(solution)/shard_map/dynamic_update_slice | solution.py:28
  57.3 13.9 %collective-permute-done.8 = f32[25,48,128]{2,1,0:T(8,128)S(1)} collective-permute-done((f32[25,48,128]{2,1,0:T(8,128)S(1)}, f32[25,48,128]{2,1,0:T(8,128)S(1)}, u32[]{:S(2)}, u32[]{:S(2)}) %collective-permute-start.8) | collective-permute-done | bytes 614432 | tf_op jit(solution)/shard_map/ppermute | solution.py:26
  71.3 1.6 %copy-done.1 = f32[25,48,640]{2,1,0:T(8,128)} copy-done((f32[25,48,640]{2,1,0:T(8,128)}, f32[25,48,640]{2,1,0:T(8,128)S(1)}, u32[]{:S(2)}) %copy-start.1) | copy-done | bytes 3072024
  73.0 7.6 %shard_map.104 = (f32[4,8,48,512]{3,2,1,0:T(8,128)}, f32[4,48,512]{2,1,0:T(8,128)}, f32[4,48,512]{2,1,0:T(8,128)}) custom-call(f32[8]{0:T(128)} %compare_convert_fusion.north_ref, f32[4,8,48,512]{3,2,1,0:T(8,128)} %q_ref.1, f32[4,48,512]{2,1,0:T(8,128)} %copy-done.4, f32[4,48,512]{2,1,0:T(8,128)} %collective-permute-done.2.qn_ref, f32[25,48,640]{2,1,0:T(8,128)} %copy-done.1, ...), custom_call_target="tpu_custom_call" | custom-call | tf_op jit(solution)/shard_map/pallas_call | solution.py:117
  80.6 1.9 %collective-permute-start.12 = (f32[4,48,512]{2,1,0:T(8,128)}, f32[4,48,512]{2,1,0:T(8,128)S(1)}, u32[]{:S(2)}, u32[]{:S(2)}) collective-permute-start(f32[4,48,512]{2,1,0:T(8,128)} %get-tuple-element.10), channel_id=1, source_target_pairs={{0,1},{1,2},{2,3},{4,5},{5,6},{6,7},{8,9},{9,10},{10,11},{12,13},{... | collective-permute-start | bytes 1179656 | tf_op jit(solution)/shard_map/ppermute | solution.py:14
  82.5 2.9 %collective-permute-start.13 = (f32[4,48,512]{2,1,0:T(8,128)}, f32[4,48,512]{2,1,0:T(8,128)S(1)}, u32[]{:S(2)}, u32[]{:S(2)}) collective-permute-start(f32[4,48,512]{2,1,0:T(8,128)} %get-tuple-element.11), channel_id=1, source_target_pairs={{1,0},{2,1},{3,2},{5,4},{6,5},{7,6},{9,8},{10,9},{11,10},{13,12},{... | collective-permute-start | bytes 1179656 | tf_op jit(solution)/shard_map/ppermute | solution.py:14
  85.5 2.1 %collective-permute-done.12.qs_ref = f32[4,48,512]{2,1,0:T(8,128)S(1)} collective-permute-done((f32[4,48,512]{2,1,0:T(8,128)}, f32[4,48,512]{2,1,0:T(8,128)S(1)}, u32[]{:S(2)}, u32[]{:S(2)}) %collective-permute-start.12) | collective-permute-done | bytes 393248 | tf_op jit(solution)/shard_map/ppermute | solution.py:14
  87.6 4.3 %collective-permute-done.13.qn_ref = f32[4,48,512]{2,1,0:T(8,128)S(1)} collective-permute-done((f32[4,48,512]{2,1,0:T(8,128)}, f32[4,48,512]{2,1,0:T(8,128)S(1)}, u32[]{:S(2)}, u32[]{:S(2)}) %collective-permute-start.13) | collective-permute-done | bytes 393248 | tf_op jit(solution)/shard_map/ppermute | solution.py:14
  91.9 0.8 copy-done.3
  92.6 7.5 %shard_map.105 = f32[4,8,48,512]{3,2,1,0:T(8,128)} custom-call(f32[8]{0:T(128)} %compare_convert_fusion.north_ref, f32[4,8,48,512]{3,2,1,0:T(8,128)} %get-tuple-element.9.q_ref, f32[4,48,512]{2,1,0:T(8,128)} %copy-done.2, f32[4,48,512]{2,1,0:T(8,128)} %copy-done.3, f32[25,48,640]{2,1,0:T(8,128)} %copy-done.1, f32[4,8,512]{2,1,0:T(8,128)} %fusion.2.src_ref), custom_call_target="tpu_custom_call" | custom-call | tf_op jit(solution)/shard_map/pallas_call | solution.py:117
  (31 shorter events, 2.9 us)
Async XLA Ops:
  0.6 9.2 %copy-start = (f32[8,8,8]{2,1,0:T(8,128)S(1)}, f32[8,8,8]{2,1,0:T(8,128)}, u32[]{:S(2)}) copy-start(f32[8,8,8]{2,1,0:T(8,128)} %param.11) | copy-start | bytes 6148
  1.4 10.3 %collective-permute-start = (f32[1,48,128]{2,1,0:T(8,128)S(1)}, f32[1,48,128]{2,1,0:T(8,128)S(1)}, u32[]{:S(2)}, u32[]{:S(2)}) collective-permute-start(f32[1,48,128]{2,1,0:T(8,128)S(1)} %slice.9), channel_id=1, source_target_pairs={{0,1},{1,2},{2,3},{4,5},{5,6},{6,7},{8,9},{9,10},{10,11},{12,13},{... | collective-permute-start | bytes 73736 | tf_op jit(solution)/shard_map/ppermute | solution.py:14
  12.3 16.4 %collective-permute-start.3 = (f32[25,48,128]{2,1,0:T(8,128)}, f32[25,48,128]{2,1,0:T(8,128)}, u32[]{:S(2)}, u32[]{:S(2)}) collective-permute-start(f32[25,48,128]{2,1,0:T(8,128)} %constant_dynamic-update-slice_fusion), channel_id=1, source_target_pairs={{0,4},{4,8},{8,12},{1,5},{5,9},{9,13},{2,6},{6,10},{10,14},{3,7},{... | collective-permute-start | bytes 1843208 | tf_op jit(solution)/shard_map/ppermute | solution.py:25
  17.9 17.2 %collective-permute-start.4 = (f32[25,48,128]{2,1,0:T(8,128)}, f32[25,48,128]{2,1,0:T(8,128)S(1)}, u32[]{:S(2)}, u32[]{:S(2)}) collective-permute-start(f32[25,48,128]{2,1,0:T(8,128)} %constant_dynamic-update-slice_fusion), channel_id=1, source_target_pairs={{4,0},{8,4},{12,8},{5,1},{9,5},{13,9},{6,2},{10,6},{14,10},{7,3},{... | collective-permute-start | bytes 1843208 | tf_op jit(solution)/shard_map/ppermute | solution.py:26
  20.2 11.7 %collective-permute-start.9 = (f32[4,8,512]{2,1,0:T(8,128)}, f32[4,8,512]{2,1,0:T(8,128)S(1)}, u32[]{:S(2)}, u32[]{:S(2)}) collective-permute-start(f32[4,8,512]{2,1,0:T(8,128)} %param.10), channel_id=1, source_target_pairs={{0,1},{1,2},{2,3},{3,0},{4,5},{5,6},{6,7},{7,4},{8,9},{9,10},{10,1... | collective-permute-start | bytes 196616 | tf_op jit(solution)/shard_map/ppermute | solution.py:150
  20.5 16.0 %collective-permute-start.11 = (f32[4,8,512]{2,1,0:T(8,128)}, f32[4,8,512]{2,1,0:T(8,128)S(1)}, u32[]{:S(2)}, u32[]{:S(2)}) collective-permute-start(f32[4,8,512]{2,1,0:T(8,128)} %param.10), channel_id=1, source_target_pairs={{0,3},{1,0},{2,1},{3,2},{4,7},{5,4},{6,5},{7,6},{8,11},{9,8},{10,9... | collective-permute-start | bytes 196616 | tf_op jit(solution)/shard_map/ppermute | solution.py:150
  20.7 18.9 %collective-permute-start.10 = (f32[4,8,512]{2,1,0:T(8,128)}, f32[4,8,512]{2,1,0:T(8,128)S(1)}, u32[]{:S(2)}, u32[]{:S(2)}) collective-permute-start(f32[4,8,512]{2,1,0:T(8,128)} %param.10), channel_id=1, source_target_pairs={{0,2},{1,3},{2,0},{3,1},{4,6},{5,7},{6,4},{7,5},{8,10},{9,11},{10,... | collective-permute-start | bytes 196616 | tf_op jit(solution)/shard_map/ppermute | solution.py:150
  28.6 10.3 %collective-permute-start.5 = (f32[25,48,128]{2,1,0:T(8,128)}, f32[25,48,128]{2,1,0:T(8,128)S(1)}, u32[]{:S(2)}, u32[]{:S(2)}) collective-permute-start(f32[25,48,128]{2,1,0:T(8,128)} %collective-permute-done.3), channel_id=1, source_target_pairs={{4,8},{8,12},{5,9},{9,13},{6,10},{10,14},{7,11},{11,15},{20,24},{2... | collective-permute-start | bytes 1843208 | tf_op jit(solution)/shard_map/ppermute | solution.py:25
  31.8 39.4 %collective-permute-start.1 = (f32[4,48,512]{2,1,0:T(8,128)S(1)}, f32[4,48,512]{2,1,0:T(8,128)S(1)}, u32[]{:S(2)}, u32[]{:S(2)}) collective-permute-start(f32[4,48,512]{2,1,0:T(8,128)S(1)} %get-tuple-element.13), channel_id=1, source_target_pairs={{0,1},{1,2},{2,3},{4,5},{5,6},{6,7},{8,9},{9,10},{10,11},{12,13},{... | collective-permute-start | bytes 1179656 | tf_op jit(solution)/shard_map/ppermute | solution.py:14
  35.1 19.6 %collective-permute-start.6 = (f32[25,48,128]{2,1,0:T(8,128)S(1)}, f32[25,48,128]{2,1,0:T(8,128)S(1)}, u32[]{:S(2)}, u32[]{:S(2)}) collective-permute-start(f32[25,48,128]{2,1,0:T(8,128)S(1)} %collective-permute-done.4), channel_id=1, source_target_pairs={{4,0},{8,4},{5,1},{9,5},{6,2},{10,6},{7,3},{11,7},{20,16},{24,20},... | collective-permute-start | bytes 1843208 | tf_op jit(solution)/shard_map/ppermute | solution.py:26
  36.6 34.7 %collective-permute-start.2 = (f32[4,48,512]{2,1,0:T(8,128)S(1)}, f32[4,48,512]{2,1,0:T(8,128)}, u32[]{:S(2)}, u32[]{:S(2)}) collective-permute-start(f32[4,48,512]{2,1,0:T(8,128)S(1)} %get-tuple-element.12), channel_id=1, source_target_pairs={{1,0},{2,1},{3,2},{5,4},{6,5},{7,6},{9,8},{10,9},{11,10},{13,12},{... | collective-permute-start | bytes 1179656 | tf_op jit(solution)/shard_map/ppermute | solution.py:14
  38.9 18.3 %collective-permute-start.7 = (f32[25,48,128]{2,1,0:T(8,128)S(1)}, f32[25,48,128]{2,1,0:T(8,128)S(1)}, u32[]{:S(2)}, u32[]{:S(2)}) collective-permute-start(f32[25,48,128]{2,1,0:T(8,128)S(1)} %collective-permute-done.5), channel_id=1, source_target_pairs={{8,12},{9,13},{10,14},{11,15},{24,28},{25,29},{26,30},{27,31}} | collective-permute-start | bytes 1843208 | tf_op jit(solution)/shard_map/ppermute | solution.py:25
  54.7 16.5 %collective-permute-start.8 = (f32[25,48,128]{2,1,0:T(8,128)S(1)}, f32[25,48,128]{2,1,0:T(8,128)S(1)}, u32[]{:S(2)}, u32[]{:S(2)}) collective-permute-start(f32[25,48,128]{2,1,0:T(8,128)S(1)} %collective-permute-done.6), channel_id=1, source_target_pairs={{4,0},{5,1},{6,2},{7,3},{20,16},{21,17},{22,18},{23,19}} | collective-permute-start | bytes 1843208 | tf_op jit(solution)/shard_map/ppermute | solution.py:26
  71.3 1.7 %copy-start.1 = (f32[25,48,640]{2,1,0:T(8,128)}, f32[25,48,640]{2,1,0:T(8,128)S(1)}, u32[]{:S(2)}) copy-start(f32[25,48,640]{2,1,0:T(8,128)S(1)} %constant_dynamic-update-slice_fusion.4.wx_ref) | copy-start | bytes 9216004
  71.3 1.7 %copy-start.4 = (f32[4,48,512]{2,1,0:T(8,128)}, f32[4,48,512]{2,1,0:T(8,128)S(1)}, u32[]{:S(2)}) copy-start(f32[4,48,512]{2,1,0:T(8,128)S(1)} %collective-permute-done.1.qs_ref) | copy-start | bytes 1179652
  80.6 6.9 %collective-permute-start.12 = (f32[4,48,512]{2,1,0:T(8,128)}, f32[4,48,512]{2,1,0:T(8,128)S(1)}, u32[]{:S(2)}, u32[]{:S(2)}) collective-permute-start(f32[4,48,512]{2,1,0:T(8,128)} %get-tuple-element.10), channel_id=1, source_target_pairs={{0,1},{1,2},{2,3},{4,5},{5,6},{6,7},{8,9},{9,10},{10,11},{12,13},{... | collective-permute-start | bytes 1179656 | tf_op jit(solution)/shard_map/ppermute | solution.py:14
  82.5 9.3 %collective-permute-start.13 = (f32[4,48,512]{2,1,0:T(8,128)}, f32[4,48,512]{2,1,0:T(8,128)S(1)}, u32[]{:S(2)}, u32[]{:S(2)}) collective-permute-start(f32[4,48,512]{2,1,0:T(8,128)} %get-tuple-element.11), channel_id=1, source_target_pairs={{1,0},{2,1},{3,2},{5,4},{6,5},{7,6},{9,8},{10,9},{11,10},{13,12},{... | collective-permute-start | bytes 1179656 | tf_op jit(solution)/shard_map/ppermute | solution.py:14
  87.6 4.3 %copy-start.2 = (f32[4,48,512]{2,1,0:T(8,128)}, f32[4,48,512]{2,1,0:T(8,128)S(1)}, u32[]{:S(2)}) copy-start(f32[4,48,512]{2,1,0:T(8,128)S(1)} %collective-permute-done.12.qs_ref) | copy-start | bytes 1179652
  91.9 0.8 copy-start.3

commit v6 on v5

--- a/solution.py
+++ b/solution.py
@@ -14,7 +14,32 @@
     return lax.ppermute(value, axis, pairs)
 
 
-def relay_gather(x, axis):
+def pack_kernel(*refs):
+    parts, out_ref, sems = refs[:-2], refs[-2], refs[-1]
+    copies = []
+    row = 0
+    for i, part in enumerate(parts):
+        rows = part.shape[0]
+        copies.append(pltpu.make_async_copy(part, out_ref.at[pl.ds(row, rows)], sems.at[i]))
+        row += rows
+    for copy in copies:
+        copy.start()
+    for copy in copies:
+        copy.wait()
+
+
+def packed(parts):
+    rows = sum(part.shape[0] for part in parts)
+    return pl.pallas_call(
+        pack_kernel,
+        in_specs=[pl.BlockSpec(memory_space=pl.ANY)] * len(parts),
+        out_specs=pl.BlockSpec(memory_space=pl.ANY),
+        out_shape=jax.ShapeDtypeStruct((rows,) + parts[0].shape[1:], parts[0].dtype),
+        scratch_shapes=[pltpu.SemaphoreType.DMA((len(parts),))],
+    )(*parts)
+
+
+def relay_gather(x, axis, hold, release_round):
     count = lax.axis_size(axis)
     me = lax.axis_index(axis)
     rows, levels, width = x.shape
@@ -24,11 +49,15 @@
     for r in range(1, count):
         right = lax.ppermute(right, axis, [(i, i + 1) for i in range(r - 1, count - 1)])
         left = lax.ppermute(left, axis, [(j, j - 1) for j in range(1, count - r + 1)])
+        if r == min(release_round, count - 1):
+            hold, right, left = lax.optimization_barrier((hold, right, left))
         slot = jnp.where(me - r >= 0, me - r, count)
         buf = lax.dynamic_update_slice(buf, right, (0, 0, slot * width))
         slot = jnp.where(me + r < count, me + r, count)
         buf = lax.dynamic_update_slice(buf, left, (0, 0, slot * width))
-    return buf
+    if count == 1:
+        hold = lax.optimization_barrier(hold)
+    return buf, hold
 
 
 def step_kernel(north_ref, q_ref, qs_ref, qn_ref, wx_ref, src_ref, *rest):
@@ -139,15 +168,17 @@
     lat_rows = control.shape[1]
 
     south_v = passed_along(meridional_courant[-1:], "band", 1)
-    pack = jnp.concatenate([zonal_courant, meridional_courant, vertical_diffusion, south_v], axis=0)
-    weather = relay_gather(pack, "tracer")
-    held_state, held_control, _ = lax.optimization_barrier((tracer_state, control, pack))
-    q_south = passed_along(held_state[:, -1], "band", 1)
-    q_north = passed_along(held_state[:, 0], "band", -1)
+    pack = packed([zonal_courant, meridional_courant, vertical_diffusion, south_v])
+    weather, held = relay_gather(
+        pack, "tracer", (tracer_state, control, prior_tiles, tile_index, region_map, region_sigma), 2
+    )
+    tracer_state, control, prior_tiles, tile_index, region_map, region_sigma = held
+    q_south = passed_along(tracer_state[:, -1], "band", 1)
+    q_north = passed_along(tracer_state[:, 0], "band", -1)
     shifted = [control]
     for s in range(1, band_count):
         pairs = [(i, (i + s) % band_count) for i in range(band_count)]
-        shifted.append(lax.ppermute(held_control, "band", pairs))
+        shifted.append(lax.ppermute(control, "band", pairs))
 
     choose = (
         tile_index[:, :, None] == lax.broadcasted_iota(jnp.int32, (1, 1, tiles_count), 2)

time: 101 us -> 117 us (1.16)
  Pallas kernels: 15.1 us -> 34.9 us
  starting transfers between devices: 23.2 us -> 27.8 us
  local copies, waits for them, and re-layouts: 13.3 us -> 9.17 us
  waiting for transfers between devices: 43.7 us -> 41.3 us
  matrix products: 3.4 us -> 1.83 us
    pallas_call x0 -> x1, Pallas kernels: none -> 19.7 us  [packed(): pl.pallas_call(pack_kernel, in_specs=[pl.BlockSpec(memory_space=pl.ANY)]...]
    ppermute x3, waiting for transfers between devices: 29.4 us -> 20.2 us  [relay_gather(): lax.ppermute(left, axis, [(j, j - 1) for j in range(1, count - r + 1)])]
    unnamed x13 -> x20, local copies, waits for them, and re-layouts: 7.35 us -> 1.72 us
    ppermute x5, waiting for transfers between devices: 6.39 us -> 10.1 us  [passed_along(): return lax.ppermute(value, axis, pairs)]
    ppermute x3, waiting for transfers between devices: 7.89 us -> 11 us  [relay_gather(): lax.ppermute(right, axis, [(i, i + 1) for i in range(r - 1, count - 1)])]
    dynamic_update_slice x3, local copies, waits for them, and re-layouts: 0.14 us -> 2.29 us  [relay_gather(): buf = lax.dynamic_update_slice(buf, left, (0, 0, slot * width))]
    ppermute x5, starting transfers between devices: 13.4 us -> 15.4 us  [passed_along(): return lax.ppermute(value, axis, pairs)]
    ppermute x3, starting transfers between devices: 0.56 us -> 2.3 us  [on_device(): shifted.append(lax.ppermute(control, 'band', pairs))]
  transfers between devices with their start and end apart: 14 -> 14, of which waited for: 6 -> 8; matrix products, arithmetic and copies ran while one was open for 13% -> 8% of each run, Pallas kernels for 0% -> 0%
where the time goes in v6:
time: 117 us
  waiting for transfers between devices  41.3 us (35%)
  Pallas kernels  34.9 us (30%)
  starting transfers between devices  27.8 us (24%)
  local copies, waits for them, and re-layouts  9.17 us (8%)
  matrix products  1.83 us (2%)
    ppermute x3, waiting for transfers between devices, relay_gather(): lax.ppermute(left, axis, [(j, j - 1) for j in range(1, count - r + 1)])  20.2 us
    pallas_call x1, Pallas kernels, packed(): pl.pallas_call(pack_kernel, in_specs=[pl.BlockSpec(memory_space=pl.ANY)]...  19.7 us
    ppermute x5, starting transfers between devices, passed_along(): return lax.ppermute(value, axis, pairs)  15.4 us
    pallas_call x2, Pallas kernels, advance(): pl.pallas_call(step_kernel, grid_spec=grid_spec, out_shape=out_shape, com...  15.2 us
    ppermute x3, waiting for transfers between devices, relay_gather(): lax.ppermute(right, axis, [(i, i + 1) for i in range(r - 1, count - 1)])  11 us
    ppermute x5, waiting for transfers between devices, passed_along(): return lax.ppermute(value, axis, pairs)  10.1 us
    ppermute x3, starting transfers between devices, relay_gather(): lax.ppermute(right, axis, [(i, i + 1) for i in range(r - 1, count - 1)])  6.23 us
    ppermute x3, starting transfers between devices, relay_gather(): lax.ppermute(left, axis, [(j, j - 1) for j in range(1, count - r + 1)])  3.85 us
  transfers between devices with their start and end apart: 14, of which 8 were waited for; matrix products, arithmetic and copies ran while one was open for 8% of the time, Pallas kernels for 0%

profile of v6, /device:TPU:1, one launch (start us, length us, event | category | flops | bytes accessed | tf_op | source)
XLA Modules:
  0.0 116.5 jit_solution(10676337138483276899)
XLA Ops:
  0.6 0.7 slice.9
  1.4 4.5 %collective-permute-start = (f32[1,48,128]{2,1,0:T(8,128)S(1)}, f32[1,48,128]{2,1,0:T(8,128)S(1)}, u32[]{:S(2)}, u32[]{:S(2)}) collective-permute-start(f32[1,48,128]{2,1,0:T(8,128)S(1)} %slice.9), channel_id=1, source_target_pairs={{0,1},{1,2},{2,3},{4,5},{5,6},{6,7},{8,9},{9,10},{10,11},{12,13},{... | collective-permute-start | bytes 73736 | tf_op jit(solution)/shard_map/ppermute | solution.py:14
  5.9 0.9 collective-permute-done.refs_3_
  7.4 19.7 %shard_map.104 = f32[25,48,128]{2,1,0:T(8,128)} custom-call(f32[8,48,128]{2,1,0:T(8,128)} %refs_0_.1, f32[8,48,128]{2,1,0:T(8,128)} %refs_1_.1, f32[8,48,128]{2,1,0:T(8,128)} %refs_2_.1, f32[1,48,128]{2,1,0:T(8,128)} %copy-done.7), custom_call_target="tpu_custom_call" | custom-call | tf_op jit(solution)/shard_map/pallas_call | solution.py:33
  27.2 4.0 %collective-permute-start.1 = (f32[25,48,128]{2,1,0:T(8,128)}, f32[25,48,128]{2,1,0:T(8,128)}, u32[]{:S(2)}, u32[]{:S(2)}) collective-permute-start(f32[25,48,128]{2,1,0:T(8,128)} %shard_map.104), channel_id=1, source_target_pairs={{0,4},{4,8},{8,12},{1,5},{5,9},{9,13},{2,6},{6,10},{10,14},{3,7},{... | collective-permute-start | bytes 1843208 | tf_op jit(solution)/shard_map/ppermute | solution.py:50
  31.2 1.3 %collective-permute-start.3 = (f32[25,48,128]{2,1,0:T(8,128)}, f32[25,48,128]{2,1,0:T(8,128)}, u32[]{:S(2)}, u32[]{:S(2)}) collective-permute-start(f32[25,48,128]{2,1,0:T(8,128)} %shard_map.104), channel_id=1, source_target_pairs={{4,0},{8,4},{12,8},{5,1},{9,5},{13,9},{6,2},{10,6},{14,10},{7,3},{... | collective-permute-start | bytes 1843208 | tf_op jit(solution)/shard_map/ppermute | solution.py:51
  32.5 11.0 %collective-permute-done.1 = f32[25,48,128]{2,1,0:T(8,128)} collective-permute-done((f32[25,48,128]{2,1,0:T(8,128)}, f32[25,48,128]{2,1,0:T(8,128)}, u32[]{:S(2)}, u32[]{:S(2)}) %collective-permute-start.1) | collective-permute-done | bytes 614432 | tf_op jit(solution)/shard_map/ppermute | solution.py:50
  43.5 1.5 %collective-permute-start.2 = (f32[25,48,128]{2,1,0:T(8,128)}, f32[25,48,128]{2,1,0:T(8,128)}, u32[]{:S(2)}, u32[]{:S(2)}) collective-permute-start(f32[25,48,128]{2,1,0:T(8,128)} %collective-permute-done.1), channel_id=1, source_target_pairs={{4,8},{8,12},{5,9},{9,13},{6,10},{10,14},{7,11},{11,15},{20,24},{2... | collective-permute-start | bytes 1843208 | tf_op jit(solution)/shard_map/ppermute | solution.py:50
  45.0 3.4 %collective-permute-done.3 = f32[25,48,128]{2,1,0:T(8,128)} collective-permute-done((f32[25,48,128]{2,1,0:T(8,128)}, f32[25,48,128]{2,1,0:T(8,128)}, u32[]{:S(2)}, u32[]{:S(2)}) %collective-permute-start.3) | collective-permute-done | bytes 614432 | tf_op jit(solution)/shard_map/ppermute | solution.py:51
  48.4 1.3 %collective-permute-start.4 = (f32[25,48,128]{2,1,0:T(8,128)}, f32[25,48,128]{2,1,0:T(8,128)}, u32[]{:S(2)}, u32[]{:S(2)}) collective-permute-start(f32[25,48,128]{2,1,0:T(8,128)} %collective-permute-done.3), channel_id=1, source_target_pairs={{4,0},{8,4},{5,1},{9,5},{6,2},{10,6},{7,3},{11,7},{20,16},{24,20},... | collective-permute-start | bytes 1843208 | tf_op jit(solution)/shard_map/ppermute | solution.py:51
  50.9 1.1 constant_dynamic-update-slice_fusion.5
  52.0 1.1 constant_dynamic-update-slice_fusion.4
  53.2 12.7 %collective-permute-done.4 = f32[25,48,128]{2,1,0:T(8,128)} collective-permute-done((f32[25,48,128]{2,1,0:T(8,128)}, f32[25,48,128]{2,1,0:T(8,128)}, u32[]{:S(2)}, u32[]{:S(2)}) %collective-permute-start.4) | collective-permute-done | bytes 614432 | tf_op jit(solution)/shard_map/ppermute | solution.py:51
  65.9 2.3 %collective-permute-start.10 = (f32[4,8,512]{2,1,0:T(8,128)S(1)}, f32[4,8,512]{2,1,0:T(8,128)S(1)}, u32[]{:S(2)}, u32[]{:S(2)}) collective-permute-start(f32[4,8,512]{2,1,0:T(8,128)S(1)} %copy-done.6), channel_id=1, source_target_pairs={{0,2},{1,3},{2,0},{3,1},{4,6},{5,7},{6,4},{7,5},{8,10},{9,11},{10,... | collective-permute-start | bytes 196616 | tf_op jit(solution)/shard_map/ppermute | solution.py:181
  68.2 0.7 collective-permute-start.7
  68.9 1.3 %collective-permute-start.8 = (f32[25,48,128]{2,1,0:T(8,128)}, f32[25,48,128]{2,1,0:T(8,128)S(1)}, u32[]{:S(2)}, u32[]{:S(2)}) collective-permute-start(f32[25,48,128]{2,1,0:T(8,128)} %collective-permute-done.4), channel_id=1, source_target_pairs={{4,0},{5,1},{6,2},{7,3},{20,16},{21,17},{22,18},{23,19}} | collective-permute-start | bytes 1843208 | tf_op jit(solution)/shard_map/ppermute | solution.py:51
  70.2 1.2 %slice_bitcast_fusion = (f32[4,48,512]{2,1,0:T(8,128)S(1)}, f32[4,48,512]{2,1,0:T(8,128)S(1)}) fusion(f32[4,8,48,512]{3,2,1,0:T(8,128)} %q_ref), kind=kLoop, calls=%fused_computation.5 | loop fusion | bytes 1572864 | tf_op jit(solution)/shard_map/squeeze | solution.py:177
  71.4 0.7 constant_dynamic-slice_fusion.4
  72.5 1.1 constant_dynamic-update-slice_fusion.3
  73.6 1.1 constant_dynamic-update-slice_fusion.2
  74.8 3.7 %collective-permute-start.5 = (f32[4,48,512]{2,1,0:T(8,128)S(1)}, f32[4,48,512]{2,1,0:T(8,128)S(1)}, u32[]{:S(2)}, u32[]{:S(2)}) collective-permute-start(f32[4,48,512]{2,1,0:T(8,128)S(1)} %get-tuple-element.25), channel_id=1, source_target_pairs={{0,1},{1,2},{2,3},{4,5},{5,6},{6,7},{8,9},{9,10},{10,11},{12,13},{... | collective-permute-start | bytes 1179656 | tf_op jit(solution)/shard_map/ppermute | solution.py:14
  78.7 1.9 %collective-permute-start.6 = (f32[4,48,512]{2,1,0:T(8,128)S(1)}, f32[4,48,512]{2,1,0:T(8,128)}, u32[]{:S(2)}, u32[]{:S(2)}) collective-permute-start(f32[4,48,512]{2,1,0:T(8,128)S(1)} %get-tuple-element.24), channel_id=1, source_target_pairs={{1,0},{2,1},{3,2},{5,4},{6,5},{7,6},{9,8},{10,9},{11,10},{13,12},{... | collective-permute-start | bytes 1179656 | tf_op jit(solution)/shard_map/ppermute | solution.py:14
  81.0 0.8 fusion.3.src_ref
  81.9 4.1 %collective-permute-done.8 = f32[25,48,128]{2,1,0:T(8,128)S(1)} collective-permute-done((f32[25,48,128]{2,1,0:T(8,128)}, f32[25,48,128]{2,1,0:T(8,128)S(1)}, u32[]{:S(2)}, u32[]{:S(2)}) %collective-permute-start.8) | collective-permute-done | bytes 614432 | tf_op jit(solution)/shard_map/ppermute | solution.py:51
  86.1 1.8 %collective-permute-done.6.qn_ref = f32[4,48,512]{2,1,0:T(8,128)} collective-permute-done((f32[4,48,512]{2,1,0:T(8,128)S(1)}, f32[4,48,512]{2,1,0:T(8,128)}, u32[]{:S(2)}, u32[]{:S(2)}) %collective-permute-start.6) | collective-permute-done | bytes 393248 | tf_op jit(solution)/shard_map/ppermute | solution.py:14
  87.9 7.6 %shard_map.105 = (f32[4,8,48,512]{3,2,1,0:T(8,128)}, f32[4,48,512]{2,1,0:T(8,128)}, f32[4,48,512]{2,1,0:T(8,128)}) custom-call(f32[8]{0:T(128)} %compare_convert_fusion.north_ref, f32[4,8,48,512]{3,2,1,0:T(8,128)} %q_ref, f32[4,48,512]{2,1,0:T(8,128)} %copy-done.5, f32[4,48,512]{2,1,0:T(8,128)} %collective-permute-done.6.qn_ref, f32[25,48,640]{2,1,0:T(8,128)} %copy-done.1, ...), custom_call_target="tpu_custom_call" | custom-call | tf_op jit(solution)/shard_map/pallas_call | solution.py:146
  95.5 3.4 %collective-permute-start.12 = (f32[4,48,512]{2,1,0:T(8,128)}, f32[4,48,512]{2,1,0:T(8,128)S(1)}, u32[]{:S(2)}, u32[]{:S(2)}) collective-permute-start(f32[4,48,512]{2,1,0:T(8,128)} %get-tuple-element.22), channel_id=1, source_target_pairs={{0,1},{1,2},{2,3},{4,5},{5,6},{6,7},{8,9},{9,10},{10,11},{12,13},{... | collective-permute-start | bytes 1179656 | tf_op jit(solution)/shard_map/ppermute | solution.py:14
  98.9 1.9 %collective-permute-start.13 = (f32[4,48,512]{2,1,0:T(8,128)}, f32[4,48,512]{2,1,0:T(8,128)S(1)}, u32[]{:S(2)}, u32[]{:S(2)}) collective-permute-start(f32[4,48,512]{2,1,0:T(8,128)} %get-tuple-element.23), channel_id=1, source_target_pairs={{1,0},{2,1},{3,2},{5,4},{6,5},{7,6},{9,8},{10,9},{11,10},{13,12},{... | collective-permute-start | bytes 1179656 | tf_op jit(solution)/shard_map/ppermute | solution.py:14
  100.9 3.1 %collective-permute-done.12.qs_ref = f32[4,48,512]{2,1,0:T(8,128)S(1)} collective-permute-done((f32[4,48,512]{2,1,0:T(8,128)}, f32[4,48,512]{2,1,0:T(8,128)S(1)}, u32[]{:S(2)}, u32[]{:S(2)}) %collective-permute-start.12) | collective-permute-done | bytes 393248 | tf_op jit(solution)/shard_map/ppermute | solution.py:14
  103.9 4.3 %collective-permute-done.13.qn_ref = f32[4,48,512]{2,1,0:T(8,128)S(1)} collective-permute-done((f32[4,48,512]{2,1,0:T(8,128)}, f32[4,48,512]{2,1,0:T(8,128)S(1)}, u32[]{:S(2)}, u32[]{:S(2)}) %collective-permute-start.13) | collective-permute-done | bytes 393248 | tf_op jit(solution)/shard_map/ppermute | solution.py:14
  108.2 0.8 copy-done.4
  109.0 7.5 %shard_map.106 = f32[4,8,48,512]{3,2,1,0:T(8,128)} custom-call(f32[8]{0:T(128)} %compare_convert_fusion.north_ref, f32[4,8,48,512]{3,2,1,0:T(8,128)} %get-tuple-element.21.q_ref, f32[4,48,512]{2,1,0:T(8,128)} %copy-done.3, f32[4,48,512]{2,1,0:T(8,128)} %copy-done.4, f32[25,48,640]{2,1,0:T(8,128)} %copy-done.1, f32[4,8,512]{2,1,0:T(8,128)} %fusion.3.src_ref), custom_call_target="tpu_custom_call" | custom-call | tf_op jit(solution)/shard_map/pallas_call | solution.py:146
  (38 shorter events, 2.9 us)
Async XLA Ops:
  0.6 71.4 %copy-start = (f32[8,8,8]{2,1,0:T(8,128)S(1)}, f32[8,8,8]{2,1,0:T(8,128)}, u32[]{:S(2)}) copy-start(f32[8,8,8]{2,1,0:T(8,128)} %param.11) | copy-start | bytes 6148
  1.4 5.4 %collective-permute-start = (f32[1,48,128]{2,1,0:T(8,128)S(1)}, f32[1,48,128]{2,1,0:T(8,128)S(1)}, u32[]{:S(2)}, u32[]{:S(2)}) collective-permute-start(f32[1,48,128]{2,1,0:T(8,128)S(1)} %slice.9), channel_id=1, source_target_pairs={{0,1},{1,2},{2,3},{4,5},{5,6},{6,7},{8,9},{9,10},{10,11},{12,13},{... | collective-permute-start | bytes 73736 | tf_op jit(solution)/shard_map/ppermute | solution.py:14
  6.8 0.6 copy-start.7
  27.2 16.3 %collective-permute-start.1 = (f32[25,48,128]{2,1,0:T(8,128)}, f32[25,48,128]{2,1,0:T(8,128)}, u32[]{:S(2)}, u32[]{:S(2)}) collective-permute-start(f32[25,48,128]{2,1,0:T(8,128)} %shard_map.104), channel_id=1, source_target_pairs={{0,4},{4,8},{8,12},{1,5},{5,9},{9,13},{2,6},{6,10},{10,14},{3,7},{... | collective-permute-start | bytes 1843208 | tf_op jit(solution)/shard_map/ppermute | solution.py:50
  31.2 17.2 %collective-permute-start.3 = (f32[25,48,128]{2,1,0:T(8,128)}, f32[25,48,128]{2,1,0:T(8,128)}, u32[]{:S(2)}, u32[]{:S(2)}) collective-permute-start(f32[25,48,128]{2,1,0:T(8,128)} %shard_map.104), channel_id=1, source_target_pairs={{4,0},{8,4},{12,8},{5,1},{9,5},{13,9},{6,2},{10,6},{14,10},{7,3},{... | collective-permute-start | bytes 1843208 | tf_op jit(solution)/shard_map/ppermute | solution.py:51
  43.5 9.7 %collective-permute-start.2 = (f32[25,48,128]{2,1,0:T(8,128)}, f32[25,48,128]{2,1,0:T(8,128)}, u32[]{:S(2)}, u32[]{:S(2)}) collective-permute-start(f32[25,48,128]{2,1,0:T(8,128)} %collective-permute-done.1), channel_id=1, source_target_pairs={{4,8},{8,12},{5,9},{9,13},{6,10},{10,14},{7,11},{11,15},{20,24},{2... | collective-permute-start | bytes 1843208 | tf_op jit(solution)/shard_map/ppermute | solution.py:50
  48.4 17.5 %collective-permute-start.4 = (f32[25,48,128]{2,1,0:T(8,128)}, f32[25,48,128]{2,1,0:T(8,128)}, u32[]{:S(2)}, u32[]{:S(2)}) collective-permute-start(f32[25,48,128]{2,1,0:T(8,128)} %collective-permute-done.3), channel_id=1, source_target_pairs={{4,0},{8,4},{5,1},{9,5},{6,2},{10,6},{7,3},{11,7},{20,16},{24,20},... | collective-permute-start | bytes 1843208 | tf_op jit(solution)/shard_map/ppermute | solution.py:51
  49.8 1.1 copy-start.2
  50.3 15.5 %copy-start.6 = (f32[4,8,512]{2,1,0:T(8,128)S(1)}, f32[4,8,512]{2,1,0:T(8,128)}, u32[]{:S(2)}) copy-start(f32[4,8,512]{2,1,0:T(8,128)} %param.10) | copy-start | bytes 196612
  50.9 21.4 %copy-start.8 = (s32[8,512]{1,0:T(8,128)S(1)}, s32[8,512]{1,0:T(8,128)}, u32[]{:S(2)}) copy-start(s32[8,512]{1,0:T(8,128)} %param.13) | copy-start | bytes 49156
  50.9 21.4 %copy-start.9 = (f32[4,22]{1,0:T(4,128)S(1)}, f32[4,22]{1,0:T(4,128)}, u32[]{:S(2)}) copy-start(f32[4,22]{1,0:T(4,128)} %param.14) | copy-start | bytes 1060
  65.9 8.9 %collective-permute-start.9 = (f32[4,8,512]{2,1,0:T(8,128)S(1)}, f32[4,8,512]{2,1,0:T(8,128)S(1)}, u32[]{:S(2)}, u32[]{:S(2)}) collective-permute-start(f32[4,8,512]{2,1,0:T(8,128)S(1)} %copy-done.6), channel_id=1, source_target_pairs={{0,1},{1,2},{2,3},{3,0},{4,5},{5,6},{6,7},{7,4},{8,9},{9,10},{10,1... | collective-permute-start | bytes 196616 | tf_op jit(solution)/shard_map/ppermute | solution.py:181
  65.9 12.8 %collective-permute-start.10 = (f32[4,8,512]{2,1,0:T(8,128)S(1)}, f32[4,8,512]{2,1,0:T(8,128)S(1)}, u32[]{:S(2)}, u32[]{:S(2)}) collective-permute-start(f32[4,8,512]{2,1,0:T(8,128)S(1)} %copy-done.6), channel_id=1, source_target_pairs={{0,2},{1,3},{2,0},{3,1},{4,6},{5,7},{6,4},{7,5},{8,10},{9,11},{10,... | collective-permute-start | bytes 196616 | tf_op jit(solution)/shard_map/ppermute | solution.py:181
  68.2 12.6 %collective-permute-start.11 = (f32[4,8,512]{2,1,0:T(8,128)S(1)}, f32[4,8,512]{2,1,0:T(8,128)S(1)}, u32[]{:S(2)}, u32[]{:S(2)}) collective-permute-start(f32[4,8,512]{2,1,0:T(8,128)S(1)} %copy-done.6), channel_id=1, source_target_pairs={{0,3},{1,0},{2,1},{3,2},{4,7},{5,4},{6,5},{7,6},{8,11},{9,8},{10,9... | collective-permute-start | bytes 196616 | tf_op jit(solution)/shard_map/ppermute | solution.py:181
  68.2 13.6 %collective-permute-start.7 = (f32[25,48,128]{2,1,0:T(8,128)}, f32[25,48,128]{2,1,0:T(8,128)S(1)}, u32[]{:S(2)}, u32[]{:S(2)}) collective-permute-start(f32[25,48,128]{2,1,0:T(8,128)} %collective-permute-done.2), channel_id=1, source_target_pairs={{8,12},{9,13},{10,14},{11,15},{24,28},{25,29},{26,30},{27,31}} | collective-permute-start | bytes 1843208 | tf_op jit(solution)/shard_map/ppermute | solution.py:50
  68.9 17.1 %collective-permute-start.8 = (f32[25,48,128]{2,1,0:T(8,128)}, f32[25,48,128]{2,1,0:T(8,128)S(1)}, u32[]{:S(2)}, u32[]{:S(2)}) collective-permute-start(f32[25,48,128]{2,1,0:T(8,128)} %collective-permute-done.4), channel_id=1, source_target_pairs={{4,0},{5,1},{6,2},{7,3},{20,16},{21,17},{22,18},{23,19}} | collective-permute-start | bytes 1843208 | tf_op jit(solution)/shard_map/ppermute | solution.py:51
  74.8 11.2 %collective-permute-start.5 = (f32[4,48,512]{2,1,0:T(8,128)S(1)}, f32[4,48,512]{2,1,0:T(8,128)S(1)}, u32[]{:S(2)}, u32[]{:S(2)}) collective-permute-start(f32[4,48,512]{2,1,0:T(8,128)S(1)} %get-tuple-element.25), channel_id=1, source_target_pairs={{0,1},{1,2},{2,3},{4,5},{5,6},{6,7},{8,9},{9,10},{10,11},{12,13},{... | collective-permute-start | bytes 1179656 | tf_op jit(solution)/shard_map/ppermute | solution.py:14
  78.7 9.2 %collective-permute-start.6 = (f32[4,48,512]{2,1,0:T(8,128)S(1)}, f32[4,48,512]{2,1,0:T(8,128)}, u32[]{:S(2)}, u32[]{:S(2)}) collective-permute-start(f32[4,48,512]{2,1,0:T(8,128)S(1)} %get-tuple-element.24), channel_id=1, source_target_pairs={{1,0},{2,1},{3,2},{5,4},{6,5},{7,6},{9,8},{10,9},{11,10},{13,12},{... | collective-permute-start | bytes 1179656 | tf_op jit(solution)/shard_map/ppermute | solution.py:14
  86.1 1.8 %copy-start.1 = (f32[25,48,640]{2,1,0:T(8,128)}, f32[25,48,640]{2,1,0:T(8,128)S(1)}, u32[]{:S(2)}) copy-start(f32[25,48,640]{2,1,0:T(8,128)S(1)} %constant_dynamic-update-slice_fusion.wx_ref) | copy-start | bytes 9216004
  86.1 1.8 %copy-start.5 = (f32[4,48,512]{2,1,0:T(8,128)}, f32[4,48,512]{2,1,0:T(8,128)S(1)}, u32[]{:S(2)}) copy-start(f32[4,48,512]{2,1,0:T(8,128)S(1)} %collective-permute-done.5.qs_ref) | copy-start | bytes 1179652
  95.5 8.4 %collective-permute-start.12 = (f32[4,48,512]{2,1,0:T(8,128)}, f32[4,48,512]{2,1,0:T(8,128)S(1)}, u32[]{:S(2)}, u32[]{:S(2)}) collective-permute-start(f32[4,48,512]{2,1,0:T(8,128)} %get-tuple-element.22), channel_id=1, source_target_pairs={{0,1},{1,2},{2,3},{4,5},{5,6},{6,7},{8,9},{9,10},{10,11},{12,13},{... | collective-permute-start | bytes 1179656 | tf_op jit(solution)/shard_map/ppermute | solution.py:14
  98.9 9.3 %collective-permute-start.13 = (f32[4,48,512]{2,1,0:T(8,128)}, f32[4,48,512]{2,1,0:T(8,128)S(1)}, u32[]{:S(2)}, u32[]{:S(2)}) collective-permute-start(f32[4,48,512]{2,1,0:T(8,128)} %get-tuple-element.23), channel_id=1, source_target_pairs={{1,0},{2,1},{3,2},{5,4},{6,5},{7,6},{9,8},{10,9},{11,10},{13,12},{... | collective-permute-start | bytes 1179656 | tf_op jit(solution)/shard_map/ppermute | solution.py:14
  103.9 4.3 %copy-start.3 = (f32[4,48,512]{2,1,0:T(8,128)}, f32[4,48,512]{2,1,0:T(8,128)S(1)}, u32[]{:S(2)}) copy-start(f32[4,48,512]{2,1,0:T(8,128)S(1)} %collective-permute-done.12.qs_ref) | copy-start | bytes 1179652
  108.2 0.8 copy-start.4

commit v7 on v5

--- a/solution.py
+++ b/solution.py
@@ -1,3 +1,5 @@
+import functools
+
 import jax
 import jax.numpy as jnp
 from jax import lax
@@ -31,11 +33,12 @@
     return buf
 
 
-def step_kernel(north_ref, q_ref, qs_ref, qn_ref, wx_ref, src_ref, *rest):
+def step_kernel(north_ref, q_ref, qs_ref, qn_ref, wx_ref, src_ref, *rest, rows=None):
     o_ref = rest[0]
     edges = rest[1:-1]
     coef_ref = rest[-1]
     lat_rows = q_ref.shape[1]
+    rows = range(lat_rows) if rows is None else rows
     levels, lon = q_ref.shape[2], q_ref.shape[3]
     level = lax.broadcasted_iota(jnp.int32, (levels, lon), 0)
     not_top = level < levels - 1
@@ -67,7 +70,7 @@
             coef_ref[5, a] = w_up
             coef_ref[6, a] = w_down
 
-    for a in range(lat_rows):
+    for a in rows:
         qa = q_ref[0, a]
         qm = qs_ref[0] if a == 0 else q_ref[0, a - 1]
         qp = qn_ref[0] if a == lat_rows - 1 else q_ref[0, a + 1]
@@ -122,6 +125,112 @@
     )(north_open, state, south, north, weather, emission)
 
 
+def interior_step(state, weather, emission, north_open):
+    tracers, lat_rows, levels, lon = state.shape
+    row = pl.BlockSpec((1, lat_rows, levels, lon), lambda k: (k, 0, 0, 0))
+    kernel = functools.partial(
+        lambda n, q, w, e, o, c, rows: step_kernel(n, q, None, None, w, e, o, c, rows=rows),
+        rows=range(1, lat_rows - 1),
+    )
+    grid_spec = pltpu.PrefetchScalarGridSpec(
+        num_scalar_prefetch=0,
+        grid=(tracers,),
+        in_specs=[
+            pl.BlockSpec(memory_space=pltpu.SMEM),
+            row,
+            pl.BlockSpec(weather.shape[:2] + (lon,), lambda k: (0, 0, 0)),
+            pl.BlockSpec((1, lat_rows, lon), lambda k: (k, 0, 0)),
+        ],
+        out_specs=row,
+        scratch_shapes=[pltpu.VMEM((7, lat_rows, levels, lon), jnp.float32)],
+    )
+    return pl.pallas_call(
+        kernel,
+        grid_spec=grid_spec,
+        out_shape=jax.ShapeDtypeStruct(state.shape, state.dtype),
+        compiler_params=pltpu.CompilerParams(dimension_semantics=("arbitrary",)),
+    )(north_open, state, weather, emission)
+
+
+def edge_kernel(north_ref, qa_ref, qi_ref, qs_ref, qn_ref, u_ref, v_ref, vm_ref, w_ref, src_ref, base_ref, o_ref):
+    del base_ref
+    lat_rows = src_ref.shape[1]
+    levels, lon = qa_ref.shape[2], qa_ref.shape[3]
+    top = pl.program_id(1)
+    level = lax.broadcasted_iota(jnp.int32, (levels, lon), 0)
+    not_top = level < levels - 1
+    not_bottom = level > 0
+    a = top * (lat_rows - 1)
+    qa = qa_ref[0, 0]
+    inner = qi_ref[0, 0]
+    is_top = jnp.full((levels, lon), top, jnp.int32) == 1
+    qm = jnp.where(is_top, inner, qs_ref[0])
+    qp = jnp.where(is_top, qn_ref[0], inner)
+    u = u_ref[0]
+    uw = pltpu.roll(u, 1, 1)
+    v = v_ref[0] * north_ref[a]
+    vm = vm_ref[0]
+    w = w_ref[0]
+    w_up = jnp.where(not_top, w, 0.0)
+    w_down = jnp.where(not_bottom, pltpu.roll(w, 1, 0), 0.0)
+    c_self = (
+        1.0
+        - jnp.maximum(u, 0.0)
+        + jnp.minimum(uw, 0.0)
+        - jnp.maximum(v, 0.0)
+        + jnp.minimum(vm, 0.0)
+        - w_up
+        - w_down
+    )
+    result = (
+        c_self * qa
+        + (-jnp.minimum(u, 0.0)) * pltpu.roll(qa, lon - 1, 1)
+        + jnp.maximum(uw, 0.0) * pltpu.roll(qa, 1, 1)
+        + (-jnp.minimum(v, 0.0)) * qp
+        + jnp.maximum(vm, 0.0) * qm
+        + w_up * pltpu.roll(qa, levels - 1, 0)
+        + w_down * pltpu.roll(qa, 1, 0)
+    )
+    first_row = src_ref[0, 0:1, :]
+    last_row = src_ref[0, lat_rows - 1 : lat_rows, :]
+    source = jnp.where(jnp.full((1, lon), top, jnp.int32) == 1, last_row, first_row)
+    o_ref[0, 0] = result
+    o_ref[0, 0, 0:1, :] = result[0:1] + source
+
+
+def edge_step(state, base, south, north, weather, emission, north_open):
+    tracers, lat_rows, levels, lon = state.shape
+    last = lat_rows - 1
+    one = lambda index: pl.BlockSpec((1, 1, levels, lon), index)
+    edge = pl.BlockSpec((1, levels, lon), lambda k, e: (k, 0, 0))
+    met = lambda index: pl.BlockSpec((1, levels, lon), index)
+    grid_spec = pltpu.PrefetchScalarGridSpec(
+        num_scalar_prefetch=0,
+        grid=(tracers, 2),
+        in_specs=[
+            pl.BlockSpec(memory_space=pltpu.SMEM),
+            one(lambda k, e: (k, e * last, 0, 0)),
+            one(lambda k, e: (k, 1 + e * (lat_rows - 3), 0, 0)),
+            edge,
+            edge,
+            met(lambda k, e: (e * last, 0, 0)),
+            met(lambda k, e: (lat_rows + e * last, 0, 0)),
+            met(lambda k, e: (3 * lat_rows - e * (lat_rows + 2), 0, 0)),
+            met(lambda k, e: (2 * lat_rows + e * last, 0, 0)),
+            pl.BlockSpec((1, lat_rows, lon), lambda k, e: (k, 0, 0)),
+            pl.BlockSpec(memory_space=pl.ANY),
+        ],
+        out_specs=one(lambda k, e: (k, e * last, 0, 0)),
+    )
+    return pl.pallas_call(
+        edge_kernel,
+        grid_spec=grid_spec,
+        out_shape=jax.ShapeDtypeStruct(state.shape, state.dtype),
+        input_output_aliases={10: 0},
+        compiler_params=pltpu.CompilerParams(dimension_semantics=("arbitrary", "arbitrary")),
+    )(north_open, state, state, south, north, weather, weather, weather, weather, emission, base)
+
+
 def on_device(
     tracer_state,
     control,
@@ -175,7 +284,8 @@
     )
     s1_south = passed_along(top_row, "band", 1)
     s1_north = passed_along(bottom_row, "band", -1)
-    (tracer_field,) = advance(first, s1_south, s1_north, weather, emission, north_open, False)
+    inside = interior_step(first, weather, emission, north_open)
+    tracer_field = edge_step(first, inside, s1_south, s1_north, weather, emission, north_open)
     return (tracer_field, emission)
 
 

time: 101 us -> 101 us (level)
  waiting for transfers between devices: 43.7 us -> 36.2 us
  Pallas kernels: 15.1 us -> 21.1 us
  starting transfers between devices: 23.2 us -> 24.3 us
    pallas_call x0 -> x2, Pallas kernels: none -> 13.5 us  [the longest x1 6.84 us: edge_step(): pl.pallas_call(edge_kernel, grid_spec=grid_spec, out_shape=jax.ShapeDtype...]
    pallas_call x2 -> x1, Pallas kernels: 15.1 us -> 7.61 us  [advance(): pl.pallas_call(step_kernel, grid_spec=grid_spec, out_shape=out_shape, com...]
    ppermute x5, waiting for transfers between devices: 6.39 us -> 0.66 us  [passed_along(): return lax.ppermute(value, axis, pairs)]
    ppermute x3, waiting for transfers between devices: 7.89 us -> 6.62 us  [relay_gather(): lax.ppermute(right, axis, [(i, i + 1) for i in range(r - 1, count - 1)])]
    ppermute x3, starting transfers between devices: 0.56 us -> 1.82 us  [on_device(): shifted.append(lax.ppermute(held_control, 'band', pairs))]
  transfers between devices with their start and end apart: 14 -> 14, of which waited for: 6 -> 5; matrix products, arithmetic and copies ran while one was open for 13% -> 13% of each run, Pallas kernels for 0% -> 7%
where the time goes in v7:
time: 101 us; the launch traced here: 99.8 us
  waiting for transfers between devices  36.2 us (36%)
  starting transfers between devices  24.3 us (24%)
  Pallas kernels  21.1 us (21%)
  local copies, waits for them, and re-layouts  13.4 us (13%)
  matrix products  3.41 us (3%)
    ppermute x3, waiting for transfers between devices, relay_gather(): lax.ppermute(left, axis, [(j, j - 1) for j in range(1, count - r + 1)])  28.9 us
    ppermute x5, starting transfers between devices, passed_along(): return lax.ppermute(value, axis, pairs)  13.1 us
    pallas_call x1, Pallas kernels, advance(): pl.pallas_call(step_kernel, grid_spec=grid_spec, out_shape=out_shape, com...  7.61 us
    unnamed x13, local copies, waits for them, and re-layouts  7.47 us
    pallas_call x1, Pallas kernels, edge_step(): pl.pallas_call(edge_kernel, grid_spec=grid_spec, out_shape=jax.ShapeDtype...  6.84 us
    pallas_call x1, Pallas kernels, interior_step(): pl.pallas_call(kernel, grid_spec=grid_spec, out_shape=jax.ShapeDtypeStruc...  6.69 us
    ppermute x3, waiting for transfers between devices, relay_gather(): lax.ppermute(right, axis, [(i, i + 1) for i in range(r - 1, count - 1)])  6.62 us
    ppermute x3, starting transfers between devices, relay_gather(): lax.ppermute(right, axis, [(i, i + 1) for i in range(r - 1, count - 1)])  5.43 us
  transfers between devices with their start and end apart: 14, of which 5 were waited for; matrix products, arithmetic and copies ran while one was open for 13% of the time, Pallas kernels for 7%

profile of v7, /device:TPU:1, one launch (start us, length us, event | category | flops | bytes accessed | tf_op | source)
XLA Modules:
  0.0 99.8 jit_solution(3337172668416602593)
XLA Ops:
  0.6 0.7 slice.9
  1.4 4.5 %collective-permute-start = (f32[1,48,128]{2,1,0:T(8,128)S(1)}, f32[1,48,128]{2,1,0:T(8,128)S(1)}, u32[]{:S(2)}, u32[]{:S(2)}) collective-permute-start(f32[1,48,128]{2,1,0:T(8,128)S(1)} %slice.9), channel_id=1, source_target_pairs={{0,1},{1,2},{2,3},{4,5},{5,6},{6,7},{8,9},{9,10},{10,11},{12,13},{... | collective-permute-start | bytes 73736 | tf_op jit(solution)/shard_map/ppermute | solution.py:16
  5.9 1.6 %constant_dynamic-update-slice_fusion.3 = f32[25,48,128]{2,1,0:T(8,128)} fusion(f32[8,48,128]{2,1,0:T(8,128)} %param.15), kind=kLoop, calls=%fused_computation.18 | loop fusion | bytes 393216
  7.5 1.6 %constant_dynamic-update-slice_fusion.2 = f32[25,48,128]{2,1,0:T(8,128)} fusion(f32[25,48,128]{2,1,0:T(8,128)} %constant_dynamic-update-slice_fusion.3, f32[8,48,128]{2,1,0:T(8,128)} %param.16), kind=kLoop, calls=%fused_computation.17 | loop fusion | bytes 393216
  9.1 0.7 constant_dynamic-slice_fusion.4
  10.0 1.6 %constant_dynamic-update-slice_fusion.1 = f32[25,48,128]{2,1,0:T(8,128)} fusion(f32[25,48,128]{2,1,0:T(8,128)} %constant_dynamic-update-slice_fusion.2, f32[8,48,128]{2,1,0:T(8,128)} %param.17), kind=kLoop, calls=%fused_computation.16 | loop fusion | bytes 393216
  12.3 4.0 %collective-permute-start.3 = (f32[25,48,128]{2,1,0:T(8,128)}, f32[25,48,128]{2,1,0:T(8,128)}, u32[]{:S(2)}, u32[]{:S(2)}) collective-permute-start(f32[25,48,128]{2,1,0:T(8,128)} %constant_dynamic-update-slice_fusion), channel_id=1, source_target_pairs={{0,4},{4,8},{8,12},{1,5},{5,9},{9,13},{2,6},{6,10},{10,14},{3,7},{... | collective-permute-start | bytes 1843208 | tf_op jit(solution)/shard_map/ppermute | solution.py:27
  16.9 1.0 %convolution_bitcast_fusion.3 = f32[4,8,512]{2,1,0:T(8,128)S(1)} fusion(f32[8,8,1]{1,0,2:T(8,128)S(1)} %bitcast.47, f32[4,8,512]{2,1,0:T(8,128)} %param.10), kind=kOutput, calls=%fused_computation.7 | convolution fusion | flops 1572864 | bytes 131328 | tf_op jit(solution)/shard_map/jm,kmn->kjn/dot_general | solution.py:270
  17.9 1.3 %collective-permute-start.4 = (f32[25,48,128]{2,1,0:T(8,128)}, f32[25,48,128]{2,1,0:T(8,128)S(1)}, u32[]{:S(2)}, u32[]{:S(2)}) collective-permute-start(f32[25,48,128]{2,1,0:T(8,128)} %constant_dynamic-update-slice_fusion), channel_id=1, source_target_pairs={{4,0},{8,4},{12,8},{5,1},{9,5},{13,9},{6,2},{10,6},{14,10},{7,3},{... | collective-permute-start | bytes 1843208 | tf_op jit(solution)/shard_map/ppermute | solution.py:28
  19.2 1.0 fusion.4
  20.6 1.4 %collective-permute-start.9 = (f32[4,8,512]{2,1,0:T(8,128)}, f32[4,8,512]{2,1,0:T(8,128)S(1)}, u32[]{:S(2)}, u32[]{:S(2)}) collective-permute-start(f32[4,8,512]{2,1,0:T(8,128)} %param.10), channel_id=1, source_target_pairs={{0,1},{1,2},{2,3},{3,0},{4,5},{5,6},{6,7},{7,4},{8,9},{9,10},{10,1... | collective-permute-start | bytes 196616 | tf_op jit(solution)/shard_map/ppermute | solution.py:259
  22.0 6.6 %collective-permute-done.3 = f32[25,48,128]{2,1,0:T(8,128)} collective-permute-done((f32[25,48,128]{2,1,0:T(8,128)}, f32[25,48,128]{2,1,0:T(8,128)}, u32[]{:S(2)}, u32[]{:S(2)}) %collective-permute-start.3) | collective-permute-done | bytes 614432 | tf_op jit(solution)/shard_map/ppermute | solution.py:27
  28.6 0.7 collective-permute-start.5
  29.3 1.2 %slice_bitcast_fusion = (f32[4,48,512]{2,1,0:T(8,128)S(1)}, f32[4,48,512]{2,1,0:T(8,128)S(1)}) fusion(f32[4,8,48,512]{3,2,1,0:T(8,128)} %q_ref.1), kind=kLoop, calls=%fused_computation.8 | loop fusion | bytes 1572864 | tf_op jit(solution)/shard_map/squeeze | solution.py:255
  30.7 1.1 %constant_dynamic-update-slice_fusion.10 = f32[25,48,640]{2,1,0:T(8,128)S(1)} fusion(f32[25,48,640]{2,1,0:T(8,128)S(1)} %broadcast_in_dim.2, f32[25,48,128]{2,1,0:T(8,128)} %constant_dynamic-update-slice_fusion, s32[]{:T(128)S(6)} %select_n.75), kind=kLoop, calls=%fused_computation.30 | loop fusion | bytes 1228804 | tf_op jit(solution)/shard_map/dynamic_update_slice | solution.py:24
  31.8 1.9 %collective-permute-start.2 = (f32[4,48,512]{2,1,0:T(8,128)S(1)}, f32[4,48,512]{2,1,0:T(8,128)S(1)}, u32[]{:S(2)}, u32[]{:S(2)}) collective-permute-start(f32[4,48,512]{2,1,0:T(8,128)S(1)} %get-tuple-element.12), channel_id=1, source_target_pairs={{1,0},{2,1},{3,2},{5,4},{6,5},{7,6},{9,8},{10,9},{11,10},{13,12},{... | collective-permute-start | bytes 1179656 | tf_op jit(solution)/shard_map/ppermute | solution.py:16
  33.8 1.3 %collective-permute-done.4 = f32[25,48,128]{2,1,0:T(8,128)S(1)} collective-permute-done((f32[25,48,128]{2,1,0:T(8,128)}, f32[25,48,128]{2,1,0:T(8,128)S(1)}, u32[]{:S(2)}, u32[]{:S(2)}) %collective-permute-start.4) | collective-permute-done | bytes 614432 | tf_op jit(solution)/shard_map/ppermute | solution.py:28
  35.1 1.3 %collective-permute-start.6 = (f32[25,48,128]{2,1,0:T(8,128)S(1)}, f32[25,48,128]{2,1,0:T(8,128)S(1)}, u32[]{:S(2)}, u32[]{:S(2)}) collective-permute-start(f32[25,48,128]{2,1,0:T(8,128)S(1)} %collective-permute-done.4), channel_id=1, source_target_pairs={{4,0},{8,4},{5,1},{9,5},{6,2},{10,6},{7,3},{11,7},{20,16},{24,20},... | collective-permute-start | bytes 1843208 | tf_op jit(solution)/shard_map/ppermute | solution.py:28
  36.6 2.4 %collective-permute-start.1 = (f32[4,48,512]{2,1,0:T(8,128)S(1)}, f32[4,48,512]{2,1,0:T(8,128)}, u32[]{:S(2)}, u32[]{:S(2)}) collective-permute-start(f32[4,48,512]{2,1,0:T(8,128)S(1)} %get-tuple-element.13), channel_id=1, source_target_pairs={{0,1},{1,2},{2,3},{4,5},{5,6},{6,7},{8,9},{9,10},{10,11},{12,13},{... | collective-permute-start | bytes 1179656 | tf_op jit(solution)/shard_map/ppermute | solution.py:16
  39.1 0.7 collective-permute-start.7
  39.9 0.8 fusion.2.src_ref.e
  40.7 13.3 %collective-permute-done.6 = f32[25,48,128]{2,1,0:T(8,128)S(1)} collective-permute-done((f32[25,48,128]{2,1,0:T(8,128)S(1)}, f32[25,48,128]{2,1,0:T(8,128)S(1)}, u32[]{:S(2)}, u32[]{:S(2)}) %collective-permute-start.6) | collective-permute-done | bytes 614432 | tf_op jit(solution)/shard_map/ppermute | solution.py:28
  54.0 1.3 %collective-permute-start.8 = (f32[25,48,128]{2,1,0:T(8,128)S(1)}, f32[25,48,128]{2,1,0:T(8,128)S(1)}, u32[]{:S(2)}, u32[]{:S(2)}) collective-permute-start(f32[25,48,128]{2,1,0:T(8,128)S(1)} %collective-permute-done.6), channel_id=1, source_target_pairs={{4,0},{5,1},{6,2},{7,3},{20,16},{21,17},{22,18},{23,19}} | collective-permute-start | bytes 1843208 | tf_op jit(solution)/shard_map/ppermute | solution.py:28
  55.3 1.1 %constant_dynamic-update-slice_fusion.9 = f32[25,48,640]{2,1,0:T(8,128)S(1)} fusion(f32[25,48,640]{2,1,0:T(8,128)S(1)} %constant_dynamic-update-slice_fusion.10, f32[25,48,128]{2,1,0:T(8,128)} %collective-permute-done.3, s32[]{:T(128)S(6)} %select_n.77), kind=kLoop, calls=%fused_computation.29 | loop fusion | bytes 1228804 | tf_op jit(solution)/shard_map/dynamic_update_slice | solution.py:30
  56.6 14.4 %collective-permute-done.8 = f32[25,48,128]{2,1,0:T(8,128)S(1)} collective-permute-done((f32[25,48,128]{2,1,0:T(8,128)S(1)}, f32[25,48,128]{2,1,0:T(8,128)S(1)}, u32[]{:S(2)}, u32[]{:S(2)}) %collective-permute-start.8) | collective-permute-done | bytes 614432 | tf_op jit(solution)/shard_map/ppermute | solution.py:28
  71.1 1.6 %copy-done.1 = f32[25,48,640]{2,1,0:T(8,128)} copy-done((f32[25,48,640]{2,1,0:T(8,128)}, f32[25,48,640]{2,1,0:T(8,128)S(1)}, u32[]{:S(2)}) %copy-start.1) | copy-done | bytes 3072024
  72.8 7.6 %shard_map.104 = (f32[4,8,48,512]{3,2,1,0:T(8,128)}, f32[4,48,512]{2,1,0:T(8,128)}, f32[4,48,512]{2,1,0:T(8,128)}) custom-call(f32[8]{0:T(128)} %compare_convert_fusion.north_ref.n, f32[4,8,48,512]{3,2,1,0:T(8,128)} %q_ref.1, f32[4,48,512]{2,1,0:T(8,128)} %collective-permute-done.1.qs_ref, f32[4,48,512]{2,1,0:T(8,128)} %copy-done.2, ...), custom_call_target="tpu_custom_call" | custom-call | tf_op jit(solution)/shard_map/pallas_call | solution.py:120
  80.4 2.4 %collective-permute-start.12 = (f32[4,48,512]{2,1,0:T(8,128)}, f32[4,48,512]{2,1,0:T(8,128)S(1)}, u32[]{:S(2)}, u32[]{:S(2)}) collective-permute-start(f32[4,48,512]{2,1,0:T(8,128)} %get-tuple-element.10), channel_id=1, source_target_pairs={{0,1},{1,2},{2,3},{4,5},{5,6},{6,7},{8,9},{9,10},{10,11},{12,13},{... | collective-permute-start | bytes 1179656 | tf_op jit(solution)/shard_map/ppermute | solution.py:16
  82.8 1.9 %collective-permute-start.13 = (f32[4,48,512]{2,1,0:T(8,128)}, f32[4,48,512]{2,1,0:T(8,128)S(1)}, u32[]{:S(2)}, u32[]{:S(2)}) collective-permute-start(f32[4,48,512]{2,1,0:T(8,128)} %get-tuple-element.11), channel_id=1, source_target_pairs={{1,0},{2,1},{3,2},{5,4},{6,5},{7,6},{9,8},{10,9},{11,10},{13,12},{... | collective-permute-start | bytes 1179656 | tf_op jit(solution)/shard_map/ppermute | solution.py:16
  84.8 6.7 %shard_map.105.base_ref = f32[4,8,48,512]{3,2,1,0:T(8,128)} custom-call(f32[8]{0:T(128)} %compare_convert_fusion.north_ref.n, f32[4,8,48,512]{3,2,1,0:T(8,128)} %get-tuple-element.9.q.qa_ref.qi_ref, f32[25,48,640]{2,1,0:T(8,128)} %copy-done.1, f32[4,8,512]{2,1,0:T(8,128)} %fusion.2.src_ref.e), custom_call_target="tpu_custom_call" | custom-call | tf_op jit(solution)/shard_map/pallas_call | solution.py:147
  92.2 0.8 copy-done.4
  93.0 6.8 %shard_map.106 = f32[4,8,48,512]{3,2,1,0:T(8,128)} custom-call(f32[8]{0:T(128)} %compare_convert_fusion.north_ref.n, f32[4,8,48,512]{3,2,1,0:T(8,128)} %get-tuple-element.9.q.qa_ref.qi_ref, f32[4,8,48,512]{3,2,1,0:T(8,128)} %get-tuple-element.9.q.qa_ref.qi_ref, f32[4,48,512]{2,1,0:T(8,128)} %copy-done.3, ...), custom_call_target="tpu_custom_call", output_to_operand_aliasing={{}: (10, {})} | custom-call | tf_op jit(solution)/shard_map/pallas_call | solution.py:225
  (32 shorter events, 3.5 us)
Async XLA Ops:
  0.6 9.2 %copy-start = (f32[8,8,8]{2,1,0:T(8,128)S(1)}, f32[8,8,8]{2,1,0:T(8,128)}, u32[]{:S(2)}) copy-start(f32[8,8,8]{2,1,0:T(8,128)} %param.11) | copy-start | bytes 6148
  1.4 10.3 %collective-permute-start = (f32[1,48,128]{2,1,0:T(8,128)S(1)}, f32[1,48,128]{2,1,0:T(8,128)S(1)}, u32[]{:S(2)}, u32[]{:S(2)}) collective-permute-start(f32[1,48,128]{2,1,0:T(8,128)S(1)} %slice.9), channel_id=1, source_target_pairs={{0,1},{1,2},{2,3},{4,5},{5,6},{6,7},{8,9},{9,10},{10,11},{12,13},{... | collective-permute-start | bytes 73736 | tf_op jit(solution)/shard_map/ppermute | solution.py:16
  12.3 16.4 %collective-permute-start.3 = (f32[25,48,128]{2,1,0:T(8,128)}, f32[25,48,128]{2,1,0:T(8,128)}, u32[]{:S(2)}, u32[]{:S(2)}) collective-permute-start(f32[25,48,128]{2,1,0:T(8,128)} %constant_dynamic-update-slice_fusion), channel_id=1, source_target_pairs={{0,4},{4,8},{8,12},{1,5},{5,9},{9,13},{2,6},{6,10},{10,14},{3,7},{... | collective-permute-start | bytes 1843208 | tf_op jit(solution)/shard_map/ppermute | solution.py:27
  17.9 17.2 %collective-permute-start.4 = (f32[25,48,128]{2,1,0:T(8,128)}, f32[25,48,128]{2,1,0:T(8,128)S(1)}, u32[]{:S(2)}, u32[]{:S(2)}) collective-permute-start(f32[25,48,128]{2,1,0:T(8,128)} %constant_dynamic-update-slice_fusion), channel_id=1, source_target_pairs={{4,0},{8,4},{12,8},{5,1},{9,5},{13,9},{6,2},{10,6},{14,10},{7,3},{... | collective-permute-start | bytes 1843208 | tf_op jit(solution)/shard_map/ppermute | solution.py:28
  20.2 16.4 %collective-permute-start.11 = (f32[4,8,512]{2,1,0:T(8,128)}, f32[4,8,512]{2,1,0:T(8,128)S(1)}, u32[]{:S(2)}, u32[]{:S(2)}) collective-permute-start(f32[4,8,512]{2,1,0:T(8,128)} %param.10), channel_id=1, source_target_pairs={{0,3},{1,0},{2,1},{3,2},{4,7},{5,4},{6,5},{7,6},{8,11},{9,8},{10,9... | collective-permute-start | bytes 196616 | tf_op jit(solution)/shard_map/ppermute | solution.py:259
  20.2 19.6 %collective-permute-start.10 = (f32[4,8,512]{2,1,0:T(8,128)}, f32[4,8,512]{2,1,0:T(8,128)S(1)}, u32[]{:S(2)}, u32[]{:S(2)}) collective-permute-start(f32[4,8,512]{2,1,0:T(8,128)} %param.10), channel_id=1, source_target_pairs={{0,2},{1,3},{2,0},{3,1},{4,6},{5,7},{6,4},{7,5},{8,10},{9,11},{10,... | collective-permute-start | bytes 196616 | tf_op jit(solution)/shard_map/ppermute | solution.py:259
  20.6 11.2 %collective-permute-start.9 = (f32[4,8,512]{2,1,0:T(8,128)}, f32[4,8,512]{2,1,0:T(8,128)S(1)}, u32[]{:S(2)}, u32[]{:S(2)}) collective-permute-start(f32[4,8,512]{2,1,0:T(8,128)} %param.10), channel_id=1, source_target_pairs={{0,1},{1,2},{2,3},{3,0},{4,5},{5,6},{6,7},{7,4},{8,9},{9,10},{10,1... | collective-permute-start | bytes 196616 | tf_op jit(solution)/shard_map/ppermute | solution.py:259
  28.6 10.5 %collective-permute-start.5 = (f32[25,48,128]{2,1,0:T(8,128)}, f32[25,48,128]{2,1,0:T(8,128)S(1)}, u32[]{:S(2)}, u32[]{:S(2)}) collective-permute-start(f32[25,48,128]{2,1,0:T(8,128)} %collective-permute-done.3), channel_id=1, source_target_pairs={{4,8},{8,12},{5,9},{9,13},{6,10},{10,14},{7,11},{11,15},{20,24},{2... | collective-permute-start | bytes 1843208 | tf_op jit(solution)/shard_map/ppermute | solution.py:27
  31.8 39.2 %collective-permute-start.2 = (f32[4,48,512]{2,1,0:T(8,128)S(1)}, f32[4,48,512]{2,1,0:T(8,128)S(1)}, u32[]{:S(2)}, u32[]{:S(2)}) collective-permute-start(f32[4,48,512]{2,1,0:T(8,128)S(1)} %get-tuple-element.12), channel_id=1, source_target_pairs={{1,0},{2,1},{3,2},{5,4},{6,5},{7,6},{9,8},{10,9},{11,10},{13,12},{... | collective-permute-start | bytes 1179656 | tf_op jit(solution)/shard_map/ppermute | solution.py:16
  35.1 18.9 %collective-permute-start.6 = (f32[25,48,128]{2,1,0:T(8,128)S(1)}, f32[25,48,128]{2,1,0:T(8,128)S(1)}, u32[]{:S(2)}, u32[]{:S(2)}) collective-permute-start(f32[25,48,128]{2,1,0:T(8,128)S(1)} %collective-permute-done.4), channel_id=1, source_target_pairs={{4,0},{8,4},{5,1},{9,5},{6,2},{10,6},{7,3},{11,7},{20,16},{24,20},... | collective-permute-start | bytes 1843208 | tf_op jit(solution)/shard_map/ppermute | solution.py:28
  36.6 34.5 %collective-permute-start.1 = (f32[4,48,512]{2,1,0:T(8,128)S(1)}, f32[4,48,512]{2,1,0:T(8,128)}, u32[]{:S(2)}, u32[]{:S(2)}) collective-permute-start(f32[4,48,512]{2,1,0:T(8,128)S(1)} %get-tuple-element.13), channel_id=1, source_target_pairs={{0,1},{1,2},{2,3},{4,5},{5,6},{6,7},{8,9},{9,10},{10,11},{12,13},{... | collective-permute-start | bytes 1179656 | tf_op jit(solution)/shard_map/ppermute | solution.py:16
  39.1 17.4 %collective-permute-start.7 = (f32[25,48,128]{2,1,0:T(8,128)S(1)}, f32[25,48,128]{2,1,0:T(8,128)S(1)}, u32[]{:S(2)}, u32[]{:S(2)}) collective-permute-start(f32[25,48,128]{2,1,0:T(8,128)S(1)} %collective-permute-done.5), channel_id=1, source_target_pairs={{8,12},{9,13},{10,14},{11,15},{24,28},{25,29},{26,30},{27,31}} | collective-permute-start | bytes 1843208 | tf_op jit(solution)/shard_map/ppermute | solution.py:27
  54.0 17.0 %collective-permute-start.8 = (f32[25,48,128]{2,1,0:T(8,128)S(1)}, f32[25,48,128]{2,1,0:T(8,128)S(1)}, u32[]{:S(2)}, u32[]{:S(2)}) collective-permute-start(f32[25,48,128]{2,1,0:T(8,128)S(1)} %collective-permute-done.6), channel_id=1, source_target_pairs={{4,0},{5,1},{6,2},{7,3},{20,16},{21,17},{22,18},{23,19}} | collective-permute-start | bytes 1843208 | tf_op jit(solution)/shard_map/ppermute | solution.py:28
  71.0 1.7 %copy-start.1 = (f32[25,48,640]{2,1,0:T(8,128)}, f32[25,48,640]{2,1,0:T(8,128)S(1)}, u32[]{:S(2)}) copy-start(f32[25,48,640]{2,1,0:T(8,128)S(1)} %constant_dynamic-update-slice_fusion.4.wx_ref.w.u_ref.v_ref.vm_ref.w_ref) | copy-start | bytes 9216004
  71.1 1.7 %copy-start.2 = (f32[4,48,512]{2,1,0:T(8,128)}, f32[4,48,512]{2,1,0:T(8,128)S(1)}, u32[]{:S(2)}) copy-start(f32[4,48,512]{2,1,0:T(8,128)S(1)} %collective-permute-done.2.qn_ref) | copy-start | bytes 1179652
  80.4 11.1 %collective-permute-start.12 = (f32[4,48,512]{2,1,0:T(8,128)}, f32[4,48,512]{2,1,0:T(8,128)S(1)}, u32[]{:S(2)}, u32[]{:S(2)}) collective-permute-start(f32[4,48,512]{2,1,0:T(8,128)} %get-tuple-element.10), channel_id=1, source_target_pairs={{0,1},{1,2},{2,3},{4,5},{5,6},{6,7},{8,9},{9,10},{10,11},{12,13},{... | collective-permute-start | bytes 1179656 | tf_op jit(solution)/shard_map/ppermute | solution.py:16
  82.8 9.3 %collective-permute-start.13 = (f32[4,48,512]{2,1,0:T(8,128)}, f32[4,48,512]{2,1,0:T(8,128)S(1)}, u32[]{:S(2)}, u32[]{:S(2)}) collective-permute-start(f32[4,48,512]{2,1,0:T(8,128)} %get-tuple-element.11), channel_id=1, source_target_pairs={{1,0},{2,1},{3,2},{5,4},{6,5},{7,6},{9,8},{10,9},{11,10},{13,12},{... | collective-permute-start | bytes 1179656 | tf_op jit(solution)/shard_map/ppermute | solution.py:16
  91.5 0.8 copy-start.3
  92.2 0.8 copy-start.4

commit v8 on v7

--- a/solution.py
+++ b/solution.py
@@ -154,18 +154,14 @@
 
 def edge_kernel(north_ref, qa_ref, qi_ref, qs_ref, qn_ref, u_ref, v_ref, vm_ref, w_ref, src_ref, base_ref, o_ref):
     del base_ref
-    lat_rows = src_ref.shape[1]
+    tracers, lat_rows = src_ref.shape[0], src_ref.shape[1]
     levels, lon = qa_ref.shape[2], qa_ref.shape[3]
-    top = pl.program_id(1)
+    top = pl.program_id(0)
     level = lax.broadcasted_iota(jnp.int32, (levels, lon), 0)
     not_top = level < levels - 1
     not_bottom = level > 0
     a = top * (lat_rows - 1)
-    qa = qa_ref[0, 0]
-    inner = qi_ref[0, 0]
     is_top = jnp.full((levels, lon), top, jnp.int32) == 1
-    qm = jnp.where(is_top, inner, qs_ref[0])
-    qp = jnp.where(is_top, qn_ref[0], inner)
     u = u_ref[0]
     uw = pltpu.roll(u, 1, 1)
     v = v_ref[0] * north_ref[a]
@@ -182,52 +178,60 @@
         - w_up
         - w_down
     )
-    result = (
-        c_self * qa
-        + (-jnp.minimum(u, 0.0)) * pltpu.roll(qa, lon - 1, 1)
-        + jnp.maximum(uw, 0.0) * pltpu.roll(qa, 1, 1)
-        + (-jnp.minimum(v, 0.0)) * qp
-        + jnp.maximum(vm, 0.0) * qm
-        + w_up * pltpu.roll(qa, levels - 1, 0)
-        + w_down * pltpu.roll(qa, 1, 0)
-    )
-    first_row = src_ref[0, 0:1, :]
-    last_row = src_ref[0, lat_rows - 1 : lat_rows, :]
-    source = jnp.where(jnp.full((1, lon), top, jnp.int32) == 1, last_row, first_row)
-    o_ref[0, 0] = result
-    o_ref[0, 0, 0:1, :] = result[0:1] + source
+    c_east = -jnp.minimum(u, 0.0)
+    c_west = jnp.maximum(uw, 0.0)
+    c_north = -jnp.minimum(v, 0.0)
+    c_south = jnp.maximum(vm, 0.0)
+    at_top = jnp.full((1, lon), top, jnp.int32) == 1
+    for k in range(tracers):
+        qa = qa_ref[k, 0]
+        inner = qi_ref[k, 0]
+        qm = jnp.where(is_top, inner, qs_ref[k])
+        qp = jnp.where(is_top, qn_ref[k], inner)
+        result = (
+            c_self * qa
+            + c_east * pltpu.roll(qa, lon - 1, 1)
+            + c_west * pltpu.roll(qa, 1, 1)
+            + c_north * qp
+            + c_south * qm
+            + w_up * pltpu.roll(qa, levels - 1, 0)
+            + w_down * pltpu.roll(qa, 1, 0)
+        )
+        source = jnp.where(at_top, src_ref[k, lat_rows - 1 : lat_rows, :], src_ref[k, 0:1, :])
+        o_ref[k, 0] = result
+        o_ref[k, 0, 0:1, :] = result[0:1] + source
 
 
 def edge_step(state, base, south, north, weather, emission, north_open):
     tracers, lat_rows, levels, lon = state.shape
     last = lat_rows - 1
-    one = lambda index: pl.BlockSpec((1, 1, levels, lon), index)
-    edge = pl.BlockSpec((1, levels, lon), lambda k, e: (k, 0, 0))
+    one = lambda index: pl.BlockSpec((tracers, 1, levels, lon), index)
+    edge = pl.BlockSpec((tracers, levels, lon), lambda e: (0, 0, 0))
     met = lambda index: pl.BlockSpec((1, levels, lon), index)
     grid_spec = pltpu.PrefetchScalarGridSpec(
         num_scalar_prefetch=0,
-        grid=(tracers, 2),
+        grid=(2,),
         in_specs=[
             pl.BlockSpec(memory_space=pltpu.SMEM),
-            one(lambda k, e: (k, e * last, 0, 0)),
-            one(lambda k, e: (k, 1 + e * (lat_rows - 3), 0, 0)),
+            one(lambda e: (0, e * last, 0, 0)),
+            one(lambda e: (0, 1 + e * (lat_rows - 3), 0, 0)),
             edge,
             edge,
-            met(lambda k, e: (e * last, 0, 0)),
-            met(lambda k, e: (lat_rows + e * last, 0, 0)),
-            met(lambda k, e: (3 * lat_rows - e * (lat_rows + 2), 0, 0)),
-            met(lambda k, e: (2 * lat_rows + e * last, 0, 0)),
-            pl.BlockSpec((1, lat_rows, lon), lambda k, e: (k, 0, 0)),
+            met(lambda e: (e * last, 0, 0)),
+            met(lambda e: (lat_rows + e * last, 0, 0)),
+            met(lambda e: (3 * lat_rows - e * (lat_rows + 2), 0, 0)),
+            met(lambda e: (2 * lat_rows + e * last, 0, 0)),
+            pl.BlockSpec((tracers, lat_rows, lon), lambda e: (0, 0, 0)),
             pl.BlockSpec(memory_space=pl.ANY),
         ],
-        out_specs=one(lambda k, e: (k, e * last, 0, 0)),
+        out_specs=one(lambda e: (0, e * last, 0, 0)),
     )
     return pl.pallas_call(
         edge_kernel,
         grid_spec=grid_spec,
         out_shape=jax.ShapeDtypeStruct(state.shape, state.dtype),
         input_output_aliases={10: 0},
-        compiler_params=pltpu.CompilerParams(dimension_semantics=("arbitrary", "arbitrary")),
+        compiler_params=pltpu.CompilerParams(dimension_semantics=("arbitrary",)),
     )(north_open, state, state, south, north, weather, weather, weather, weather, emission, base)
 
 

time: 101 us -> 97.1 us (0.961)
  Pallas kernels: 21.1 us -> 17.5 us
    pallas_call x1, Pallas kernels: 6.84 us -> 3.23 us  [edge_step(): pl.pallas_call(edge_kernel, grid_spec=grid_spec, out_shape=jax.ShapeDtype...]
  transfers between devices with their start and end apart: 14 -> 14, of which waited for: 5 -> 5; matrix products, arithmetic and copies ran while one was open for 13% -> 14% of each run, Pallas kernels for 7% -> 7%
where the time goes in v8:
time: 97.1 us; the launch traced here: 96.2 us
  waiting for transfers between devices  36.2 us (37%)
  starting transfers between devices  24.3 us (25%)
  Pallas kernels  17.5 us (18%)
  local copies, waits for them, and re-layouts  13.4 us (14%)
  matrix products  3.41 us (4%)
    ppermute x3, waiting for transfers between devices, relay_gather(): lax.ppermute(left, axis, [(j, j - 1) for j in range(1, count - r + 1)])  28.9 us
    ppermute x5, starting transfers between devices, passed_along(): return lax.ppermute(value, axis, pairs)  13.1 us
    pallas_call x1, Pallas kernels, advance(): pl.pallas_call(step_kernel, grid_spec=grid_spec, out_shape=out_shape, com...  7.61 us
    unnamed x13, local copies, waits for them, and re-layouts  7.47 us
    pallas_call x1, Pallas kernels, interior_step(): pl.pallas_call(kernel, grid_spec=grid_spec, out_shape=jax.ShapeDtypeStruc...  6.69 us
    ppermute x3, waiting for transfers between devices, relay_gather(): lax.ppermute(right, axis, [(i, i + 1) for i in range(r - 1, count - 1)])  6.62 us
    ppermute x3, starting transfers between devices, relay_gather(): lax.ppermute(right, axis, [(i, i + 1) for i in range(r - 1, count - 1)])  5.43 us
    ppermute x3, starting transfers between devices, relay_gather(): lax.ppermute(left, axis, [(j, j - 1) for j in range(1, count - r + 1)])  3.85 us
  transfers between devices with their start and end apart: 14, of which 5 were waited for; matrix products, arithmetic and copies ran while one was open for 14% of the time, Pallas kernels for 7%

profile of v8, /device:TPU:1, one launch (start us, length us, event | category | flops | bytes accessed | tf_op | source)
XLA Modules:
  0.0 96.2 jit_solution(197112372748698772)
XLA Ops:
  0.6 0.7 slice.9
  1.4 4.5 %collective-permute-start = (f32[1,48,128]{2,1,0:T(8,128)S(1)}, f32[1,48,128]{2,1,0:T(8,128)S(1)}, u32[]{:S(2)}, u32[]{:S(2)}) collective-permute-start(f32[1,48,128]{2,1,0:T(8,128)S(1)} %slice.9), channel_id=1, source_target_pairs={{0,1},{1,2},{2,3},{4,5},{5,6},{6,7},{8,9},{9,10},{10,11},{12,13},{... | collective-permute-start | bytes 73736 | tf_op jit(solution)/shard_map/ppermute | solution.py:16
  5.9 1.6 %constant_dynamic-update-slice_fusion.3 = f32[25,48,128]{2,1,0:T(8,128)} fusion(f32[8,48,128]{2,1,0:T(8,128)} %param.15), kind=kLoop, calls=%fused_computation.18 | loop fusion | bytes 393216
  7.5 1.6 %constant_dynamic-update-slice_fusion.2 = f32[25,48,128]{2,1,0:T(8,128)} fusion(f32[25,48,128]{2,1,0:T(8,128)} %constant_dynamic-update-slice_fusion.3, f32[8,48,128]{2,1,0:T(8,128)} %param.16), kind=kLoop, calls=%fused_computation.17 | loop fusion | bytes 393216
  9.1 0.7 constant_dynamic-slice_fusion.4
  10.0 1.6 %constant_dynamic-update-slice_fusion.1 = f32[25,48,128]{2,1,0:T(8,128)} fusion(f32[25,48,128]{2,1,0:T(8,128)} %constant_dynamic-update-slice_fusion.2, f32[8,48,128]{2,1,0:T(8,128)} %param.17), kind=kLoop, calls=%fused_computation.16 | loop fusion | bytes 393216
  12.3 4.0 %collective-permute-start.3 = (f32[25,48,128]{2,1,0:T(8,128)}, f32[25,48,128]{2,1,0:T(8,128)}, u32[]{:S(2)}, u32[]{:S(2)}) collective-permute-start(f32[25,48,128]{2,1,0:T(8,128)} %constant_dynamic-update-slice_fusion), channel_id=1, source_target_pairs={{0,4},{4,8},{8,12},{1,5},{5,9},{9,13},{2,6},{6,10},{10,14},{3,7},{... | collective-permute-start | bytes 1843208 | tf_op jit(solution)/shard_map/ppermute | solution.py:27
  16.9 1.0 %convolution_bitcast_fusion.3 = f32[4,8,512]{2,1,0:T(8,128)S(1)} fusion(f32[8,8,1]{1,0,2:T(8,128)S(1)} %bitcast.47, f32[4,8,512]{2,1,0:T(8,128)} %param.10), kind=kOutput, calls=%fused_computation.7 | convolution fusion | flops 1572864 | bytes 131328 | tf_op jit(solution)/shard_map/jm,kmn->kjn/dot_general | solution.py:274
  17.9 1.3 %collective-permute-start.4 = (f32[25,48,128]{2,1,0:T(8,128)}, f32[25,48,128]{2,1,0:T(8,128)S(1)}, u32[]{:S(2)}, u32[]{:S(2)}) collective-permute-start(f32[25,48,128]{2,1,0:T(8,128)} %constant_dynamic-update-slice_fusion), channel_id=1, source_target_pairs={{4,0},{8,4},{12,8},{5,1},{9,5},{13,9},{6,2},{10,6},{14,10},{7,3},{... | collective-permute-start | bytes 1843208 | tf_op jit(solution)/shard_map/ppermute | solution.py:28
  19.2 1.0 %fusion.4 = f32[8,512,4]{1,2,0:T(4,128)S(1)} fusion(s32[8,512]{1,0:T(8,128)} %param.13, f32[4,22]{1,0:T(4,128)} %param.14), kind=kOutput, calls=%fused_computation.11 | convolution fusion | flops 4415488 | bytes 82272 | tf_op jit(solution)/shard_map/kr,jnr->kjn/dot_general | solution.py:280
  20.6 1.4 %collective-permute-start.9 = (f32[4,8,512]{2,1,0:T(8,128)}, f32[4,8,512]{2,1,0:T(8,128)S(1)}, u32[]{:S(2)}, u32[]{:S(2)}) collective-permute-start(f32[4,8,512]{2,1,0:T(8,128)} %param.10), channel_id=1, source_target_pairs={{0,1},{1,2},{2,3},{3,0},{4,5},{5,6},{6,7},{7,4},{8,9},{9,10},{10,1... | collective-permute-start | bytes 196616 | tf_op jit(solution)/shard_map/ppermute | solution.py:263
  22.0 6.6 %collective-permute-done.3 = f32[25,48,128]{2,1,0:T(8,128)} collective-permute-done((f32[25,48,128]{2,1,0:T(8,128)}, f32[25,48,128]{2,1,0:T(8,128)}, u32[]{:S(2)}, u32[]{:S(2)}) %collective-permute-start.3) | collective-permute-done | bytes 614432 | tf_op jit(solution)/shard_map/ppermute | solution.py:27
  28.6 0.7 collective-permute-start.5
  29.3 1.2 %slice_bitcast_fusion = (f32[4,48,512]{2,1,0:T(8,128)S(1)}, f32[4,48,512]{2,1,0:T(8,128)S(1)}) fusion(f32[4,8,48,512]{3,2,1,0:T(8,128)} %q_ref.1), kind=kLoop, calls=%fused_computation.8 | loop fusion | bytes 1572864 | tf_op jit(solution)/shard_map/squeeze | solution.py:259
  30.7 1.1 %constant_dynamic-update-slice_fusion.10 = f32[25,48,640]{2,1,0:T(8,128)S(1)} fusion(f32[25,48,640]{2,1,0:T(8,128)S(1)} %broadcast_in_dim.2, f32[25,48,128]{2,1,0:T(8,128)} %constant_dynamic-update-slice_fusion, s32[]{:T(128)S(6)} %select_n.75), kind=kLoop, calls=%fused_computation.30 | loop fusion | bytes 1228804 | tf_op jit(solution)/shard_map/dynamic_update_slice | solution.py:24
  31.8 1.9 %collective-permute-start.2 = (f32[4,48,512]{2,1,0:T(8,128)S(1)}, f32[4,48,512]{2,1,0:T(8,128)S(1)}, u32[]{:S(2)}, u32[]{:S(2)}) collective-permute-start(f32[4,48,512]{2,1,0:T(8,128)S(1)} %get-tuple-element.12), channel_id=1, source_target_pairs={{1,0},{2,1},{3,2},{5,4},{6,5},{7,6},{9,8},{10,9},{11,10},{13,12},{... | collective-permute-start | bytes 1179656 | tf_op jit(solution)/shard_map/ppermute | solution.py:16
  33.8 1.3 %collective-permute-done.4 = f32[25,48,128]{2,1,0:T(8,128)S(1)} collective-permute-done((f32[25,48,128]{2,1,0:T(8,128)}, f32[25,48,128]{2,1,0:T(8,128)S(1)}, u32[]{:S(2)}, u32[]{:S(2)}) %collective-permute-start.4) | collective-permute-done | bytes 614432 | tf_op jit(solution)/shard_map/ppermute | solution.py:28
  35.1 1.3 %collective-permute-start.6 = (f32[25,48,128]{2,1,0:T(8,128)S(1)}, f32[25,48,128]{2,1,0:T(8,128)S(1)}, u32[]{:S(2)}, u32[]{:S(2)}) collective-permute-start(f32[25,48,128]{2,1,0:T(8,128)S(1)} %collective-permute-done.4), channel_id=1, source_target_pairs={{4,0},{8,4},{5,1},{9,5},{6,2},{10,6},{7,3},{11,7},{20,16},{24,20},... | collective-permute-start | bytes 1843208 | tf_op jit(solution)/shard_map/ppermute | solution.py:28
  36.6 2.4 %collective-permute-start.1 = (f32[4,48,512]{2,1,0:T(8,128)S(1)}, f32[4,48,512]{2,1,0:T(8,128)}, u32[]{:S(2)}, u32[]{:S(2)}) collective-permute-start(f32[4,48,512]{2,1,0:T(8,128)S(1)} %get-tuple-element.13), channel_id=1, source_target_pairs={{0,1},{1,2},{2,3},{4,5},{5,6},{6,7},{8,9},{9,10},{10,11},{12,13},{... | collective-permute-start | bytes 1179656 | tf_op jit(solution)/shard_map/ppermute | solution.py:16
  39.1 0.7 collective-permute-start.7
  39.9 0.8 fusion.2.src_ref.e
  40.7 13.3 %collective-permute-done.6 = f32[25,48,128]{2,1,0:T(8,128)S(1)} collective-permute-done((f32[25,48,128]{2,1,0:T(8,128)S(1)}, f32[25,48,128]{2,1,0:T(8,128)S(1)}, u32[]{:S(2)}, u32[]{:S(2)}) %collective-permute-start.6) | collective-permute-done | bytes 614432 | tf_op jit(solution)/shard_map/ppermute | solution.py:28
  54.0 1.3 %collective-permute-start.8 = (f32[25,48,128]{2,1,0:T(8,128)S(1)}, f32[25,48,128]{2,1,0:T(8,128)S(1)}, u32[]{:S(2)}, u32[]{:S(2)}) collective-permute-start(f32[25,48,128]{2,1,0:T(8,128)S(1)} %collective-permute-done.6), channel_id=1, source_target_pairs={{4,0},{5,1},{6,2},{7,3},{20,16},{21,17},{22,18},{23,19}} | collective-permute-start | bytes 1843208 | tf_op jit(solution)/shard_map/ppermute | solution.py:28
  55.3 1.1 %constant_dynamic-update-slice_fusion.9 = f32[25,48,640]{2,1,0:T(8,128)S(1)} fusion(f32[25,48,640]{2,1,0:T(8,128)S(1)} %constant_dynamic-update-slice_fusion.10, f32[25,48,128]{2,1,0:T(8,128)} %collective-permute-done.3, s32[]{:T(128)S(6)} %select_n.77), kind=kLoop, calls=%fused_computation.29 | loop fusion | bytes 1228804 | tf_op jit(solution)/shard_map/dynamic_update_slice | solution.py:30
  56.6 14.4 %collective-permute-done.8 = f32[25,48,128]{2,1,0:T(8,128)S(1)} collective-permute-done((f32[25,48,128]{2,1,0:T(8,128)S(1)}, f32[25,48,128]{2,1,0:T(8,128)S(1)}, u32[]{:S(2)}, u32[]{:S(2)}) %collective-permute-start.8) | collective-permute-done | bytes 614432 | tf_op jit(solution)/shard_map/ppermute | solution.py:28
  71.1 1.6 %copy-done.1 = f32[25,48,640]{2,1,0:T(8,128)} copy-done((f32[25,48,640]{2,1,0:T(8,128)}, f32[25,48,640]{2,1,0:T(8,128)S(1)}, u32[]{:S(2)}) %copy-start.1) | copy-done | bytes 3072024
  72.8 7.6 %shard_map.104 = (f32[4,8,48,512]{3,2,1,0:T(8,128)}, f32[4,48,512]{2,1,0:T(8,128)}, f32[4,48,512]{2,1,0:T(8,128)}) custom-call(f32[8]{0:T(128)} %compare_convert_fusion.north_ref.n, f32[4,8,48,512]{3,2,1,0:T(8,128)} %q_ref.1, f32[4,48,512]{2,1,0:T(8,128)} %collective-permute-done.1.qs_ref, f32[4,48,512]{2,1,0:T(8,128)} %copy-done.2, ...), custom_call_target="tpu_custom_call" | custom-call | tf_op jit(solution)/shard_map/pallas_call | solution.py:120
  80.4 2.4 %collective-permute-start.12 = (f32[4,48,512]{2,1,0:T(8,128)}, f32[4,48,512]{2,1,0:T(8,128)S(1)}, u32[]{:S(2)}, u32[]{:S(2)}) collective-permute-start(f32[4,48,512]{2,1,0:T(8,128)} %get-tuple-element.10), channel_id=1, source_target_pairs={{0,1},{1,2},{2,3},{4,5},{5,6},{6,7},{8,9},{9,10},{10,11},{12,13},{... | collective-permute-start | bytes 1179656 | tf_op jit(solution)/shard_map/ppermute | solution.py:16
  82.8 1.9 %collective-permute-start.13 = (f32[4,48,512]{2,1,0:T(8,128)}, f32[4,48,512]{2,1,0:T(8,128)S(1)}, u32[]{:S(2)}, u32[]{:S(2)}) collective-permute-start(f32[4,48,512]{2,1,0:T(8,128)} %get-tuple-element.11), channel_id=1, source_target_pairs={{1,0},{2,1},{3,2},{5,4},{6,5},{7,6},{9,8},{10,9},{11,10},{13,12},{... | collective-permute-start | bytes 1179656 | tf_op jit(solution)/shard_map/ppermute | solution.py:16
  84.8 6.7 %shard_map.105.base_ref = f32[4,8,48,512]{3,2,1,0:T(8,128)} custom-call(f32[8]{0:T(128)} %compare_convert_fusion.north_ref.n, f32[4,8,48,512]{3,2,1,0:T(8,128)} %get-tuple-element.9.q.qa_ref.qi_ref, f32[25,48,640]{2,1,0:T(8,128)} %copy-done.1, f32[4,8,512]{2,1,0:T(8,128)} %fusion.2.src_ref.e), custom_call_target="tpu_custom_call" | custom-call | tf_op jit(solution)/shard_map/pallas_call | solution.py:147
  92.2 0.8 copy-done.4
  93.0 3.2 %shard_map.106 = f32[4,8,48,512]{3,2,1,0:T(8,128)} custom-call(f32[8]{0:T(128)} %compare_convert_fusion.north_ref.n, f32[4,8,48,512]{3,2,1,0:T(8,128)} %get-tuple-element.9.q.qa_ref.qi_ref, f32[4,8,48,512]{3,2,1,0:T(8,128)} %get-tuple-element.9.q.qa_ref.qi_ref, f32[4,48,512]{2,1,0:T(8,128)} %copy-done.3, ...), custom_call_target="tpu_custom_call", output_to_operand_aliasing={{}: (10, {})} | custom-call | tf_op jit(solution)/shard_map/pallas_call | solution.py:229
  (32 shorter events, 3.5 us)
Async XLA Ops:
  0.6 9.2 %copy-start = (f32[8,8,8]{2,1,0:T(8,128)S(1)}, f32[8,8,8]{2,1,0:T(8,128)}, u32[]{:S(2)}) copy-start(f32[8,8,8]{2,1,0:T(8,128)} %param.11) | copy-start | bytes 6148
  1.4 10.3 %collective-permute-start = (f32[1,48,128]{2,1,0:T(8,128)S(1)}, f32[1,48,128]{2,1,0:T(8,128)S(1)}, u32[]{:S(2)}, u32[]{:S(2)}) collective-permute-start(f32[1,48,128]{2,1,0:T(8,128)S(1)} %slice.9), channel_id=1, source_target_pairs={{0,1},{1,2},{2,3},{4,5},{5,6},{6,7},{8,9},{9,10},{10,11},{12,13},{... | collective-permute-start | bytes 73736 | tf_op jit(solution)/shard_map/ppermute | solution.py:16
  12.3 16.4 %collective-permute-start.3 = (f32[25,48,128]{2,1,0:T(8,128)}, f32[25,48,128]{2,1,0:T(8,128)}, u32[]{:S(2)}, u32[]{:S(2)}) collective-permute-start(f32[25,48,128]{2,1,0:T(8,128)} %constant_dynamic-update-slice_fusion), channel_id=1, source_target_pairs={{0,4},{4,8},{8,12},{1,5},{5,9},{9,13},{2,6},{6,10},{10,14},{3,7},{... | collective-permute-start | bytes 1843208 | tf_op jit(solution)/shard_map/ppermute | solution.py:27
  17.9 17.2 %collective-permute-start.4 = (f32[25,48,128]{2,1,0:T(8,128)}, f32[25,48,128]{2,1,0:T(8,128)S(1)}, u32[]{:S(2)}, u32[]{:S(2)}) collective-permute-start(f32[25,48,128]{2,1,0:T(8,128)} %constant_dynamic-update-slice_fusion), channel_id=1, source_target_pairs={{4,0},{8,4},{12,8},{5,1},{9,5},{13,9},{6,2},{10,6},{14,10},{7,3},{... | collective-permute-start | bytes 1843208 | tf_op jit(solution)/shard_map/ppermute | solution.py:28
  20.2 16.4 %collective-permute-start.11 = (f32[4,8,512]{2,1,0:T(8,128)}, f32[4,8,512]{2,1,0:T(8,128)S(1)}, u32[]{:S(2)}, u32[]{:S(2)}) collective-permute-start(f32[4,8,512]{2,1,0:T(8,128)} %param.10), channel_id=1, source_target_pairs={{0,3},{1,0},{2,1},{3,2},{4,7},{5,4},{6,5},{7,6},{8,11},{9,8},{10,9... | collective-permute-start | bytes 196616 | tf_op jit(solution)/shard_map/ppermute | solution.py:263
  20.2 19.6 %collective-permute-start.10 = (f32[4,8,512]{2,1,0:T(8,128)}, f32[4,8,512]{2,1,0:T(8,128)S(1)}, u32[]{:S(2)}, u32[]{:S(2)}) collective-permute-start(f32[4,8,512]{2,1,0:T(8,128)} %param.10), channel_id=1, source_target_pairs={{0,2},{1,3},{2,0},{3,1},{4,6},{5,7},{6,4},{7,5},{8,10},{9,11},{10,... | collective-permute-start | bytes 196616 | tf_op jit(solution)/shard_map/ppermute | solution.py:263
  20.6 11.2 %collective-permute-start.9 = (f32[4,8,512]{2,1,0:T(8,128)}, f32[4,8,512]{2,1,0:T(8,128)S(1)}, u32[]{:S(2)}, u32[]{:S(2)}) collective-permute-start(f32[4,8,512]{2,1,0:T(8,128)} %param.10), channel_id=1, source_target_pairs={{0,1},{1,2},{2,3},{3,0},{4,5},{5,6},{6,7},{7,4},{8,9},{9,10},{10,1... | collective-permute-start | bytes 196616 | tf_op jit(solution)/shard_map/ppermute | solution.py:263
  28.6 10.5 %collective-permute-start.5 = (f32[25,48,128]{2,1,0:T(8,128)}, f32[25,48,128]{2,1,0:T(8,128)S(1)}, u32[]{:S(2)}, u32[]{:S(2)}) collective-permute-start(f32[25,48,128]{2,1,0:T(8,128)} %collective-permute-done.3), channel_id=1, source_target_pairs={{4,8},{8,12},{5,9},{9,13},{6,10},{10,14},{7,11},{11,15},{20,24},{2... | collective-permute-start | bytes 1843208 | tf_op jit(solution)/shard_map/ppermute | solution.py:27
  31.8 39.2 %collective-permute-start.2 = (f32[4,48,512]{2,1,0:T(8,128)S(1)}, f32[4,48,512]{2,1,0:T(8,128)S(1)}, u32[]{:S(2)}, u32[]{:S(2)}) collective-permute-start(f32[4,48,512]{2,1,0:T(8,128)S(1)} %get-tuple-element.12), channel_id=1, source_target_pairs={{1,0},{2,1},{3,2},{5,4},{6,5},{7,6},{9,8},{10,9},{11,10},{13,12},{... | collective-permute-start | bytes 1179656 | tf_op jit(solution)/shard_map/ppermute | solution.py:16
  35.1 18.9 %collective-permute-start.6 = (f32[25,48,128]{2,1,0:T(8,128)S(1)}, f32[25,48,128]{2,1,0:T(8,128)S(1)}, u32[]{:S(2)}, u32[]{:S(2)}) collective-permute-start(f32[25,48,128]{2,1,0:T(8,128)S(1)} %collective-permute-done.4), channel_id=1, source_target_pairs={{4,0},{8,4},{5,1},{9,5},{6,2},{10,6},{7,3},{11,7},{20,16},{24,20},... | collective-permute-start | bytes 1843208 | tf_op jit(solution)/shard_map/ppermute | solution.py:28
  36.6 34.5 %collective-permute-start.1 = (f32[4,48,512]{2,1,0:T(8,128)S(1)}, f32[4,48,512]{2,1,0:T(8,128)}, u32[]{:S(2)}, u32[]{:S(2)}) collective-permute-start(f32[4,48,512]{2,1,0:T(8,128)S(1)} %get-tuple-element.13), channel_id=1, source_target_pairs={{0,1},{1,2},{2,3},{4,5},{5,6},{6,7},{8,9},{9,10},{10,11},{12,13},{... | collective-permute-start | bytes 1179656 | tf_op jit(solution)/shard_map/ppermute | solution.py:16
  39.1 17.4 %collective-permute-start.7 = (f32[25,48,128]{2,1,0:T(8,128)S(1)}, f32[25,48,128]{2,1,0:T(8,128)S(1)}, u32[]{:S(2)}, u32[]{:S(2)}) collective-permute-start(f32[25,48,128]{2,1,0:T(8,128)S(1)} %collective-permute-done.5), channel_id=1, source_target_pairs={{8,12},{9,13},{10,14},{11,15},{24,28},{25,29},{26,30},{27,31}} | collective-permute-start | bytes 1843208 | tf_op jit(solution)/shard_map/ppermute | solution.py:27
  54.0 17.0 %collective-permute-start.8 = (f32[25,48,128]{2,1,0:T(8,128)S(1)}, f32[25,48,128]{2,1,0:T(8,128)S(1)}, u32[]{:S(2)}, u32[]{:S(2)}) collective-permute-start(f32[25,48,128]{2,1,0:T(8,128)S(1)} %collective-permute-done.6), channel_id=1, source_target_pairs={{4,0},{5,1},{6,2},{7,3},{20,16},{21,17},{22,18},{23,19}} | collective-permute-start | bytes 1843208 | tf_op jit(solution)/shard_map/ppermute | solution.py:28
  71.0 1.7 %copy-start.1 = (f32[25,48,640]{2,1,0:T(8,128)}, f32[25,48,640]{2,1,0:T(8,128)S(1)}, u32[]{:S(2)}) copy-start(f32[25,48,640]{2,1,0:T(8,128)S(1)} %constant_dynamic-update-slice_fusion.4.wx_ref.w.u_ref.v_ref.vm_ref.w_ref) | copy-start | bytes 9216004
  71.1 1.7 %copy-start.2 = (f32[4,48,512]{2,1,0:T(8,128)}, f32[4,48,512]{2,1,0:T(8,128)S(1)}, u32[]{:S(2)}) copy-start(f32[4,48,512]{2,1,0:T(8,128)S(1)} %collective-permute-done.2.qn_ref) | copy-start | bytes 1179652
  80.4 11.1 %collective-permute-start.12 = (f32[4,48,512]{2,1,0:T(8,128)}, f32[4,48,512]{2,1,0:T(8,128)S(1)}, u32[]{:S(2)}, u32[]{:S(2)}) collective-permute-start(f32[4,48,512]{2,1,0:T(8,128)} %get-tuple-element.10), channel_id=1, source_target_pairs={{0,1},{1,2},{2,3},{4,5},{5,6},{6,7},{8,9},{9,10},{10,11},{12,13},{... | collective-permute-start | bytes 1179656 | tf_op jit(solution)/shard_map/ppermute | solution.py:16
  82.8 9.3 %collective-permute-start.13 = (f32[4,48,512]{2,1,0:T(8,128)}, f32[4,48,512]{2,1,0:T(8,128)S(1)}, u32[]{:S(2)}, u32[]{:S(2)}) collective-permute-start(f32[4,48,512]{2,1,0:T(8,128)} %get-tuple-element.11), channel_id=1, source_target_pairs={{1,0},{2,1},{3,2},{5,4},{6,5},{7,6},{9,8},{10,9},{11,10},{13,12},{... | collective-permute-start | bytes 1179656 | tf_op jit(solution)/shard_map/ppermute | solution.py:16
  91.5 0.8 copy-start.3
  92.2 0.8 copy-start.4

commit v9 on v8

--- a/solution.py
+++ b/solution.py
@@ -33,6 +33,37 @@
     return buf
 
 
+def fill_coefficients(north_ref, wx_ref, coef_ref):
+    lat_rows = coef_ref.shape[1]
+    levels, lon = coef_ref.shape[2], coef_ref.shape[3]
+    level = lax.broadcasted_iota(jnp.int32, (levels, lon), 0)
+    not_top = level < levels - 1
+    not_bottom = level > 0
+    for a in range(lat_rows):
+        u = wx_ref[a]
+        uw = pltpu.roll(u, 1, 1)
+        v = wx_ref[lat_rows + a] * north_ref[a]
+        vm = wx_ref[3 * lat_rows] if a == 0 else wx_ref[lat_rows + a - 1]
+        w = wx_ref[2 * lat_rows + a]
+        w_up = jnp.where(not_top, w, 0.0)
+        w_down = jnp.where(not_bottom, pltpu.roll(w, 1, 0), 0.0)
+        coef_ref[0, a] = (
+            1.0
+            - jnp.maximum(u, 0.0)
+            + jnp.minimum(uw, 0.0)
+            - jnp.maximum(v, 0.0)
+            + jnp.minimum(vm, 0.0)
+            - w_up
+            - w_down
+        )
+        coef_ref[1, a] = -jnp.minimum(u, 0.0)
+        coef_ref[2, a] = jnp.maximum(uw, 0.0)
+        coef_ref[3, a] = -jnp.minimum(v, 0.0)
+        coef_ref[4, a] = jnp.maximum(vm, 0.0)
+        coef_ref[5, a] = w_up
+        coef_ref[6, a] = w_down
+
+
 def step_kernel(north_ref, q_ref, qs_ref, qn_ref, wx_ref, src_ref, *rest, rows=None):
     o_ref = rest[0]
     edges = rest[1:-1]
@@ -46,29 +77,7 @@
 
     @pl.when(pl.program_id(0) == 0)
     def _():
-        for a in range(lat_rows):
-            u = wx_ref[a]
-            uw = pltpu.roll(u, 1, 1)
-            v = wx_ref[lat_rows + a] * north_ref[a]
-            vm = wx_ref[3 * lat_rows] if a == 0 else wx_ref[lat_rows + a - 1]
-            w = wx_ref[2 * lat_rows + a]
-            w_up = jnp.where(not_top, w, 0.0)
-            w_down = jnp.where(not_bottom, pltpu.roll(w, 1, 0), 0.0)
-            coef_ref[0, a] = (
-                1.0
-                - jnp.maximum(u, 0.0)
-                + jnp.minimum(uw, 0.0)
-                - jnp.maximum(v, 0.0)
-                + jnp.minimum(vm, 0.0)
-                - w_up
-                - w_down
-            )
-            coef_ref[1, a] = -jnp.minimum(u, 0.0)
-            coef_ref[2, a] = jnp.maximum(uw, 0.0)
-            coef_ref[3, a] = -jnp.minimum(v, 0.0)
-            coef_ref[4, a] = jnp.maximum(vm, 0.0)
-            coef_ref[5, a] = w_up
-            coef_ref[6, a] = w_down
+        fill_coefficients(north_ref, wx_ref, coef_ref)
 
     for a in rows:
         qa = q_ref[0, a]
@@ -152,10 +161,10 @@
     )(north_open, state, weather, emission)
 
 
-def edge_kernel(north_ref, qa_ref, qi_ref, qs_ref, qn_ref, u_ref, v_ref, vm_ref, w_ref, src_ref, base_ref, o_ref):
-    del base_ref
+def edge_kernel(north_ref, lo_ref, hi_ref, lo_in_ref, hi_in_ref, qs_ref, qn_ref, u_ref, v_ref, vm_ref, w_ref, src_ref, *outs):
+    split = len(outs) == 2
     tracers, lat_rows = src_ref.shape[0], src_ref.shape[1]
-    levels, lon = qa_ref.shape[2], qa_ref.shape[3]
+    levels, lon = lo_ref.shape[1], lo_ref.shape[2]
     top = pl.program_id(0)
     level = lax.broadcasted_iota(jnp.int32, (levels, lon), 0)
     not_top = level < levels - 1
@@ -184,8 +193,8 @@
     c_south = jnp.maximum(vm, 0.0)
     at_top = jnp.full((1, lon), top, jnp.int32) == 1
     for k in range(tracers):
-        qa = qa_ref[k, 0]
-        inner = qi_ref[k, 0]
+        qa = jnp.where(is_top, hi_ref[k], lo_ref[k])
+        inner = jnp.where(is_top, hi_in_ref[k], lo_in_ref[k])
         qm = jnp.where(is_top, inner, qs_ref[k])
         qp = jnp.where(is_top, qn_ref[k], inner)
         result = (
@@ -198,41 +207,129 @@
             + w_down * pltpu.roll(qa, 1, 0)
         )
         source = jnp.where(at_top, src_ref[k, lat_rows - 1 : lat_rows, :], src_ref[k, 0:1, :])
-        o_ref[k, 0] = result
-        o_ref[k, 0, 0:1, :] = result[0:1] + source
-
-
-def edge_step(state, base, south, north, weather, emission, north_open):
-    tracers, lat_rows, levels, lon = state.shape
+        surface = result[0:1] + source
+        if split:
+
+            def put(ref, result=result, surface=surface, k=k):
+                ref[k] = result
+                ref[k, 0:1, :] = surface
+
+            pl.when(top == 0)(functools.partial(put, outs[0]))
+            pl.when(top == 1)(functools.partial(put, outs[1]))
+        else:
+            outs[-1][k, 0] = result
+            outs[-1][k, 0, 0:1, :] = surface
+
+
+def edge_step(rows, base, south, north, weather, emission, north_open):
+    tracers, levels, lon = rows[0].shape
+    lat_rows = emission.shape[1]
     last = lat_rows - 1
-    one = lambda index: pl.BlockSpec((tracers, 1, levels, lon), index)
     edge = pl.BlockSpec((tracers, levels, lon), lambda e: (0, 0, 0))
     met = lambda index: pl.BlockSpec((1, levels, lon), index)
+    in_specs = [
+        pl.BlockSpec(memory_space=pltpu.SMEM),
+        edge,
+        edge,
+        edge,
+        edge,
+        edge,
+        edge,
+        met(lambda e: (e * last, 0, 0)),
+        met(lambda e: (lat_rows + e * last, 0, 0)),
+        met(lambda e: (3 * lat_rows - e * (lat_rows + 2), 0, 0)),
+        met(lambda e: (2 * lat_rows + e * last, 0, 0)),
+        pl.BlockSpec((tracers, lat_rows, lon), lambda e: (0, 0, 0)),
+    ]
+    args = [north_open, *rows, south, north, weather, weather, weather, weather, emission]
+    if base is None:
+        out_specs = [edge, edge]
+        out_shape = [jax.ShapeDtypeStruct((tracers, levels, lon), jnp.float32)] * 2
+        aliases = {}
+        kernel = edge_kernel
+    else:
+        in_specs.append(pl.BlockSpec(memory_space=pl.ANY))
+        args.append(base)
+        out_specs = pl.BlockSpec((tracers, 1, levels, lon), lambda e: (0, e * last, 0, 0))
+        out_shape = jax.ShapeDtypeStruct(base.shape, base.dtype)
+        aliases = {len(args) - 1: 0}
+        kernel = lambda *refs: edge_kernel(*refs[:-2], refs[-1])
+    grid_spec = pltpu.PrefetchScalarGridSpec(
+        num_scalar_prefetch=0, grid=(2,), in_specs=in_specs, out_specs=out_specs
+    )
+    return pl.pallas_call(
+        kernel,
+        grid_spec=grid_spec,
+        out_shape=out_shape,
+        input_output_aliases=aliases,
+        compiler_params=pltpu.CompilerParams(dimension_semantics=("arbitrary",)),
+    )(*args)
+
+
+def fused_kernel(north_ref, q_ref, lo_ref, hi_ref, wx_ref, src_ref, o_ref, lo_in_ref, hi_in_ref, coef_ref, mid_ref):
+    lat_rows = q_ref.shape[1]
+    levels, lon = q_ref.shape[2], q_ref.shape[3]
+
+    @pl.when(pl.program_id(0) == 0)
+    def _():
+        fill_coefficients(north_ref, wx_ref, coef_ref)
+
+    def stencil(a, qa, qm, qp):
+        result = (
+            coef_ref[0, a] * qa
+            + coef_ref[1, a] * pltpu.roll(qa, lon - 1, 1)
+            + coef_ref[2, a] * pltpu.roll(qa, 1, 1)
+            + coef_ref[3, a] * qp
+            + coef_ref[4, a] * qm
+            + coef_ref[5, a] * pltpu.roll(qa, levels - 1, 0)
+            + coef_ref[6, a] * pltpu.roll(qa, 1, 0)
+        )
+        return result, result[0:1] + src_ref[0, a : a + 1, :]
+
+    mid_ref[0] = lo_ref[0]
+    mid_ref[lat_rows - 1] = hi_ref[0]
+    for a in range(1, lat_rows - 1):
+        result, surface = stencil(a, q_ref[0, a], q_ref[0, a - 1], q_ref[0, a + 1])
+        mid_ref[a] = result
+        mid_ref[a, 0:1, :] = surface
+        if a == 1:
+            lo_in_ref[0] = mid_ref[a]
+        if a == lat_rows - 2:
+            hi_in_ref[0] = mid_ref[a]
+    for a in range(1, lat_rows - 1):
+        result, surface = stencil(a, mid_ref[a], mid_ref[a - 1], mid_ref[a + 1])
+        o_ref[0, a] = result
+        o_ref[0, a, 0:1, :] = surface
+
+
+def fused_steps(state, lo, hi, weather, emission, north_open):
+    tracers, lat_rows, levels, lon = state.shape
+    row = pl.BlockSpec((1, lat_rows, levels, lon), lambda k: (k, 0, 0, 0))
+    edge = pl.BlockSpec((1, levels, lon), lambda k: (k, 0, 0))
     grid_spec = pltpu.PrefetchScalarGridSpec(
         num_scalar_prefetch=0,
-        grid=(2,),
+        grid=(tracers,),
         in_specs=[
             pl.BlockSpec(memory_space=pltpu.SMEM),
-            one(lambda e: (0, e * last, 0, 0)),
-            one(lambda e: (0, 1 + e * (lat_rows - 3), 0, 0)),
+            row,
             edge,
             edge,
-            met(lambda e: (e * last, 0, 0)),
-            met(lambda e: (lat_rows + e * last, 0, 0)),
-            met(lambda e: (3 * lat_rows - e * (lat_rows + 2), 0, 0)),
-            met(lambda e: (2 * lat_rows + e * last, 0, 0)),
-            pl.BlockSpec((tracers, lat_rows, lon), lambda e: (0, 0, 0)),
-            pl.BlockSpec(memory_space=pl.ANY),
+            pl.BlockSpec(weather.shape[:2] + (lon,), lambda k: (0, 0, 0)),
+            pl.BlockSpec((1, lat_rows, lon), lambda k: (k, 0, 0)),
         ],
-        out_specs=one(lambda e: (0, e * last, 0, 0)),
+        out_specs=[row, edge, edge],
+        scratch_shapes=[
+            pltpu.VMEM((7, lat_rows, levels, lon), jnp.float32),
+            pltpu.VMEM((lat_rows, levels, lon), jnp.float32),
+        ],
     )
     return pl.pallas_call(
-        edge_kernel,
+        fused_kernel,
         grid_spec=grid_spec,
-        out_shape=jax.ShapeDtypeStruct(state.shape, state.dtype),
-        input_output_aliases={10: 0},
+        out_shape=[jax.ShapeDtypeStruct(state.shape, state.dtype)]
+        + [jax.ShapeDtypeStruct((tracers, levels, lon), state.dtype)] * 2,
         compiler_params=pltpu.CompilerParams(dimension_semantics=("arbitrary",)),
-    )(north_open, state, state, south, north, weather, weather, weather, weather, emission, base)
+    )(north_open, state, lo, hi, weather, emission)
 
 
 def on_device(
@@ -283,13 +380,13 @@
     latitude = band_index * lat_rows + jnp.arange(lat_rows, dtype=jnp.int32)
     north_open = (latitude < band_count * lat_rows - 1).astype(jnp.float32)
 
-    first, bottom_row, top_row = advance(
-        tracer_state, q_south, q_north, weather, emission, north_open, True
-    )
+    rim = (tracer_state[:, 0], tracer_state[:, lat_rows - 1], tracer_state[:, 1], tracer_state[:, lat_rows - 2])
+    bottom_row, top_row = edge_step(rim, None, q_south, q_north, weather, emission, north_open)
     s1_south = passed_along(top_row, "band", 1)
     s1_north = passed_along(bottom_row, "band", -1)
-    inside = interior_step(first, weather, emission, north_open)
-    tracer_field = edge_step(first, inside, s1_south, s1_north, weather, emission, north_open)
+    inside, bottom_in, top_in = fused_steps(tracer_state, bottom_row, top_row, weather, emission, north_open)
+    rim = (bottom_row, top_row, bottom_in, top_in)
+    tracer_field = edge_step(rim, inside, s1_south, s1_north, weather, emission, north_open)
     return (tracer_field, emission)
 
 

time: 97.1 us -> 97.9 us (level)
  local copies, waits for them, and re-layouts: 13.4 us -> 16 us
  Pallas kernels: 17.5 us -> 16.4 us
  starting transfers between devices: 24.3 us -> 23.3 us
    squeeze x0 -> x1, local copies, waits for them, and re-layouts: none -> 2.51 us  [on_device(): tracer_state[:, lat_rows - 2]]
    ppermute x3, starting transfers between devices: 1.82 us -> 0.56 us  [on_device(): shifted.append(lax.ppermute(held_control, 'band', pairs))]
    pallas_call x3, Pallas kernels: 17.5 us -> 16.4 us  [the longest x1 8.67 us: fused_steps(): pl.pallas_call(fused_kernel, grid_spec=grid_spec, out_shape=[jax.ShapeDty...]
    unnamed x13 -> x21, local copies, waits for them, and re-layouts: 7.47 us -> 7.58 us
  transfers between devices with their start and end apart: 14 -> 14, of which waited for: 5 -> 4; matrix products, arithmetic and copies ran while one was open for 14% -> 16% of each run, Pallas kernels for 7% -> 9%
where the time goes in v9:
time: 97.9 us; the launch traced here: 97.1 us
  waiting for transfers between devices  36.4 us (37%)
  starting transfers between devices  23.3 us (24%)
  Pallas kernels  16.4 us (17%)
  local copies, waits for them, and re-layouts  16 us (16%)
  matrix products  3.32 us (3%)
  between operations  1.03 us (1%)
    ppermute x3, waiting for transfers between devices, relay_gather(): lax.ppermute(left, axis, [(j, j - 1) for j in range(1, count - r + 1)])  29.4 us
    ppermute x5, starting transfers between devices, passed_along(): return lax.ppermute(value, axis, pairs)  13.4 us
    pallas_call x1, Pallas kernels, fused_steps(): pl.pallas_call(fused_kernel, grid_spec=grid_spec, out_shape=[jax.ShapeDty...  8.67 us
    pallas_call x2, Pallas kernels, edge_step(): pl.pallas_call(kernel, grid_spec=grid_spec, out_shape=out_shape, input_ou...  7.72 us
    unnamed x21, local copies, waits for them, and re-layouts  7.58 us
    ppermute x3, waiting for transfers between devices, relay_gather(): lax.ppermute(right, axis, [(i, i + 1) for i in range(r - 1, count - 1)])  7.03 us
    ppermute x3, starting transfers between devices, relay_gather(): lax.ppermute(right, axis, [(i, i + 1) for i in range(r - 1, count - 1)])  5.43 us
    ppermute x3, starting transfers between devices, relay_gather(): lax.ppermute(left, axis, [(j, j - 1) for j in range(1, count - r + 1)])  3.97 us
  transfers between devices with their start and end apart: 14, of which 4 were waited for; matrix products, arithmetic and copies ran while one was open for 16% of the time, Pallas kernels for 9%

profile of v9, /device:TPU:1, one launch (start us, length us, event | category | flops | bytes accessed | tf_op | source)
XLA Modules:
  0.0 97.1 jit_solution(2491080838425587998)
XLA Ops:
  0.7 0.8 slice.25
  1.4 4.5 %collective-permute-start = (f32[1,48,128]{2,1,0:T(8,128)S(1)}, f32[1,48,128]{2,1,0:T(8,128)S(1)}, u32[]{:S(2)}, u32[]{:S(2)}) collective-permute-start(f32[1,48,128]{2,1,0:T(8,128)S(1)} %slice.25), channel_id=1, source_target_pairs={{0,1},{1,2},{2,3},{4,5},{5,6},{6,7},{8,9},{9,10},{10,11},{12,13},{... | collective-permute-start | bytes 73736 | tf_op jit(solution)/shard_map/ppermute | solution.py:16
  6.0 1.6 %constant_dynamic-update-slice_fusion.3 = f32[25,48,128]{2,1,0:T(8,128)} fusion(f32[8,48,128]{2,1,0:T(8,128)} %param.15), kind=kLoop, calls=%fused_computation.22 | loop fusion | bytes 393216
  7.6 1.6 %constant_dynamic-update-slice_fusion.2 = f32[25,48,128]{2,1,0:T(8,128)} fusion(f32[25,48,128]{2,1,0:T(8,128)} %constant_dynamic-update-slice_fusion.3, f32[8,48,128]{2,1,0:T(8,128)} %param.16), kind=kLoop, calls=%fused_computation.21 | loop fusion | bytes 393216
  9.2 0.7 constant_dynamic-slice_fusion.4
  10.2 1.7 %convolution_bitcast_fusion.3 = f32[4,8,512]{2,1,0:T(8,128)} fusion(f32[8,8,1]{1,0,2:T(8,128)S(1)} %bitcast.63, f32[4,8,512]{2,1,0:T(8,128)} %param.10), kind=kOutput, calls=%fused_computation.7 | convolution fusion | flops 1572864 | bytes 131328 | tf_op jit(solution)/shard_map/jm,kmn->kjn/dot_general | solution.py:371
  11.8 1.6 %constant_dynamic-update-slice_fusion.1 = f32[25,48,128]{2,1,0:T(8,128)} fusion(f32[25,48,128]{2,1,0:T(8,128)} %constant_dynamic-update-slice_fusion.2, f32[8,48,128]{2,1,0:T(8,128)} %param.17), kind=kLoop, calls=%fused_computation.20 | loop fusion | bytes 393216
  14.0 4.0 %collective-permute-start.3 = (f32[25,48,128]{2,1,0:T(8,128)}, f32[25,48,128]{2,1,0:T(8,128)}, u32[]{:S(2)}, u32[]{:S(2)}) collective-permute-start(f32[25,48,128]{2,1,0:T(8,128)} %constant_dynamic-update-slice_fusion), channel_id=1, source_target_pairs={{0,4},{4,8},{8,12},{1,5},{5,9},{9,13},{2,6},{6,10},{10,14},{3,7},{... | collective-permute-start | bytes 1843208 | tf_op jit(solution)/shard_map/ppermute | solution.py:27
  18.6 2.5 %slice_bitcast_fusion.2 = (f32[4,48,512]{2,1,0:T(8,128)}, f32[4,48,512]{2,1,0:T(8,128)}, f32[4,48,512]{2,1,0:T(8,128)}, f32[4,48,512]{2,1,0:T(8,128)}) fusion(f32[4,8,48,512]{3,2,1,0:T(8,128)} %q_ref.1), kind=kLoop, calls=%fused_computation.11 | loop fusion | bytes 3145728 | tf_op jit(solution)/shard_map/squeeze | solution.py:383
  21.1 1.4 %collective-permute-start.4 = (f32[25,48,128]{2,1,0:T(8,128)}, f32[25,48,128]{2,1,0:T(8,128)S(1)}, u32[]{:S(2)}, u32[]{:S(2)}) collective-permute-start(f32[25,48,128]{2,1,0:T(8,128)} %constant_dynamic-update-slice_fusion), channel_id=1, source_target_pairs={{4,0},{8,4},{12,8},{5,1},{9,5},{13,9},{6,2},{10,6},{14,10},{7,3},{... | collective-permute-start | bytes 1843208 | tf_op jit(solution)/shard_map/ppermute | solution.py:28
  23.4 7.0 %collective-permute-done.3 = f32[25,48,128]{2,1,0:T(8,128)} collective-permute-done((f32[25,48,128]{2,1,0:T(8,128)}, f32[25,48,128]{2,1,0:T(8,128)}, u32[]{:S(2)}, u32[]{:S(2)}) %collective-permute-start.3) | collective-permute-done | bytes 614432 | tf_op jit(solution)/shard_map/ppermute | solution.py:27
  30.4 0.7 collective-permute-start.5
  31.1 1.2 %slice_bitcast_fusion = (f32[4,48,512]{2,1,0:T(8,128)S(1)}, f32[4,48,512]{2,1,0:T(8,128)S(1)}) fusion(f32[4,8,48,512]{3,2,1,0:T(8,128)} %q_ref.1), kind=kLoop, calls=%fused_computation.8 | loop fusion | bytes 1572864 | tf_op jit(solution)/shard_map/squeeze | solution.py:356
  32.5 1.1 %constant_dynamic-update-slice_fusion.10 = f32[25,48,640]{2,1,0:T(8,128)S(1)} fusion(f32[25,48,640]{2,1,0:T(8,128)S(1)} %broadcast_in_dim.2, f32[25,48,128]{2,1,0:T(8,128)} %constant_dynamic-update-slice_fusion, s32[]{:T(128)S(6)} %select_n.75), kind=kLoop, calls=%fused_computation.34 | loop fusion | bytes 1228804 | tf_op jit(solution)/shard_map/dynamic_update_slice | solution.py:24
  33.6 1.9 %collective-permute-start.1 = (f32[4,48,512]{2,1,0:T(8,128)S(1)}, f32[4,48,512]{2,1,0:T(8,128)S(1)}, u32[]{:S(2)}, u32[]{:S(2)}) collective-permute-start(f32[4,48,512]{2,1,0:T(8,128)S(1)} %get-tuple-element.17), channel_id=1, source_target_pairs={{0,1},{1,2},{2,3},{4,5},{5,6},{6,7},{8,9},{9,10},{10,11},{12,13},{... | collective-permute-start | bytes 1179656 | tf_op jit(solution)/shard_map/ppermute | solution.py:16
  35.6 2.8 %collective-permute-done.4 = f32[25,48,128]{2,1,0:T(8,128)S(1)} collective-permute-done((f32[25,48,128]{2,1,0:T(8,128)}, f32[25,48,128]{2,1,0:T(8,128)S(1)}, u32[]{:S(2)}, u32[]{:S(2)}) %collective-permute-start.4) | collective-permute-done | bytes 614432 | tf_op jit(solution)/shard_map/ppermute | solution.py:28
  38.4 1.3 %collective-permute-start.6 = (f32[25,48,128]{2,1,0:T(8,128)S(1)}, f32[25,48,128]{2,1,0:T(8,128)S(1)}, u32[]{:S(2)}, u32[]{:S(2)}) collective-permute-start(f32[25,48,128]{2,1,0:T(8,128)S(1)} %collective-permute-done.4), channel_id=1, source_target_pairs={{4,0},{8,4},{5,1},{9,5},{6,2},{10,6},{7,3},{11,7},{20,16},{24,20},... | collective-permute-start | bytes 1843208 | tf_op jit(solution)/shard_map/ppermute | solution.py:28
  39.9 2.1 %collective-permute-start.2 = (f32[4,48,512]{2,1,0:T(8,128)S(1)}, f32[4,48,512]{2,1,0:T(8,128)S(1)}, u32[]{:S(2)}, u32[]{:S(2)}) collective-permute-start(f32[4,48,512]{2,1,0:T(8,128)S(1)} %get-tuple-element.16), channel_id=1, source_target_pairs={{1,0},{2,1},{3,2},{5,4},{6,5},{7,6},{9,8},{10,9},{11,10},{13,12},{... | collective-permute-start | bytes 1179656 | tf_op jit(solution)/shard_map/ppermute | solution.py:16
  42.3 0.7 collective-permute-start.7
  43.0 0.8 fusion.2.src_ref.refs_11_
  43.8 12.7 %collective-permute-done.6 = f32[25,48,128]{2,1,0:T(8,128)S(1)} collective-permute-done((f32[25,48,128]{2,1,0:T(8,128)S(1)}, f32[25,48,128]{2,1,0:T(8,128)S(1)}, u32[]{:S(2)}, u32[]{:S(2)}) %collective-permute-start.6) | collective-permute-done | bytes 614432 | tf_op jit(solution)/shard_map/ppermute | solution.py:28
  56.5 1.3 %collective-permute-start.8 = (f32[25,48,128]{2,1,0:T(8,128)S(1)}, f32[25,48,128]{2,1,0:T(8,128)S(1)}, u32[]{:S(2)}, u32[]{:S(2)}) collective-permute-start(f32[25,48,128]{2,1,0:T(8,128)S(1)} %collective-permute-done.6), channel_id=1, source_target_pairs={{4,0},{5,1},{6,2},{7,3},{20,16},{21,17},{22,18},{23,19}} | collective-permute-start | bytes 1843208 | tf_op jit(solution)/shard_map/ppermute | solution.py:28
  57.7 1.1 %constant_dynamic-update-slice_fusion.9 = f32[25,48,640]{2,1,0:T(8,128)S(1)} fusion(f32[25,48,640]{2,1,0:T(8,128)S(1)} %constant_dynamic-update-slice_fusion.10, f32[25,48,128]{2,1,0:T(8,128)} %collective-permute-done.3, s32[]{:T(128)S(6)} %select_n.77), kind=kLoop, calls=%fused_computation.33 | loop fusion | bytes 1228804 | tf_op jit(solution)/shard_map/dynamic_update_slice | solution.py:30
  59.1 13.9 %collective-permute-done.8 = f32[25,48,128]{2,1,0:T(8,128)S(1)} collective-permute-done((f32[25,48,128]{2,1,0:T(8,128)S(1)}, f32[25,48,128]{2,1,0:T(8,128)S(1)}, u32[]{:S(2)}, u32[]{:S(2)}) %collective-permute-start.8) | collective-permute-done | bytes 614432 | tf_op jit(solution)/shard_map/ppermute | solution.py:28
  73.1 0.8 copy-done.3
  73.9 0.9 copy-done.1
  74.9 4.1 %shard_map.104 = (f32[4,48,512]{2,1,0:T(8,128)}, f32[4,48,512]{2,1,0:T(8,128)}) custom-call(f32[8]{0:T(128)} %compare_convert_fusion.north_ref.refs_0_, f32[4,48,512]{2,1,0:T(8,128)} %get-tuple-element.21.lo_ref, f32[4,48,512]{2,1,0:T(8,128)} %get-tuple-element.20.hi_ref, f32[4,48,512]{2,1,0:T(8,128)} %get-tuple-element.19.lo_in_ref, ...), custom_call_target="tpu_custom_call" | custom-call | tf_op jit(solution)/shard_map/pallas_call | solution.py:260
  79.1 1.9 %collective-permute-start.12 = (f32[4,48,512]{2,1,0:T(8,128)}, f32[4,48,512]{2,1,0:T(8,128)S(1)}, u32[]{:S(2)}, u32[]{:S(2)}) collective-permute-start(f32[4,48,512]{2,1,0:T(8,128)} %get-tuple-element.12.hi_ref.refs_2_), channel_id=1, source_target_pairs={{0,1},{1,2},{2,3},{4,5},{5,6},{6,7},{8,9},{9,10},{10,11},{12,13},{... | collective-permute-start | bytes 1179656 | tf_op jit(solution)/shard_map/ppermute | solution.py:16
  81.0 2.9 %collective-permute-start.13 = (f32[4,48,512]{2,1,0:T(8,128)}, f32[4,48,512]{2,1,0:T(8,128)S(1)}, u32[]{:S(2)}, u32[]{:S(2)}) collective-permute-start(f32[4,48,512]{2,1,0:T(8,128)} %get-tuple-element.11.lo_ref.refs_1_), channel_id=1, source_target_pairs={{1,0},{2,1},{3,2},{5,4},{6,5},{7,6},{9,8},{10,9},{11,10},{13,12},{... | collective-permute-start | bytes 1179656 | tf_op jit(solution)/shard_map/ppermute | solution.py:16
  83.9 8.7 %shard_map.105 = (f32[4,8,48,512]{3,2,1,0:T(8,128)}, f32[4,48,512]{2,1,0:T(8,128)}, f32[4,48,512]{2,1,0:T(8,128)}) custom-call(f32[8]{0:T(128)} %compare_convert_fusion.north_ref.refs_0_, f32[4,8,48,512]{3,2,1,0:T(8,128)} %q_ref.1, f32[4,48,512]{2,1,0:T(8,128)} %get-tuple-element.11.lo_ref.refs_1_, f32[4,48,512]{2,1,0:T(8,128)} %get-tuple-element.12.hi_ref.refs_2_, ...), custom_call_target="tpu_custom_call" | custom-call | tf_op jit(solution)/shard_map/pallas_call | solution.py:326
  92.6 0.7 copy-done.4
  93.5 3.6 %shard_map.106 = f32[4,8,48,512]{3,2,1,0:T(8,128)} custom-call(f32[8]{0:T(128)} %compare_convert_fusion.north_ref.refs_0_, f32[4,48,512]{2,1,0:T(8,128)} %get-tuple-element.11.lo_ref.refs_1_, f32[4,48,512]{2,1,0:T(8,128)} %get-tuple-element.12.hi_ref.refs_2_, f32[4,48,512]{2,1,0:T(8,128)} %get-tuple-element.13.refs_3_, ...), custom_call_target="tpu_custom_call", output_to_operand_aliasing={{}: (12, {})} | custom-call | tf_op jit(solution)/shard_map/pallas_call | solution.py:260
  (41 shorter events, 3.3 us)
Async XLA Ops:
  0.6 9.3 %copy-start = (f32[8,8,8]{2,1,0:T(8,128)S(1)}, f32[8,8,8]{2,1,0:T(8,128)}, u32[]{:S(2)}) copy-start(f32[8,8,8]{2,1,0:T(8,128)} %param.11) | copy-start | bytes 6148
  0.6 21.9 %copy-start.7 = (s32[8,512]{1,0:T(8,128)S(1)}, s32[8,512]{1,0:T(8,128)}, u32[]{:S(2)}) copy-start(s32[8,512]{1,0:T(8,128)} %param.13) | copy-start | bytes 49156
  0.7 21.9 %copy-start.8 = (f32[4,22]{1,0:T(4,128)S(1)}, f32[4,22]{1,0:T(4,128)}, u32[]{:S(2)}) copy-start(f32[4,22]{1,0:T(4,128)} %param.14) | copy-start | bytes 1060
  1.4 12.0 %collective-permute-start = (f32[1,48,128]{2,1,0:T(8,128)S(1)}, f32[1,48,128]{2,1,0:T(8,128)S(1)}, u32[]{:S(2)}, u32[]{:S(2)}) collective-permute-start(f32[1,48,128]{2,1,0:T(8,128)S(1)} %slice.25), channel_id=1, source_target_pairs={{0,1},{1,2},{2,3},{4,5},{5,6},{6,7},{8,9},{9,10},{10,11},{12,13},{... | collective-permute-start | bytes 73736 | tf_op jit(solution)/shard_map/ppermute | solution.py:16
  14.0 16.4 %collective-permute-start.3 = (f32[25,48,128]{2,1,0:T(8,128)}, f32[25,48,128]{2,1,0:T(8,128)}, u32[]{:S(2)}, u32[]{:S(2)}) collective-permute-start(f32[25,48,128]{2,1,0:T(8,128)} %constant_dynamic-update-slice_fusion), channel_id=1, source_target_pairs={{0,4},{4,8},{8,12},{1,5},{5,9},{9,13},{2,6},{6,10},{10,14},{3,7},{... | collective-permute-start | bytes 1843208 | tf_op jit(solution)/shard_map/ppermute | solution.py:27
  21.1 18.6 %copy-start.6 = (f32[4,8,512]{2,1,0:T(8,128)S(1)}, f32[4,8,512]{2,1,0:T(8,128)}, u32[]{:S(2)}) copy-start(f32[4,8,512]{2,1,0:T(8,128)} %convolution_bitcast_fusion.3) | copy-start | bytes 196612
  21.1 17.3 %collective-permute-start.4 = (f32[25,48,128]{2,1,0:T(8,128)}, f32[25,48,128]{2,1,0:T(8,128)S(1)}, u32[]{:S(2)}, u32[]{:S(2)}) collective-permute-start(f32[25,48,128]{2,1,0:T(8,128)} %constant_dynamic-update-slice_fusion), channel_id=1, source_target_pairs={{4,0},{8,4},{12,8},{5,1},{9,5},{13,9},{6,2},{10,6},{14,10},{7,3},{... | collective-permute-start | bytes 1843208 | tf_op jit(solution)/shard_map/ppermute | solution.py:28
  22.8 10.8 %collective-permute-start.9 = (f32[4,8,512]{2,1,0:T(8,128)}, f32[4,8,512]{2,1,0:T(8,128)S(1)}, u32[]{:S(2)}, u32[]{:S(2)}) collective-permute-start(f32[4,8,512]{2,1,0:T(8,128)} %param.10), channel_id=1, source_target_pairs={{0,1},{1,2},{2,3},{3,0},{4,5},{5,6},{6,7},{7,4},{8,9},{9,10},{10,1... | collective-permute-start | bytes 196616 | tf_op jit(solution)/shard_map/ppermute | solution.py:360
  23.2 16.7 %collective-permute-start.11 = (f32[4,8,512]{2,1,0:T(8,128)}, f32[4,8,512]{2,1,0:T(8,128)S(1)}, u32[]{:S(2)}, u32[]{:S(2)}) collective-permute-start(f32[4,8,512]{2,1,0:T(8,128)} %param.10), channel_id=1, source_target_pairs={{0,3},{1,0},{2,1},{3,2},{4,7},{5,4},{6,5},{7,6},{8,11},{9,8},{10,9... | collective-permute-start | bytes 196616 | tf_op jit(solution)/shard_map/ppermute | solution.py:360
  23.4 19.6 %collective-permute-start.10 = (f32[4,8,512]{2,1,0:T(8,128)}, f32[4,8,512]{2,1,0:T(8,128)S(1)}, u32[]{:S(2)}, u32[]{:S(2)}) collective-permute-start(f32[4,8,512]{2,1,0:T(8,128)} %param.10), channel_id=1, source_target_pairs={{0,2},{1,3},{2,0},{3,1},{4,6},{5,7},{6,4},{7,5},{8,10},{9,11},{10,... | collective-permute-start | bytes 196616 | tf_op jit(solution)/shard_map/ppermute | solution.py:360
  30.4 11.8 %collective-permute-start.5 = (f32[25,48,128]{2,1,0:T(8,128)}, f32[25,48,128]{2,1,0:T(8,128)S(1)}, u32[]{:S(2)}, u32[]{:S(2)}) collective-permute-start(f32[25,48,128]{2,1,0:T(8,128)} %collective-permute-done.3), channel_id=1, source_target_pairs={{4,8},{8,12},{5,9},{9,13},{6,10},{10,14},{7,11},{11,15},{20,24},{2... | collective-permute-start | bytes 1843208 | tf_op jit(solution)/shard_map/ppermute | solution.py:27
  33.6 39.4 %collective-permute-start.1 = (f32[4,48,512]{2,1,0:T(8,128)S(1)}, f32[4,48,512]{2,1,0:T(8,128)S(1)}, u32[]{:S(2)}, u32[]{:S(2)}) collective-permute-start(f32[4,48,512]{2,1,0:T(8,128)S(1)} %get-tuple-element.17), channel_id=1, source_target_pairs={{0,1},{1,2},{2,3},{4,5},{5,6},{6,7},{8,9},{9,10},{10,11},{12,13},{... | collective-permute-start | bytes 1179656 | tf_op jit(solution)/shard_map/ppermute | solution.py:16
  38.4 18.1 %collective-permute-start.6 = (f32[25,48,128]{2,1,0:T(8,128)S(1)}, f32[25,48,128]{2,1,0:T(8,128)S(1)}, u32[]{:S(2)}, u32[]{:S(2)}) collective-permute-start(f32[25,48,128]{2,1,0:T(8,128)S(1)} %collective-permute-done.4), channel_id=1, source_target_pairs={{4,0},{8,4},{5,1},{9,5},{6,2},{10,6},{7,3},{11,7},{20,16},{24,20},... | collective-permute-start | bytes 1843208 | tf_op jit(solution)/shard_map/ppermute | solution.py:28
  39.9 33.2 %collective-permute-start.2 = (f32[4,48,512]{2,1,0:T(8,128)S(1)}, f32[4,48,512]{2,1,0:T(8,128)S(1)}, u32[]{:S(2)}, u32[]{:S(2)}) collective-permute-start(f32[4,48,512]{2,1,0:T(8,128)S(1)} %get-tuple-element.16), channel_id=1, source_target_pairs={{1,0},{2,1},{3,2},{5,4},{6,5},{7,6},{9,8},{10,9},{11,10},{13,12},{... | collective-permute-start | bytes 1179656 | tf_op jit(solution)/shard_map/ppermute | solution.py:16
  42.3 16.8 %collective-permute-start.7 = (f32[25,48,128]{2,1,0:T(8,128)S(1)}, f32[25,48,128]{2,1,0:T(8,128)S(1)}, u32[]{:S(2)}, u32[]{:S(2)}) collective-permute-start(f32[25,48,128]{2,1,0:T(8,128)S(1)} %collective-permute-done.5), channel_id=1, source_target_pairs={{8,12},{9,13},{10,14},{11,15},{24,28},{25,29},{26,30},{27,31}} | collective-permute-start | bytes 1843208 | tf_op jit(solution)/shard_map/ppermute | solution.py:27
  56.5 16.5 %collective-permute-start.8 = (f32[25,48,128]{2,1,0:T(8,128)S(1)}, f32[25,48,128]{2,1,0:T(8,128)S(1)}, u32[]{:S(2)}, u32[]{:S(2)}) collective-permute-start(f32[25,48,128]{2,1,0:T(8,128)S(1)} %collective-permute-done.6), channel_id=1, source_target_pairs={{4,0},{5,1},{6,2},{7,3},{20,16},{21,17},{22,18},{23,19}} | collective-permute-start | bytes 1843208 | tf_op jit(solution)/shard_map/ppermute | solution.py:28
  73.1 1.7 %copy-start.1 = (f32[25,48,640]{2,1,0:T(8,128)}, f32[25,48,640]{2,1,0:T(8,128)S(1)}, u32[]{:S(2)}) copy-start(f32[25,48,640]{2,1,0:T(8,128)S(1)} %constant_dynamic-update-slice_fusion.4.u_ref.v_ref.vm_ref.w_ref.wx_ref.refs_7_.refs_8_.refs_9_.refs_10_) | copy-start | bytes 9216004
  73.1 1.9 %copy-start.2 = (f32[4,48,512]{2,1,0:T(8,128)}, f32[4,48,512]{2,1,0:T(8,128)S(1)}, u32[]{:S(2)}) copy-start(f32[4,48,512]{2,1,0:T(8,128)S(1)} %collective-permute-done.1.qs_ref) | copy-start | bytes 1179652
  73.1 0.8 copy-start.3
  79.1 13.5 %collective-permute-start.12 = (f32[4,48,512]{2,1,0:T(8,128)}, f32[4,48,512]{2,1,0:T(8,128)S(1)}, u32[]{:S(2)}, u32[]{:S(2)}) collective-permute-start(f32[4,48,512]{2,1,0:T(8,128)} %get-tuple-element.12.hi_ref.refs_2_), channel_id=1, source_target_pairs={{0,1},{1,2},{2,3},{4,5},{5,6},{6,7},{8,9},{9,10},{10,11},{12,13},{... | collective-permute-start | bytes 1179656 | tf_op jit(solution)/shard_map/ppermute | solution.py:16
  81.0 11.6 %collective-permute-start.13 = (f32[4,48,512]{2,1,0:T(8,128)}, f32[4,48,512]{2,1,0:T(8,128)S(1)}, u32[]{:S(2)}, u32[]{:S(2)}) collective-permute-start(f32[4,48,512]{2,1,0:T(8,128)} %get-tuple-element.11.lo_ref.refs_1_), channel_id=1, source_target_pairs={{1,0},{2,1},{3,2},{5,4},{6,5},{7,6},{9,8},{10,9},{11,10},{13,12},{... | collective-permute-start | bytes 1179656 | tf_op jit(solution)/shard_map/ppermute | solution.py:16
  92.6 0.8 copy-start.4
  92.6 0.9 copy-start.5

commit v10 on v8

--- a/solution.py
+++ b/solution.py
@@ -14,6 +14,23 @@
     count = lax.axis_size(axis)
     pairs = [(i, i + by) for i in range(count) if 0 <= i + by < count]
     return lax.ppermute(value, axis, pairs)
+
+
+def pack_kernel(*refs):
+    parts, out_ref = refs[:-1], refs[-1]
+    row = 0
+    for part in parts:
+        rows = part.shape[0]
+        out_ref[row : row + rows] = part[...]
+        row += rows
+
+
+def packed(parts):
+    rows = sum(part.shape[0] for part in parts)
+    return pl.pallas_call(
+        pack_kernel,
+        out_shape=jax.ShapeDtypeStruct((rows,) + parts[0].shape[1:], parts[0].dtype),
+    )(*parts)
 
 
 def relay_gather(x, axis):
@@ -252,7 +269,7 @@
     lat_rows = control.shape[1]
 
     south_v = passed_along(meridional_courant[-1:], "band", 1)
-    pack = jnp.concatenate([zonal_courant, meridional_courant, vertical_diffusion, south_v], axis=0)
+    pack = packed([zonal_courant, meridional_courant, vertical_diffusion, south_v])
     weather = relay_gather(pack, "tracer")
     held_state, held_control, _ = lax.optimization_barrier((tracer_state, control, pack))
     q_south = passed_along(held_state[:, -1], "band", 1)

time: 97.1 us -> 95.2 us (0.980)
  local copies, waits for them, and re-layouts: 13.4 us -> 7.42 us
  starting transfers between devices: 24.3 us -> 27.4 us
  Pallas kernels: 17.5 us -> 19.5 us
  waiting for transfers between devices: 36.2 us -> 35.2 us
    unnamed x13 -> x14, local copies, waits for them, and re-layouts: 7.47 us -> 3.18 us
    ppermute x5, starting transfers between devices: 13.1 us -> 15.4 us  [passed_along(): return lax.ppermute(value, axis, pairs)]
    pallas_call x0 -> x1, Pallas kernels: none -> 1.98 us  [packed(): pl.pallas_call(pack_kernel, out_shape=jax.ShapeDtypeStruct((rows,) + part...]
    ppermute x3, waiting for transfers between devices: 6.62 us -> 5.55 us  [relay_gather(): lax.ppermute(right, axis, [(i, i + 1) for i in range(r - 1, count - 1)])]
    dynamic_update_slice x1, local copies, waits for them, and re-layouts: 1.12 us -> 0.05 us  [relay_gather(): buf = lax.dynamic_update_slice(buf, x, (0, 0, me * width))]
  transfers between devices with their start and end apart: 14 -> 14, of which waited for: 5 -> 5; matrix products, arithmetic and copies ran while one was open for 14% -> 8% of each run, Pallas kernels for 7% -> 7%
where the time goes in v10:
time: 95.2 us; the launch traced here: 94.5 us
  waiting for transfers between devices  35.2 us (37%)
  starting transfers between devices  27.4 us (29%)
  Pallas kernels  19.5 us (20%)
  local copies, waits for them, and re-layouts  7.42 us (8%)
  matrix products  3.47 us (4%)
    ppermute x3, waiting for transfers between devices, relay_gather(): lax.ppermute(left, axis, [(j, j - 1) for j in range(1, count - r + 1)])  28.9 us
    ppermute x5, starting transfers between devices, passed_along(): return lax.ppermute(value, axis, pairs)  15.4 us
    pallas_call x1, Pallas kernels, advance(): pl.pallas_call(step_kernel, grid_spec=grid_spec, out_shape=out_shape, com...  7.61 us
    pallas_call x1, Pallas kernels, interior_step(): pl.pallas_call(kernel, grid_spec=grid_spec, out_shape=jax.ShapeDtypeStruc...  6.69 us
    ppermute x3, waiting for transfers between devices, relay_gather(): lax.ppermute(right, axis, [(i, i + 1) for i in range(r - 1, count - 1)])  5.55 us
    ppermute x3, starting transfers between devices, relay_gather(): lax.ppermute(right, axis, [(i, i + 1) for i in range(r - 1, count - 1)])  5.42 us
    ppermute x3, starting transfers between devices, relay_gather(): lax.ppermute(left, axis, [(j, j - 1) for j in range(1, count - r + 1)])  3.85 us
    pallas_call x1, Pallas kernels, edge_step(): pl.pallas_call(edge_kernel, grid_spec=grid_spec, out_shape=jax.ShapeDtype...  3.23 us
  transfers between devices with their start and end apart: 14, of which 5 were waited for; matrix products, arithmetic and copies ran while one was open for 8% of the time, Pallas kernels for 7%

profile of v10, /device:TPU:1, one launch (start us, length us, event | category | flops | bytes accessed | tf_op | source)
XLA Modules:
  0.0 94.5 jit_solution(4317169534968769562)
XLA Ops:
  0.6 0.7 slice.9
  1.4 4.5 %collective-permute-start = (f32[1,48,128]{2,1,0:T(8,128)S(1)}, f32[1,48,128]{2,1,0:T(8,128)S(1)}, u32[]{:S(2)}, u32[]{:S(2)}) collective-permute-start(f32[1,48,128]{2,1,0:T(8,128)S(1)} %slice.9), channel_id=1, source_target_pairs={{0,1},{1,2},{2,3},{4,5},{5,6},{6,7},{8,9},{9,10},{10,11},{12,13},{... | collective-permute-start | bytes 73736 | tf_op jit(solution)/shard_map/ppermute | solution.py:16
  5.9 0.7 constant_dynamic-slice_fusion.4
  6.8 0.6 copy-done.6
  7.4 2.0 %shard_map.104 = f32[25,48,128]{2,1,0:T(8,128)} custom-call(f32[8,48,128]{2,1,0:T(8,128)} %refs_0_.1, f32[8,48,128]{2,1,0:T(8,128)} %refs_1_.1, f32[8,48,128]{2,1,0:T(8,128)} %refs_2_.1, f32[1,48,128]{2,1,0:T(8,128)} %copy-done.6), custom_call_target="tpu_custom_call" | custom-call | tf_op jit(solution)/shard_map/pallas_call | solution.py:30
  9.4 4.0 %collective-permute-start.3 = (f32[25,48,128]{2,1,0:T(8,128)}, f32[25,48,128]{2,1,0:T(8,128)}, u32[]{:S(2)}, u32[]{:S(2)}) collective-permute-start(f32[25,48,128]{2,1,0:T(8,128)} %shard_map.104), channel_id=1, source_target_pairs={{0,4},{4,8},{8,12},{1,5},{5,9},{9,13},{2,6},{6,10},{10,14},{3,7},{... | collective-permute-start | bytes 1843208 | tf_op jit(solution)/shard_map/ppermute | solution.py:44
  13.4 0.6 compare_convert_fusion.north_ref.n
  14.0 1.1 %convolution_bitcast_fusion.3 = f32[4,8,512]{2,1,0:T(8,128)S(1)} fusion(f32[8,8,1]{1,0,2:T(8,128)S(1)} %bitcast.47, f32[4,8,512]{2,1,0:T(8,128)} %param.10), kind=kOutput, calls=%fused_computation.7 | convolution fusion | flops 1572864 | bytes 131328 | tf_op jit(solution)/shard_map/jm,kmn->kjn/dot_general | solution.py:291
  15.1 1.3 %collective-permute-start.4 = (f32[25,48,128]{2,1,0:T(8,128)}, f32[25,48,128]{2,1,0:T(8,128)S(1)}, u32[]{:S(2)}, u32[]{:S(2)}) collective-permute-start(f32[25,48,128]{2,1,0:T(8,128)} %shard_map.104), channel_id=1, source_target_pairs={{4,0},{8,4},{12,8},{5,1},{9,5},{13,9},{6,2},{10,6},{14,10},{7,3},{... | collective-permute-start | bytes 1843208 | tf_op jit(solution)/shard_map/ppermute | solution.py:45
  16.4 1.0 %fusion.4 = f32[8,512,4]{1,2,0:T(4,128)S(1)} fusion(s32[8,512]{1,0:T(8,128)} %param.13, f32[4,22]{1,0:T(4,128)} %param.14), kind=kOutput, calls=%fused_computation.11 | convolution fusion | flops 4415488 | bytes 82272 | tf_op jit(solution)/shard_map/kr,jnr->kjn/dot_general | solution.py:297
  17.5 2.7 %collective-permute-start.10 = (f32[4,8,512]{2,1,0:T(8,128)}, f32[4,8,512]{2,1,0:T(8,128)S(1)}, u32[]{:S(2)}, u32[]{:S(2)}) collective-permute-start(f32[4,8,512]{2,1,0:T(8,128)} %param.10), channel_id=1, source_target_pairs={{0,2},{1,3},{2,0},{3,1},{4,6},{5,7},{6,4},{7,5},{8,10},{9,11},{10,... | collective-permute-start | bytes 196616 | tf_op jit(solution)/shard_map/ppermute | solution.py:280
  20.2 5.5 %collective-permute-done.3 = f32[25,48,128]{2,1,0:T(8,128)} collective-permute-done((f32[25,48,128]{2,1,0:T(8,128)}, f32[25,48,128]{2,1,0:T(8,128)}, u32[]{:S(2)}, u32[]{:S(2)}) %collective-permute-start.3) | collective-permute-done | bytes 614432 | tf_op jit(solution)/shard_map/ppermute | solution.py:44
  25.8 0.7 collective-permute-start.5
  26.5 1.2 %slice_bitcast_fusion = (f32[4,48,512]{2,1,0:T(8,128)S(1)}, f32[4,48,512]{2,1,0:T(8,128)S(1)}) fusion(f32[4,8,48,512]{3,2,1,0:T(8,128)} %q_ref.1), kind=kLoop, calls=%fused_computation.8 | loop fusion | bytes 1572864 | tf_op jit(solution)/shard_map/squeeze | solution.py:276
  27.9 1.9 %collective-permute-start.2 = (f32[4,48,512]{2,1,0:T(8,128)S(1)}, f32[4,48,512]{2,1,0:T(8,128)S(1)}, u32[]{:S(2)}, u32[]{:S(2)}) collective-permute-start(f32[4,48,512]{2,1,0:T(8,128)S(1)} %get-tuple-element.12), channel_id=1, source_target_pairs={{1,0},{2,1},{3,2},{5,4},{6,5},{7,6},{9,8},{10,9},{11,10},{13,12},{... | collective-permute-start | bytes 1179656 | tf_op jit(solution)/shard_map/ppermute | solution.py:16
  29.8 2.4 %collective-permute-done.4 = f32[25,48,128]{2,1,0:T(8,128)S(1)} collective-permute-done((f32[25,48,128]{2,1,0:T(8,128)}, f32[25,48,128]{2,1,0:T(8,128)S(1)}, u32[]{:S(2)}, u32[]{:S(2)}) %collective-permute-start.4) | collective-permute-done | bytes 614432 | tf_op jit(solution)/shard_map/ppermute | solution.py:45
  32.3 1.3 %collective-permute-start.6 = (f32[25,48,128]{2,1,0:T(8,128)S(1)}, f32[25,48,128]{2,1,0:T(8,128)S(1)}, u32[]{:S(2)}, u32[]{:S(2)}) collective-permute-start(f32[25,48,128]{2,1,0:T(8,128)S(1)} %collective-permute-done.4), channel_id=1, source_target_pairs={{4,0},{8,4},{5,1},{9,5},{6,2},{10,6},{7,3},{11,7},{20,16},{24,20},... | collective-permute-start | bytes 1843208 | tf_op jit(solution)/shard_map/ppermute | solution.py:45
  33.8 2.9 %collective-permute-start.1 = (f32[4,48,512]{2,1,0:T(8,128)S(1)}, f32[4,48,512]{2,1,0:T(8,128)}, u32[]{:S(2)}, u32[]{:S(2)}) collective-permute-start(f32[4,48,512]{2,1,0:T(8,128)S(1)} %get-tuple-element.13), channel_id=1, source_target_pairs={{0,1},{1,2},{2,3},{4,5},{5,6},{6,7},{8,9},{9,10},{10,11},{12,13},{... | collective-permute-start | bytes 1179656 | tf_op jit(solution)/shard_map/ppermute | solution.py:16
  36.9 0.7 collective-permute-start.7
  37.6 0.8 fusion.2.src_ref.e
  38.4 12.2 %collective-permute-done.6 = f32[25,48,128]{2,1,0:T(8,128)S(1)} collective-permute-done((f32[25,48,128]{2,1,0:T(8,128)S(1)}, f32[25,48,128]{2,1,0:T(8,128)S(1)}, u32[]{:S(2)}, u32[]{:S(2)}) %collective-permute-start.6) | collective-permute-done | bytes 614432 | tf_op jit(solution)/shard_map/ppermute | solution.py:45
  50.6 1.3 %collective-permute-start.8 = (f32[25,48,128]{2,1,0:T(8,128)S(1)}, f32[25,48,128]{2,1,0:T(8,128)S(1)}, u32[]{:S(2)}, u32[]{:S(2)}) collective-permute-start(f32[25,48,128]{2,1,0:T(8,128)S(1)} %collective-permute-done.6), channel_id=1, source_target_pairs={{4,0},{5,1},{6,2},{7,3},{20,16},{21,17},{22,18},{23,19}} | collective-permute-start | bytes 1843208 | tf_op jit(solution)/shard_map/ppermute | solution.py:45
  51.9 1.1 %constant_dynamic-update-slice_fusion.5 = f32[25,48,640]{2,1,0:T(8,128)S(1)} fusion(f32[25,48,640]{2,1,0:T(8,128)S(1)} %constant_dynamic-update-slice_fusion.6, f32[25,48,128]{2,1,0:T(8,128)} %collective-permute-done.3, s32[]{:T(128)S(6)} %select_n.77), kind=kLoop, calls=%fused_computation.25 | loop fusion | bytes 1228804 | tf_op jit(solution)/shard_map/dynamic_update_slice | solution.py:47
  53.3 14.3 %collective-permute-done.8 = f32[25,48,128]{2,1,0:T(8,128)S(1)} collective-permute-done((f32[25,48,128]{2,1,0:T(8,128)S(1)}, f32[25,48,128]{2,1,0:T(8,128)S(1)}, u32[]{:S(2)}, u32[]{:S(2)}) %collective-permute-start.8) | collective-permute-done | bytes 614432 | tf_op jit(solution)/shard_map/ppermute | solution.py:45
  67.6 1.6 %copy-done.1 = f32[25,48,640]{2,1,0:T(8,128)} copy-done((f32[25,48,640]{2,1,0:T(8,128)}, f32[25,48,640]{2,1,0:T(8,128)S(1)}, u32[]{:S(2)}) %copy-start.1) | copy-done | bytes 3072024
  69.4 7.6 %shard_map.105 = (f32[4,8,48,512]{3,2,1,0:T(8,128)}, f32[4,48,512]{2,1,0:T(8,128)}, f32[4,48,512]{2,1,0:T(8,128)}) custom-call(f32[8]{0:T(128)} %compare_convert_fusion.north_ref.n, f32[4,8,48,512]{3,2,1,0:T(8,128)} %q_ref.1, f32[4,48,512]{2,1,0:T(8,128)} %collective-permute-done.1.qs_ref, f32[4,48,512]{2,1,0:T(8,128)} %copy-done.3, ...), custom_call_target="tpu_custom_call" | custom-call | tf_op jit(solution)/shard_map/pallas_call | solution.py:137
  77.0 4.2 %collective-permute-start.12 = (f32[4,48,512]{2,1,0:T(8,128)}, f32[4,48,512]{2,1,0:T(8,128)S(1)}, u32[]{:S(2)}, u32[]{:S(2)}) collective-permute-start(f32[4,48,512]{2,1,0:T(8,128)} %get-tuple-element.10), channel_id=1, source_target_pairs={{0,1},{1,2},{2,3},{4,5},{5,6},{6,7},{8,9},{9,10},{10,11},{12,13},{... | collective-permute-start | bytes 1179656 | tf_op jit(solution)/shard_map/ppermute | solution.py:16
  81.1 1.9 %collective-permute-start.13 = (f32[4,48,512]{2,1,0:T(8,128)}, f32[4,48,512]{2,1,0:T(8,128)S(1)}, u32[]{:S(2)}, u32[]{:S(2)}) collective-permute-start(f32[4,48,512]{2,1,0:T(8,128)} %get-tuple-element.11), channel_id=1, source_target_pairs={{1,0},{2,1},{3,2},{5,4},{6,5},{7,6},{9,8},{10,9},{11,10},{13,12},{... | collective-permute-start | bytes 1179656 | tf_op jit(solution)/shard_map/ppermute | solution.py:16
  83.1 6.7 %shard_map.106.base_ref = f32[4,8,48,512]{3,2,1,0:T(8,128)} custom-call(f32[8]{0:T(128)} %compare_convert_fusion.north_ref.n, f32[4,8,48,512]{3,2,1,0:T(8,128)} %get-tuple-element.9.q.qa_ref.qi_ref, f32[25,48,640]{2,1,0:T(8,128)} %copy-done.1, f32[4,8,512]{2,1,0:T(8,128)} %fusion.2.src_ref.e), custom_call_target="tpu_custom_call" | custom-call | tf_op jit(solution)/shard_map/pallas_call | solution.py:164
  89.8 0.7 collective-permute-done.13.qn_ref
  90.5 0.8 copy-done.5
  91.3 3.2 %shard_map.107 = f32[4,8,48,512]{3,2,1,0:T(8,128)} custom-call(f32[8]{0:T(128)} %compare_convert_fusion.north_ref.n, f32[4,8,48,512]{3,2,1,0:T(8,128)} %get-tuple-element.9.q.qa_ref.qi_ref, f32[4,8,48,512]{3,2,1,0:T(8,128)} %get-tuple-element.9.q.qa_ref.qi_ref, f32[4,48,512]{2,1,0:T(8,128)} %copy-done.4, ...), custom_call_target="tpu_custom_call", output_to_operand_aliasing={{}: (10, {})} | custom-call | tf_op jit(solution)/shard_map/pallas_call | solution.py:246
  (33 shorter events, 1.4 us)
Async XLA Ops:
  0.6 6.0 %copy-start = (f32[8,8,8]{2,1,0:T(8,128)S(1)}, f32[8,8,8]{2,1,0:T(8,128)}, u32[]{:S(2)}) copy-start(f32[8,8,8]{2,1,0:T(8,128)} %param.11) | copy-start | bytes 6148
  1.4 5.4 %collective-permute-start = (f32[1,48,128]{2,1,0:T(8,128)S(1)}, f32[1,48,128]{2,1,0:T(8,128)S(1)}, u32[]{:S(2)}, u32[]{:S(2)}) collective-permute-start(f32[1,48,128]{2,1,0:T(8,128)S(1)} %slice.9), channel_id=1, source_target_pairs={{0,1},{1,2},{2,3},{4,5},{5,6},{6,7},{8,9},{9,10},{10,11},{12,13},{... | collective-permute-start | bytes 73736 | tf_op jit(solution)/shard_map/ppermute | solution.py:16
  6.8 0.6 copy-start.6
  9.4 16.4 %collective-permute-start.3 = (f32[25,48,128]{2,1,0:T(8,128)}, f32[25,48,128]{2,1,0:T(8,128)}, u32[]{:S(2)}, u32[]{:S(2)}) collective-permute-start(f32[25,48,128]{2,1,0:T(8,128)} %shard_map.104), channel_id=1, source_target_pairs={{0,4},{4,8},{8,12},{1,5},{5,9},{9,13},{2,6},{6,10},{10,14},{3,7},{... | collective-permute-start | bytes 1843208 | tf_op jit(solution)/shard_map/ppermute | solution.py:44
  14.0 13.8 %copy-start.2 = (f32[25,48,128]{2,1,0:T(8,128)S(1)}, f32[25,48,128]{2,1,0:T(8,128)}, u32[]{:S(2)}) copy-start(f32[25,48,128]{2,1,0:T(8,128)} %shard_map.104) | copy-start | bytes 1843204
  15.1 17.1 %collective-permute-start.4 = (f32[25,48,128]{2,1,0:T(8,128)}, f32[25,48,128]{2,1,0:T(8,128)S(1)}, u32[]{:S(2)}, u32[]{:S(2)}) collective-permute-start(f32[25,48,128]{2,1,0:T(8,128)} %shard_map.104), channel_id=1, source_target_pairs={{4,0},{8,4},{12,8},{5,1},{9,5},{13,9},{6,2},{10,6},{14,10},{7,3},{... | collective-permute-start | bytes 1843208 | tf_op jit(solution)/shard_map/ppermute | solution.py:45
  17.4 16.4 %collective-permute-start.11 = (f32[4,8,512]{2,1,0:T(8,128)}, f32[4,8,512]{2,1,0:T(8,128)S(1)}, u32[]{:S(2)}, u32[]{:S(2)}) collective-permute-start(f32[4,8,512]{2,1,0:T(8,128)} %param.10), channel_id=1, source_target_pairs={{0,3},{1,0},{2,1},{3,2},{4,7},{5,4},{6,5},{7,6},{8,11},{9,8},{10,9... | collective-permute-start | bytes 196616 | tf_op jit(solution)/shard_map/ppermute | solution.py:280
  17.5 20.1 %collective-permute-start.10 = (f32[4,8,512]{2,1,0:T(8,128)}, f32[4,8,512]{2,1,0:T(8,128)S(1)}, u32[]{:S(2)}, u32[]{:S(2)}) collective-permute-start(f32[4,8,512]{2,1,0:T(8,128)} %param.10), channel_id=1, source_target_pairs={{0,2},{1,3},{2,0},{3,1},{4,6},{5,7},{6,4},{7,5},{8,10},{9,11},{10,... | collective-permute-start | bytes 196616 | tf_op jit(solution)/shard_map/ppermute | solution.py:280
  20.2 7.7 %collective-permute-start.9 = (f32[4,8,512]{2,1,0:T(8,128)}, f32[4,8,512]{2,1,0:T(8,128)S(1)}, u32[]{:S(2)}, u32[]{:S(2)}) collective-permute-start(f32[4,8,512]{2,1,0:T(8,128)} %param.10), channel_id=1, source_target_pairs={{0,1},{1,2},{2,3},{3,0},{4,5},{5,6},{6,7},{7,4},{8,9},{9,10},{10,1... | collective-permute-start | bytes 196616 | tf_op jit(solution)/shard_map/ppermute | solution.py:280
  25.8 11.1 %collective-permute-start.5 = (f32[25,48,128]{2,1,0:T(8,128)}, f32[25,48,128]{2,1,0:T(8,128)S(1)}, u32[]{:S(2)}, u32[]{:S(2)}) collective-permute-start(f32[25,48,128]{2,1,0:T(8,128)} %collective-permute-done.3), channel_id=1, source_target_pairs={{4,8},{8,12},{5,9},{9,13},{6,10},{10,14},{7,11},{11,15},{20,24},{2... | collective-permute-start | bytes 1843208 | tf_op jit(solution)/shard_map/ppermute | solution.py:44
  27.9 39.7 %collective-permute-start.2 = (f32[4,48,512]{2,1,0:T(8,128)S(1)}, f32[4,48,512]{2,1,0:T(8,128)S(1)}, u32[]{:S(2)}, u32[]{:S(2)}) collective-permute-start(f32[4,48,512]{2,1,0:T(8,128)S(1)} %get-tuple-element.12), channel_id=1, source_target_pairs={{1,0},{2,1},{3,2},{5,4},{6,5},{7,6},{9,8},{10,9},{11,10},{13,12},{... | collective-permute-start | bytes 1179656 | tf_op jit(solution)/shard_map/ppermute | solution.py:16
  32.3 18.3 %collective-permute-start.6 = (f32[25,48,128]{2,1,0:T(8,128)S(1)}, f32[25,48,128]{2,1,0:T(8,128)S(1)}, u32[]{:S(2)}, u32[]{:S(2)}) collective-permute-start(f32[25,48,128]{2,1,0:T(8,128)S(1)} %collective-permute-done.4), channel_id=1, source_target_pairs={{4,0},{8,4},{5,1},{9,5},{6,2},{10,6},{7,3},{11,7},{20,16},{24,20},... | collective-permute-start | bytes 1843208 | tf_op jit(solution)/shard_map/ppermute | solution.py:45
  33.8 33.9 %collective-permute-start.1 = (f32[4,48,512]{2,1,0:T(8,128)S(1)}, f32[4,48,512]{2,1,0:T(8,128)}, u32[]{:S(2)}, u32[]{:S(2)}) collective-permute-start(f32[4,48,512]{2,1,0:T(8,128)S(1)} %get-tuple-element.13), channel_id=1, source_target_pairs={{0,1},{1,2},{2,3},{4,5},{5,6},{6,7},{8,9},{9,10},{10,11},{12,13},{... | collective-permute-start | bytes 1179656 | tf_op jit(solution)/shard_map/ppermute | solution.py:16
  36.9 16.3 %collective-permute-start.7 = (f32[25,48,128]{2,1,0:T(8,128)S(1)}, f32[25,48,128]{2,1,0:T(8,128)S(1)}, u32[]{:S(2)}, u32[]{:S(2)}) collective-permute-start(f32[25,48,128]{2,1,0:T(8,128)S(1)} %collective-permute-done.5), channel_id=1, source_target_pairs={{8,12},{9,13},{10,14},{11,15},{24,28},{25,29},{26,30},{27,31}} | collective-permute-start | bytes 1843208 | tf_op jit(solution)/shard_map/ppermute | solution.py:44
  50.6 16.9 %collective-permute-start.8 = (f32[25,48,128]{2,1,0:T(8,128)S(1)}, f32[25,48,128]{2,1,0:T(8,128)S(1)}, u32[]{:S(2)}, u32[]{:S(2)}) collective-permute-start(f32[25,48,128]{2,1,0:T(8,128)S(1)} %collective-permute-done.6), channel_id=1, source_target_pairs={{4,0},{5,1},{6,2},{7,3},{20,16},{21,17},{22,18},{23,19}} | collective-permute-start | bytes 1843208 | tf_op jit(solution)/shard_map/ppermute | solution.py:45
  67.6 1.7 %copy-start.1 = (f32[25,48,640]{2,1,0:T(8,128)}, f32[25,48,640]{2,1,0:T(8,128)S(1)}, u32[]{:S(2)}) copy-start(f32[25,48,640]{2,1,0:T(8,128)S(1)} %constant_dynamic-update-slice_fusion.wx_ref.w.u_ref.v_ref.vm_ref.w_ref) | copy-start | bytes 9216004
  67.6 1.7 %copy-start.3 = (f32[4,48,512]{2,1,0:T(8,128)}, f32[4,48,512]{2,1,0:T(8,128)S(1)}, u32[]{:S(2)}) copy-start(f32[4,48,512]{2,1,0:T(8,128)S(1)} %collective-permute-done.2.qn_ref) | copy-start | bytes 1179652
  77.0 12.8 %collective-permute-start.12 = (f32[4,48,512]{2,1,0:T(8,128)}, f32[4,48,512]{2,1,0:T(8,128)S(1)}, u32[]{:S(2)}, u32[]{:S(2)}) collective-permute-start(f32[4,48,512]{2,1,0:T(8,128)} %get-tuple-element.10), channel_id=1, source_target_pairs={{0,1},{1,2},{2,3},{4,5},{5,6},{6,7},{8,9},{9,10},{10,11},{12,13},{... | collective-permute-start | bytes 1179656 | tf_op jit(solution)/shard_map/ppermute | solution.py:16
  81.1 9.3 %collective-permute-start.13 = (f32[4,48,512]{2,1,0:T(8,128)}, f32[4,48,512]{2,1,0:T(8,128)S(1)}, u32[]{:S(2)}, u32[]{:S(2)}) collective-permute-start(f32[4,48,512]{2,1,0:T(8,128)} %get-tuple-element.11), channel_id=1, source_target_pairs={{1,0},{2,1},{3,2},{5,4},{6,5},{7,6},{9,8},{10,9},{11,10},{13,12},{... | collective-permute-start | bytes 1179656 | tf_op jit(solution)/shard_map/ppermute | solution.py:16
  89.8 0.8 copy-start.4
  90.5 0.8 copy-start.5

commit v11 on v10

--- a/solution.py
+++ b/solution.py
@@ -33,7 +33,7 @@
     )(*parts)
 
 
-def relay_gather(x, axis):
+def relay_gather(x, axis, hold):
     count = lax.axis_size(axis)
     me = lax.axis_index(axis)
     rows, levels, width = x.shape
@@ -43,11 +43,15 @@
     for r in range(1, count):
         right = lax.ppermute(right, axis, [(i, i + 1) for i in range(r - 1, count - 1)])
         left = lax.ppermute(left, axis, [(j, j - 1) for j in range(1, count - r + 1)])
+        if r == 1:
+            hold, right = lax.optimization_barrier((hold, right))
         slot = jnp.where(me - r >= 0, me - r, count)
         buf = lax.dynamic_update_slice(buf, right, (0, 0, slot * width))
         slot = jnp.where(me + r < count, me + r, count)
         buf = lax.dynamic_update_slice(buf, left, (0, 0, slot * width))
-    return buf
+    if count == 1:
+        hold = lax.optimization_barrier(hold)
+    return buf, hold
 
 
 def step_kernel(north_ref, q_ref, qs_ref, qn_ref, wx_ref, src_ref, *rest, rows=None):
@@ -270,14 +274,16 @@
 
     south_v = passed_along(meridional_courant[-1:], "band", 1)
     pack = packed([zonal_courant, meridional_courant, vertical_diffusion, south_v])
-    weather = relay_gather(pack, "tracer")
-    held_state, held_control, _ = lax.optimization_barrier((tracer_state, control, pack))
-    q_south = passed_along(held_state[:, -1], "band", 1)
-    q_north = passed_along(held_state[:, 0], "band", -1)
+    weather, held = relay_gather(
+        pack, "tracer", (tracer_state, control, prior_tiles, tile_index, region_map, region_sigma)
+    )
+    tracer_state, control, prior_tiles, tile_index, region_map, region_sigma = held
+    q_south = passed_along(tracer_state[:, -1], "band", 1)
+    q_north = passed_along(tracer_state[:, 0], "band", -1)
     shifted = [control]
     for s in range(1, band_count):
         pairs = [(i, (i + s) % band_count) for i in range(band_count)]
-        shifted.append(lax.ppermute(held_control, "band", pairs))
+        shifted.append(lax.ppermute(control, "band", pairs))
 
     choose = (
         tile_index[:, :, None] == lax.broadcasted_iota(jnp.int32, (1, 1, tiles_count), 2)
@@ -297,7 +303,7 @@
     cell_sigma = jnp.einsum("kr,jnr->kjn", region_sigma, onehot, precision=exact_dot)
     emission = cell_sigma * prior_field
 
-    latitude = band_index * lat_rows + jnp.arange(lat_rows, dtype=jnp.int32)
+    latitude = band_index * lat_rows + lax.broadcasted_iota(jnp.int32, (lat_rows,), 0) + tile_index[0, 0] * 0
     north_open = (latitude < band_count * lat_rows - 1).astype(jnp.float32)
 
     first, bottom_row, top_row = advance(

time: 95.2 us -> 98.4 us (1.034)
  waiting for transfers between devices: 35.2 us -> 40.2 us
  starting transfers between devices: 27.4 us -> 26.4 us
    ppermute x3, waiting for transfers between devices: 5.55 us -> 10.1 us  [relay_gather(): lax.ppermute(right, axis, [(i, i + 1) for i in range(r - 1, count - 1)])]
    ppermute x3, starting transfers between devices: 2.79 us -> 1.78 us  [on_device(): shifted.append(lax.ppermute(control, 'band', pairs))]
    unnamed x14 -> x18, local copies, waits for them, and re-layouts: 3.18 us -> 3.17 us
  transfers between devices with their start and end apart: 14 -> 14, of which waited for: 5 -> 5; matrix products, arithmetic and copies ran while one was open for 8% -> 7% of each run, Pallas kernels for 7% -> 7%
where the time goes in v11:
time: 98.4 us; the launch traced here: 97.7 us
  waiting for transfers between devices  40.2 us (41%)
  starting transfers between devices  26.4 us (27%)
  Pallas kernels  19.5 us (20%)
  local copies, waits for them, and re-layouts  7.42 us (8%)
  matrix products  2.67 us (3%)
    ppermute x3, waiting for transfers between devices, relay_gather(): lax.ppermute(left, axis, [(j, j - 1) for j in range(1, count - r + 1)])  28.4 us
    ppermute x5, starting transfers between devices, passed_along(): return lax.ppermute(value, axis, pairs)  15.2 us
    ppermute x3, waiting for transfers between devices, relay_gather(): lax.ppermute(right, axis, [(i, i + 1) for i in range(r - 1, count - 1)])  10.1 us
    pallas_call x1, Pallas kernels, advance(): pl.pallas_call(step_kernel, grid_spec=grid_spec, out_shape=out_shape, com...  7.63 us
    pallas_call x1, Pallas kernels, interior_step(): pl.pallas_call(kernel, grid_spec=grid_spec, out_shape=jax.ShapeDtypeStruc...  6.69 us
    ppermute x3, starting transfers between devices, relay_gather(): lax.ppermute(right, axis, [(i, i + 1) for i in range(r - 1, count - 1)])  5.58 us
    ppermute x3, starting transfers between devices, relay_gather(): lax.ppermute(left, axis, [(j, j - 1) for j in range(1, count - r + 1)])  3.85 us
    pallas_call x1, Pallas kernels, edge_step(): pl.pallas_call(edge_kernel, grid_spec=grid_spec, out_shape=jax.ShapeDtype...  3.23 us
  transfers between devices with their start and end apart: 14, of which 5 were waited for; matrix products, arithmetic and copies ran while one was open for 7% of the time, Pallas kernels for 7%

profile of v11, /device:TPU:1, one launch (start us, length us, event | category | flops | bytes accessed | tf_op | source)
XLA Modules:
  0.0 97.7 jit_solution(17526089196016671282)
XLA Ops:
  0.6 0.7 slice.9
  1.4 4.5 %collective-permute-start = (f32[1,48,128]{2,1,0:T(8,128)S(1)}, f32[1,48,128]{2,1,0:T(8,128)S(1)}, u32[]{:S(2)}, u32[]{:S(2)}) collective-permute-start(f32[1,48,128]{2,1,0:T(8,128)S(1)} %slice.9), channel_id=1, source_target_pairs={{0,1},{1,2},{2,3},{4,5},{5,6},{6,7},{8,9},{9,10},{10,11},{12,13},{... | collective-permute-start | bytes 73736 | tf_op jit(solution)/shard_map/ppermute | solution.py:16
  5.9 0.9 collective-permute-done.refs_3_
  6.8 0.6 copy-done.6
  7.4 2.0 %shard_map.104 = f32[25,48,128]{2,1,0:T(8,128)} custom-call(f32[8,48,128]{2,1,0:T(8,128)} %refs_0_.1, f32[8,48,128]{2,1,0:T(8,128)} %refs_1_.1, f32[8,48,128]{2,1,0:T(8,128)} %refs_2_.1, f32[1,48,128]{2,1,0:T(8,128)} %copy-done.6), custom_call_target="tpu_custom_call" | custom-call | tf_op jit(solution)/shard_map/pallas_call | solution.py:30
  9.4 4.2 %collective-permute-start.1 = (f32[25,48,128]{2,1,0:T(8,128)}, f32[25,48,128]{2,1,0:T(8,128)}, u32[]{:S(2)}, u32[]{:S(2)}) collective-permute-start(f32[25,48,128]{2,1,0:T(8,128)} %shard_map.104), channel_id=1, source_target_pairs={{0,4},{4,8},{8,12},{1,5},{5,9},{9,13},{2,6},{6,10},{10,14},{3,7},{... | collective-permute-start | bytes 1843208 | tf_op jit(solution)/shard_map/ppermute | solution.py:44
  13.6 0.5 compare_convert_fusion.north_ref.n
  14.1 1.3 %collective-permute-start.4 = (f32[25,48,128]{2,1,0:T(8,128)}, f32[25,48,128]{2,1,0:T(8,128)S(1)}, u32[]{:S(2)}, u32[]{:S(2)}) collective-permute-start(f32[25,48,128]{2,1,0:T(8,128)} %shard_map.104), channel_id=1, source_target_pairs={{4,0},{8,4},{12,8},{5,1},{9,5},{13,9},{6,2},{10,6},{14,10},{7,3},{... | collective-permute-start | bytes 1843208 | tf_op jit(solution)/shard_map/ppermute | solution.py:45
  15.7 10.1 %collective-permute-done.1 = f32[25,48,128]{2,1,0:T(8,128)} collective-permute-done((f32[25,48,128]{2,1,0:T(8,128)}, f32[25,48,128]{2,1,0:T(8,128)}, u32[]{:S(2)}, u32[]{:S(2)}) %collective-permute-start.1) | collective-permute-done | bytes 614432 | tf_op jit(solution)/shard_map/ppermute | solution.py:44
  25.8 1.2 %collective-permute-start.10 = (f32[4,8,512]{2,1,0:T(8,128)}, f32[4,8,512]{2,1,0:T(8,128)S(1)}, u32[]{:S(2)}, u32[]{:S(2)}) collective-permute-start(f32[4,8,512]{2,1,0:T(8,128)} %param.10), channel_id=1, source_target_pairs={{0,2},{1,3},{2,0},{3,1},{4,6},{5,7},{6,4},{7,5},{8,10},{9,11},{10,... | collective-permute-start | bytes 196616 | tf_op jit(solution)/shard_map/ppermute | solution.py:286
  27.0 0.6 collective-permute-start.9
  27.6 0.7 collective-permute-start.5
  28.3 0.7 constant_dynamic-slice_fusion.4
  29.2 1.1 %constant_dynamic-update-slice_fusion.5 = f32[25,48,640]{2,1,0:T(8,128)S(1)} fusion(f32[25,48,640]{2,1,0:T(8,128)S(1)} %constant_dynamic-update-slice_fusion.6, f32[25,48,128]{2,1,0:T(8,128)} %collective-permute-done.1, s32[]{:T(128)S(6)} %select_n.77), kind=kLoop, calls=%fused_computation.22 | loop fusion | bytes 1228804 | tf_op jit(solution)/shard_map/dynamic_update_slice | solution.py:49
  30.3 0.2 fusion.4
  30.6 1.2 %slice_bitcast_fusion = (f32[4,48,512]{2,1,0:T(8,128)S(1)}, f32[4,48,512]{2,1,0:T(8,128)S(1)}) fusion(f32[4,8,48,512]{3,2,1,0:T(8,128)} %q_ref), kind=kLoop, calls=%fused_computation.5 | loop fusion | bytes 1572864 | tf_op jit(solution)/shard_map/squeeze | solution.py:282
  31.8 2.3 %collective-permute-start.3 = (f32[4,48,512]{2,1,0:T(8,128)S(1)}, f32[4,48,512]{2,1,0:T(8,128)S(1)}, u32[]{:S(2)}, u32[]{:S(2)}) collective-permute-start(f32[4,48,512]{2,1,0:T(8,128)S(1)} %get-tuple-element.22), channel_id=1, source_target_pairs={{1,0},{2,1},{3,2},{5,4},{6,5},{7,6},{9,8},{10,9},{11,10},{13,12},{... | collective-permute-start | bytes 1179656 | tf_op jit(solution)/shard_map/ppermute | solution.py:16
  34.2 1.3 %collective-permute-start.6 = (f32[25,48,128]{2,1,0:T(8,128)S(1)}, f32[25,48,128]{2,1,0:T(8,128)S(1)}, u32[]{:S(2)}, u32[]{:S(2)}) collective-permute-start(f32[25,48,128]{2,1,0:T(8,128)S(1)} %collective-permute-done.4), channel_id=1, source_target_pairs={{4,0},{8,4},{5,1},{9,5},{6,2},{10,6},{7,3},{11,7},{20,16},{24,20},... | collective-permute-start | bytes 1843208 | tf_op jit(solution)/shard_map/ppermute | solution.py:45
  35.7 3.3 %collective-permute-start.2 = (f32[4,48,512]{2,1,0:T(8,128)S(1)}, f32[4,48,512]{2,1,0:T(8,128)}, u32[]{:S(2)}, u32[]{:S(2)}) collective-permute-start(f32[4,48,512]{2,1,0:T(8,128)S(1)} %get-tuple-element.23), channel_id=1, source_target_pairs={{0,1},{1,2},{2,3},{4,5},{5,6},{6,7},{8,9},{9,10},{10,11},{12,13},{... | collective-permute-start | bytes 1179656 | tf_op jit(solution)/shard_map/ppermute | solution.py:16
  39.2 0.7 collective-permute-start.7
  40.1 14.6 %collective-permute-done.6 = f32[25,48,128]{2,1,0:T(8,128)S(1)} collective-permute-done((f32[25,48,128]{2,1,0:T(8,128)S(1)}, f32[25,48,128]{2,1,0:T(8,128)S(1)}, u32[]{:S(2)}, u32[]{:S(2)}) %collective-permute-start.6) | collective-permute-done | bytes 614432 | tf_op jit(solution)/shard_map/ppermute | solution.py:45
  54.7 1.3 %collective-permute-start.8 = (f32[25,48,128]{2,1,0:T(8,128)S(1)}, f32[25,48,128]{2,1,0:T(8,128)S(1)}, u32[]{:S(2)}, u32[]{:S(2)}) collective-permute-start(f32[25,48,128]{2,1,0:T(8,128)S(1)} %collective-permute-done.6), channel_id=1, source_target_pairs={{4,0},{5,1},{6,2},{7,3},{20,16},{21,17},{22,18},{23,19}} | collective-permute-start | bytes 1843208 | tf_op jit(solution)/shard_map/ppermute | solution.py:45
  55.9 1.7 %fusion.3.src_ref.e = f32[4,8,512]{2,1,0:T(8,128)} fusion(f32[4,512,8]{1,2,0:T(8,128)S(1)} %fusion.14, f32[4,512,8]{1,2,0:T(8,128)S(1)} %fusion.13, f32[4,512,8]{1,2,0:T(8,128)S(1)} %fusion.12, f32[4,8,512]{2,1,0:T(8,128)} %param.10, f32[8,8,1]{1,0,2:T(8,128)S(1)} %bitcast.31, f32[4,8,512]{2,0,1:T(4,128)S(1)} %fusion.4), kind=kOutput, calls=%fused_computation.4 | convolution fusion | flops 1638400 | bytes 393472 | tf_op jit(solution)/shard_map/jm,kmn->kjn/dot_general | solution.py:297
  57.8 13.9 %collective-permute-done.8 = f32[25,48,128]{2,1,0:T(8,128)S(1)} collective-permute-done((f32[25,48,128]{2,1,0:T(8,128)S(1)}, f32[25,48,128]{2,1,0:T(8,128)S(1)}, u32[]{:S(2)}, u32[]{:S(2)}) %collective-permute-start.8) | collective-permute-done | bytes 614432 | tf_op jit(solution)/shard_map/ppermute | solution.py:45
  71.7 1.6 %copy-done.1 = f32[25,48,640]{2,1,0:T(8,128)} copy-done((f32[25,48,640]{2,1,0:T(8,128)}, f32[25,48,640]{2,1,0:T(8,128)S(1)}, u32[]{:S(2)}) %copy-start.1) | copy-done | bytes 3072024
  73.5 7.6 %shard_map.105 = (f32[4,8,48,512]{3,2,1,0:T(8,128)}, f32[4,48,512]{2,1,0:T(8,128)}, f32[4,48,512]{2,1,0:T(8,128)}) custom-call(f32[8]{0:T(128)} %compare_convert_fusion.north_ref.n, f32[4,8,48,512]{3,2,1,0:T(8,128)} %q_ref, f32[4,48,512]{2,1,0:T(8,128)} %collective-permute-done.2.qs_ref, f32[4,48,512]{2,1,0:T(8,128)} %copy-done.3, f32[25,48,640]{2,1,0:T(8,128)} %copy-done.1, ...), custom_call_target="tpu_custom_call" | custom-call | tf_op jit(solution)/shard_map/pallas_call | solution.py:141
  81.1 3.2 %collective-permute-start.12 = (f32[4,48,512]{2,1,0:T(8,128)}, f32[4,48,512]{2,1,0:T(8,128)S(1)}, u32[]{:S(2)}, u32[]{:S(2)}) collective-permute-start(f32[4,48,512]{2,1,0:T(8,128)} %get-tuple-element.20), channel_id=1, source_target_pairs={{0,1},{1,2},{2,3},{4,5},{5,6},{6,7},{8,9},{9,10},{10,11},{12,13},{... | collective-permute-start | bytes 1179656 | tf_op jit(solution)/shard_map/ppermute | solution.py:16
  84.3 1.9 %collective-permute-start.13 = (f32[4,48,512]{2,1,0:T(8,128)}, f32[4,48,512]{2,1,0:T(8,128)S(1)}, u32[]{:S(2)}, u32[]{:S(2)}) collective-permute-start(f32[4,48,512]{2,1,0:T(8,128)} %get-tuple-element.21), channel_id=1, source_target_pairs={{1,0},{2,1},{3,2},{5,4},{6,5},{7,6},{9,8},{10,9},{11,10},{13,12},{... | collective-permute-start | bytes 1179656 | tf_op jit(solution)/shard_map/ppermute | solution.py:16
  86.2 6.7 %shard_map.106.base_ref = f32[4,8,48,512]{3,2,1,0:T(8,128)} custom-call(f32[8]{0:T(128)} %compare_convert_fusion.north_ref.n, f32[4,8,48,512]{3,2,1,0:T(8,128)} %get-tuple-element.19.q.qa_ref.qi_ref, f32[25,48,640]{2,1,0:T(8,128)} %copy-done.1, f32[4,8,512]{2,1,0:T(8,128)} %fusion.3.src_ref.e), custom_call_target="tpu_custom_call" | custom-call | tf_op jit(solution)/shard_map/pallas_call | solution.py:168
  92.9 0.7 collective-permute-done.13.qn_ref
  93.7 0.8 copy-done.5
  94.4 3.2 %shard_map.107 = f32[4,8,48,512]{3,2,1,0:T(8,128)} custom-call(f32[8]{0:T(128)} %compare_convert_fusion.north_ref.n, f32[4,8,48,512]{3,2,1,0:T(8,128)} %get-tuple-element.19.q.qa_ref.qi_ref, f32[4,8,48,512]{3,2,1,0:T(8,128)} %get-tuple-element.19.q.qa_ref.qi_ref, f32[4,48,512]{2,1,0:T(8,128)} %copy-done.4, ...), custom_call_target="tpu_custom_call", output_to_operand_aliasing={{}: (10, {})} | custom-call | tf_op jit(solution)/shard_map/pallas_call | solution.py:250
  (37 shorter events, 1.5 us)
Async XLA Ops:
  0.6 28.4 %copy-start = (f32[8,8,8]{2,1,0:T(8,128)S(1)}, f32[8,8,8]{2,1,0:T(8,128)}, u32[]{:S(2)}) copy-start(f32[8,8,8]{2,1,0:T(8,128)} %param.11) | copy-start | bytes 6148
  1.4 5.4 %collective-permute-start = (f32[1,48,128]{2,1,0:T(8,128)S(1)}, f32[1,48,128]{2,1,0:T(8,128)S(1)}, u32[]{:S(2)}, u32[]{:S(2)}) collective-permute-start(f32[1,48,128]{2,1,0:T(8,128)S(1)} %slice.9), channel_id=1, source_target_pairs={{0,1},{1,2},{2,3},{4,5},{5,6},{6,7},{8,9},{9,10},{10,11},{12,13},{... | collective-permute-start | bytes 73736 | tf_op jit(solution)/shard_map/ppermute | solution.py:16
  6.8 0.6 copy-start.6
  9.4 20.9 %copy-start.7 = (s32[8,512]{1,0:T(8,128)S(1)}, s32[8,512]{1,0:T(8,128)}, u32[]{:S(2)}) copy-start(s32[8,512]{1,0:T(8,128)} %param.13) | copy-start | bytes 49156
  9.4 20.9 %copy-start.8 = (f32[4,22]{1,0:T(4,128)S(1)}, f32[4,22]{1,0:T(4,128)}, u32[]{:S(2)}) copy-start(f32[4,22]{1,0:T(4,128)} %param.14) | copy-start | bytes 1060
  9.4 16.4 %collective-permute-start.1 = (f32[25,48,128]{2,1,0:T(8,128)}, f32[25,48,128]{2,1,0:T(8,128)}, u32[]{:S(2)}, u32[]{:S(2)}) collective-permute-start(f32[25,48,128]{2,1,0:T(8,128)} %shard_map.104), channel_id=1, source_target_pairs={{0,4},{4,8},{8,12},{1,5},{5,9},{9,13},{2,6},{6,10},{10,14},{3,7},{... | collective-permute-start | bytes 1843208 | tf_op jit(solution)/shard_map/ppermute | solution.py:44
  13.6 2.0 %copy-start.2 = (f32[25,48,128]{2,1,0:T(8,128)S(1)}, f32[25,48,128]{2,1,0:T(8,128)}, u32[]{:S(2)}) copy-start(f32[25,48,128]{2,1,0:T(8,128)} %shard_map.104) | copy-start | bytes 1843204
  14.1 17.6 %collective-permute-start.4 = (f32[25,48,128]{2,1,0:T(8,128)}, f32[25,48,128]{2,1,0:T(8,128)S(1)}, u32[]{:S(2)}, u32[]{:S(2)}) collective-permute-start(f32[25,48,128]{2,1,0:T(8,128)} %shard_map.104), channel_id=1, source_target_pairs={{4,0},{8,4},{12,8},{5,1},{9,5},{13,9},{6,2},{10,6},{14,10},{7,3},{... | collective-permute-start | bytes 1843208 | tf_op jit(solution)/shard_map/ppermute | solution.py:45
  25.8 8.3 %collective-permute-start.11 = (f32[4,8,512]{2,1,0:T(8,128)}, f32[4,8,512]{2,1,0:T(8,128)S(1)}, u32[]{:S(2)}, u32[]{:S(2)}) collective-permute-start(f32[4,8,512]{2,1,0:T(8,128)} %param.10), channel_id=1, source_target_pairs={{0,3},{1,0},{2,1},{3,2},{4,7},{5,4},{6,5},{7,6},{8,11},{9,8},{10,9... | collective-permute-start | bytes 196616 | tf_op jit(solution)/shard_map/ppermute | solution.py:286
  25.8 9.8 %collective-permute-start.10 = (f32[4,8,512]{2,1,0:T(8,128)}, f32[4,8,512]{2,1,0:T(8,128)S(1)}, u32[]{:S(2)}, u32[]{:S(2)}) collective-permute-start(f32[4,8,512]{2,1,0:T(8,128)} %param.10), channel_id=1, source_target_pairs={{0,2},{1,3},{2,0},{3,1},{4,6},{5,7},{6,4},{7,5},{8,10},{9,11},{10,... | collective-permute-start | bytes 196616 | tf_op jit(solution)/shard_map/ppermute | solution.py:286
  27.0 12.9 %collective-permute-start.9 = (f32[4,8,512]{2,1,0:T(8,128)}, f32[4,8,512]{2,1,0:T(8,128)S(1)}, u32[]{:S(2)}, u32[]{:S(2)}) collective-permute-start(f32[4,8,512]{2,1,0:T(8,128)} %param.10), channel_id=1, source_target_pairs={{0,1},{1,2},{2,3},{3,0},{4,5},{5,6},{6,7},{7,4},{8,9},{9,10},{10,1... | collective-permute-start | bytes 196616 | tf_op jit(solution)/shard_map/ppermute | solution.py:286
  27.6 11.6 %collective-permute-start.5 = (f32[25,48,128]{2,1,0:T(8,128)}, f32[25,48,128]{2,1,0:T(8,128)S(1)}, u32[]{:S(2)}, u32[]{:S(2)}) collective-permute-start(f32[25,48,128]{2,1,0:T(8,128)} %collective-permute-done.1), channel_id=1, source_target_pairs={{4,8},{8,12},{5,9},{9,13},{6,10},{10,14},{7,11},{11,15},{20,24},{2... | collective-permute-start | bytes 1843208 | tf_op jit(solution)/shard_map/ppermute | solution.py:44
  31.8 39.9 %collective-permute-start.3 = (f32[4,48,512]{2,1,0:T(8,128)S(1)}, f32[4,48,512]{2,1,0:T(8,128)S(1)}, u32[]{:S(2)}, u32[]{:S(2)}) collective-permute-start(f32[4,48,512]{2,1,0:T(8,128)S(1)} %get-tuple-element.22), channel_id=1, source_target_pairs={{1,0},{2,1},{3,2},{5,4},{6,5},{7,6},{9,8},{10,9},{11,10},{13,12},{... | collective-permute-start | bytes 1179656 | tf_op jit(solution)/shard_map/ppermute | solution.py:16
  34.2 20.5 %collective-permute-start.6 = (f32[25,48,128]{2,1,0:T(8,128)S(1)}, f32[25,48,128]{2,1,0:T(8,128)S(1)}, u32[]{:S(2)}, u32[]{:S(2)}) collective-permute-start(f32[25,48,128]{2,1,0:T(8,128)S(1)} %collective-permute-done.4), channel_id=1, source_target_pairs={{4,0},{8,4},{5,1},{9,5},{6,2},{10,6},{7,3},{11,7},{20,16},{24,20},... | collective-permute-start | bytes 1843208 | tf_op jit(solution)/shard_map/ppermute | solution.py:45
  35.7 36.1 %collective-permute-start.2 = (f32[4,48,512]{2,1,0:T(8,128)S(1)}, f32[4,48,512]{2,1,0:T(8,128)}, u32[]{:S(2)}, u32[]{:S(2)}) collective-permute-start(f32[4,48,512]{2,1,0:T(8,128)S(1)} %get-tuple-element.23), channel_id=1, source_target_pairs={{0,1},{1,2},{2,3},{4,5},{5,6},{6,7},{8,9},{9,10},{10,11},{12,13},{... | collective-permute-start | bytes 1179656 | tf_op jit(solution)/shard_map/ppermute | solution.py:16
  39.2 18.6 %collective-permute-start.7 = (f32[25,48,128]{2,1,0:T(8,128)S(1)}, f32[25,48,128]{2,1,0:T(8,128)S(1)}, u32[]{:S(2)}, u32[]{:S(2)}) collective-permute-start(f32[25,48,128]{2,1,0:T(8,128)S(1)} %collective-permute-done.5), channel_id=1, source_target_pairs={{8,12},{9,13},{10,14},{11,15},{24,28},{25,29},{26,30},{27,31}} | collective-permute-start | bytes 1843208 | tf_op jit(solution)/shard_map/ppermute | solution.py:44
  54.7 17.0 %collective-permute-start.8 = (f32[25,48,128]{2,1,0:T(8,128)S(1)}, f32[25,48,128]{2,1,0:T(8,128)S(1)}, u32[]{:S(2)}, u32[]{:S(2)}) collective-permute-start(f32[25,48,128]{2,1,0:T(8,128)S(1)} %collective-permute-done.6), channel_id=1, source_target_pairs={{4,0},{5,1},{6,2},{7,3},{20,16},{21,17},{22,18},{23,19}} | collective-permute-start | bytes 1843208 | tf_op jit(solution)/shard_map/ppermute | solution.py:45
  71.7 1.7 %copy-start.1 = (f32[25,48,640]{2,1,0:T(8,128)}, f32[25,48,640]{2,1,0:T(8,128)S(1)}, u32[]{:S(2)}) copy-start(f32[25,48,640]{2,1,0:T(8,128)S(1)} %constant_dynamic-update-slice_fusion.wx_ref.w.u_ref.v_ref.vm_ref.w_ref) | copy-start | bytes 9216004
  71.7 1.7 %copy-start.3 = (f32[4,48,512]{2,1,0:T(8,128)}, f32[4,48,512]{2,1,0:T(8,128)S(1)}, u32[]{:S(2)}) copy-start(f32[4,48,512]{2,1,0:T(8,128)S(1)} %collective-permute-done.3.qn_ref) | copy-start | bytes 1179652
  81.1 11.9 %collective-permute-start.12 = (f32[4,48,512]{2,1,0:T(8,128)}, f32[4,48,512]{2,1,0:T(8,128)S(1)}, u32[]{:S(2)}, u32[]{:S(2)}) collective-permute-start(f32[4,48,512]{2,1,0:T(8,128)} %get-tuple-element.20), channel_id=1, source_target_pairs={{0,1},{1,2},{2,3},{4,5},{5,6},{6,7},{8,9},{9,10},{10,11},{12,13},{... | collective-permute-start | bytes 1179656 | tf_op jit(solution)/shard_map/ppermute | solution.py:16
  84.3 9.3 %collective-permute-start.13 = (f32[4,48,512]{2,1,0:T(8,128)}, f32[4,48,512]{2,1,0:T(8,128)S(1)}, u32[]{:S(2)}, u32[]{:S(2)}) collective-permute-start(f32[4,48,512]{2,1,0:T(8,128)} %get-tuple-element.21), channel_id=1, source_target_pairs={{1,0},{2,1},{3,2},{5,4},{6,5},{7,6},{9,8},{10,9},{11,10},{13,12},{... | collective-permute-start | bytes 1179656 | tf_op jit(solution)/shard_map/ppermute | solution.py:16
  92.9 0.7 copy-start.4
  93.7 0.8 copy-start.5

commit v12 on v9

--- a/solution.py
+++ b/solution.py
@@ -14,6 +14,23 @@
     count = lax.axis_size(axis)
     pairs = [(i, i + by) for i in range(count) if 0 <= i + by < count]
     return lax.ppermute(value, axis, pairs)
+
+
+def pack_kernel(*refs):
+    parts, out_ref = refs[:-1], refs[-1]
+    row = 0
+    for part in parts:
+        rows = part.shape[0]
+        out_ref[row : row + rows] = part[...]
+        row += rows
+
+
+def packed(parts):
+    rows = sum(part.shape[0] for part in parts)
+    return pl.pallas_call(
+        pack_kernel,
+        out_shape=jax.ShapeDtypeStruct((rows,) + parts[0].shape[1:], parts[0].dtype),
+    )(*parts)
 
 
 def relay_gather(x, axis):
@@ -349,7 +366,7 @@
     lat_rows = control.shape[1]
 
     south_v = passed_along(meridional_courant[-1:], "band", 1)
-    pack = jnp.concatenate([zonal_courant, meridional_courant, vertical_diffusion, south_v], axis=0)
+    pack = packed([zonal_courant, meridional_courant, vertical_diffusion, south_v])
     weather = relay_gather(pack, "tracer")
     held_state, held_control, _ = lax.optimization_barrier((tracer_state, control, pack))
     q_south = passed_along(held_state[:, -1], "band", 1)

time: 97.9 us -> 95 us (0.970)
  local copies, waits for them, and re-layouts: 16 us -> 11.2 us
  Pallas kernels: 16.4 us -> 18.4 us
    unnamed x21 -> x20, local copies, waits for them, and re-layouts: 7.58 us -> 3.35 us
    pallas_call x0 -> x1, Pallas kernels: none -> 1.98 us  [packed(): pl.pallas_call(pack_kernel, out_shape=jax.ShapeDtypeStruct((rows,) + part...]
  transfers between devices with their start and end apart: 14 -> 14, of which waited for: 4 -> 4; matrix products, arithmetic and copies ran while one was open for 16% -> 12% of each run, Pallas kernels for 9% -> 9%
where the time goes in v12:
time: 95 us; the launch traced here: 94.2 us
  waiting for transfers between devices  35.9 us (38%)
  starting transfers between devices  23.9 us (25%)
  Pallas kernels  18.4 us (19%)
  local copies, waits for them, and re-layouts  11.2 us (12%)
  matrix products  3.32 us (3%)
  between operations  1.03 us (1%)
    ppermute x3, waiting for transfers between devices, relay_gather(): lax.ppermute(left, axis, [(j, j - 1) for j in range(1, count - r + 1)])  29.4 us
    ppermute x5, starting transfers between devices, passed_along(): return lax.ppermute(value, axis, pairs)  13.4 us
    pallas_call x1, Pallas kernels, fused_steps(): pl.pallas_call(fused_kernel, grid_spec=grid_spec, out_shape=[jax.ShapeDty...  8.67 us
    pallas_call x2, Pallas kernels, edge_step(): pl.pallas_call(kernel, grid_spec=grid_spec, out_shape=out_shape, input_ou...  7.72 us
    ppermute x3, waiting for transfers between devices, relay_gather(): lax.ppermute(right, axis, [(i, i + 1) for i in range(r - 1, count - 1)])  6.48 us
    ppermute x3, starting transfers between devices, relay_gather(): lax.ppermute(right, axis, [(i, i + 1) for i in range(r - 1, count - 1)])  5.43 us
    ppermute x3, starting transfers between devices, relay_gather(): lax.ppermute(left, axis, [(j, j - 1) for j in range(1, count - r + 1)])  3.97 us
    unnamed x20, local copies, waits for them, and re-layouts  3.35 us
  transfers between devices with their start and end apart: 14, of which 4 were waited for; matrix products, arithmetic and copies ran while one was open for 12% of the time, Pallas kernels for 9%

profile of v12, /device:TPU:1, one launch (start us, length us, event | category | flops | bytes accessed | tf_op | source)
XLA Modules:
  0.0 94.2 jit_solution(3148443960259531202)
XLA Ops:
  0.7 0.8 slice.25
  1.4 4.5 %collective-permute-start = (f32[1,48,128]{2,1,0:T(8,128)S(1)}, f32[1,48,128]{2,1,0:T(8,128)S(1)}, u32[]{:S(2)}, u32[]{:S(2)}) collective-permute-start(f32[1,48,128]{2,1,0:T(8,128)S(1)} %slice.25), channel_id=1, source_target_pairs={{0,1},{1,2},{2,3},{4,5},{5,6},{6,7},{8,9},{9,10},{10,11},{12,13},{... | collective-permute-start | bytes 73736 | tf_op jit(solution)/shard_map/ppermute | solution.py:16
  6.0 0.7 constant_dynamic-slice_fusion.4
  6.9 1.7 %convolution_bitcast_fusion.3 = f32[4,8,512]{2,1,0:T(8,128)} fusion(f32[8,8,1]{1,0,2:T(8,128)S(1)} %bitcast.63, f32[4,8,512]{2,1,0:T(8,128)} %param.10), kind=kOutput, calls=%fused_computation.7 | convolution fusion | flops 1572864 | bytes 131328 | tf_op jit(solution)/shard_map/jm,kmn->kjn/dot_general | solution.py:388
  8.6 0.6 copy-done.7
  9.2 2.0 %shard_map.104 = f32[25,48,128]{2,1,0:T(8,128)} custom-call(f32[8,48,128]{2,1,0:T(8,128)} %refs_0_.1, f32[8,48,128]{2,1,0:T(8,128)} %refs_1_.1, f32[8,48,128]{2,1,0:T(8,128)} %refs_2_.1, f32[1,48,128]{2,1,0:T(8,128)} %copy-done.7), custom_call_target="tpu_custom_call" | custom-call | tf_op jit(solution)/shard_map/pallas_call | solution.py:30
  11.2 4.0 %collective-permute-start.3 = (f32[25,48,128]{2,1,0:T(8,128)}, f32[25,48,128]{2,1,0:T(8,128)}, u32[]{:S(2)}, u32[]{:S(2)}) collective-permute-start(f32[25,48,128]{2,1,0:T(8,128)} %shard_map.104), channel_id=1, source_target_pairs={{0,4},{4,8},{8,12},{1,5},{5,9},{9,13},{2,6},{6,10},{10,14},{3,7},{... | collective-permute-start | bytes 1843208 | tf_op jit(solution)/shard_map/ppermute | solution.py:44
  15.8 2.5 %slice_bitcast_fusion.2 = (f32[4,48,512]{2,1,0:T(8,128)}, f32[4,48,512]{2,1,0:T(8,128)}, f32[4,48,512]{2,1,0:T(8,128)}, f32[4,48,512]{2,1,0:T(8,128)}) fusion(f32[4,8,48,512]{3,2,1,0:T(8,128)} %q_ref.1), kind=kLoop, calls=%fused_computation.11 | loop fusion | bytes 3145728 | tf_op jit(solution)/shard_map/squeeze | solution.py:400
  18.3 1.4 %collective-permute-start.4 = (f32[25,48,128]{2,1,0:T(8,128)}, f32[25,48,128]{2,1,0:T(8,128)S(1)}, u32[]{:S(2)}, u32[]{:S(2)}) collective-permute-start(f32[25,48,128]{2,1,0:T(8,128)} %shard_map.104), channel_id=1, source_target_pairs={{4,0},{8,4},{12,8},{5,1},{9,5},{13,9},{6,2},{10,6},{14,10},{7,3},{... | collective-permute-start | bytes 1843208 | tf_op jit(solution)/shard_map/ppermute | solution.py:45
  20.0 0.9 collective-permute-start.9
  21.1 6.5 %collective-permute-done.3 = f32[25,48,128]{2,1,0:T(8,128)} collective-permute-done((f32[25,48,128]{2,1,0:T(8,128)}, f32[25,48,128]{2,1,0:T(8,128)}, u32[]{:S(2)}, u32[]{:S(2)}) %collective-permute-start.3) | collective-permute-done | bytes 614432 | tf_op jit(solution)/shard_map/ppermute | solution.py:44
  27.5 0.7 collective-permute-start.5
  28.2 1.2 %slice_bitcast_fusion = (f32[4,48,512]{2,1,0:T(8,128)S(1)}, f32[4,48,512]{2,1,0:T(8,128)S(1)}) fusion(f32[4,8,48,512]{3,2,1,0:T(8,128)} %q_ref.1), kind=kLoop, calls=%fused_computation.8 | loop fusion | bytes 1572864 | tf_op jit(solution)/shard_map/squeeze | solution.py:373
  29.6 1.1 %constant_dynamic-update-slice_fusion.6 = f32[25,48,640]{2,1,0:T(8,128)S(1)} fusion(f32[25,48,640]{2,1,0:T(8,128)S(1)} %broadcast_in_dim.2, f32[25,48,128]{2,1,0:T(8,128)} %shard_map.104, s32[]{:T(128)S(6)} %select_n.75), kind=kLoop, calls=%fused_computation.30 | loop fusion | bytes 1228804 | tf_op jit(solution)/shard_map/dynamic_update_slice | solution.py:41
  30.8 1.9 %collective-permute-start.1 = (f32[4,48,512]{2,1,0:T(8,128)S(1)}, f32[4,48,512]{2,1,0:T(8,128)S(1)}, u32[]{:S(2)}, u32[]{:S(2)}) collective-permute-start(f32[4,48,512]{2,1,0:T(8,128)S(1)} %get-tuple-element.17), channel_id=1, source_target_pairs={{0,1},{1,2},{2,3},{4,5},{5,6},{6,7},{8,9},{9,10},{10,11},{12,13},{... | collective-permute-start | bytes 1179656 | tf_op jit(solution)/shard_map/ppermute | solution.py:16
  32.7 2.9 %collective-permute-done.4 = f32[25,48,128]{2,1,0:T(8,128)S(1)} collective-permute-done((f32[25,48,128]{2,1,0:T(8,128)}, f32[25,48,128]{2,1,0:T(8,128)S(1)}, u32[]{:S(2)}, u32[]{:S(2)}) %collective-permute-start.4) | collective-permute-done | bytes 614432 | tf_op jit(solution)/shard_map/ppermute | solution.py:45
  35.6 1.3 %collective-permute-start.6 = (f32[25,48,128]{2,1,0:T(8,128)S(1)}, f32[25,48,128]{2,1,0:T(8,128)S(1)}, u32[]{:S(2)}, u32[]{:S(2)}) collective-permute-start(f32[25,48,128]{2,1,0:T(8,128)S(1)} %collective-permute-done.4), channel_id=1, source_target_pairs={{4,0},{8,4},{5,1},{9,5},{6,2},{10,6},{7,3},{11,7},{20,16},{24,20},... | collective-permute-start | bytes 1843208 | tf_op jit(solution)/shard_map/ppermute | solution.py:45
  37.1 2.1 %collective-permute-start.2 = (f32[4,48,512]{2,1,0:T(8,128)S(1)}, f32[4,48,512]{2,1,0:T(8,128)S(1)}, u32[]{:S(2)}, u32[]{:S(2)}) collective-permute-start(f32[4,48,512]{2,1,0:T(8,128)S(1)} %get-tuple-element.16), channel_id=1, source_target_pairs={{1,0},{2,1},{3,2},{5,4},{6,5},{7,6},{9,8},{10,9},{11,10},{13,12},{... | collective-permute-start | bytes 1179656 | tf_op jit(solution)/shard_map/ppermute | solution.py:16
  39.4 0.7 collective-permute-start.7
  40.1 0.8 fusion.2.src_ref.refs_11_
  41.0 12.6 %collective-permute-done.6 = f32[25,48,128]{2,1,0:T(8,128)S(1)} collective-permute-done((f32[25,48,128]{2,1,0:T(8,128)S(1)}, f32[25,48,128]{2,1,0:T(8,128)S(1)}, u32[]{:S(2)}, u32[]{:S(2)}) %collective-permute-start.6) | collective-permute-done | bytes 614432 | tf_op jit(solution)/shard_map/ppermute | solution.py:45
  53.6 1.3 %collective-permute-start.8 = (f32[25,48,128]{2,1,0:T(8,128)S(1)}, f32[25,48,128]{2,1,0:T(8,128)S(1)}, u32[]{:S(2)}, u32[]{:S(2)}) collective-permute-start(f32[25,48,128]{2,1,0:T(8,128)S(1)} %collective-permute-done.6), channel_id=1, source_target_pairs={{4,0},{5,1},{6,2},{7,3},{20,16},{21,17},{22,18},{23,19}} | collective-permute-start | bytes 1843208 | tf_op jit(solution)/shard_map/ppermute | solution.py:45
  54.9 1.1 %constant_dynamic-update-slice_fusion.5 = f32[25,48,640]{2,1,0:T(8,128)S(1)} fusion(f32[25,48,640]{2,1,0:T(8,128)S(1)} %constant_dynamic-update-slice_fusion.6, f32[25,48,128]{2,1,0:T(8,128)} %collective-permute-done.3, s32[]{:T(128)S(6)} %select_n.77), kind=kLoop, calls=%fused_computation.29 | loop fusion | bytes 1228804 | tf_op jit(solution)/shard_map/dynamic_update_slice | solution.py:47
  56.2 13.9 %collective-permute-done.8 = f32[25,48,128]{2,1,0:T(8,128)S(1)} collective-permute-done((f32[25,48,128]{2,1,0:T(8,128)S(1)}, f32[25,48,128]{2,1,0:T(8,128)S(1)}, u32[]{:S(2)}, u32[]{:S(2)}) %collective-permute-start.8) | collective-permute-done | bytes 614432 | tf_op jit(solution)/shard_map/ppermute | solution.py:45
  70.2 0.8 copy-done.3
  71.0 0.9 copy-done.1
  72.1 4.1 %shard_map.105 = (f32[4,48,512]{2,1,0:T(8,128)}, f32[4,48,512]{2,1,0:T(8,128)}) custom-call(f32[8]{0:T(128)} %compare_convert_fusion.north_ref.refs_0_, f32[4,48,512]{2,1,0:T(8,128)} %get-tuple-element.21.lo_ref, f32[4,48,512]{2,1,0:T(8,128)} %get-tuple-element.20.hi_ref, f32[4,48,512]{2,1,0:T(8,128)} %get-tuple-element.19.lo_in_ref, ...), custom_call_target="tpu_custom_call" | custom-call | tf_op jit(solution)/shard_map/pallas_call | solution.py:277
  76.2 1.9 %collective-permute-start.12 = (f32[4,48,512]{2,1,0:T(8,128)}, f32[4,48,512]{2,1,0:T(8,128)S(1)}, u32[]{:S(2)}, u32[]{:S(2)}) collective-permute-start(f32[4,48,512]{2,1,0:T(8,128)} %get-tuple-element.12.hi_ref.refs_2_), channel_id=1, source_target_pairs={{0,1},{1,2},{2,3},{4,5},{5,6},{6,7},{8,9},{9,10},{10,11},{12,13},{... | collective-permute-start | bytes 1179656 | tf_op jit(solution)/shard_map/ppermute | solution.py:16
  78.1 2.9 %collective-permute-start.13 = (f32[4,48,512]{2,1,0:T(8,128)}, f32[4,48,512]{2,1,0:T(8,128)S(1)}, u32[]{:S(2)}, u32[]{:S(2)}) collective-permute-start(f32[4,48,512]{2,1,0:T(8,128)} %get-tuple-element.11.lo_ref.refs_1_), channel_id=1, source_target_pairs={{1,0},{2,1},{3,2},{5,4},{6,5},{7,6},{9,8},{10,9},{11,10},{13,12},{... | collective-permute-start | bytes 1179656 | tf_op jit(solution)/shard_map/ppermute | solution.py:16
  81.0 8.7 %shard_map.106 = (f32[4,8,48,512]{3,2,1,0:T(8,128)}, f32[4,48,512]{2,1,0:T(8,128)}, f32[4,48,512]{2,1,0:T(8,128)}) custom-call(f32[8]{0:T(128)} %compare_convert_fusion.north_ref.refs_0_, f32[4,8,48,512]{3,2,1,0:T(8,128)} %q_ref.1, f32[4,48,512]{2,1,0:T(8,128)} %get-tuple-element.11.lo_ref.refs_1_, f32[4,48,512]{2,1,0:T(8,128)} %get-tuple-element.12.hi_ref.refs_2_, ...), custom_call_target="tpu_custom_call" | custom-call | tf_op jit(solution)/shard_map/pallas_call | solution.py:343
  89.7 0.7 copy-done.4
  90.6 3.6 %shard_map.107 = f32[4,8,48,512]{3,2,1,0:T(8,128)} custom-call(f32[8]{0:T(128)} %compare_convert_fusion.north_ref.refs_0_, f32[4,48,512]{2,1,0:T(8,128)} %get-tuple-element.11.lo_ref.refs_1_, f32[4,48,512]{2,1,0:T(8,128)} %get-tuple-element.12.hi_ref.refs_2_, f32[4,48,512]{2,1,0:T(8,128)} %get-tuple-element.13.refs_3_, ...), custom_call_target="tpu_custom_call", output_to_operand_aliasing={{}: (12, {})} | custom-call | tf_op jit(solution)/shard_map/pallas_call | solution.py:277
  (40 shorter events, 2.4 us)
Async XLA Ops:
  0.6 6.1 %copy-start = (f32[8,8,8]{2,1,0:T(8,128)S(1)}, f32[8,8,8]{2,1,0:T(8,128)}, u32[]{:S(2)}) copy-start(f32[8,8,8]{2,1,0:T(8,128)} %param.11) | copy-start | bytes 6148
  0.6 19.1 %copy-start.8 = (s32[8,512]{1,0:T(8,128)S(1)}, s32[8,512]{1,0:T(8,128)}, u32[]{:S(2)}) copy-start(s32[8,512]{1,0:T(8,128)} %param.13) | copy-start | bytes 49156
  0.7 19.1 %copy-start.9 = (f32[4,22]{1,0:T(4,128)S(1)}, f32[4,22]{1,0:T(4,128)}, u32[]{:S(2)}) copy-start(f32[4,22]{1,0:T(4,128)} %param.14) | copy-start | bytes 1060
  1.4 7.2 %collective-permute-start = (f32[1,48,128]{2,1,0:T(8,128)S(1)}, f32[1,48,128]{2,1,0:T(8,128)S(1)}, u32[]{:S(2)}, u32[]{:S(2)}) collective-permute-start(f32[1,48,128]{2,1,0:T(8,128)S(1)} %slice.25), channel_id=1, source_target_pairs={{0,1},{1,2},{2,3},{4,5},{5,6},{6,7},{8,9},{9,10},{10,11},{12,13},{... | collective-permute-start | bytes 73736 | tf_op jit(solution)/shard_map/ppermute | solution.py:16
  8.6 0.6 copy-start.7
  11.2 16.4 %collective-permute-start.3 = (f32[25,48,128]{2,1,0:T(8,128)}, f32[25,48,128]{2,1,0:T(8,128)}, u32[]{:S(2)}, u32[]{:S(2)}) collective-permute-start(f32[25,48,128]{2,1,0:T(8,128)} %shard_map.104), channel_id=1, source_target_pairs={{0,4},{4,8},{8,12},{1,5},{5,9},{9,13},{2,6},{6,10},{10,14},{3,7},{... | collective-permute-start | bytes 1843208 | tf_op jit(solution)/shard_map/ppermute | solution.py:44
  18.3 18.6 %copy-start.6 = (f32[4,8,512]{2,1,0:T(8,128)S(1)}, f32[4,8,512]{2,1,0:T(8,128)}, u32[]{:S(2)}) copy-start(f32[4,8,512]{2,1,0:T(8,128)} %convolution_bitcast_fusion.3) | copy-start | bytes 196612
  18.3 17.3 %collective-permute-start.4 = (f32[25,48,128]{2,1,0:T(8,128)}, f32[25,48,128]{2,1,0:T(8,128)S(1)}, u32[]{:S(2)}, u32[]{:S(2)}) collective-permute-start(f32[25,48,128]{2,1,0:T(8,128)} %shard_map.104), channel_id=1, source_target_pairs={{4,0},{8,4},{12,8},{5,1},{9,5},{13,9},{6,2},{10,6},{14,10},{7,3},{... | collective-permute-start | bytes 1843208 | tf_op jit(solution)/shard_map/ppermute | solution.py:45
  20.0 10.8 %collective-permute-start.9 = (f32[4,8,512]{2,1,0:T(8,128)}, f32[4,8,512]{2,1,0:T(8,128)S(1)}, u32[]{:S(2)}, u32[]{:S(2)}) collective-permute-start(f32[4,8,512]{2,1,0:T(8,128)} %param.10), channel_id=1, source_target_pairs={{0,1},{1,2},{2,3},{3,0},{4,5},{5,6},{6,7},{7,4},{8,9},{9,10},{10,1... | collective-permute-start | bytes 196616 | tf_op jit(solution)/shard_map/ppermute | solution.py:377
  20.9 16.2 %collective-permute-start.11 = (f32[4,8,512]{2,1,0:T(8,128)}, f32[4,8,512]{2,1,0:T(8,128)S(1)}, u32[]{:S(2)}, u32[]{:S(2)}) collective-permute-start(f32[4,8,512]{2,1,0:T(8,128)} %param.10), channel_id=1, source_target_pairs={{0,3},{1,0},{2,1},{3,2},{4,7},{5,4},{6,5},{7,6},{8,11},{9,8},{10,9... | collective-permute-start | bytes 196616 | tf_op jit(solution)/shard_map/ppermute | solution.py:377
  20.9 19.3 %collective-permute-start.10 = (f32[4,8,512]{2,1,0:T(8,128)}, f32[4,8,512]{2,1,0:T(8,128)S(1)}, u32[]{:S(2)}, u32[]{:S(2)}) collective-permute-start(f32[4,8,512]{2,1,0:T(8,128)} %param.10), channel_id=1, source_target_pairs={{0,2},{1,3},{2,0},{3,1},{4,6},{5,7},{6,4},{7,5},{8,10},{9,11},{10,... | collective-permute-start | bytes 196616 | tf_op jit(solution)/shard_map/ppermute | solution.py:377
  27.5 11.9 %collective-permute-start.5 = (f32[25,48,128]{2,1,0:T(8,128)}, f32[25,48,128]{2,1,0:T(8,128)S(1)}, u32[]{:S(2)}, u32[]{:S(2)}) collective-permute-start(f32[25,48,128]{2,1,0:T(8,128)} %collective-permute-done.3), channel_id=1, source_target_pairs={{4,8},{8,12},{5,9},{9,13},{6,10},{10,14},{7,11},{11,15},{20,24},{2... | collective-permute-start | bytes 1843208 | tf_op jit(solution)/shard_map/ppermute | solution.py:44
  30.8 39.4 %collective-permute-start.1 = (f32[4,48,512]{2,1,0:T(8,128)S(1)}, f32[4,48,512]{2,1,0:T(8,128)S(1)}, u32[]{:S(2)}, u32[]{:S(2)}) collective-permute-start(f32[4,48,512]{2,1,0:T(8,128)S(1)} %get-tuple-element.17), channel_id=1, source_target_pairs={{0,1},{1,2},{2,3},{4,5},{5,6},{6,7},{8,9},{9,10},{10,11},{12,13},{... | collective-permute-start | bytes 1179656 | tf_op jit(solution)/shard_map/ppermute | solution.py:16
  35.6 18.0 %collective-permute-start.6 = (f32[25,48,128]{2,1,0:T(8,128)S(1)}, f32[25,48,128]{2,1,0:T(8,128)S(1)}, u32[]{:S(2)}, u32[]{:S(2)}) collective-permute-start(f32[25,48,128]{2,1,0:T(8,128)S(1)} %collective-permute-done.4), channel_id=1, source_target_pairs={{4,0},{8,4},{5,1},{9,5},{6,2},{10,6},{7,3},{11,7},{20,16},{24,20},... | collective-permute-start | bytes 1843208 | tf_op jit(solution)/shard_map/ppermute | solution.py:45
  37.1 33.1 %collective-permute-start.2 = (f32[4,48,512]{2,1,0:T(8,128)S(1)}, f32[4,48,512]{2,1,0:T(8,128)S(1)}, u32[]{:S(2)}, u32[]{:S(2)}) collective-permute-start(f32[4,48,512]{2,1,0:T(8,128)S(1)} %get-tuple-element.16), channel_id=1, source_target_pairs={{1,0},{2,1},{3,2},{5,4},{6,5},{7,6},{9,8},{10,9},{11,10},{13,12},{... | collective-permute-start | bytes 1179656 | tf_op jit(solution)/shard_map/ppermute | solution.py:16
  39.4 16.7 %collective-permute-start.7 = (f32[25,48,128]{2,1,0:T(8,128)S(1)}, f32[25,48,128]{2,1,0:T(8,128)S(1)}, u32[]{:S(2)}, u32[]{:S(2)}) collective-permute-start(f32[25,48,128]{2,1,0:T(8,128)S(1)} %collective-permute-done.5), channel_id=1, source_target_pairs={{8,12},{9,13},{10,14},{11,15},{24,28},{25,29},{26,30},{27,31}} | collective-permute-start | bytes 1843208 | tf_op jit(solution)/shard_map/ppermute | solution.py:44
  53.6 16.5 %collective-permute-start.8 = (f32[25,48,128]{2,1,0:T(8,128)S(1)}, f32[25,48,128]{2,1,0:T(8,128)S(1)}, u32[]{:S(2)}, u32[]{:S(2)}) collective-permute-start(f32[25,48,128]{2,1,0:T(8,128)S(1)} %collective-permute-done.6), channel_id=1, source_target_pairs={{4,0},{5,1},{6,2},{7,3},{20,16},{21,17},{22,18},{23,19}} | collective-permute-start | bytes 1843208 | tf_op jit(solution)/shard_map/ppermute | solution.py:45
  70.2 1.7 %copy-start.1 = (f32[25,48,640]{2,1,0:T(8,128)}, f32[25,48,640]{2,1,0:T(8,128)S(1)}, u32[]{:S(2)}) copy-start(f32[25,48,640]{2,1,0:T(8,128)S(1)} %constant_dynamic-update-slice_fusion.u_ref.v_ref.vm_ref.w_ref.wx_ref.refs_7_.refs_8_.refs_9_.refs_10_) | copy-start | bytes 9216004
  70.2 1.9 %copy-start.2 = (f32[4,48,512]{2,1,0:T(8,128)}, f32[4,48,512]{2,1,0:T(8,128)S(1)}, u32[]{:S(2)}) copy-start(f32[4,48,512]{2,1,0:T(8,128)S(1)} %collective-permute-done.1.qs_ref) | copy-start | bytes 1179652
  70.2 0.8 copy-start.3
  76.2 13.5 %collective-permute-start.12 = (f32[4,48,512]{2,1,0:T(8,128)}, f32[4,48,512]{2,1,0:T(8,128)S(1)}, u32[]{:S(2)}, u32[]{:S(2)}) collective-permute-start(f32[4,48,512]{2,1,0:T(8,128)} %get-tuple-element.12.hi_ref.refs_2_), channel_id=1, source_target_pairs={{0,1},{1,2},{2,3},{4,5},{5,6},{6,7},{8,9},{9,10},{10,11},{12,13},{... | collective-permute-start | bytes 1179656 | tf_op jit(solution)/shard_map/ppermute | solution.py:16
  78.1 11.6 %collective-permute-start.13 = (f32[4,48,512]{2,1,0:T(8,128)}, f32[4,48,512]{2,1,0:T(8,128)S(1)}, u32[]{:S(2)}, u32[]{:S(2)}) collective-permute-start(f32[4,48,512]{2,1,0:T(8,128)} %get-tuple-element.11.lo_ref.refs_1_), channel_id=1, source_target_pairs={{1,0},{2,1},{3,2},{5,4},{6,5},{7,6},{9,8},{10,9},{11,10},{13,12},{... | collective-permute-start | bytes 1179656 | tf_op jit(solution)/shard_map/ppermute | solution.py:16
  89.7 0.8 copy-start.4
  89.7 0.9 copy-start.5

commit v13 on v12

--- a/solution.py
+++ b/solution.py
@@ -365,37 +365,36 @@
     tiles_count = prior_tiles.shape[0]
     lat_rows = control.shape[1]
 
-    south_v = passed_along(meridional_courant[-1:], "band", 1)
-    pack = packed([zonal_courant, meridional_courant, vertical_diffusion, south_v])
-    weather = relay_gather(pack, "tracer")
-    held_state, held_control, _ = lax.optimization_barrier((tracer_state, control, pack))
-    q_south = passed_along(held_state[:, -1], "band", 1)
-    q_north = passed_along(held_state[:, 0], "band", -1)
-    shifted = [control]
-    for s in range(1, band_count):
-        pairs = [(i, (i + s) % band_count) for i in range(band_count)]
-        shifted.append(lax.ppermute(held_control, "band", pairs))
-
+    latitude = band_index * lat_rows + jnp.arange(lat_rows, dtype=jnp.int32)
+    north_open = (latitude < band_count * lat_rows - 1).astype(jnp.float32)
     choose = (
         tile_index[:, :, None] == lax.broadcasted_iota(jnp.int32, (1, 1, tiles_count), 2)
     ).astype(jnp.float32)
     own_row = lax.dynamic_slice_in_dim(choose, band_index, 1, 0)[0]
     row_tiles = jnp.einsum("bt,tmn->bmn", own_row, prior_tiles, precision=exact_dot)
-    prior_field = None
-    for s, part in enumerate(shifted):
+    own_tile = lax.dynamic_index_in_dim(row_tiles, band_index, 0, keepdims=False)
+    prior_field = jnp.einsum("jm,kmn->kjn", own_tile, control, precision=exact_dot)
+    south_v = passed_along(meridional_courant[-1:], "band", 1)
+    parts, (north_open, row_tiles, prior_field) = lax.optimization_barrier(
+        ((zonal_courant, meridional_courant, vertical_diffusion, south_v), (north_open, row_tiles, prior_field))
+    )
+    pack = packed(list(parts))
+    weather = relay_gather(pack, "tracer")
+    held_state, held_control, _ = lax.optimization_barrier((tracer_state, control, pack))
+    q_south = passed_along(held_state[:, -1], "band", 1)
+    q_north = passed_along(held_state[:, 0], "band", -1)
+    for s in range(1, band_count):
+        pairs = [(i, (i + s) % band_count) for i in range(band_count)]
+        part = lax.ppermute(held_control, "band", pairs)
         source_band = (band_index - s) % band_count
         tile = lax.dynamic_index_in_dim(row_tiles, source_band, 0, keepdims=False)
-        term = jnp.einsum("jm,kmn->kjn", tile, part, precision=exact_dot)
-        prior_field = term if prior_field is None else prior_field + term
+        prior_field = prior_field + jnp.einsum("jm,kmn->kjn", tile, part, precision=exact_dot)
     regions = region_sigma.shape[1]
     onehot = (region_map[:, :, None] == lax.broadcasted_iota(jnp.int32, (1, 1, regions), 2)).astype(
         jnp.float32
     )
     cell_sigma = jnp.einsum("kr,jnr->kjn", region_sigma, onehot, precision=exact_dot)
     emission = cell_sigma * prior_field
-
-    latitude = band_index * lat_rows + jnp.arange(lat_rows, dtype=jnp.int32)
-    north_open = (latitude < band_count * lat_rows - 1).astype(jnp.float32)
 
     rim = (tracer_state[:, 0], tracer_state[:, lat_rows - 1], tracer_state[:, 1], tracer_state[:, lat_rows - 2])
     bottom_row, top_row = edge_step(rim, None, q_south, q_north, weather, emission, north_open)

time: 95 us -> 94.3 us (level)
  waiting for transfers between devices: 35.9 us -> 33.7 us
  local copies, waits for them, and re-layouts: 11.2 us -> 12.3 us
    ppermute x3, waiting for transfers between devices: 29.4 us -> 27.9 us  [relay_gather(): lax.ppermute(left, axis, [(j, j - 1) for j in range(1, count - r + 1)])]
    dynamic_update_slice x3, local copies, waits for them, and re-layouts: 0.14 us -> 1.21 us  [relay_gather(): buf = lax.dynamic_update_slice(buf, left, (0, 0, slot * width))]
    unnamed x20 -> x22, local copies, waits for them, and re-layouts: 3.35 us -> 3.35 us
  transfers between devices with their start and end apart: 14 -> 14, of which waited for: 4 -> 4; matrix products, arithmetic and copies ran while one was open for 12% -> 14% of each run, Pallas kernels for 9% -> 9%
where the time goes in v13:
time: 94.3 us; the launch traced here: 93.5 us
  waiting for transfers between devices  33.7 us (36%)
  starting transfers between devices  23.7 us (25%)
  Pallas kernels  18.4 us (20%)
  local copies, waits for them, and re-layouts  12.3 us (13%)
  matrix products  3.94 us (4%)
  between operations  0.97 us (1%)
    ppermute x3, waiting for transfers between devices, relay_gather(): lax.ppermute(left, axis, [(j, j - 1) for j in range(1, count - r + 1)])  27.9 us
    ppermute x5, starting transfers between devices, passed_along(): return lax.ppermute(value, axis, pairs)  13.7 us
    pallas_call x1, Pallas kernels, fused_steps(): pl.pallas_call(fused_kernel, grid_spec=grid_spec, out_shape=[jax.ShapeDty...  8.67 us
    pallas_call x2, Pallas kernels, edge_step(): pl.pallas_call(kernel, grid_spec=grid_spec, out_shape=out_shape, input_ou...  7.73 us
    ppermute x3, waiting for transfers between devices, relay_gather(): lax.ppermute(right, axis, [(i, i + 1) for i in range(r - 1, count - 1)])  5.7 us
    ppermute x3, starting transfers between devices, relay_gather(): lax.ppermute(right, axis, [(i, i + 1) for i in range(r - 1, count - 1)])  5.41 us
    ppermute x3, starting transfers between devices, relay_gather(): lax.ppermute(left, axis, [(j, j - 1) for j in range(1, count - r + 1)])  3.84 us
    unnamed x22, local copies, waits for them, and re-layouts  3.35 us
  transfers between devices with their start and end apart: 14, of which 4 were waited for; matrix products, arithmetic and copies ran while one was open for 14% of the time, Pallas kernels for 9%

profile of v13, /device:TPU:1, one launch (start us, length us, event | category | flops | bytes accessed | tf_op | source)
XLA Modules:
  0.0 93.5 jit_solution(15308091233379095579)
XLA Ops:
  0.7 0.8 slice.21
  1.4 4.5 %collective-permute-start = (f32[1,48,128]{2,1,0:T(8,128)S(1)}, f32[1,48,128]{2,1,0:T(8,128)S(1)}, u32[]{:S(2)}, u32[]{:S(2)}) collective-permute-start(f32[1,48,128]{2,1,0:T(8,128)S(1)} %slice.21), channel_id=1, source_target_pairs={{0,1},{1,2},{2,3},{4,5},{5,6},{6,7},{8,9},{9,10},{10,11},{12,13},{... | collective-permute-start | bytes 73736 | tf_op jit(solution)/shard_map/ppermute | solution.py:16
  5.9 0.7 constant_dynamic-slice_fusion.4
  6.8 1.7 %convolution_bitcast_fusion.3 = f32[4,8,512]{2,1,0:T(8,128)} fusion(f32[8,8,1]{1,0,2:T(8,128)S(1)} %bitcast.56, f32[4,8,512]{2,1,0:T(8,128)} %param.10), kind=kOutput, calls=%fused_computation.3 | convolution fusion | flops 1572864 | bytes 131328 | tf_op jit(solution)/shard_map/jm,kmn->kjn/dot_general | solution.py:376
  9.7 2.0 %shard_map.104 = f32[25,48,128]{2,1,0:T(8,128)} custom-call(f32[8,48,128]{2,1,0:T(8,128)} %refs_0_, f32[8,48,128]{2,1,0:T(8,128)} %refs_1_, f32[8,48,128]{2,1,0:T(8,128)} %refs_2_, f32[1,48,128]{2,1,0:T(8,128)} %copy-done.8), custom_call_target="tpu_custom_call" | custom-call | tf_op jit(solution)/shard_map/pallas_call | solution.py:30
  11.7 4.0 %collective-permute-start.3 = (f32[25,48,128]{2,1,0:T(8,128)}, f32[25,48,128]{2,1,0:T(8,128)}, u32[]{:S(2)}, u32[]{:S(2)}) collective-permute-start(f32[25,48,128]{2,1,0:T(8,128)} %shard_map.104), channel_id=1, source_target_pairs={{0,4},{4,8},{8,12},{1,5},{5,9},{9,13},{2,6},{6,10},{10,14},{3,7},{... | collective-permute-start | bytes 1843208 | tf_op jit(solution)/shard_map/ppermute | solution.py:44
  15.7 2.5 %slice_bitcast_fusion.2 = (f32[4,48,512]{2,1,0:T(8,128)}, f32[4,48,512]{2,1,0:T(8,128)}, f32[4,48,512]{2,1,0:T(8,128)}, f32[4,48,512]{2,1,0:T(8,128)}) fusion(f32[4,8,48,512]{3,2,1,0:T(8,128)} %q_ref.1), kind=kLoop, calls=%fused_computation.7 | loop fusion | bytes 3145728 | tf_op jit(solution)/shard_map/squeeze | solution.py:399
  18.2 1.3 %collective-permute-start.4 = (f32[25,48,128]{2,1,0:T(8,128)}, f32[25,48,128]{2,1,0:T(8,128)}, u32[]{:S(2)}, u32[]{:S(2)}) collective-permute-start(f32[25,48,128]{2,1,0:T(8,128)} %shard_map.104), channel_id=1, source_target_pairs={{4,0},{8,4},{12,8},{5,1},{9,5},{13,9},{6,2},{10,6},{14,10},{7,3},{... | collective-permute-start | bytes 1843208 | tf_op jit(solution)/shard_map/ppermute | solution.py:45
  19.5 0.9 fusion
  21.2 1.2 %slice_bitcast_fusion = (f32[4,48,512]{2,1,0:T(8,128)S(1)}, f32[4,48,512]{2,1,0:T(8,128)S(1)}) fusion(f32[4,8,48,512]{3,2,1,0:T(8,128)} %q_ref.1), kind=kLoop, calls=%fused_computation.4 | loop fusion | bytes 1572864 | tf_op jit(solution)/shard_map/squeeze | solution.py:385
  22.3 5.7 %collective-permute-done.3 = f32[25,48,128]{2,1,0:T(8,128)} collective-permute-done((f32[25,48,128]{2,1,0:T(8,128)}, f32[25,48,128]{2,1,0:T(8,128)}, u32[]{:S(2)}, u32[]{:S(2)}) %collective-permute-start.3) | collective-permute-done | bytes 614432 | tf_op jit(solution)/shard_map/ppermute | solution.py:44
  28.0 0.7 collective-permute-start.5
  28.9 1.1 %constant_dynamic-update-slice_fusion.6 = f32[25,48,640]{2,1,0:T(8,128)S(1)} fusion(f32[25,48,640]{2,1,0:T(8,128)S(1)} %broadcast_in_dim.2, f32[25,48,128]{2,1,0:T(8,128)} %shard_map.104, s32[]{:T(128)S(6)} %select_n.70), kind=kLoop, calls=%fused_computation.25 | loop fusion | bytes 1228804 | tf_op jit(solution)/shard_map/dynamic_update_slice | solution.py:41
  30.1 1.9 %collective-permute-start.1 = (f32[4,48,512]{2,1,0:T(8,128)S(1)}, f32[4,48,512]{2,1,0:T(8,128)S(1)}, u32[]{:S(2)}, u32[]{:S(2)}) collective-permute-start(f32[4,48,512]{2,1,0:T(8,128)S(1)} %get-tuple-element.31), channel_id=1, source_target_pairs={{0,1},{1,2},{2,3},{4,5},{5,6},{6,7},{8,9},{9,10},{10,11},{12,13},{... | collective-permute-start | bytes 1179656 | tf_op jit(solution)/shard_map/ppermute | solution.py:16
  32.0 3.4 %collective-permute-done.4 = f32[25,48,128]{2,1,0:T(8,128)} collective-permute-done((f32[25,48,128]{2,1,0:T(8,128)}, f32[25,48,128]{2,1,0:T(8,128)}, u32[]{:S(2)}, u32[]{:S(2)}) %collective-permute-start.4) | collective-permute-done | bytes 614432 | tf_op jit(solution)/shard_map/ppermute | solution.py:45
  35.5 1.3 %collective-permute-start.6 = (f32[25,48,128]{2,1,0:T(8,128)}, f32[25,48,128]{2,1,0:T(8,128)S(1)}, u32[]{:S(2)}, u32[]{:S(2)}) collective-permute-start(f32[25,48,128]{2,1,0:T(8,128)} %collective-permute-done.4), channel_id=1, source_target_pairs={{4,0},{8,4},{5,1},{9,5},{6,2},{10,6},{7,3},{11,7},{20,16},{24,20},... | collective-permute-start | bytes 1843208 | tf_op jit(solution)/shard_map/ppermute | solution.py:45
  37.0 2.1 %collective-permute-start.2 = (f32[4,48,512]{2,1,0:T(8,128)S(1)}, f32[4,48,512]{2,1,0:T(8,128)S(1)}, u32[]{:S(2)}, u32[]{:S(2)}) collective-permute-start(f32[4,48,512]{2,1,0:T(8,128)S(1)} %get-tuple-element.30), channel_id=1, source_target_pairs={{1,0},{2,1},{3,2},{5,4},{6,5},{7,6},{9,8},{10,9},{11,10},{13,12},{... | collective-permute-start | bytes 1179656 | tf_op jit(solution)/shard_map/ppermute | solution.py:16
  39.3 0.7 collective-permute-start.7
  40.1 0.8 bitcast_multiply_fusion.src_ref.refs_11_
  40.9 12.0 %collective-permute-done.6 = f32[25,48,128]{2,1,0:T(8,128)S(1)} collective-permute-done((f32[25,48,128]{2,1,0:T(8,128)}, f32[25,48,128]{2,1,0:T(8,128)S(1)}, u32[]{:S(2)}, u32[]{:S(2)}) %collective-permute-start.6) | collective-permute-done | bytes 614432 | tf_op jit(solution)/shard_map/ppermute | solution.py:45
  52.9 1.3 %collective-permute-start.8 = (f32[25,48,128]{2,1,0:T(8,128)S(1)}, f32[25,48,128]{2,1,0:T(8,128)S(1)}, u32[]{:S(2)}, u32[]{:S(2)}) collective-permute-start(f32[25,48,128]{2,1,0:T(8,128)S(1)} %collective-permute-done.6), channel_id=1, source_target_pairs={{4,0},{5,1},{6,2},{7,3},{20,16},{21,17},{22,18},{23,19}} | collective-permute-start | bytes 1843208 | tf_op jit(solution)/shard_map/ppermute | solution.py:45
  54.2 1.1 %constant_dynamic-update-slice_fusion.5 = f32[25,48,640]{2,1,0:T(8,128)S(1)} fusion(f32[25,48,640]{2,1,0:T(8,128)S(1)} %constant_dynamic-update-slice_fusion.6, f32[25,48,128]{2,1,0:T(8,128)} %collective-permute-done.3, s32[]{:T(128)S(6)} %select_n.72), kind=kLoop, calls=%fused_computation.24 | loop fusion | bytes 1228804 | tf_op jit(solution)/shard_map/dynamic_update_slice | solution.py:47
  55.3 1.1 %constant_dynamic-update-slice_fusion.4 = f32[25,48,640]{2,1,0:T(8,128)S(1)} fusion(f32[25,48,640]{2,1,0:T(8,128)S(1)} %constant_dynamic-update-slice_fusion.5, f32[25,48,128]{2,1,0:T(8,128)} %collective-permute-done.4, s32[]{:T(128)S(6)} %select_n.74), kind=kLoop, calls=%fused_computation.23 | loop fusion | bytes 1228804 | tf_op jit(solution)/shard_map/dynamic_update_slice | solution.py:49
  56.6 12.5 %collective-permute-done.8 = f32[25,48,128]{2,1,0:T(8,128)S(1)} collective-permute-done((f32[25,48,128]{2,1,0:T(8,128)S(1)}, f32[25,48,128]{2,1,0:T(8,128)S(1)}, u32[]{:S(2)}, u32[]{:S(2)}) %collective-permute-start.8) | collective-permute-done | bytes 614432 | tf_op jit(solution)/shard_map/ppermute | solution.py:45
  69.2 0.8 copy-done.3
  70.0 0.9 copy-done.1
  71.0 4.1 %shard_map.105 = (f32[4,48,512]{2,1,0:T(8,128)}, f32[4,48,512]{2,1,0:T(8,128)}) custom-call(f32[8]{0:T(128)} %compare_convert_fusion.north_ref.refs_0_, f32[4,48,512]{2,1,0:T(8,128)} %get-tuple-element.35.lo_ref, f32[4,48,512]{2,1,0:T(8,128)} %get-tuple-element.34.hi_ref, f32[4,48,512]{2,1,0:T(8,128)} %get-tuple-element.33.lo_in_ref, ...), custom_call_target="tpu_custom_call" | custom-call | tf_op jit(solution)/shard_map/pallas_call | solution.py:277
  75.2 1.9 %collective-permute-start.12 = (f32[4,48,512]{2,1,0:T(8,128)}, f32[4,48,512]{2,1,0:T(8,128)S(1)}, u32[]{:S(2)}, u32[]{:S(2)}) collective-permute-start(f32[4,48,512]{2,1,0:T(8,128)} %get-tuple-element.26.hi_ref.refs_2_), channel_id=1, source_target_pairs={{0,1},{1,2},{2,3},{4,5},{5,6},{6,7},{8,9},{9,10},{10,11},{12,13},{... | collective-permute-start | bytes 1179656 | tf_op jit(solution)/shard_map/ppermute | solution.py:16
  77.1 3.2 %collective-permute-start.13 = (f32[4,48,512]{2,1,0:T(8,128)}, f32[4,48,512]{2,1,0:T(8,128)S(1)}, u32[]{:S(2)}, u32[]{:S(2)}) collective-permute-start(f32[4,48,512]{2,1,0:T(8,128)} %get-tuple-element.25.lo_ref.refs_1_), channel_id=1, source_target_pairs={{1,0},{2,1},{3,2},{5,4},{6,5},{7,6},{9,8},{10,9},{11,10},{13,12},{... | collective-permute-start | bytes 1179656 | tf_op jit(solution)/shard_map/ppermute | solution.py:16
  80.3 8.7 %shard_map.106 = (f32[4,8,48,512]{3,2,1,0:T(8,128)}, f32[4,48,512]{2,1,0:T(8,128)}, f32[4,48,512]{2,1,0:T(8,128)}) custom-call(f32[8]{0:T(128)} %compare_convert_fusion.north_ref.refs_0_, f32[4,8,48,512]{3,2,1,0:T(8,128)} %q_ref.1, f32[4,48,512]{2,1,0:T(8,128)} %get-tuple-element.25.lo_ref.refs_1_, f32[4,48,512]{2,1,0:T(8,128)} %get-tuple-element.26.hi_ref.refs_2_, ...), custom_call_target="tpu_custom_call" | custom-call | tf_op jit(solution)/shard_map/pallas_call | solution.py:343
  89.0 0.7 copy-done.4
  89.9 3.6 %shard_map.107 = f32[4,8,48,512]{3,2,1,0:T(8,128)} custom-call(f32[8]{0:T(128)} %compare_convert_fusion.north_ref.refs_0_, f32[4,48,512]{2,1,0:T(8,128)} %get-tuple-element.25.lo_ref.refs_1_, f32[4,48,512]{2,1,0:T(8,128)} %get-tuple-element.26.hi_ref.refs_2_, f32[4,48,512]{2,1,0:T(8,128)} %get-tuple-element.27.refs_3_, ...), custom_call_target="tpu_custom_call", output_to_operand_aliasing={{}: (12, {})} | custom-call | tf_op jit(solution)/shard_map/pallas_call | solution.py:277
  (43 shorter events, 3.3 us)
Async XLA Ops:
  0.6 6.0 %copy-start = (f32[8,8,8]{2,1,0:T(8,128)S(1)}, f32[8,8,8]{2,1,0:T(8,128)}, u32[]{:S(2)}) copy-start(f32[8,8,8]{2,1,0:T(8,128)} %param.11) | copy-start | bytes 6148
  0.6 18.9 %copy-start.9 = (s32[8,512]{1,0:T(8,128)S(1)}, s32[8,512]{1,0:T(8,128)}, u32[]{:S(2)}) copy-start(s32[8,512]{1,0:T(8,128)} %param.13) | copy-start | bytes 49156
  0.7 18.9 %copy-start.10 = (f32[4,22]{1,0:T(4,128)S(1)}, f32[4,22]{1,0:T(4,128)}, u32[]{:S(2)}) copy-start(f32[4,22]{1,0:T(4,128)} %param.14) | copy-start | bytes 1060
  1.4 7.7 %collective-permute-start = (f32[1,48,128]{2,1,0:T(8,128)S(1)}, f32[1,48,128]{2,1,0:T(8,128)S(1)}, u32[]{:S(2)}, u32[]{:S(2)}) collective-permute-start(f32[1,48,128]{2,1,0:T(8,128)S(1)} %slice.21), channel_id=1, source_target_pairs={{0,1},{1,2},{2,3},{4,5},{5,6},{6,7},{8,9},{9,10},{10,11},{12,13},{... | collective-permute-start | bytes 73736 | tf_op jit(solution)/shard_map/ppermute | solution.py:16
  9.1 0.6 copy-start.8
  11.7 16.4 %collective-permute-start.3 = (f32[25,48,128]{2,1,0:T(8,128)}, f32[25,48,128]{2,1,0:T(8,128)}, u32[]{:S(2)}, u32[]{:S(2)}) collective-permute-start(f32[25,48,128]{2,1,0:T(8,128)} %shard_map.104), channel_id=1, source_target_pairs={{0,4},{4,8},{8,12},{1,5},{5,9},{9,13},{2,6},{6,10},{10,14},{3,7},{... | collective-permute-start | bytes 1843208 | tf_op jit(solution)/shard_map/ppermute | solution.py:44
  18.2 17.3 %collective-permute-start.4 = (f32[25,48,128]{2,1,0:T(8,128)}, f32[25,48,128]{2,1,0:T(8,128)}, u32[]{:S(2)}, u32[]{:S(2)}) collective-permute-start(f32[25,48,128]{2,1,0:T(8,128)} %shard_map.104), channel_id=1, source_target_pairs={{4,0},{8,4},{12,8},{5,1},{9,5},{13,9},{6,2},{10,6},{14,10},{7,3},{... | collective-permute-start | bytes 1843208 | tf_op jit(solution)/shard_map/ppermute | solution.py:45
  20.4 19.6 %copy-start.6 = (f32[4,8,512]{2,1,0:T(8,128)S(1)}, f32[4,8,512]{2,1,0:T(8,128)}, u32[]{:S(2)}) copy-start(f32[4,8,512]{2,1,0:T(8,128)} %convolution_bitcast_fusion.3) | copy-start | bytes 196612
  20.4 19.6 %copy-start.7 = (f32[8,512,4]{1,2,0:T(4,128)S(1)}, f32[8,512,4]{1,2,0:T(4,128)}, u32[]{:S(2)}) copy-start(f32[8,512,4]{1,2,0:T(4,128)} %fusion) | copy-start | bytes 196612
  20.4 9.7 %collective-permute-start.10 = (f32[4,8,512]{2,1,0:T(8,128)}, f32[4,8,512]{2,1,0:T(8,128)S(1)}, u32[]{:S(2)}, u32[]{:S(2)}) collective-permute-start(f32[4,8,512]{2,1,0:T(8,128)} %param.10), channel_id=1, source_target_pairs={{0,2},{1,3},{2,0},{3,1},{4,6},{5,7},{6,4},{7,5},{8,10},{9,11},{10,... | collective-permute-start | bytes 196616 | tf_op jit(solution)/shard_map/ppermute | solution.py:388
  20.4 16.5 %collective-permute-start.9 = (f32[4,8,512]{2,1,0:T(8,128)}, f32[4,8,512]{2,1,0:T(8,128)S(1)}, u32[]{:S(2)}, u32[]{:S(2)}) collective-permute-start(f32[4,8,512]{2,1,0:T(8,128)} %param.10), channel_id=1, source_target_pairs={{0,1},{1,2},{2,3},{3,0},{4,5},{5,6},{6,7},{7,4},{8,9},{9,10},{10,1... | collective-permute-start | bytes 196616 | tf_op jit(solution)/shard_map/ppermute | solution.py:388
  21.1 19.0 %collective-permute-start.11 = (f32[4,8,512]{2,1,0:T(8,128)}, f32[4,8,512]{2,1,0:T(8,128)S(1)}, u32[]{:S(2)}, u32[]{:S(2)}) collective-permute-start(f32[4,8,512]{2,1,0:T(8,128)} %param.10), channel_id=1, source_target_pairs={{0,3},{1,0},{2,1},{3,2},{4,7},{5,4},{6,5},{7,6},{8,11},{9,8},{10,9... | collective-permute-start | bytes 196616 | tf_op jit(solution)/shard_map/ppermute | solution.py:388
  28.0 11.3 %collective-permute-start.5 = (f32[25,48,128]{2,1,0:T(8,128)}, f32[25,48,128]{2,1,0:T(8,128)S(1)}, u32[]{:S(2)}, u32[]{:S(2)}) collective-permute-start(f32[25,48,128]{2,1,0:T(8,128)} %collective-permute-done.3), channel_id=1, source_target_pairs={{4,8},{8,12},{5,9},{9,13},{6,10},{10,14},{7,11},{11,15},{20,24},{2... | collective-permute-start | bytes 1843208 | tf_op jit(solution)/shard_map/ppermute | solution.py:44
  30.1 39.1 %collective-permute-start.1 = (f32[4,48,512]{2,1,0:T(8,128)S(1)}, f32[4,48,512]{2,1,0:T(8,128)S(1)}, u32[]{:S(2)}, u32[]{:S(2)}) collective-permute-start(f32[4,48,512]{2,1,0:T(8,128)S(1)} %get-tuple-element.31), channel_id=1, source_target_pairs={{0,1},{1,2},{2,3},{4,5},{5,6},{6,7},{8,9},{9,10},{10,11},{12,13},{... | collective-permute-start | bytes 1179656 | tf_op jit(solution)/shard_map/ppermute | solution.py:16
  35.5 17.4 %collective-permute-start.6 = (f32[25,48,128]{2,1,0:T(8,128)}, f32[25,48,128]{2,1,0:T(8,128)S(1)}, u32[]{:S(2)}, u32[]{:S(2)}) collective-permute-start(f32[25,48,128]{2,1,0:T(8,128)} %collective-permute-done.4), channel_id=1, source_target_pairs={{4,0},{8,4},{5,1},{9,5},{6,2},{10,6},{7,3},{11,7},{20,16},{24,20},... | collective-permute-start | bytes 1843208 | tf_op jit(solution)/shard_map/ppermute | solution.py:45
  37.0 32.2 %collective-permute-start.2 = (f32[4,48,512]{2,1,0:T(8,128)S(1)}, f32[4,48,512]{2,1,0:T(8,128)S(1)}, u32[]{:S(2)}, u32[]{:S(2)}) collective-permute-start(f32[4,48,512]{2,1,0:T(8,128)S(1)} %get-tuple-element.30), channel_id=1, source_target_pairs={{1,0},{2,1},{3,2},{5,4},{6,5},{7,6},{9,8},{10,9},{11,10},{13,12},{... | collective-permute-start | bytes 1179656 | tf_op jit(solution)/shard_map/ppermute | solution.py:16
  39.3 17.2 %collective-permute-start.7 = (f32[25,48,128]{2,1,0:T(8,128)S(1)}, f32[25,48,128]{2,1,0:T(8,128)S(1)}, u32[]{:S(2)}, u32[]{:S(2)}) collective-permute-start(f32[25,48,128]{2,1,0:T(8,128)S(1)} %collective-permute-done.5), channel_id=1, source_target_pairs={{8,12},{9,13},{10,14},{11,15},{24,28},{25,29},{26,30},{27,31}} | collective-permute-start | bytes 1843208 | tf_op jit(solution)/shard_map/ppermute | solution.py:44
  52.9 16.2 %collective-permute-start.8 = (f32[25,48,128]{2,1,0:T(8,128)S(1)}, f32[25,48,128]{2,1,0:T(8,128)S(1)}, u32[]{:S(2)}, u32[]{:S(2)}) collective-permute-start(f32[25,48,128]{2,1,0:T(8,128)S(1)} %collective-permute-done.6), channel_id=1, source_target_pairs={{4,0},{5,1},{6,2},{7,3},{20,16},{21,17},{22,18},{23,19}} | collective-permute-start | bytes 1843208 | tf_op jit(solution)/shard_map/ppermute | solution.py:45
  69.1 1.7 %copy-start.1 = (f32[25,48,640]{2,1,0:T(8,128)}, f32[25,48,640]{2,1,0:T(8,128)S(1)}, u32[]{:S(2)}) copy-start(f32[25,48,640]{2,1,0:T(8,128)S(1)} %constant_dynamic-update-slice_fusion.u_ref.v_ref.vm_ref.w_ref.wx_ref.refs_7_.refs_8_.refs_9_.refs_10_) | copy-start | bytes 9216004
  69.2 1.9 %copy-start.2 = (f32[4,48,512]{2,1,0:T(8,128)}, f32[4,48,512]{2,1,0:T(8,128)S(1)}, u32[]{:S(2)}) copy-start(f32[4,48,512]{2,1,0:T(8,128)S(1)} %collective-permute-done.1.qs_ref) | copy-start | bytes 1179652
  69.2 0.8 copy-start.3
  75.2 13.8 %collective-permute-start.12 = (f32[4,48,512]{2,1,0:T(8,128)}, f32[4,48,512]{2,1,0:T(8,128)S(1)}, u32[]{:S(2)}, u32[]{:S(2)}) collective-permute-start(f32[4,48,512]{2,1,0:T(8,128)} %get-tuple-element.26.hi_ref.refs_2_), channel_id=1, source_target_pairs={{0,1},{1,2},{2,3},{4,5},{5,6},{6,7},{8,9},{9,10},{10,11},{12,13},{... | collective-permute-start | bytes 1179656 | tf_op jit(solution)/shard_map/ppermute | solution.py:16
  77.1 11.9 %collective-permute-start.13 = (f32[4,48,512]{2,1,0:T(8,128)}, f32[4,48,512]{2,1,0:T(8,128)S(1)}, u32[]{:S(2)}, u32[]{:S(2)}) collective-permute-start(f32[4,48,512]{2,1,0:T(8,128)} %get-tuple-element.25.lo_ref.refs_1_), channel_id=1, source_target_pairs={{1,0},{2,1},{3,2},{5,4},{6,5},{7,6},{9,8},{10,9},{11,10},{13,12},{... | collective-permute-start | bytes 1179656 | tf_op jit(solution)/shard_map/ppermute | solution.py:16
  89.0 0.8 copy-start.4
  89.0 0.9 copy-start.5

commit v14 on v13

--- a/solution.py
+++ b/solution.py
@@ -375,8 +375,9 @@
     own_tile = lax.dynamic_index_in_dim(row_tiles, band_index, 0, keepdims=False)
     prior_field = jnp.einsum("jm,kmn->kjn", own_tile, control, precision=exact_dot)
     south_v = passed_along(meridional_courant[-1:], "band", 1)
-    parts, (north_open, row_tiles, prior_field) = lax.optimization_barrier(
-        ((zonal_courant, meridional_courant, vertical_diffusion, south_v), (north_open, row_tiles, prior_field))
+    rim = (tracer_state[:, 0], tracer_state[:, lat_rows - 1], tracer_state[:, 1], tracer_state[:, lat_rows - 2])
+    parts, (north_open, row_tiles, prior_field, rim) = lax.optimization_barrier(
+        ((zonal_courant, meridional_courant, vertical_diffusion, south_v), (north_open, row_tiles, prior_field, rim))
     )
     pack = packed(list(parts))
     weather = relay_gather(pack, "tracer")
@@ -396,7 +397,6 @@
     cell_sigma = jnp.einsum("kr,jnr->kjn", region_sigma, onehot, precision=exact_dot)
     emission = cell_sigma * prior_field
 
-    rim = (tracer_state[:, 0], tracer_state[:, lat_rows - 1], tracer_state[:, 1], tracer_state[:, lat_rows - 2])
     bottom_row, top_row = edge_step(rim, None, q_south, q_north, weather, emission, north_open)
     s1_south = passed_along(top_row, "band", 1)
     s1_north = passed_along(bottom_row, "band", -1)

time: 94.3 us -> 95.8 us (1.016)
  waiting for transfers between devices: 33.7 us -> 36.6 us
  local copies, waits for them, and re-layouts: 12.3 us -> 11.1 us
    ppermute x3, waiting for transfers between devices: 5.7 us -> 8.29 us  [relay_gather(): lax.ppermute(right, axis, [(i, i + 1) for i in range(r - 1, count - 1)])]
    dynamic_update_slice x1, local copies, waits for them, and re-layouts: 1.12 us -> 0.05 us  [relay_gather(): buf = lax.dynamic_update_slice(buf, x, (0, 0, me * width))]
  transfers between devices with their start and end apart: 14 -> 14, of which waited for: 4 -> 4; matrix products, arithmetic and copies ran while one was open for 14% -> 12% of each run, Pallas kernels for 9% -> 9%
where the time goes in v14:
time: 95.8 us; the launch traced here: 95 us
  waiting for transfers between devices  36.6 us (38%)
  starting transfers between devices  23.4 us (24%)
  Pallas kernels  18.4 us (19%)
  local copies, waits for them, and re-layouts  11.1 us (12%)
  matrix products  3.93 us (4%)
  between operations  0.98 us (1%)
    ppermute x3, waiting for transfers between devices, relay_gather(): lax.ppermute(left, axis, [(j, j - 1) for j in range(1, count - r + 1)])  28.3 us
    ppermute x5, starting transfers between devices, passed_along(): return lax.ppermute(value, axis, pairs)  13.5 us
    pallas_call x1, Pallas kernels, fused_steps(): pl.pallas_call(fused_kernel, grid_spec=grid_spec, out_shape=[jax.ShapeDty...  8.67 us
    ppermute x3, waiting for transfers between devices, relay_gather(): lax.ppermute(right, axis, [(i, i + 1) for i in range(r - 1, count - 1)])  8.29 us
    pallas_call x2, Pallas kernels, edge_step(): pl.pallas_call(kernel, grid_spec=grid_spec, out_shape=out_shape, input_ou...  7.74 us
    ppermute x3, starting transfers between devices, relay_gather(): lax.ppermute(right, axis, [(i, i + 1) for i in range(r - 1, count - 1)])  5.41 us
    ppermute x3, starting transfers between devices, relay_gather(): lax.ppermute(left, axis, [(j, j - 1) for j in range(1, count - r + 1)])  3.84 us
    unnamed x22, local copies, waits for them, and re-layouts  3.21 us
  transfers between devices with their start and end apart: 14, of which 4 were waited for; matrix products, arithmetic and copies ran while one was open for 12% of the time, Pallas kernels for 9%

profile of v14, /device:TPU:1, one launch (start us, length us, event | category | flops | bytes accessed | tf_op | source)
XLA Modules:
  0.0 95.0 jit_solution(637258046315839661)
XLA Ops:
  0.7 0.8 slice.21
  1.4 4.5 %collective-permute-start = (f32[1,48,128]{2,1,0:T(8,128)S(1)}, f32[1,48,128]{2,1,0:T(8,128)S(1)}, u32[]{:S(2)}, u32[]{:S(2)}) collective-permute-start(f32[1,48,128]{2,1,0:T(8,128)S(1)} %slice.21), channel_id=1, source_target_pairs={{0,1},{1,2},{2,3},{4,5},{5,6},{6,7},{8,9},{9,10},{10,11},{12,13},{... | collective-permute-start | bytes 73736 | tf_op jit(solution)/shard_map/ppermute | solution.py:16
  5.9 0.7 constant_dynamic-slice_fusion.4
  6.8 2.6 %slice_bitcast_fusion.2 = (f32[4,48,512]{2,1,0:T(8,128)}, f32[4,48,512]{2,1,0:T(8,128)}, f32[4,48,512]{2,1,0:T(8,128)}, f32[4,48,512]{2,1,0:T(8,128)}) fusion(f32[4,8,48,512]{3,2,1,0:T(8,128)} %q_ref.1), kind=kLoop, calls=%fused_computation.7 | loop fusion | bytes 3145728 | tf_op jit(solution)/shard_map/squeeze | solution.py:378
  9.4 1.6 %convolution_bitcast_fusion.3 = f32[4,8,512]{2,1,0:T(8,128)} fusion(f32[8,8,1]{1,0,2:T(8,128)S(1)} %bitcast.56, f32[4,8,512]{2,1,0:T(8,128)} %param.10), kind=kOutput, calls=%fused_computation.3 | convolution fusion | flops 1572864 | bytes 131328 | tf_op jit(solution)/shard_map/jm,kmn->kjn/dot_general | solution.py:376
  11.6 0.6 copy-done.8
  12.2 2.0 %shard_map.104 = f32[25,48,128]{2,1,0:T(8,128)} custom-call(f32[8,48,128]{2,1,0:T(8,128)} %refs_0_, f32[8,48,128]{2,1,0:T(8,128)} %refs_1_, f32[8,48,128]{2,1,0:T(8,128)} %refs_2_, f32[1,48,128]{2,1,0:T(8,128)} %copy-done.8), custom_call_target="tpu_custom_call" | custom-call | tf_op jit(solution)/shard_map/pallas_call | solution.py:30
  14.2 4.0 %collective-permute-start.3 = (f32[25,48,128]{2,1,0:T(8,128)}, f32[25,48,128]{2,1,0:T(8,128)}, u32[]{:S(2)}, u32[]{:S(2)}) collective-permute-start(f32[25,48,128]{2,1,0:T(8,128)} %shard_map.104), channel_id=1, source_target_pairs={{0,4},{4,8},{8,12},{1,5},{5,9},{9,13},{2,6},{6,10},{10,14},{3,7},{... | collective-permute-start | bytes 1843208 | tf_op jit(solution)/shard_map/ppermute | solution.py:44
  18.2 1.3 %collective-permute-start.4 = (f32[25,48,128]{2,1,0:T(8,128)}, f32[25,48,128]{2,1,0:T(8,128)}, u32[]{:S(2)}, u32[]{:S(2)}) collective-permute-start(f32[25,48,128]{2,1,0:T(8,128)} %shard_map.104), channel_id=1, source_target_pairs={{4,0},{8,4},{12,8},{5,1},{9,5},{13,9},{6,2},{10,6},{14,10},{7,3},{... | collective-permute-start | bytes 1843208 | tf_op jit(solution)/shard_map/ppermute | solution.py:45
  19.6 0.9 fusion
  20.5 0.6 collective-permute-start.9
  21.1 1.2 %slice_bitcast_fusion = (f32[4,48,512]{2,1,0:T(8,128)S(1)}, f32[4,48,512]{2,1,0:T(8,128)S(1)}) fusion(f32[4,8,48,512]{3,2,1,0:T(8,128)} %q_ref.1), kind=kLoop, calls=%fused_computation.4 | loop fusion | bytes 1572864 | tf_op jit(solution)/shard_map/squeeze | solution.py:386
  22.3 8.3 %collective-permute-done.3 = f32[25,48,128]{2,1,0:T(8,128)} collective-permute-done((f32[25,48,128]{2,1,0:T(8,128)}, f32[25,48,128]{2,1,0:T(8,128)}, u32[]{:S(2)}, u32[]{:S(2)}) %collective-permute-start.3) | collective-permute-done | bytes 614432 | tf_op jit(solution)/shard_map/ppermute | solution.py:44
  30.6 0.7 collective-permute-start.5
  31.6 1.9 %collective-permute-start.1 = (f32[4,48,512]{2,1,0:T(8,128)S(1)}, f32[4,48,512]{2,1,0:T(8,128)S(1)}, u32[]{:S(2)}, u32[]{:S(2)}) collective-permute-start(f32[4,48,512]{2,1,0:T(8,128)S(1)} %get-tuple-element.39), channel_id=1, source_target_pairs={{0,1},{1,2},{2,3},{4,5},{5,6},{6,7},{8,9},{9,10},{10,11},{12,13},{... | collective-permute-start | bytes 1179656 | tf_op jit(solution)/shard_map/ppermute | solution.py:16
  33.5 2.0 %collective-permute-done.4 = f32[25,48,128]{2,1,0:T(8,128)} collective-permute-done((f32[25,48,128]{2,1,0:T(8,128)}, f32[25,48,128]{2,1,0:T(8,128)}, u32[]{:S(2)}, u32[]{:S(2)}) %collective-permute-start.4) | collective-permute-done | bytes 614432 | tf_op jit(solution)/shard_map/ppermute | solution.py:45
  35.5 1.3 %collective-permute-start.6 = (f32[25,48,128]{2,1,0:T(8,128)}, f32[25,48,128]{2,1,0:T(8,128)S(1)}, u32[]{:S(2)}, u32[]{:S(2)}) collective-permute-start(f32[25,48,128]{2,1,0:T(8,128)} %collective-permute-done.4), channel_id=1, source_target_pairs={{4,0},{8,4},{5,1},{9,5},{6,2},{10,6},{7,3},{11,7},{20,16},{24,20},... | collective-permute-start | bytes 1843208 | tf_op jit(solution)/shard_map/ppermute | solution.py:45
  37.0 2.1 %collective-permute-start.2 = (f32[4,48,512]{2,1,0:T(8,128)S(1)}, f32[4,48,512]{2,1,0:T(8,128)}, u32[]{:S(2)}, u32[]{:S(2)}) collective-permute-start(f32[4,48,512]{2,1,0:T(8,128)S(1)} %get-tuple-element.38), channel_id=1, source_target_pairs={{1,0},{2,1},{3,2},{5,4},{6,5},{7,6},{9,8},{10,9},{11,10},{13,12},{... | collective-permute-start | bytes 1179656 | tf_op jit(solution)/shard_map/ppermute | solution.py:16
  39.4 0.7 collective-permute-start.7
  40.1 0.8 bitcast_multiply_fusion.src_ref.refs_11_
  40.9 13.6 %collective-permute-done.6 = f32[25,48,128]{2,1,0:T(8,128)S(1)} collective-permute-done((f32[25,48,128]{2,1,0:T(8,128)}, f32[25,48,128]{2,1,0:T(8,128)S(1)}, u32[]{:S(2)}, u32[]{:S(2)}) %collective-permute-start.6) | collective-permute-done | bytes 614432 | tf_op jit(solution)/shard_map/ppermute | solution.py:45
  54.5 1.3 %collective-permute-start.8 = (f32[25,48,128]{2,1,0:T(8,128)S(1)}, f32[25,48,128]{2,1,0:T(8,128)S(1)}, u32[]{:S(2)}, u32[]{:S(2)}) collective-permute-start(f32[25,48,128]{2,1,0:T(8,128)S(1)} %collective-permute-done.6), channel_id=1, source_target_pairs={{4,0},{5,1},{6,2},{7,3},{20,16},{21,17},{22,18},{23,19}} | collective-permute-start | bytes 1843208 | tf_op jit(solution)/shard_map/ppermute | solution.py:45
  55.8 1.1 %constant_dynamic-update-slice_fusion.5 = f32[25,48,640]{2,1,0:T(8,128)S(1)} fusion(f32[25,48,640]{2,1,0:T(8,128)S(1)} %constant_dynamic-update-slice_fusion.6, f32[25,48,128]{2,1,0:T(8,128)} %collective-permute-done.3, s32[]{:T(128)S(6)} %select_n.72), kind=kLoop, calls=%fused_computation.24 | loop fusion | bytes 1228804 | tf_op jit(solution)/shard_map/dynamic_update_slice | solution.py:47
  56.9 1.1 %constant_dynamic-update-slice_fusion.4 = f32[25,48,640]{2,1,0:T(8,128)S(1)} fusion(f32[25,48,640]{2,1,0:T(8,128)S(1)} %constant_dynamic-update-slice_fusion.5, f32[25,48,128]{2,1,0:T(8,128)} %collective-permute-done.4, s32[]{:T(128)S(6)} %select_n.74), kind=kLoop, calls=%fused_computation.23 | loop fusion | bytes 1228804 | tf_op jit(solution)/shard_map/dynamic_update_slice | solution.py:49
  58.2 12.7 %collective-permute-done.8 = f32[25,48,128]{2,1,0:T(8,128)S(1)} collective-permute-done((f32[25,48,128]{2,1,0:T(8,128)S(1)}, f32[25,48,128]{2,1,0:T(8,128)S(1)}, u32[]{:S(2)}, u32[]{:S(2)}) %collective-permute-start.8) | collective-permute-done | bytes 614432 | tf_op jit(solution)/shard_map/ppermute | solution.py:45
  71.0 1.6 %copy-done.1 = f32[25,48,640]{2,1,0:T(8,128)} copy-done((f32[25,48,640]{2,1,0:T(8,128)}, f32[25,48,640]{2,1,0:T(8,128)S(1)}, u32[]{:S(2)}) %copy-start.1) | copy-done | bytes 3072024
  72.7 4.1 %shard_map.105 = (f32[4,48,512]{2,1,0:T(8,128)}, f32[4,48,512]{2,1,0:T(8,128)}) custom-call(f32[8]{0:T(128)} %compare_convert_fusion.north_ref.refs_0_, f32[4,48,512]{2,1,0:T(8,128)} %get-tuple-element.21.lo_ref, f32[4,48,512]{2,1,0:T(8,128)} %get-tuple-element.22.hi_ref, f32[4,48,512]{2,1,0:T(8,128)} %get-tuple-element.23.lo_in_ref, ...), custom_call_target="tpu_custom_call" | custom-call | tf_op jit(solution)/shard_map/pallas_call | solution.py:277
  76.9 1.9 %collective-permute-start.12 = (f32[4,48,512]{2,1,0:T(8,128)}, f32[4,48,512]{2,1,0:T(8,128)S(1)}, u32[]{:S(2)}, u32[]{:S(2)}) collective-permute-start(f32[4,48,512]{2,1,0:T(8,128)} %get-tuple-element.34.hi_ref.refs_2_), channel_id=1, source_target_pairs={{0,1},{1,2},{2,3},{4,5},{5,6},{6,7},{8,9},{9,10},{10,11},{12,13},{... | collective-permute-start | bytes 1179656 | tf_op jit(solution)/shard_map/ppermute | solution.py:16
  78.8 3.0 %collective-permute-start.13 = (f32[4,48,512]{2,1,0:T(8,128)}, f32[4,48,512]{2,1,0:T(8,128)S(1)}, u32[]{:S(2)}, u32[]{:S(2)}) collective-permute-start(f32[4,48,512]{2,1,0:T(8,128)} %get-tuple-element.33.lo_ref.refs_1_), channel_id=1, source_target_pairs={{1,0},{2,1},{3,2},{5,4},{6,5},{7,6},{9,8},{10,9},{11,10},{13,12},{... | collective-permute-start | bytes 1179656 | tf_op jit(solution)/shard_map/ppermute | solution.py:16
  81.8 8.7 %shard_map.106 = (f32[4,8,48,512]{3,2,1,0:T(8,128)}, f32[4,48,512]{2,1,0:T(8,128)}, f32[4,48,512]{2,1,0:T(8,128)}) custom-call(f32[8]{0:T(128)} %compare_convert_fusion.north_ref.refs_0_, f32[4,8,48,512]{3,2,1,0:T(8,128)} %q_ref.1, f32[4,48,512]{2,1,0:T(8,128)} %get-tuple-element.33.lo_ref.refs_1_, f32[4,48,512]{2,1,0:T(8,128)} %get-tuple-element.34.hi_ref.refs_2_, ...), custom_call_target="tpu_custom_call" | custom-call | tf_op jit(solution)/shard_map/pallas_call | solution.py:343
  90.5 0.7 copy-done.4
  91.4 3.6 %shard_map.107 = f32[4,8,48,512]{3,2,1,0:T(8,128)} custom-call(f32[8]{0:T(128)} %compare_convert_fusion.north_ref.refs_0_, f32[4,48,512]{2,1,0:T(8,128)} %get-tuple-element.33.lo_ref.refs_1_, f32[4,48,512]{2,1,0:T(8,128)} %get-tuple-element.34.hi_ref.refs_2_, f32[4,48,512]{2,1,0:T(8,128)} %get-tuple-element.35.refs_3_, ...), custom_call_target="tpu_custom_call", output_to_operand_aliasing={{}: (12, {})} | custom-call | tf_op jit(solution)/shard_map/pallas_call | solution.py:277
  (43 shorter events, 2.0 us)
Async XLA Ops:
  0.6 6.0 %copy-start = (f32[8,8,8]{2,1,0:T(8,128)S(1)}, f32[8,8,8]{2,1,0:T(8,128)}, u32[]{:S(2)}) copy-start(f32[8,8,8]{2,1,0:T(8,128)} %param.11) | copy-start | bytes 6148
  0.6 18.9 %copy-start.9 = (s32[8,512]{1,0:T(8,128)S(1)}, s32[8,512]{1,0:T(8,128)}, u32[]{:S(2)}) copy-start(s32[8,512]{1,0:T(8,128)} %param.13) | copy-start | bytes 49156
  0.7 18.9 %copy-start.10 = (f32[4,22]{1,0:T(4,128)S(1)}, f32[4,22]{1,0:T(4,128)}, u32[]{:S(2)}) copy-start(f32[4,22]{1,0:T(4,128)} %param.14) | copy-start | bytes 1060
  1.4 10.2 %collective-permute-start = (f32[1,48,128]{2,1,0:T(8,128)S(1)}, f32[1,48,128]{2,1,0:T(8,128)S(1)}, u32[]{:S(2)}, u32[]{:S(2)}) collective-permute-start(f32[1,48,128]{2,1,0:T(8,128)S(1)} %slice.21), channel_id=1, source_target_pairs={{0,1},{1,2},{2,3},{4,5},{5,6},{6,7},{8,9},{9,10},{10,11},{12,13},{... | collective-permute-start | bytes 73736 | tf_op jit(solution)/shard_map/ppermute | solution.py:16
  11.6 0.6 copy-start.8
  14.2 16.4 %collective-permute-start.3 = (f32[25,48,128]{2,1,0:T(8,128)}, f32[25,48,128]{2,1,0:T(8,128)}, u32[]{:S(2)}, u32[]{:S(2)}) collective-permute-start(f32[25,48,128]{2,1,0:T(8,128)} %shard_map.104), channel_id=1, source_target_pairs={{0,4},{4,8},{8,12},{1,5},{5,9},{9,13},{2,6},{6,10},{10,14},{3,7},{... | collective-permute-start | bytes 1843208 | tf_op jit(solution)/shard_map/ppermute | solution.py:44
  18.2 17.3 %collective-permute-start.4 = (f32[25,48,128]{2,1,0:T(8,128)}, f32[25,48,128]{2,1,0:T(8,128)}, u32[]{:S(2)}, u32[]{:S(2)}) collective-permute-start(f32[25,48,128]{2,1,0:T(8,128)} %shard_map.104), channel_id=1, source_target_pairs={{4,0},{8,4},{12,8},{5,1},{9,5},{13,9},{6,2},{10,6},{14,10},{7,3},{... | collective-permute-start | bytes 1843208 | tf_op jit(solution)/shard_map/ppermute | solution.py:45
  20.4 11.1 %copy-start.2 = (f32[25,48,128]{2,1,0:T(8,128)S(1)}, f32[25,48,128]{2,1,0:T(8,128)}, u32[]{:S(2)}) copy-start(f32[25,48,128]{2,1,0:T(8,128)} %shard_map.104) | copy-start | bytes 1843204
  20.4 19.6 %copy-start.6 = (f32[4,8,512]{2,1,0:T(8,128)S(1)}, f32[4,8,512]{2,1,0:T(8,128)}, u32[]{:S(2)}) copy-start(f32[4,8,512]{2,1,0:T(8,128)} %convolution_bitcast_fusion.3) | copy-start | bytes 196612
  20.4 19.6 %copy-start.7 = (f32[8,512,4]{1,2,0:T(4,128)S(1)}, f32[8,512,4]{1,2,0:T(4,128)}, u32[]{:S(2)}) copy-start(f32[8,512,4]{1,2,0:T(4,128)} %fusion) | copy-start | bytes 196612
  20.4 11.1 %collective-permute-start.10 = (f32[4,8,512]{2,1,0:T(8,128)}, f32[4,8,512]{2,1,0:T(8,128)S(1)}, u32[]{:S(2)}, u32[]{:S(2)}) collective-permute-start(f32[4,8,512]{2,1,0:T(8,128)} %param.10), channel_id=1, source_target_pairs={{0,2},{1,3},{2,0},{3,1},{4,6},{5,7},{6,4},{7,5},{8,10},{9,11},{10,... | collective-permute-start | bytes 196616 | tf_op jit(solution)/shard_map/ppermute | solution.py:389
  20.5 16.5 %collective-permute-start.9 = (f32[4,8,512]{2,1,0:T(8,128)}, f32[4,8,512]{2,1,0:T(8,128)S(1)}, u32[]{:S(2)}, u32[]{:S(2)}) collective-permute-start(f32[4,8,512]{2,1,0:T(8,128)} %param.10), channel_id=1, source_target_pairs={{0,1},{1,2},{2,3},{3,0},{4,5},{5,6},{6,7},{7,4},{8,9},{9,10},{10,1... | collective-permute-start | bytes 196616 | tf_op jit(solution)/shard_map/ppermute | solution.py:389
  21.1 19.0 %collective-permute-start.11 = (f32[4,8,512]{2,1,0:T(8,128)}, f32[4,8,512]{2,1,0:T(8,128)S(1)}, u32[]{:S(2)}, u32[]{:S(2)}) collective-permute-start(f32[4,8,512]{2,1,0:T(8,128)} %param.10), channel_id=1, source_target_pairs={{0,3},{1,0},{2,1},{3,2},{4,7},{5,4},{6,5},{7,6},{8,11},{9,8},{10,9... | collective-permute-start | bytes 196616 | tf_op jit(solution)/shard_map/ppermute | solution.py:389
  30.6 8.8 %collective-permute-start.5 = (f32[25,48,128]{2,1,0:T(8,128)}, f32[25,48,128]{2,1,0:T(8,128)S(1)}, u32[]{:S(2)}, u32[]{:S(2)}) collective-permute-start(f32[25,48,128]{2,1,0:T(8,128)} %collective-permute-done.3), channel_id=1, source_target_pairs={{4,8},{8,12},{5,9},{9,13},{6,10},{10,14},{7,11},{11,15},{20,24},{2... | collective-permute-start | bytes 1843208 | tf_op jit(solution)/shard_map/ppermute | solution.py:44
  31.6 39.4 %collective-permute-start.1 = (f32[4,48,512]{2,1,0:T(8,128)S(1)}, f32[4,48,512]{2,1,0:T(8,128)S(1)}, u32[]{:S(2)}, u32[]{:S(2)}) collective-permute-start(f32[4,48,512]{2,1,0:T(8,128)S(1)} %get-tuple-element.39), channel_id=1, source_target_pairs={{0,1},{1,2},{2,3},{4,5},{5,6},{6,7},{8,9},{9,10},{10,11},{12,13},{... | collective-permute-start | bytes 1179656 | tf_op jit(solution)/shard_map/ppermute | solution.py:16
  35.5 19.0 %collective-permute-start.6 = (f32[25,48,128]{2,1,0:T(8,128)}, f32[25,48,128]{2,1,0:T(8,128)S(1)}, u32[]{:S(2)}, u32[]{:S(2)}) collective-permute-start(f32[25,48,128]{2,1,0:T(8,128)} %collective-permute-done.4), channel_id=1, source_target_pairs={{4,0},{8,4},{5,1},{9,5},{6,2},{10,6},{7,3},{11,7},{20,16},{24,20},... | collective-permute-start | bytes 1843208 | tf_op jit(solution)/shard_map/ppermute | solution.py:45
  37.0 34.0 %collective-permute-start.2 = (f32[4,48,512]{2,1,0:T(8,128)S(1)}, f32[4,48,512]{2,1,0:T(8,128)}, u32[]{:S(2)}, u32[]{:S(2)}) collective-permute-start(f32[4,48,512]{2,1,0:T(8,128)S(1)} %get-tuple-element.38), channel_id=1, source_target_pairs={{1,0},{2,1},{3,2},{5,4},{6,5},{7,6},{9,8},{10,9},{11,10},{13,12},{... | collective-permute-start | bytes 1179656 | tf_op jit(solution)/shard_map/ppermute | solution.py:16
  39.4 18.8 %collective-permute-start.7 = (f32[25,48,128]{2,1,0:T(8,128)S(1)}, f32[25,48,128]{2,1,0:T(8,128)S(1)}, u32[]{:S(2)}, u32[]{:S(2)}) collective-permute-start(f32[25,48,128]{2,1,0:T(8,128)S(1)} %collective-permute-done.5), channel_id=1, source_target_pairs={{8,12},{9,13},{10,14},{11,15},{24,28},{25,29},{26,30},{27,31}} | collective-permute-start | bytes 1843208 | tf_op jit(solution)/shard_map/ppermute | solution.py:44
  54.5 16.4 %collective-permute-start.8 = (f32[25,48,128]{2,1,0:T(8,128)S(1)}, f32[25,48,128]{2,1,0:T(8,128)S(1)}, u32[]{:S(2)}, u32[]{:S(2)}) collective-permute-start(f32[25,48,128]{2,1,0:T(8,128)S(1)} %collective-permute-done.6), channel_id=1, source_target_pairs={{4,0},{5,1},{6,2},{7,3},{20,16},{21,17},{22,18},{23,19}} | collective-permute-start | bytes 1843208 | tf_op jit(solution)/shard_map/ppermute | solution.py:45
  71.0 1.6 %copy-start.1 = (f32[25,48,640]{2,1,0:T(8,128)}, f32[25,48,640]{2,1,0:T(8,128)S(1)}, u32[]{:S(2)}) copy-start(f32[25,48,640]{2,1,0:T(8,128)S(1)} %constant_dynamic-update-slice_fusion.u_ref.v_ref.vm_ref.w_ref.wx_ref.refs_7_.refs_8_.refs_9_.refs_10_) | copy-start | bytes 9216004
  71.0 1.7 %copy-start.3 = (f32[4,48,512]{2,1,0:T(8,128)}, f32[4,48,512]{2,1,0:T(8,128)S(1)}, u32[]{:S(2)}) copy-start(f32[4,48,512]{2,1,0:T(8,128)S(1)} %collective-permute-done.1.qs_ref) | copy-start | bytes 1179652
  76.9 13.6 %collective-permute-start.12 = (f32[4,48,512]{2,1,0:T(8,128)}, f32[4,48,512]{2,1,0:T(8,128)S(1)}, u32[]{:S(2)}, u32[]{:S(2)}) collective-permute-start(f32[4,48,512]{2,1,0:T(8,128)} %get-tuple-element.34.hi_ref.refs_2_), channel_id=1, source_target_pairs={{0,1},{1,2},{2,3},{4,5},{5,6},{6,7},{8,9},{9,10},{10,11},{12,13},{... | collective-permute-start | bytes 1179656 | tf_op jit(solution)/shard_map/ppermute | solution.py:16
  78.8 11.7 %collective-permute-start.13 = (f32[4,48,512]{2,1,0:T(8,128)}, f32[4,48,512]{2,1,0:T(8,128)S(1)}, u32[]{:S(2)}, u32[]{:S(2)}) collective-permute-start(f32[4,48,512]{2,1,0:T(8,128)} %get-tuple-element.33.lo_ref.refs_1_), channel_id=1, source_target_pairs={{1,0},{2,1},{3,2},{5,4},{6,5},{7,6},{9,8},{10,9},{11,10},{13,12},{... | collective-permute-start | bytes 1179656 | tf_op jit(solution)/shard_map/ppermute | solution.py:16
  90.5 0.8 copy-start.4
  90.5 0.9 copy-start.5

commit v15 on v13

--- a/solution.py
+++ b/solution.py
@@ -178,87 +178,76 @@
     )(north_open, state, weather, emission)
 
 
-def edge_kernel(north_ref, lo_ref, hi_ref, lo_in_ref, hi_in_ref, qs_ref, qn_ref, u_ref, v_ref, vm_ref, w_ref, src_ref, *outs):
+def edge_kernel(north_ref, lo_ref, hi_ref, lo_in_ref, hi_in_ref, qs_ref, qn_ref, wx_ref, src_ref, *outs):
     split = len(outs) == 2
+    if not split:
+        o_hbm, stage, sems = outs
     tracers, lat_rows = src_ref.shape[0], src_ref.shape[1]
     levels, lon = lo_ref.shape[1], lo_ref.shape[2]
-    top = pl.program_id(0)
     level = lax.broadcasted_iota(jnp.int32, (levels, lon), 0)
     not_top = level < levels - 1
     not_bottom = level > 0
-    a = top * (lat_rows - 1)
-    is_top = jnp.full((levels, lon), top, jnp.int32) == 1
-    u = u_ref[0]
-    uw = pltpu.roll(u, 1, 1)
-    v = v_ref[0] * north_ref[a]
-    vm = vm_ref[0]
-    w = w_ref[0]
-    w_up = jnp.where(not_top, w, 0.0)
-    w_down = jnp.where(not_bottom, pltpu.roll(w, 1, 0), 0.0)
-    c_self = (
-        1.0
-        - jnp.maximum(u, 0.0)
-        + jnp.minimum(uw, 0.0)
-        - jnp.maximum(v, 0.0)
-        + jnp.minimum(vm, 0.0)
-        - w_up
-        - w_down
-    )
-    c_east = -jnp.minimum(u, 0.0)
-    c_west = jnp.maximum(uw, 0.0)
-    c_north = -jnp.minimum(v, 0.0)
-    c_south = jnp.maximum(vm, 0.0)
-    at_top = jnp.full((1, lon), top, jnp.int32) == 1
-    for k in range(tracers):
-        qa = jnp.where(is_top, hi_ref[k], lo_ref[k])
-        inner = jnp.where(is_top, hi_in_ref[k], lo_in_ref[k])
-        qm = jnp.where(is_top, inner, qs_ref[k])
-        qp = jnp.where(is_top, qn_ref[k], inner)
-        result = (
-            c_self * qa
-            + c_east * pltpu.roll(qa, lon - 1, 1)
-            + c_west * pltpu.roll(qa, 1, 1)
-            + c_north * qp
-            + c_south * qm
-            + w_up * pltpu.roll(qa, levels - 1, 0)
-            + w_down * pltpu.roll(qa, 1, 0)
+    last = lat_rows - 1
+    for top in (0, 1):
+        a = top * last
+        u = wx_ref[a]
+        uw = pltpu.roll(u, 1, 1)
+        v = wx_ref[lat_rows + a] * north_ref[a]
+        vm = wx_ref[3 * lat_rows] if top == 0 else wx_ref[lat_rows + a - 1]
+        w = wx_ref[2 * lat_rows + a]
+        w_up = jnp.where(not_top, w, 0.0)
+        w_down = jnp.where(not_bottom, pltpu.roll(w, 1, 0), 0.0)
+        c_self = (
+            1.0
+            - jnp.maximum(u, 0.0)
+            + jnp.minimum(uw, 0.0)
+            - jnp.maximum(v, 0.0)
+            + jnp.minimum(vm, 0.0)
+            - w_up
+            - w_down
         )
-        source = jnp.where(at_top, src_ref[k, lat_rows - 1 : lat_rows, :], src_ref[k, 0:1, :])
-        surface = result[0:1] + source
-        if split:
-
-            def put(ref, result=result, surface=surface, k=k):
-                ref[k] = result
-                ref[k, 0:1, :] = surface
-
-            pl.when(top == 0)(functools.partial(put, outs[0]))
-            pl.when(top == 1)(functools.partial(put, outs[1]))
-        else:
-            outs[-1][k, 0] = result
-            outs[-1][k, 0, 0:1, :] = surface
+        c_east = -jnp.minimum(u, 0.0)
+        c_west = jnp.maximum(uw, 0.0)
+        c_north = -jnp.minimum(v, 0.0)
+        c_south = jnp.maximum(vm, 0.0)
+        for k in range(tracers):
+            qa = hi_ref[k] if top else lo_ref[k]
+            inner = hi_in_ref[k] if top else lo_in_ref[k]
+            qm = inner if top else qs_ref[k]
+            qp = qn_ref[k] if top else inner
+            result = (
+                c_self * qa
+                + c_east * pltpu.roll(qa, lon - 1, 1)
+                + c_west * pltpu.roll(qa, 1, 1)
+                + c_north * qp
+                + c_south * qm
+                + w_up * pltpu.roll(qa, levels - 1, 0)
+                + w_down * pltpu.roll(qa, 1, 0)
+            )
+            surface = result[0:1] + src_ref[k, a : a + 1, :]
+            target = outs[top].at[k] if split else stage.at[top, k, 0]
+            target[...] = result
+            target[0:1, :] = surface
+    if not split:
+        copies = [
+            pltpu.make_async_copy(stage.at[top], o_hbm.at[:, pl.ds(top * last, 1)], sems.at[top])
+            for top in (0, 1)
+        ]
+        for copy in copies:
+            copy.start()
+        for copy in copies:
+            copy.wait()
 
 
 def edge_step(rows, base, south, north, weather, emission, north_open):
     tracers, levels, lon = rows[0].shape
     lat_rows = emission.shape[1]
-    last = lat_rows - 1
-    edge = pl.BlockSpec((tracers, levels, lon), lambda e: (0, 0, 0))
-    met = lambda index: pl.BlockSpec((1, levels, lon), index)
-    in_specs = [
-        pl.BlockSpec(memory_space=pltpu.SMEM),
-        edge,
-        edge,
-        edge,
-        edge,
-        edge,
-        edge,
-        met(lambda e: (e * last, 0, 0)),
-        met(lambda e: (lat_rows + e * last, 0, 0)),
-        met(lambda e: (3 * lat_rows - e * (lat_rows + 2), 0, 0)),
-        met(lambda e: (2 * lat_rows + e * last, 0, 0)),
-        pl.BlockSpec((tracers, lat_rows, lon), lambda e: (0, 0, 0)),
-    ]
-    args = [north_open, *rows, south, north, weather, weather, weather, weather, emission]
+    vmem = pl.BlockSpec(memory_space=pltpu.VMEM)
+    in_specs = [pl.BlockSpec(memory_space=pltpu.SMEM)] + [vmem] * 6
+    in_specs += [pl.BlockSpec(weather.shape[:2] + (lon,), lambda i: (0, 0, 0)), vmem]
+    args = [north_open, *rows, south, north, weather, emission]
+    edge = pl.BlockSpec((tracers, levels, lon), lambda i: (0, 0, 0))
+    scratch = []
     if base is None:
         out_specs = [edge, edge]
         out_shape = [jax.ShapeDtypeStruct((tracers, levels, lon), jnp.float32)] * 2
@@ -267,19 +256,19 @@
     else:
         in_specs.append(pl.BlockSpec(memory_space=pl.ANY))
         args.append(base)
-        out_specs = pl.BlockSpec((tracers, 1, levels, lon), lambda e: (0, e * last, 0, 0))
+        out_specs = pl.BlockSpec(memory_space=pl.ANY)
         out_shape = jax.ShapeDtypeStruct(base.shape, base.dtype)
         aliases = {len(args) - 1: 0}
-        kernel = lambda *refs: edge_kernel(*refs[:-2], refs[-1])
+        scratch = [pltpu.VMEM((2, tracers, 1, levels, lon), jnp.float32), pltpu.SemaphoreType.DMA((2,))]
+        kernel = lambda *refs: edge_kernel(*refs[:9], *refs[10:])
     grid_spec = pltpu.PrefetchScalarGridSpec(
-        num_scalar_prefetch=0, grid=(2,), in_specs=in_specs, out_specs=out_specs
+        num_scalar_prefetch=0, grid=(1,), in_specs=in_specs, out_specs=out_specs, scratch_shapes=scratch
     )
     return pl.pallas_call(
         kernel,
         grid_spec=grid_spec,
         out_shape=out_shape,
         input_output_aliases=aliases,
-        compiler_params=pltpu.CompilerParams(dimension_semantics=("arbitrary",)),
     )(*args)
 
 

time: 94.3 us -> 94.4 us (level)
    unnamed x22 -> x20, local copies, waits for them, and re-layouts: 3.35 us -> 3.23 us
where the time goes in v15:
time: 94.4 us; the launch traced here: 93.6 us
  waiting for transfers between devices  33.6 us (36%)
  starting transfers between devices  23.8 us (25%)
  Pallas kernels  18.7 us (20%)
  local copies, waits for them, and re-layouts  12.1 us (13%)
  matrix products  3.94 us (4%)
  between operations  0.96 us (1%)
    ppermute x3, waiting for transfers between devices, relay_gather(): lax.ppermute(left, axis, [(j, j - 1) for j in range(1, count - r + 1)])  27.9 us
    ppermute x5, starting transfers between devices, passed_along(): return lax.ppermute(value, axis, pairs)  13.7 us
    pallas_call x1, Pallas kernels, fused_steps(): pl.pallas_call(fused_kernel, grid_spec=grid_spec, out_shape=[jax.ShapeDty...  8.67 us
    pallas_call x2, Pallas kernels, edge_step(): pl.pallas_call(kernel, grid_spec=grid_spec, out_shape=out_shape, input_ou...  8.05 us
    ppermute x3, waiting for transfers between devices, relay_gather(): lax.ppermute(right, axis, [(i, i + 1) for i in range(r - 1, count - 1)])  5.64 us
    ppermute x3, starting transfers between devices, relay_gather(): lax.ppermute(right, axis, [(i, i + 1) for i in range(r - 1, count - 1)])  5.43 us
    ppermute x3, starting transfers between devices, relay_gather(): lax.ppermute(left, axis, [(j, j - 1) for j in range(1, count - r + 1)])  3.84 us
    unnamed x20, local copies, waits for them, and re-layouts  3.23 us
  transfers between devices with their start and end apart: 14, of which 4 were waited for; matrix products, arithmetic and copies ran while one was open for 14% of the time, Pallas kernels for 9%

profile of v15, /device:TPU:1, one launch (start us, length us, event | category | flops | bytes accessed | tf_op | source)
XLA Modules:
  0.0 93.6 jit_solution(7258645013767678605)
XLA Ops:
  0.7 0.8 slice.21
  1.4 4.5 %collective-permute-start = (f32[1,48,128]{2,1,0:T(8,128)S(1)}, f32[1,48,128]{2,1,0:T(8,128)S(1)}, u32[]{:S(2)}, u32[]{:S(2)}) collective-permute-start(f32[1,48,128]{2,1,0:T(8,128)S(1)} %slice.21), channel_id=1, source_target_pairs={{0,1},{1,2},{2,3},{4,5},{5,6},{6,7},{8,9},{9,10},{10,11},{12,13},{... | collective-permute-start | bytes 73736 | tf_op jit(solution)/shard_map/ppermute | solution.py:16
  5.9 0.7 constant_dynamic-slice_fusion.4
  6.8 1.7 %convolution_bitcast_fusion.3 = f32[4,8,512]{2,1,0:T(8,128)} fusion(f32[8,8,1]{1,0,2:T(8,128)S(1)} %bitcast.56, f32[4,8,512]{2,1,0:T(8,128)} %param.10), kind=kOutput, calls=%fused_computation.3 | convolution fusion | flops 1572864 | bytes 131328 | tf_op jit(solution)/shard_map/jm,kmn->kjn/dot_general | solution.py:365
  9.7 2.0 %shard_map.104 = f32[25,48,128]{2,1,0:T(8,128)} custom-call(f32[8,48,128]{2,1,0:T(8,128)} %refs_0_, f32[8,48,128]{2,1,0:T(8,128)} %refs_1_, f32[8,48,128]{2,1,0:T(8,128)} %refs_2_, f32[1,48,128]{2,1,0:T(8,128)} %copy-done.7), custom_call_target="tpu_custom_call" | custom-call | tf_op jit(solution)/shard_map/pallas_call | solution.py:30
  11.6 4.0 %collective-permute-start.3 = (f32[25,48,128]{2,1,0:T(8,128)}, f32[25,48,128]{2,1,0:T(8,128)}, u32[]{:S(2)}, u32[]{:S(2)}) collective-permute-start(f32[25,48,128]{2,1,0:T(8,128)} %shard_map.104), channel_id=1, source_target_pairs={{0,4},{4,8},{8,12},{1,5},{5,9},{9,13},{2,6},{6,10},{10,14},{3,7},{... | collective-permute-start | bytes 1843208 | tf_op jit(solution)/shard_map/ppermute | solution.py:44
  15.7 2.5 %slice_bitcast_fusion.2 = (f32[4,48,512]{2,1,0:T(8,128)}, f32[4,48,512]{2,1,0:T(8,128)}, f32[4,48,512]{2,1,0:T(8,128)}, f32[4,48,512]{2,1,0:T(8,128)}) fusion(f32[4,8,48,512]{3,2,1,0:T(8,128)} %q_ref.1), kind=kLoop, calls=%fused_computation.7 | loop fusion | bytes 3145728 | tf_op jit(solution)/shard_map/squeeze | solution.py:388
  18.2 1.3 %collective-permute-start.4 = (f32[25,48,128]{2,1,0:T(8,128)}, f32[25,48,128]{2,1,0:T(8,128)}, u32[]{:S(2)}, u32[]{:S(2)}) collective-permute-start(f32[25,48,128]{2,1,0:T(8,128)} %shard_map.104), channel_id=1, source_target_pairs={{4,0},{8,4},{12,8},{5,1},{9,5},{13,9},{6,2},{10,6},{14,10},{7,3},{... | collective-permute-start | bytes 1843208 | tf_op jit(solution)/shard_map/ppermute | solution.py:45
  19.5 0.9 fusion
  20.4 0.6 collective-permute-start.9
  21.2 1.2 %slice_bitcast_fusion = (f32[4,48,512]{2,1,0:T(8,128)S(1)}, f32[4,48,512]{2,1,0:T(8,128)S(1)}) fusion(f32[4,8,48,512]{3,2,1,0:T(8,128)} %q_ref.1), kind=kLoop, calls=%fused_computation.4 | loop fusion | bytes 1572864 | tf_op jit(solution)/shard_map/squeeze | solution.py:374
  22.4 5.6 %collective-permute-done.3 = f32[25,48,128]{2,1,0:T(8,128)} collective-permute-done((f32[25,48,128]{2,1,0:T(8,128)}, f32[25,48,128]{2,1,0:T(8,128)}, u32[]{:S(2)}, u32[]{:S(2)}) %collective-permute-start.3) | collective-permute-done | bytes 614432 | tf_op jit(solution)/shard_map/ppermute | solution.py:44
  28.0 0.7 collective-permute-start.5
  28.9 1.1 %constant_dynamic-update-slice_fusion.6 = f32[25,48,640]{2,1,0:T(8,128)S(1)} fusion(f32[25,48,640]{2,1,0:T(8,128)S(1)} %broadcast_in_dim.2, f32[25,48,128]{2,1,0:T(8,128)} %shard_map.104, s32[]{:T(128)S(6)} %select_n.70), kind=kLoop, calls=%fused_computation.25 | loop fusion | bytes 1228804 | tf_op jit(solution)/shard_map/dynamic_update_slice | solution.py:41
  30.1 1.9 %collective-permute-start.1 = (f32[4,48,512]{2,1,0:T(8,128)S(1)}, f32[4,48,512]{2,1,0:T(8,128)S(1)}, u32[]{:S(2)}, u32[]{:S(2)}) collective-permute-start(f32[4,48,512]{2,1,0:T(8,128)S(1)} %get-tuple-element.31), channel_id=1, source_target_pairs={{0,1},{1,2},{2,3},{4,5},{5,6},{6,7},{8,9},{9,10},{10,11},{12,13},{... | collective-permute-start | bytes 1179656 | tf_op jit(solution)/shard_map/ppermute | solution.py:16
  32.0 3.5 %collective-permute-done.4 = f32[25,48,128]{2,1,0:T(8,128)} collective-permute-done((f32[25,48,128]{2,1,0:T(8,128)}, f32[25,48,128]{2,1,0:T(8,128)}, u32[]{:S(2)}, u32[]{:S(2)}) %collective-permute-start.4) | collective-permute-done | bytes 614432 | tf_op jit(solution)/shard_map/ppermute | solution.py:45
  35.5 1.3 %collective-permute-start.6 = (f32[25,48,128]{2,1,0:T(8,128)}, f32[25,48,128]{2,1,0:T(8,128)S(1)}, u32[]{:S(2)}, u32[]{:S(2)}) collective-permute-start(f32[25,48,128]{2,1,0:T(8,128)} %collective-permute-done.4), channel_id=1, source_target_pairs={{4,0},{8,4},{5,1},{9,5},{6,2},{10,6},{7,3},{11,7},{20,16},{24,20},... | collective-permute-start | bytes 1843208 | tf_op jit(solution)/shard_map/ppermute | solution.py:45
  36.9 2.1 %collective-permute-start.2 = (f32[4,48,512]{2,1,0:T(8,128)S(1)}, f32[4,48,512]{2,1,0:T(8,128)}, u32[]{:S(2)}, u32[]{:S(2)}) collective-permute-start(f32[4,48,512]{2,1,0:T(8,128)S(1)} %get-tuple-element.30), channel_id=1, source_target_pairs={{1,0},{2,1},{3,2},{5,4},{6,5},{7,6},{9,8},{10,9},{11,10},{13,12},{... | collective-permute-start | bytes 1179656 | tf_op jit(solution)/shard_map/ppermute | solution.py:16
  39.3 0.7 collective-permute-start.7
  40.0 0.8 bitcast_multiply_fusion.src_ref.refs_8_
  40.9 11.9 %collective-permute-done.6 = f32[25,48,128]{2,1,0:T(8,128)S(1)} collective-permute-done((f32[25,48,128]{2,1,0:T(8,128)}, f32[25,48,128]{2,1,0:T(8,128)S(1)}, u32[]{:S(2)}, u32[]{:S(2)}) %collective-permute-start.6) | collective-permute-done | bytes 614432 | tf_op jit(solution)/shard_map/ppermute | solution.py:45
  52.8 1.3 %collective-permute-start.8 = (f32[25,48,128]{2,1,0:T(8,128)S(1)}, f32[25,48,128]{2,1,0:T(8,128)S(1)}, u32[]{:S(2)}, u32[]{:S(2)}) collective-permute-start(f32[25,48,128]{2,1,0:T(8,128)S(1)} %collective-permute-done.6), channel_id=1, source_target_pairs={{4,0},{5,1},{6,2},{7,3},{20,16},{21,17},{22,18},{23,19}} | collective-permute-start | bytes 1843208 | tf_op jit(solution)/shard_map/ppermute | solution.py:45
  54.1 1.1 %constant_dynamic-update-slice_fusion.5 = f32[25,48,640]{2,1,0:T(8,128)S(1)} fusion(f32[25,48,640]{2,1,0:T(8,128)S(1)} %constant_dynamic-update-slice_fusion.6, f32[25,48,128]{2,1,0:T(8,128)} %collective-permute-done.3, s32[]{:T(128)S(6)} %select_n.72), kind=kLoop, calls=%fused_computation.24 | loop fusion | bytes 1228804 | tf_op jit(solution)/shard_map/dynamic_update_slice | solution.py:47
  55.2 1.1 %constant_dynamic-update-slice_fusion.4 = f32[25,48,640]{2,1,0:T(8,128)S(1)} fusion(f32[25,48,640]{2,1,0:T(8,128)S(1)} %constant_dynamic-update-slice_fusion.5, f32[25,48,128]{2,1,0:T(8,128)} %collective-permute-done.4, s32[]{:T(128)S(6)} %select_n.74), kind=kLoop, calls=%fused_computation.23 | loop fusion | bytes 1228804 | tf_op jit(solution)/shard_map/dynamic_update_slice | solution.py:49
  56.5 12.5 %collective-permute-done.8 = f32[25,48,128]{2,1,0:T(8,128)S(1)} collective-permute-done((f32[25,48,128]{2,1,0:T(8,128)S(1)}, f32[25,48,128]{2,1,0:T(8,128)S(1)}, u32[]{:S(2)}, u32[]{:S(2)}) %collective-permute-start.8) | collective-permute-done | bytes 614432 | tf_op jit(solution)/shard_map/ppermute | solution.py:45
  69.1 1.6 %copy-done.1 = f32[25,48,640]{2,1,0:T(8,128)} copy-done((f32[25,48,640]{2,1,0:T(8,128)}, f32[25,48,640]{2,1,0:T(8,128)S(1)}, u32[]{:S(2)}) %copy-start.1) | copy-done | bytes 3072024
  70.8 4.0 %shard_map.105 = (f32[4,48,512]{2,1,0:T(8,128)}, f32[4,48,512]{2,1,0:T(8,128)}) custom-call(f32[8]{0:T(128)} %compare_convert_fusion.north_ref.refs_0_, f32[4,48,512]{2,1,0:T(8,128)} %get-tuple-element.35.lo_ref, f32[4,48,512]{2,1,0:T(8,128)} %get-tuple-element.34.hi_ref, f32[4,48,512]{2,1,0:T(8,128)} %get-tuple-element.33.lo_in_ref, ...), custom_call_target="tpu_custom_call" | custom-call | tf_op jit(solution)/shard_map/pallas_call | solution.py:267
  74.8 1.9 %collective-permute-start.12 = (f32[4,48,512]{2,1,0:T(8,128)}, f32[4,48,512]{2,1,0:T(8,128)S(1)}, u32[]{:S(2)}, u32[]{:S(2)}) collective-permute-start(f32[4,48,512]{2,1,0:T(8,128)} %get-tuple-element.26.hi_ref.refs_2_), channel_id=1, source_target_pairs={{0,1},{1,2},{2,3},{4,5},{5,6},{6,7},{8,9},{9,10},{10,11},{12,13},{... | collective-permute-start | bytes 1179656 | tf_op jit(solution)/shard_map/ppermute | solution.py:16
  76.7 3.2 %collective-permute-start.13 = (f32[4,48,512]{2,1,0:T(8,128)}, f32[4,48,512]{2,1,0:T(8,128)S(1)}, u32[]{:S(2)}, u32[]{:S(2)}) collective-permute-start(f32[4,48,512]{2,1,0:T(8,128)} %get-tuple-element.25.lo_ref.refs_1_), channel_id=1, source_target_pairs={{1,0},{2,1},{3,2},{5,4},{6,5},{7,6},{9,8},{10,9},{11,10},{13,12},{... | collective-permute-start | bytes 1179656 | tf_op jit(solution)/shard_map/ppermute | solution.py:16
  80.0 8.7 %shard_map.106 = (f32[4,8,48,512]{3,2,1,0:T(8,128)}, f32[4,48,512]{2,1,0:T(8,128)}, f32[4,48,512]{2,1,0:T(8,128)}) custom-call(f32[8]{0:T(128)} %compare_convert_fusion.north_ref.refs_0_, f32[4,8,48,512]{3,2,1,0:T(8,128)} %q_ref.1, f32[4,48,512]{2,1,0:T(8,128)} %get-tuple-element.25.lo_ref.refs_1_, f32[4,48,512]{2,1,0:T(8,128)} %get-tuple-element.26.hi_ref.refs_2_, ...), custom_call_target="tpu_custom_call" | custom-call | tf_op jit(solution)/shard_map/pallas_call | solution.py:332
  88.7 0.7 copy-done.2
  89.5 4.1 %shard_map.107 = f32[4,8,48,512]{3,2,1,0:T(8,128)} custom-call(f32[8]{0:T(128)} %compare_convert_fusion.north_ref.refs_0_, f32[4,48,512]{2,1,0:T(8,128)} %get-tuple-element.25.lo_ref.refs_1_, f32[4,48,512]{2,1,0:T(8,128)} %get-tuple-element.26.hi_ref.refs_2_, f32[4,48,512]{2,1,0:T(8,128)} %get-tuple-element.27.refs_3_, ...), custom_call_target="tpu_custom_call", output_to_operand_aliasing={{}: (9, {})} | custom-call | tf_op jit(solution)/shard_map/pallas_call | solution.py:267
  (41 shorter events, 2.6 us)
Async XLA Ops:
  0.6 6.0 %copy-start = (f32[8,8,8]{2,1,0:T(8,128)S(1)}, f32[8,8,8]{2,1,0:T(8,128)}, u32[]{:S(2)}) copy-start(f32[8,8,8]{2,1,0:T(8,128)} %param.11) | copy-start | bytes 6148
  0.6 18.8 %copy-start.8 = (s32[8,512]{1,0:T(8,128)S(1)}, s32[8,512]{1,0:T(8,128)}, u32[]{:S(2)}) copy-start(s32[8,512]{1,0:T(8,128)} %param.13) | copy-start | bytes 49156
  0.7 18.8 %copy-start.9 = (f32[4,22]{1,0:T(4,128)S(1)}, f32[4,22]{1,0:T(4,128)}, u32[]{:S(2)}) copy-start(f32[4,22]{1,0:T(4,128)} %param.14) | copy-start | bytes 1060
  1.4 7.6 %collective-permute-start = (f32[1,48,128]{2,1,0:T(8,128)S(1)}, f32[1,48,128]{2,1,0:T(8,128)S(1)}, u32[]{:S(2)}, u32[]{:S(2)}) collective-permute-start(f32[1,48,128]{2,1,0:T(8,128)S(1)} %slice.21), channel_id=1, source_target_pairs={{0,1},{1,2},{2,3},{4,5},{5,6},{6,7},{8,9},{9,10},{10,11},{12,13},{... | collective-permute-start | bytes 73736 | tf_op jit(solution)/shard_map/ppermute | solution.py:16
  9.0 0.6 copy-start.7
  11.6 16.4 %collective-permute-start.3 = (f32[25,48,128]{2,1,0:T(8,128)}, f32[25,48,128]{2,1,0:T(8,128)}, u32[]{:S(2)}, u32[]{:S(2)}) collective-permute-start(f32[25,48,128]{2,1,0:T(8,128)} %shard_map.104), channel_id=1, source_target_pairs={{0,4},{4,8},{8,12},{1,5},{5,9},{9,13},{2,6},{6,10},{10,14},{3,7},{... | collective-permute-start | bytes 1843208 | tf_op jit(solution)/shard_map/ppermute | solution.py:44
  18.2 17.3 %collective-permute-start.4 = (f32[25,48,128]{2,1,0:T(8,128)}, f32[25,48,128]{2,1,0:T(8,128)}, u32[]{:S(2)}, u32[]{:S(2)}) collective-permute-start(f32[25,48,128]{2,1,0:T(8,128)} %shard_map.104), channel_id=1, source_target_pairs={{4,0},{8,4},{12,8},{5,1},{9,5},{13,9},{6,2},{10,6},{14,10},{7,3},{... | collective-permute-start | bytes 1843208 | tf_op jit(solution)/shard_map/ppermute | solution.py:45
  20.4 19.6 %copy-start.5 = (f32[4,8,512]{2,1,0:T(8,128)S(1)}, f32[4,8,512]{2,1,0:T(8,128)}, u32[]{:S(2)}) copy-start(f32[4,8,512]{2,1,0:T(8,128)} %convolution_bitcast_fusion.3) | copy-start | bytes 196612
  20.4 19.6 %copy-start.6 = (f32[8,512,4]{1,2,0:T(4,128)S(1)}, f32[8,512,4]{1,2,0:T(4,128)}, u32[]{:S(2)}) copy-start(f32[8,512,4]{1,2,0:T(4,128)} %fusion) | copy-start | bytes 196612
  20.4 9.7 %collective-permute-start.10 = (f32[4,8,512]{2,1,0:T(8,128)}, f32[4,8,512]{2,1,0:T(8,128)S(1)}, u32[]{:S(2)}, u32[]{:S(2)}) collective-permute-start(f32[4,8,512]{2,1,0:T(8,128)} %param.10), channel_id=1, source_target_pairs={{0,2},{1,3},{2,0},{3,1},{4,6},{5,7},{6,4},{7,5},{8,10},{9,11},{10,... | collective-permute-start | bytes 196616 | tf_op jit(solution)/shard_map/ppermute | solution.py:377
  20.4 16.5 %collective-permute-start.9 = (f32[4,8,512]{2,1,0:T(8,128)}, f32[4,8,512]{2,1,0:T(8,128)S(1)}, u32[]{:S(2)}, u32[]{:S(2)}) collective-permute-start(f32[4,8,512]{2,1,0:T(8,128)} %param.10), channel_id=1, source_target_pairs={{0,1},{1,2},{2,3},{3,0},{4,5},{5,6},{6,7},{7,4},{8,9},{9,10},{10,1... | collective-permute-start | bytes 196616 | tf_op jit(solution)/shard_map/ppermute | solution.py:377
  21.0 19.0 %collective-permute-start.11 = (f32[4,8,512]{2,1,0:T(8,128)}, f32[4,8,512]{2,1,0:T(8,128)S(1)}, u32[]{:S(2)}, u32[]{:S(2)}) collective-permute-start(f32[4,8,512]{2,1,0:T(8,128)} %param.10), channel_id=1, source_target_pairs={{0,3},{1,0},{2,1},{3,2},{4,7},{5,4},{6,5},{7,6},{8,11},{9,8},{10,9... | collective-permute-start | bytes 196616 | tf_op jit(solution)/shard_map/ppermute | solution.py:377
  28.0 11.3 %collective-permute-start.5 = (f32[25,48,128]{2,1,0:T(8,128)}, f32[25,48,128]{2,1,0:T(8,128)S(1)}, u32[]{:S(2)}, u32[]{:S(2)}) collective-permute-start(f32[25,48,128]{2,1,0:T(8,128)} %collective-permute-done.3), channel_id=1, source_target_pairs={{4,8},{8,12},{5,9},{9,13},{6,10},{10,14},{7,11},{11,15},{20,24},{2... | collective-permute-start | bytes 1843208 | tf_op jit(solution)/shard_map/ppermute | solution.py:44
  30.1 39.0 %collective-permute-start.1 = (f32[4,48,512]{2,1,0:T(8,128)S(1)}, f32[4,48,512]{2,1,0:T(8,128)S(1)}, u32[]{:S(2)}, u32[]{:S(2)}) collective-permute-start(f32[4,48,512]{2,1,0:T(8,128)S(1)} %get-tuple-element.31), channel_id=1, source_target_pairs={{0,1},{1,2},{2,3},{4,5},{5,6},{6,7},{8,9},{9,10},{10,11},{12,13},{... | collective-permute-start | bytes 1179656 | tf_op jit(solution)/shard_map/ppermute | solution.py:16
  35.5 17.4 %collective-permute-start.6 = (f32[25,48,128]{2,1,0:T(8,128)}, f32[25,48,128]{2,1,0:T(8,128)S(1)}, u32[]{:S(2)}, u32[]{:S(2)}) collective-permute-start(f32[25,48,128]{2,1,0:T(8,128)} %collective-permute-done.4), channel_id=1, source_target_pairs={{4,0},{8,4},{5,1},{9,5},{6,2},{10,6},{7,3},{11,7},{20,16},{24,20},... | collective-permute-start | bytes 1843208 | tf_op jit(solution)/shard_map/ppermute | solution.py:45
  36.9 32.2 %collective-permute-start.2 = (f32[4,48,512]{2,1,0:T(8,128)S(1)}, f32[4,48,512]{2,1,0:T(8,128)}, u32[]{:S(2)}, u32[]{:S(2)}) collective-permute-start(f32[4,48,512]{2,1,0:T(8,128)S(1)} %get-tuple-element.30), channel_id=1, source_target_pairs={{1,0},{2,1},{3,2},{5,4},{6,5},{7,6},{9,8},{10,9},{11,10},{13,12},{... | collective-permute-start | bytes 1179656 | tf_op jit(solution)/shard_map/ppermute | solution.py:16
  39.3 17.2 %collective-permute-start.7 = (f32[25,48,128]{2,1,0:T(8,128)S(1)}, f32[25,48,128]{2,1,0:T(8,128)S(1)}, u32[]{:S(2)}, u32[]{:S(2)}) collective-permute-start(f32[25,48,128]{2,1,0:T(8,128)S(1)} %collective-permute-done.5), channel_id=1, source_target_pairs={{8,12},{9,13},{10,14},{11,15},{24,28},{25,29},{26,30},{27,31}} | collective-permute-start | bytes 1843208 | tf_op jit(solution)/shard_map/ppermute | solution.py:44
  52.8 16.2 %collective-permute-start.8 = (f32[25,48,128]{2,1,0:T(8,128)S(1)}, f32[25,48,128]{2,1,0:T(8,128)S(1)}, u32[]{:S(2)}, u32[]{:S(2)}) collective-permute-start(f32[25,48,128]{2,1,0:T(8,128)S(1)} %collective-permute-done.6), channel_id=1, source_target_pairs={{4,0},{5,1},{6,2},{7,3},{20,16},{21,17},{22,18},{23,19}} | collective-permute-start | bytes 1843208 | tf_op jit(solution)/shard_map/ppermute | solution.py:45
  69.1 1.6 %copy-start.1 = (f32[25,48,640]{2,1,0:T(8,128)}, f32[25,48,640]{2,1,0:T(8,128)S(1)}, u32[]{:S(2)}) copy-start(f32[25,48,640]{2,1,0:T(8,128)S(1)} %constant_dynamic-update-slice_fusion.wx_ref.refs_7_) | copy-start | bytes 9216004
  69.1 1.7 %copy-start.4 = (f32[4,48,512]{2,1,0:T(8,128)}, f32[4,48,512]{2,1,0:T(8,128)S(1)}, u32[]{:S(2)}) copy-start(f32[4,48,512]{2,1,0:T(8,128)S(1)} %collective-permute-done.1.qs_ref) | copy-start | bytes 1179652
  74.8 13.8 %collective-permute-start.12 = (f32[4,48,512]{2,1,0:T(8,128)}, f32[4,48,512]{2,1,0:T(8,128)S(1)}, u32[]{:S(2)}, u32[]{:S(2)}) collective-permute-start(f32[4,48,512]{2,1,0:T(8,128)} %get-tuple-element.26.hi_ref.refs_2_), channel_id=1, source_target_pairs={{0,1},{1,2},{2,3},{4,5},{5,6},{6,7},{8,9},{9,10},{10,11},{12,13},{... | collective-permute-start | bytes 1179656 | tf_op jit(solution)/shard_map/ppermute | solution.py:16
  76.7 11.9 %collective-permute-start.13 = (f32[4,48,512]{2,1,0:T(8,128)}, f32[4,48,512]{2,1,0:T(8,128)S(1)}, u32[]{:S(2)}, u32[]{:S(2)}) collective-permute-start(f32[4,48,512]{2,1,0:T(8,128)} %get-tuple-element.25.lo_ref.refs_1_), channel_id=1, source_target_pairs={{1,0},{2,1},{3,2},{5,4},{6,5},{7,6},{9,8},{10,9},{11,10},{13,12},{... | collective-permute-start | bytes 1179656 | tf_op jit(solution)/shard_map/ppermute | solution.py:16
  88.6 0.8 copy-start.2
  88.6 0.9 copy-start.3

commit v16 on v15

--- a/solution.py
+++ b/solution.py
@@ -178,7 +178,8 @@
     )(north_open, state, weather, emission)
 
 
-def edge_kernel(north_ref, lo_ref, hi_ref, lo_in_ref, hi_in_ref, qs_ref, qn_ref, wx_ref, src_ref, *outs):
+def edge_kernel(north_ref, lo_ref, hi_ref, lo_in_ref, hi_in_ref, qs_ref, qn_ref, *rest):
+    met_refs, src_ref, outs = rest[:8], rest[8], rest[9:]
     split = len(outs) == 2
     if not split:
         o_hbm, stage, sems = outs
@@ -190,11 +191,12 @@
     last = lat_rows - 1
     for top in (0, 1):
         a = top * last
-        u = wx_ref[a]
+        u_ref, v_ref, vm_ref, w_ref = met_refs[4 * top : 4 * top + 4]
+        u = u_ref[0]
         uw = pltpu.roll(u, 1, 1)
-        v = wx_ref[lat_rows + a] * north_ref[a]
-        vm = wx_ref[3 * lat_rows] if top == 0 else wx_ref[lat_rows + a - 1]
-        w = wx_ref[2 * lat_rows + a]
+        v = v_ref[0] * north_ref[a]
+        vm = vm_ref[0]
+        w = w_ref[0]
         w_up = jnp.where(not_top, w, 0.0)
         w_down = jnp.where(not_bottom, pltpu.roll(w, 1, 0), 0.0)
         c_self = (
@@ -244,8 +246,12 @@
     lat_rows = emission.shape[1]
     vmem = pl.BlockSpec(memory_space=pltpu.VMEM)
     in_specs = [pl.BlockSpec(memory_space=pltpu.SMEM)] + [vmem] * 6
-    in_specs += [pl.BlockSpec(weather.shape[:2] + (lon,), lambda i: (0, 0, 0)), vmem]
-    args = [north_open, *rows, south, north, weather, emission]
+    last = lat_rows - 1
+    met_rows = []
+    for a, below in ((0, 3 * lat_rows), (last, lat_rows + last - 1)):
+        met_rows += [a, lat_rows + a, below, 2 * lat_rows + a]
+    in_specs += [pl.BlockSpec((1, levels, lon), lambda i, r=r: (r, 0, 0)) for r in met_rows] + [vmem]
+    args = [north_open, *rows, south, north] + [weather] * len(met_rows) + [emission]
     edge = pl.BlockSpec((tracers, levels, lon), lambda i: (0, 0, 0))
     scratch = []
     if base is None:
@@ -260,7 +266,7 @@
         out_shape = jax.ShapeDtypeStruct(base.shape, base.dtype)
         aliases = {len(args) - 1: 0}
         scratch = [pltpu.VMEM((2, tracers, 1, levels, lon), jnp.float32), pltpu.SemaphoreType.DMA((2,))]
-        kernel = lambda *refs: edge_kernel(*refs[:9], *refs[10:])
+        kernel = lambda *refs: edge_kernel(*refs[:16], *refs[17:])
     grid_spec = pltpu.PrefetchScalarGridSpec(
         num_scalar_prefetch=0, grid=(1,), in_specs=in_specs, out_specs=out_specs, scratch_shapes=scratch
     )

time: 94.4 us -> 93.4 us (0.989)
  Pallas kernels: 18.7 us -> 17.5 us
    pallas_call x2, Pallas kernels: 8.05 us -> 6.84 us  [edge_step(): pl.pallas_call(kernel, grid_spec=grid_spec, out_shape=out_shape, input_ou...]
    unnamed x20 -> x22, local copies, waits for them, and re-layouts: 3.23 us -> 3.35 us
where the time goes in v16:
time: 93.4 us; the launch traced here: 92.6 us
  waiting for transfers between devices  33.7 us (36%)
  starting transfers between devices  23.7 us (25%)
  Pallas kernels  17.5 us (19%)
  local copies, waits for them, and re-layouts  12.3 us (13%)
  matrix products  3.94 us (4%)
  between operations  0.97 us (1%)
    ppermute x3, waiting for transfers between devices, relay_gather(): lax.ppermute(left, axis, [(j, j - 1) for j in range(1, count - r + 1)])  27.9 us
    ppermute x5, starting transfers between devices, passed_along(): return lax.ppermute(value, axis, pairs)  13.7 us
    pallas_call x1, Pallas kernels, fused_steps(): pl.pallas_call(fused_kernel, grid_spec=grid_spec, out_shape=[jax.ShapeDty...  8.67 us
    pallas_call x2, Pallas kernels, edge_step(): pl.pallas_call(kernel, grid_spec=grid_spec, out_shape=out_shape, input_ou...  6.84 us
    ppermute x3, waiting for transfers between devices, relay_gather(): lax.ppermute(right, axis, [(i, i + 1) for i in range(r - 1, count - 1)])  5.7 us
    ppermute x3, starting transfers between devices, relay_gather(): lax.ppermute(right, axis, [(i, i + 1) for i in range(r - 1, count - 1)])  5.41 us
    ppermute x3, starting transfers between devices, relay_gather(): lax.ppermute(left, axis, [(j, j - 1) for j in range(1, count - r + 1)])  3.84 us
    unnamed x22, local copies, waits for them, and re-layouts  3.35 us
  transfers between devices with their start and end apart: 14, of which 4 were waited for; matrix products, arithmetic and copies ran while one was open for 14% of the time, Pallas kernels for 9%

profile of v16, /device:TPU:1, one launch (start us, length us, event | category | flops | bytes accessed | tf_op | source)
XLA Modules:
  0.0 92.6 jit_solution(15321481333532520554)
XLA Ops:
  0.7 0.8 slice.21
  1.4 4.5 %collective-permute-start = (f32[1,48,128]{2,1,0:T(8,128)S(1)}, f32[1,48,128]{2,1,0:T(8,128)S(1)}, u32[]{:S(2)}, u32[]{:S(2)}) collective-permute-start(f32[1,48,128]{2,1,0:T(8,128)S(1)} %slice.21), channel_id=1, source_target_pairs={{0,1},{1,2},{2,3},{4,5},{5,6},{6,7},{8,9},{9,10},{10,11},{12,13},{... | collective-permute-start | bytes 73736 | tf_op jit(solution)/shard_map/ppermute | solution.py:16
  5.9 0.7 constant_dynamic-slice_fusion.4
  6.8 1.7 %convolution_bitcast_fusion.3 = f32[4,8,512]{2,1,0:T(8,128)} fusion(f32[8,8,1]{1,0,2:T(8,128)S(1)} %bitcast.56, f32[4,8,512]{2,1,0:T(8,128)} %param.10), kind=kOutput, calls=%fused_computation.3 | convolution fusion | flops 1572864 | bytes 131328 | tf_op jit(solution)/shard_map/jm,kmn->kjn/dot_general | solution.py:371
  9.7 2.0 %shard_map.104 = f32[25,48,128]{2,1,0:T(8,128)} custom-call(f32[8,48,128]{2,1,0:T(8,128)} %refs_0_, f32[8,48,128]{2,1,0:T(8,128)} %refs_1_, f32[8,48,128]{2,1,0:T(8,128)} %refs_2_, f32[1,48,128]{2,1,0:T(8,128)} %copy-done.8), custom_call_target="tpu_custom_call" | custom-call | tf_op jit(solution)/shard_map/pallas_call | solution.py:30
  11.7 4.0 %collective-permute-start.3 = (f32[25,48,128]{2,1,0:T(8,128)}, f32[25,48,128]{2,1,0:T(8,128)}, u32[]{:S(2)}, u32[]{:S(2)}) collective-permute-start(f32[25,48,128]{2,1,0:T(8,128)} %shard_map.104), channel_id=1, source_target_pairs={{0,4},{4,8},{8,12},{1,5},{5,9},{9,13},{2,6},{6,10},{10,14},{3,7},{... | collective-permute-start | bytes 1843208 | tf_op jit(solution)/shard_map/ppermute | solution.py:44
  15.7 2.5 %slice_bitcast_fusion.2 = (f32[4,48,512]{2,1,0:T(8,128)}, f32[4,48,512]{2,1,0:T(8,128)}, f32[4,48,512]{2,1,0:T(8,128)}, f32[4,48,512]{2,1,0:T(8,128)}) fusion(f32[4,8,48,512]{3,2,1,0:T(8,128)} %q_ref.1), kind=kLoop, calls=%fused_computation.7 | loop fusion | bytes 3145728 | tf_op jit(solution)/shard_map/squeeze | solution.py:394
  18.2 1.3 %collective-permute-start.4 = (f32[25,48,128]{2,1,0:T(8,128)}, f32[25,48,128]{2,1,0:T(8,128)}, u32[]{:S(2)}, u32[]{:S(2)}) collective-permute-start(f32[25,48,128]{2,1,0:T(8,128)} %shard_map.104), channel_id=1, source_target_pairs={{4,0},{8,4},{12,8},{5,1},{9,5},{13,9},{6,2},{10,6},{14,10},{7,3},{... | collective-permute-start | bytes 1843208 | tf_op jit(solution)/shard_map/ppermute | solution.py:45
  19.5 0.9 fusion
  21.2 1.2 %slice_bitcast_fusion = (f32[4,48,512]{2,1,0:T(8,128)S(1)}, f32[4,48,512]{2,1,0:T(8,128)S(1)}) fusion(f32[4,8,48,512]{3,2,1,0:T(8,128)} %q_ref.1), kind=kLoop, calls=%fused_computation.4 | loop fusion | bytes 1572864 | tf_op jit(solution)/shard_map/squeeze | solution.py:380
  22.3 5.7 %collective-permute-done.3 = f32[25,48,128]{2,1,0:T(8,128)} collective-permute-done((f32[25,48,128]{2,1,0:T(8,128)}, f32[25,48,128]{2,1,0:T(8,128)}, u32[]{:S(2)}, u32[]{:S(2)}) %collective-permute-start.3) | collective-permute-done | bytes 614432 | tf_op jit(solution)/shard_map/ppermute | solution.py:44
  28.0 0.7 collective-permute-start.5
  28.9 1.1 %constant_dynamic-update-slice_fusion.6 = f32[25,48,640]{2,1,0:T(8,128)S(1)} fusion(f32[25,48,640]{2,1,0:T(8,128)S(1)} %broadcast_in_dim.2, f32[25,48,128]{2,1,0:T(8,128)} %shard_map.104, s32[]{:T(128)S(6)} %select_n.70), kind=kLoop, calls=%fused_computation.25 | loop fusion | bytes 1228804 | tf_op jit(solution)/shard_map/dynamic_update_slice | solution.py:41
  30.1 1.9 %collective-permute-start.1 = (f32[4,48,512]{2,1,0:T(8,128)S(1)}, f32[4,48,512]{2,1,0:T(8,128)S(1)}, u32[]{:S(2)}, u32[]{:S(2)}) collective-permute-start(f32[4,48,512]{2,1,0:T(8,128)S(1)} %get-tuple-element.31), channel_id=1, source_target_pairs={{0,1},{1,2},{2,3},{4,5},{5,6},{6,7},{8,9},{9,10},{10,11},{12,13},{... | collective-permute-start | bytes 1179656 | tf_op jit(solution)/shard_map/ppermute | solution.py:16
  32.0 3.4 %collective-permute-done.4 = f32[25,48,128]{2,1,0:T(8,128)} collective-permute-done((f32[25,48,128]{2,1,0:T(8,128)}, f32[25,48,128]{2,1,0:T(8,128)}, u32[]{:S(2)}, u32[]{:S(2)}) %collective-permute-start.4) | collective-permute-done | bytes 614432 | tf_op jit(solution)/shard_map/ppermute | solution.py:45
  35.5 1.3 %collective-permute-start.6 = (f32[25,48,128]{2,1,0:T(8,128)}, f32[25,48,128]{2,1,0:T(8,128)S(1)}, u32[]{:S(2)}, u32[]{:S(2)}) collective-permute-start(f32[25,48,128]{2,1,0:T(8,128)} %collective-permute-done.4), channel_id=1, source_target_pairs={{4,0},{8,4},{5,1},{9,5},{6,2},{10,6},{7,3},{11,7},{20,16},{24,20},... | collective-permute-start | bytes 1843208 | tf_op jit(solution)/shard_map/ppermute | solution.py:45
  37.0 2.1 %collective-permute-start.2 = (f32[4,48,512]{2,1,0:T(8,128)S(1)}, f32[4,48,512]{2,1,0:T(8,128)S(1)}, u32[]{:S(2)}, u32[]{:S(2)}) collective-permute-start(f32[4,48,512]{2,1,0:T(8,128)S(1)} %get-tuple-element.30), channel_id=1, source_target_pairs={{1,0},{2,1},{3,2},{5,4},{6,5},{7,6},{9,8},{10,9},{11,10},{13,12},{... | collective-permute-start | bytes 1179656 | tf_op jit(solution)/shard_map/ppermute | solution.py:16
  39.3 0.7 collective-permute-start.7
  40.1 0.8 bitcast_multiply_fusion.rest_8_.src_ref.refs_15_
  40.9 12.0 %collective-permute-done.6 = f32[25,48,128]{2,1,0:T(8,128)S(1)} collective-permute-done((f32[25,48,128]{2,1,0:T(8,128)}, f32[25,48,128]{2,1,0:T(8,128)S(1)}, u32[]{:S(2)}, u32[]{:S(2)}) %collective-permute-start.6) | collective-permute-done | bytes 614432 | tf_op jit(solution)/shard_map/ppermute | solution.py:45
  52.9 1.3 %collective-permute-start.8 = (f32[25,48,128]{2,1,0:T(8,128)S(1)}, f32[25,48,128]{2,1,0:T(8,128)S(1)}, u32[]{:S(2)}, u32[]{:S(2)}) collective-permute-start(f32[25,48,128]{2,1,0:T(8,128)S(1)} %collective-permute-done.6), channel_id=1, source_target_pairs={{4,0},{5,1},{6,2},{7,3},{20,16},{21,17},{22,18},{23,19}} | collective-permute-start | bytes 1843208 | tf_op jit(solution)/shard_map/ppermute | solution.py:45
  54.2 1.1 %constant_dynamic-update-slice_fusion.5 = f32[25,48,640]{2,1,0:T(8,128)S(1)} fusion(f32[25,48,640]{2,1,0:T(8,128)S(1)} %constant_dynamic-update-slice_fusion.6, f32[25,48,128]{2,1,0:T(8,128)} %collective-permute-done.3, s32[]{:T(128)S(6)} %select_n.72), kind=kLoop, calls=%fused_computation.24 | loop fusion | bytes 1228804 | tf_op jit(solution)/shard_map/dynamic_update_slice | solution.py:47
  55.3 1.1 %constant_dynamic-update-slice_fusion.4 = f32[25,48,640]{2,1,0:T(8,128)S(1)} fusion(f32[25,48,640]{2,1,0:T(8,128)S(1)} %constant_dynamic-update-slice_fusion.5, f32[25,48,128]{2,1,0:T(8,128)} %collective-permute-done.4, s32[]{:T(128)S(6)} %select_n.74), kind=kLoop, calls=%fused_computation.23 | loop fusion | bytes 1228804 | tf_op jit(solution)/shard_map/dynamic_update_slice | solution.py:49
  56.6 12.5 %collective-permute-done.8 = f32[25,48,128]{2,1,0:T(8,128)S(1)} collective-permute-done((f32[25,48,128]{2,1,0:T(8,128)S(1)}, f32[25,48,128]{2,1,0:T(8,128)S(1)}, u32[]{:S(2)}, u32[]{:S(2)}) %collective-permute-start.8) | collective-permute-done | bytes 614432 | tf_op jit(solution)/shard_map/ppermute | solution.py:45
  69.2 0.8 copy-done.5
  70.0 0.9 copy-done.1
  71.0 3.4 %shard_map.105 = (f32[4,48,512]{2,1,0:T(8,128)}, f32[4,48,512]{2,1,0:T(8,128)}) custom-call(f32[8]{0:T(128)} %compare_convert_fusion.north_ref.refs_0_, f32[4,48,512]{2,1,0:T(8,128)} %get-tuple-element.35.lo_ref, f32[4,48,512]{2,1,0:T(8,128)} %get-tuple-element.34.hi_ref, f32[4,48,512]{2,1,0:T(8,128)} %get-tuple-element.33.lo_in_ref, ...), custom_call_target="tpu_custom_call" | custom-call | tf_op jit(solution)/shard_map/pallas_call | solution.py:273
  74.4 1.9 %collective-permute-start.12 = (f32[4,48,512]{2,1,0:T(8,128)}, f32[4,48,512]{2,1,0:T(8,128)S(1)}, u32[]{:S(2)}, u32[]{:S(2)}) collective-permute-start(f32[4,48,512]{2,1,0:T(8,128)} %get-tuple-element.26.hi_ref.refs_2_), channel_id=1, source_target_pairs={{0,1},{1,2},{2,3},{4,5},{5,6},{6,7},{8,9},{9,10},{10,11},{12,13},{... | collective-permute-start | bytes 1179656 | tf_op jit(solution)/shard_map/ppermute | solution.py:16
  76.3 3.2 %collective-permute-start.13 = (f32[4,48,512]{2,1,0:T(8,128)}, f32[4,48,512]{2,1,0:T(8,128)S(1)}, u32[]{:S(2)}, u32[]{:S(2)}) collective-permute-start(f32[4,48,512]{2,1,0:T(8,128)} %get-tuple-element.25.lo_ref.refs_1_), channel_id=1, source_target_pairs={{1,0},{2,1},{3,2},{5,4},{6,5},{7,6},{9,8},{10,9},{11,10},{13,12},{... | collective-permute-start | bytes 1179656 | tf_op jit(solution)/shard_map/ppermute | solution.py:16
  79.5 8.7 %shard_map.106 = (f32[4,8,48,512]{3,2,1,0:T(8,128)}, f32[4,48,512]{2,1,0:T(8,128)}, f32[4,48,512]{2,1,0:T(8,128)}) custom-call(f32[8]{0:T(128)} %compare_convert_fusion.north_ref.refs_0_, f32[4,8,48,512]{3,2,1,0:T(8,128)} %q_ref.1, f32[4,48,512]{2,1,0:T(8,128)} %get-tuple-element.25.lo_ref.refs_1_, f32[4,48,512]{2,1,0:T(8,128)} %get-tuple-element.26.hi_ref.refs_2_, ...), custom_call_target="tpu_custom_call" | custom-call | tf_op jit(solution)/shard_map/pallas_call | solution.py:338
  88.2 0.7 copy-done.2
  89.1 3.5 %shard_map.107 = f32[4,8,48,512]{3,2,1,0:T(8,128)} custom-call(f32[8]{0:T(128)} %compare_convert_fusion.north_ref.refs_0_, f32[4,48,512]{2,1,0:T(8,128)} %get-tuple-element.25.lo_ref.refs_1_, f32[4,48,512]{2,1,0:T(8,128)} %get-tuple-element.26.hi_ref.refs_2_, f32[4,48,512]{2,1,0:T(8,128)} %get-tuple-element.27.refs_3_, ...), custom_call_target="tpu_custom_call", output_to_operand_aliasing={{}: (16, {})} | custom-call | tf_op jit(solution)/shard_map/pallas_call | solution.py:273
  (43 shorter events, 3.3 us)
Async XLA Ops:
  0.6 6.0 %copy-start = (f32[8,8,8]{2,1,0:T(8,128)S(1)}, f32[8,8,8]{2,1,0:T(8,128)}, u32[]{:S(2)}) copy-start(f32[8,8,8]{2,1,0:T(8,128)} %param.11) | copy-start | bytes 6148
  0.6 18.9 %copy-start.9 = (s32[8,512]{1,0:T(8,128)S(1)}, s32[8,512]{1,0:T(8,128)}, u32[]{:S(2)}) copy-start(s32[8,512]{1,0:T(8,128)} %param.13) | copy-start | bytes 49156
  0.7 18.9 %copy-start.10 = (f32[4,22]{1,0:T(4,128)S(1)}, f32[4,22]{1,0:T(4,128)}, u32[]{:S(2)}) copy-start(f32[4,22]{1,0:T(4,128)} %param.14) | copy-start | bytes 1060
  1.4 7.7 %collective-permute-start = (f32[1,48,128]{2,1,0:T(8,128)S(1)}, f32[1,48,128]{2,1,0:T(8,128)S(1)}, u32[]{:S(2)}, u32[]{:S(2)}) collective-permute-start(f32[1,48,128]{2,1,0:T(8,128)S(1)} %slice.21), channel_id=1, source_target_pairs={{0,1},{1,2},{2,3},{4,5},{5,6},{6,7},{8,9},{9,10},{10,11},{12,13},{... | collective-permute-start | bytes 73736 | tf_op jit(solution)/shard_map/ppermute | solution.py:16
  9.1 0.6 copy-start.8
  11.7 16.4 %collective-permute-start.3 = (f32[25,48,128]{2,1,0:T(8,128)}, f32[25,48,128]{2,1,0:T(8,128)}, u32[]{:S(2)}, u32[]{:S(2)}) collective-permute-start(f32[25,48,128]{2,1,0:T(8,128)} %shard_map.104), channel_id=1, source_target_pairs={{0,4},{4,8},{8,12},{1,5},{5,9},{9,13},{2,6},{6,10},{10,14},{3,7},{... | collective-permute-start | bytes 1843208 | tf_op jit(solution)/shard_map/ppermute | solution.py:44
  18.2 17.3 %collective-permute-start.4 = (f32[25,48,128]{2,1,0:T(8,128)}, f32[25,48,128]{2,1,0:T(8,128)}, u32[]{:S(2)}, u32[]{:S(2)}) collective-permute-start(f32[25,48,128]{2,1,0:T(8,128)} %shard_map.104), channel_id=1, source_target_pairs={{4,0},{8,4},{12,8},{5,1},{9,5},{13,9},{6,2},{10,6},{14,10},{7,3},{... | collective-permute-start | bytes 1843208 | tf_op jit(solution)/shard_map/ppermute | solution.py:45
  20.4 19.6 %copy-start.6 = (f32[4,8,512]{2,1,0:T(8,128)S(1)}, f32[4,8,512]{2,1,0:T(8,128)}, u32[]{:S(2)}) copy-start(f32[4,8,512]{2,1,0:T(8,128)} %convolution_bitcast_fusion.3) | copy-start | bytes 196612
  20.4 19.6 %copy-start.7 = (f32[8,512,4]{1,2,0:T(4,128)S(1)}, f32[8,512,4]{1,2,0:T(4,128)}, u32[]{:S(2)}) copy-start(f32[8,512,4]{1,2,0:T(4,128)} %fusion) | copy-start | bytes 196612
  20.4 9.7 %collective-permute-start.10 = (f32[4,8,512]{2,1,0:T(8,128)}, f32[4,8,512]{2,1,0:T(8,128)S(1)}, u32[]{:S(2)}, u32[]{:S(2)}) collective-permute-start(f32[4,8,512]{2,1,0:T(8,128)} %param.10), channel_id=1, source_target_pairs={{0,2},{1,3},{2,0},{3,1},{4,6},{5,7},{6,4},{7,5},{8,10},{9,11},{10,... | collective-permute-start | bytes 196616 | tf_op jit(solution)/shard_map/ppermute | solution.py:383
  20.4 16.5 %collective-permute-start.9 = (f32[4,8,512]{2,1,0:T(8,128)}, f32[4,8,512]{2,1,0:T(8,128)S(1)}, u32[]{:S(2)}, u32[]{:S(2)}) collective-permute-start(f32[4,8,512]{2,1,0:T(8,128)} %param.10), channel_id=1, source_target_pairs={{0,1},{1,2},{2,3},{3,0},{4,5},{5,6},{6,7},{7,4},{8,9},{9,10},{10,1... | collective-permute-start | bytes 196616 | tf_op jit(solution)/shard_map/ppermute | solution.py:383
  21.1 19.0 %collective-permute-start.11 = (f32[4,8,512]{2,1,0:T(8,128)}, f32[4,8,512]{2,1,0:T(8,128)S(1)}, u32[]{:S(2)}, u32[]{:S(2)}) collective-permute-start(f32[4,8,512]{2,1,0:T(8,128)} %param.10), channel_id=1, source_target_pairs={{0,3},{1,0},{2,1},{3,2},{4,7},{5,4},{6,5},{7,6},{8,11},{9,8},{10,9... | collective-permute-start | bytes 196616 | tf_op jit(solution)/shard_map/ppermute | solution.py:383
  28.0 11.3 %collective-permute-start.5 = (f32[25,48,128]{2,1,0:T(8,128)}, f32[25,48,128]{2,1,0:T(8,128)S(1)}, u32[]{:S(2)}, u32[]{:S(2)}) collective-permute-start(f32[25,48,128]{2,1,0:T(8,128)} %collective-permute-done.3), channel_id=1, source_target_pairs={{4,8},{8,12},{5,9},{9,13},{6,10},{10,14},{7,11},{11,15},{20,24},{2... | collective-permute-start | bytes 1843208 | tf_op jit(solution)/shard_map/ppermute | solution.py:44
  30.1 39.1 %collective-permute-start.1 = (f32[4,48,512]{2,1,0:T(8,128)S(1)}, f32[4,48,512]{2,1,0:T(8,128)S(1)}, u32[]{:S(2)}, u32[]{:S(2)}) collective-permute-start(f32[4,48,512]{2,1,0:T(8,128)S(1)} %get-tuple-element.31), channel_id=1, source_target_pairs={{0,1},{1,2},{2,3},{4,5},{5,6},{6,7},{8,9},{9,10},{10,11},{12,13},{... | collective-permute-start | bytes 1179656 | tf_op jit(solution)/shard_map/ppermute | solution.py:16
  35.5 17.4 %collective-permute-start.6 = (f32[25,48,128]{2,1,0:T(8,128)}, f32[25,48,128]{2,1,0:T(8,128)S(1)}, u32[]{:S(2)}, u32[]{:S(2)}) collective-permute-start(f32[25,48,128]{2,1,0:T(8,128)} %collective-permute-done.4), channel_id=1, source_target_pairs={{4,0},{8,4},{5,1},{9,5},{6,2},{10,6},{7,3},{11,7},{20,16},{24,20},... | collective-permute-start | bytes 1843208 | tf_op jit(solution)/shard_map/ppermute | solution.py:45
  37.0 32.2 %collective-permute-start.2 = (f32[4,48,512]{2,1,0:T(8,128)S(1)}, f32[4,48,512]{2,1,0:T(8,128)S(1)}, u32[]{:S(2)}, u32[]{:S(2)}) collective-permute-start(f32[4,48,512]{2,1,0:T(8,128)S(1)} %get-tuple-element.30), channel_id=1, source_target_pairs={{1,0},{2,1},{3,2},{5,4},{6,5},{7,6},{9,8},{10,9},{11,10},{13,12},{... | collective-permute-start | bytes 1179656 | tf_op jit(solution)/shard_map/ppermute | solution.py:16
  39.3 17.2 %collective-permute-start.7 = (f32[25,48,128]{2,1,0:T(8,128)S(1)}, f32[25,48,128]{2,1,0:T(8,128)S(1)}, u32[]{:S(2)}, u32[]{:S(2)}) collective-permute-start(f32[25,48,128]{2,1,0:T(8,128)S(1)} %collective-permute-done.5), channel_id=1, source_target_pairs={{8,12},{9,13},{10,14},{11,15},{24,28},{25,29},{26,30},{27,31}} | collective-permute-start | bytes 1843208 | tf_op jit(solution)/shard_map/ppermute | solution.py:44
  52.9 16.2 %collective-permute-start.8 = (f32[25,48,128]{2,1,0:T(8,128)S(1)}, f32[25,48,128]{2,1,0:T(8,128)S(1)}, u32[]{:S(2)}, u32[]{:S(2)}) collective-permute-start(f32[25,48,128]{2,1,0:T(8,128)S(1)} %collective-permute-done.6), channel_id=1, source_target_pairs={{4,0},{5,1},{6,2},{7,3},{20,16},{21,17},{22,18},{23,19}} | collective-permute-start | bytes 1843208 | tf_op jit(solution)/shard_map/ppermute | solution.py:45
  69.1 1.7 %copy-start.1 = (f32[25,48,640]{2,1,0:T(8,128)}, f32[25,48,640]{2,1,0:T(8,128)S(1)}, u32[]{:S(2)}) copy-start(f32[25,48,640]{2,1,0:T(8,128)S(1)} %constant_dynamic-update-slice_fusion.rest_0_.rest_1_.rest_2_.rest_3_.rest_4_.rest_5_.rest_6_.rest_7_.wx_ref.refs_7_.refs_8_.refs_9_.refs_10_.refs_11_.refs_12_.refs_13_.refs_14_) | copy-start | bytes 9216004
  69.2 1.9 %copy-start.4 = (f32[4,48,512]{2,1,0:T(8,128)}, f32[4,48,512]{2,1,0:T(8,128)S(1)}, u32[]{:S(2)}) copy-start(f32[4,48,512]{2,1,0:T(8,128)S(1)} %collective-permute-done.1.qs_ref) | copy-start | bytes 1179652
  69.2 0.8 copy-start.5
  74.4 13.8 %collective-permute-start.12 = (f32[4,48,512]{2,1,0:T(8,128)}, f32[4,48,512]{2,1,0:T(8,128)S(1)}, u32[]{:S(2)}, u32[]{:S(2)}) collective-permute-start(f32[4,48,512]{2,1,0:T(8,128)} %get-tuple-element.26.hi_ref.refs_2_), channel_id=1, source_target_pairs={{0,1},{1,2},{2,3},{4,5},{5,6},{6,7},{8,9},{9,10},{10,11},{12,13},{... | collective-permute-start | bytes 1179656 | tf_op jit(solution)/shard_map/ppermute | solution.py:16
  76.3 11.9 %collective-permute-start.13 = (f32[4,48,512]{2,1,0:T(8,128)}, f32[4,48,512]{2,1,0:T(8,128)S(1)}, u32[]{:S(2)}, u32[]{:S(2)}) collective-permute-start(f32[4,48,512]{2,1,0:T(8,128)} %get-tuple-element.25.lo_ref.refs_1_), channel_id=1, source_target_pairs={{1,0},{2,1},{3,2},{5,4},{6,5},{7,6},{9,8},{10,9},{11,10},{13,12},{... | collective-permute-start | bytes 1179656 | tf_op jit(solution)/shard_map/ppermute | solution.py:16
  88.2 0.8 copy-start.2
  88.2 0.9 copy-start.3

commit v17 on v16

--- a/solution.py
+++ b/solution.py
@@ -50,13 +50,15 @@
     return buf
 
 
-def fill_coefficients(north_ref, wx_ref, coef_ref):
+def fill_coefficients(north_ref, wx_ref, coef_ref, ready=None):
     lat_rows = coef_ref.shape[1]
     levels, lon = coef_ref.shape[2], coef_ref.shape[3]
     level = lax.broadcasted_iota(jnp.int32, (levels, lon), 0)
     not_top = level < levels - 1
     not_bottom = level > 0
     for a in range(lat_rows):
+        if ready is not None:
+            ready(a)
         u = wx_ref[a]
         uw = pltpu.roll(u, 1, 1)
         v = wx_ref[lat_rows + a] * north_ref[a]
@@ -278,13 +280,32 @@
     )(*args)
 
 
-def fused_kernel(north_ref, q_ref, lo_ref, hi_ref, wx_ref, src_ref, o_ref, lo_in_ref, hi_in_ref, coef_ref, mid_ref):
+def fused_kernel(north_ref, q_ref, lo_ref, hi_ref, wx_hbm, src_ref, o_ref, lo_in_ref, hi_in_ref, coef_ref, mid_ref, wx_ref, sems):
     lat_rows = q_ref.shape[1]
     levels, lon = q_ref.shape[2], q_ref.shape[3]
 
     @pl.when(pl.program_id(0) == 0)
     def _():
-        fill_coefficients(north_ref, wx_ref, coef_ref)
+        copies = [
+            pltpu.make_async_copy(wx_hbm.at[pl.ds(r, 1), :, pl.ds(0, lon)], wx_ref.at[pl.ds(r, 1)], sems.at[r])
+            for r in range(wx_ref.shape[0])
+        ]
+        order = []
+        for a in range(lat_rows):
+            for r in (a, lat_rows + a, 2 * lat_rows + a, 3 * lat_rows if a == 0 else lat_rows + a - 1):
+                if r not in order:
+                    order.append(r)
+        for r in order:
+            copies[r].start()
+        waited = set()
+
+        def ready(a):
+            for r in (a, lat_rows + a, 2 * lat_rows + a, 3 * lat_rows if a == 0 else lat_rows + a - 1):
+                if r not in waited:
+                    copies[r].wait()
+                    waited.add(r)
+
+        fill_coefficients(north_ref, wx_ref, coef_ref, ready)
 
     def stencil(a, qa, qm, qp):
         result = (
@@ -326,13 +347,15 @@
             row,
             edge,
             edge,
-            pl.BlockSpec(weather.shape[:2] + (lon,), lambda k: (0, 0, 0)),
+            pl.BlockSpec(memory_space=pl.ANY),
             pl.BlockSpec((1, lat_rows, lon), lambda k: (k, 0, 0)),
         ],
         out_specs=[row, edge, edge],
         scratch_shapes=[
             pltpu.VMEM((7, lat_rows, levels, lon), jnp.float32),
             pltpu.VMEM((lat_rows, levels, lon), jnp.float32),
+            pltpu.VMEM((weather.shape[0], levels, lon), jnp.float32),
+            pltpu.SemaphoreType.DMA((weather.shape[0],)),
         ],
     )
     return pl.pallas_call(

time: 93.4 us -> 94.2 us (level)
  transfers between devices with their start and end apart: 14 -> 14, of which waited for: 4 -> 4; matrix products, arithmetic and copies ran while one was open for 14% -> 14% of each run, Pallas kernels for 9% -> 10%
where the time goes in v17:
time: 94.2 us; the launch traced here: 93.4 us
  waiting for transfers between devices  33.7 us (36%)
  starting transfers between devices  23.7 us (25%)
  Pallas kernels  18.3 us (19%)
  local copies, waits for them, and re-layouts  12.3 us (13%)
  matrix products  3.94 us (4%)
  between operations  0.98 us (1%)
    ppermute x3, waiting for transfers between devices, relay_gather(): lax.ppermute(left, axis, [(j, j - 1) for j in range(1, count - r + 1)])  27.9 us
    ppermute x5, starting transfers between devices, passed_along(): return lax.ppermute(value, axis, pairs)  13.7 us
    pallas_call x1, Pallas kernels, fused_steps(): pl.pallas_call(fused_kernel, grid_spec=grid_spec, out_shape=[jax.ShapeDty...  9.45 us
    pallas_call x2, Pallas kernels, edge_step(): pl.pallas_call(kernel, grid_spec=grid_spec, out_shape=out_shape, input_ou...  6.84 us
    ppermute x3, waiting for transfers between devices, relay_gather(): lax.ppermute(right, axis, [(i, i + 1) for i in range(r - 1, count - 1)])  5.7 us
    ppermute x3, starting transfers between devices, relay_gather(): lax.ppermute(right, axis, [(i, i + 1) for i in range(r - 1, count - 1)])  5.41 us
    ppermute x3, starting transfers between devices, relay_gather(): lax.ppermute(left, axis, [(j, j - 1) for j in range(1, count - r + 1)])  3.84 us
    unnamed x22, local copies, waits for them, and re-layouts  3.35 us
  transfers between devices with their start and end apart: 14, of which 4 were waited for; matrix products, arithmetic and copies ran while one was open for 14% of the time, Pallas kernels for 10%

profile of v17, /device:TPU:1, one launch (start us, length us, event | category | flops | bytes accessed | tf_op | source)
XLA Modules:
  0.0 93.4 jit_solution(11014001572365710453)
XLA Ops:
  0.7 0.8 slice.21
  1.4 4.5 %collective-permute-start = (f32[1,48,128]{2,1,0:T(8,128)S(1)}, f32[1,48,128]{2,1,0:T(8,128)S(1)}, u32[]{:S(2)}, u32[]{:S(2)}) collective-permute-start(f32[1,48,128]{2,1,0:T(8,128)S(1)} %slice.21), channel_id=1, source_target_pairs={{0,1},{1,2},{2,3},{4,5},{5,6},{6,7},{8,9},{9,10},{10,11},{12,13},{... | collective-permute-start | bytes 73736 | tf_op jit(solution)/shard_map/ppermute | solution.py:16
  5.9 0.7 constant_dynamic-slice_fusion.4
  6.8 1.7 %convolution_bitcast_fusion.3 = f32[4,8,512]{2,1,0:T(8,128)} fusion(f32[8,8,1]{1,0,2:T(8,128)S(1)} %bitcast.56, f32[4,8,512]{2,1,0:T(8,128)} %param.10), kind=kOutput, calls=%fused_computation.3 | convolution fusion | flops 1572864 | bytes 131328 | tf_op jit(solution)/shard_map/jm,kmn->kjn/dot_general | solution.py:394
  9.7 2.0 %shard_map.104 = f32[25,48,128]{2,1,0:T(8,128)} custom-call(f32[8,48,128]{2,1,0:T(8,128)} %refs_0_, f32[8,48,128]{2,1,0:T(8,128)} %refs_1_, f32[8,48,128]{2,1,0:T(8,128)} %refs_2_, f32[1,48,128]{2,1,0:T(8,128)} %copy-done.8), custom_call_target="tpu_custom_call" | custom-call | tf_op jit(solution)/shard_map/pallas_call | solution.py:30
  11.7 4.0 %collective-permute-start.3 = (f32[25,48,128]{2,1,0:T(8,128)}, f32[25,48,128]{2,1,0:T(8,128)}, u32[]{:S(2)}, u32[]{:S(2)}) collective-permute-start(f32[25,48,128]{2,1,0:T(8,128)} %shard_map.104), channel_id=1, source_target_pairs={{0,4},{4,8},{8,12},{1,5},{5,9},{9,13},{2,6},{6,10},{10,14},{3,7},{... | collective-permute-start | bytes 1843208 | tf_op jit(solution)/shard_map/ppermute | solution.py:44
  15.7 2.5 %slice_bitcast_fusion.2 = (f32[4,48,512]{2,1,0:T(8,128)}, f32[4,48,512]{2,1,0:T(8,128)}, f32[4,48,512]{2,1,0:T(8,128)}, f32[4,48,512]{2,1,0:T(8,128)}) fusion(f32[4,8,48,512]{3,2,1,0:T(8,128)} %q_ref.1), kind=kLoop, calls=%fused_computation.7 | loop fusion | bytes 3145728 | tf_op jit(solution)/shard_map/squeeze | solution.py:417
  18.2 1.3 %collective-permute-start.4 = (f32[25,48,128]{2,1,0:T(8,128)}, f32[25,48,128]{2,1,0:T(8,128)}, u32[]{:S(2)}, u32[]{:S(2)}) collective-permute-start(f32[25,48,128]{2,1,0:T(8,128)} %shard_map.104), channel_id=1, source_target_pairs={{4,0},{8,4},{12,8},{5,1},{9,5},{13,9},{6,2},{10,6},{14,10},{7,3},{... | collective-permute-start | bytes 1843208 | tf_op jit(solution)/shard_map/ppermute | solution.py:45
  19.5 0.9 fusion
  21.2 1.2 %slice_bitcast_fusion = (f32[4,48,512]{2,1,0:T(8,128)S(1)}, f32[4,48,512]{2,1,0:T(8,128)S(1)}) fusion(f32[4,8,48,512]{3,2,1,0:T(8,128)} %q_ref.1), kind=kLoop, calls=%fused_computation.4 | loop fusion | bytes 1572864 | tf_op jit(solution)/shard_map/squeeze | solution.py:403
  22.3 5.7 %collective-permute-done.3 = f32[25,48,128]{2,1,0:T(8,128)} collective-permute-done((f32[25,48,128]{2,1,0:T(8,128)}, f32[25,48,128]{2,1,0:T(8,128)}, u32[]{:S(2)}, u32[]{:S(2)}) %collective-permute-start.3) | collective-permute-done | bytes 614432 | tf_op jit(solution)/shard_map/ppermute | solution.py:44
  28.0 0.7 collective-permute-start.5
  28.9 1.1 %constant_dynamic-update-slice_fusion.6 = f32[25,48,640]{2,1,0:T(8,128)S(1)} fusion(f32[25,48,640]{2,1,0:T(8,128)S(1)} %broadcast_in_dim.2, f32[25,48,128]{2,1,0:T(8,128)} %shard_map.104, s32[]{:T(128)S(6)} %select_n.70), kind=kLoop, calls=%fused_computation.25 | loop fusion | bytes 1228804 | tf_op jit(solution)/shard_map/dynamic_update_slice | solution.py:41
  30.1 1.9 %collective-permute-start.1 = (f32[4,48,512]{2,1,0:T(8,128)S(1)}, f32[4,48,512]{2,1,0:T(8,128)S(1)}, u32[]{:S(2)}, u32[]{:S(2)}) collective-permute-start(f32[4,48,512]{2,1,0:T(8,128)S(1)} %get-tuple-element.31), channel_id=1, source_target_pairs={{0,1},{1,2},{2,3},{4,5},{5,6},{6,7},{8,9},{9,10},{10,11},{12,13},{... | collective-permute-start | bytes 1179656 | tf_op jit(solution)/shard_map/ppermute | solution.py:16
  32.0 3.4 %collective-permute-done.4 = f32[25,48,128]{2,1,0:T(8,128)} collective-permute-done((f32[25,48,128]{2,1,0:T(8,128)}, f32[25,48,128]{2,1,0:T(8,128)}, u32[]{:S(2)}, u32[]{:S(2)}) %collective-permute-start.4) | collective-permute-done | bytes 614432 | tf_op jit(solution)/shard_map/ppermute | solution.py:45
  35.5 1.3 %collective-permute-start.6 = (f32[25,48,128]{2,1,0:T(8,128)}, f32[25,48,128]{2,1,0:T(8,128)S(1)}, u32[]{:S(2)}, u32[]{:S(2)}) collective-permute-start(f32[25,48,128]{2,1,0:T(8,128)} %collective-permute-done.4), channel_id=1, source_target_pairs={{4,0},{8,4},{5,1},{9,5},{6,2},{10,6},{7,3},{11,7},{20,16},{24,20},... | collective-permute-start | bytes 1843208 | tf_op jit(solution)/shard_map/ppermute | solution.py:45
  37.0 2.1 %collective-permute-start.2 = (f32[4,48,512]{2,1,0:T(8,128)S(1)}, f32[4,48,512]{2,1,0:T(8,128)S(1)}, u32[]{:S(2)}, u32[]{:S(2)}) collective-permute-start(f32[4,48,512]{2,1,0:T(8,128)S(1)} %get-tuple-element.30), channel_id=1, source_target_pairs={{1,0},{2,1},{3,2},{5,4},{6,5},{7,6},{9,8},{10,9},{11,10},{13,12},{... | collective-permute-start | bytes 1179656 | tf_op jit(solution)/shard_map/ppermute | solution.py:16
  39.3 0.7 collective-permute-start.7
  40.1 0.8 bitcast_multiply_fusion.rest_8_.src_ref.refs_15_
  40.9 12.0 %collective-permute-done.6 = f32[25,48,128]{2,1,0:T(8,128)S(1)} collective-permute-done((f32[25,48,128]{2,1,0:T(8,128)}, f32[25,48,128]{2,1,0:T(8,128)S(1)}, u32[]{:S(2)}, u32[]{:S(2)}) %collective-permute-start.6) | collective-permute-done | bytes 614432 | tf_op jit(solution)/shard_map/ppermute | solution.py:45
  52.9 1.3 %collective-permute-start.8 = (f32[25,48,128]{2,1,0:T(8,128)S(1)}, f32[25,48,128]{2,1,0:T(8,128)S(1)}, u32[]{:S(2)}, u32[]{:S(2)}) collective-permute-start(f32[25,48,128]{2,1,0:T(8,128)S(1)} %collective-permute-done.6), channel_id=1, source_target_pairs={{4,0},{5,1},{6,2},{7,3},{20,16},{21,17},{22,18},{23,19}} | collective-permute-start | bytes 1843208 | tf_op jit(solution)/shard_map/ppermute | solution.py:45
  54.2 1.1 %constant_dynamic-update-slice_fusion.5 = f32[25,48,640]{2,1,0:T(8,128)S(1)} fusion(f32[25,48,640]{2,1,0:T(8,128)S(1)} %constant_dynamic-update-slice_fusion.6, f32[25,48,128]{2,1,0:T(8,128)} %collective-permute-done.3, s32[]{:T(128)S(6)} %select_n.72), kind=kLoop, calls=%fused_computation.24 | loop fusion | bytes 1228804 | tf_op jit(solution)/shard_map/dynamic_update_slice | solution.py:47
  55.3 1.1 %constant_dynamic-update-slice_fusion.4 = f32[25,48,640]{2,1,0:T(8,128)S(1)} fusion(f32[25,48,640]{2,1,0:T(8,128)S(1)} %constant_dynamic-update-slice_fusion.5, f32[25,48,128]{2,1,0:T(8,128)} %collective-permute-done.4, s32[]{:T(128)S(6)} %select_n.74), kind=kLoop, calls=%fused_computation.23 | loop fusion | bytes 1228804 | tf_op jit(solution)/shard_map/dynamic_update_slice | solution.py:49
  56.6 12.5 %collective-permute-done.8 = f32[25,48,128]{2,1,0:T(8,128)S(1)} collective-permute-done((f32[25,48,128]{2,1,0:T(8,128)S(1)}, f32[25,48,128]{2,1,0:T(8,128)S(1)}, u32[]{:S(2)}, u32[]{:S(2)}) %collective-permute-start.8) | collective-permute-done | bytes 614432 | tf_op jit(solution)/shard_map/ppermute | solution.py:45
  69.2 0.8 copy-done.5
  70.0 0.9 copy-done.1
  71.0 3.4 %shard_map.105 = (f32[4,48,512]{2,1,0:T(8,128)}, f32[4,48,512]{2,1,0:T(8,128)}) custom-call(f32[8]{0:T(128)} %compare_convert_fusion.north_ref.refs_0_, f32[4,48,512]{2,1,0:T(8,128)} %get-tuple-element.35.lo_ref, f32[4,48,512]{2,1,0:T(8,128)} %get-tuple-element.34.hi_ref, f32[4,48,512]{2,1,0:T(8,128)} %get-tuple-element.33.lo_in_ref, ...), custom_call_target="tpu_custom_call" | custom-call | tf_op jit(solution)/shard_map/pallas_call | solution.py:275
  74.4 1.9 %collective-permute-start.12 = (f32[4,48,512]{2,1,0:T(8,128)}, f32[4,48,512]{2,1,0:T(8,128)S(1)}, u32[]{:S(2)}, u32[]{:S(2)}) collective-permute-start(f32[4,48,512]{2,1,0:T(8,128)} %get-tuple-element.26.hi_ref.refs_2_), channel_id=1, source_target_pairs={{0,1},{1,2},{2,3},{4,5},{5,6},{6,7},{8,9},{9,10},{10,11},{12,13},{... | collective-permute-start | bytes 1179656 | tf_op jit(solution)/shard_map/ppermute | solution.py:16
  76.3 3.2 %collective-permute-start.13 = (f32[4,48,512]{2,1,0:T(8,128)}, f32[4,48,512]{2,1,0:T(8,128)S(1)}, u32[]{:S(2)}, u32[]{:S(2)}) collective-permute-start(f32[4,48,512]{2,1,0:T(8,128)} %get-tuple-element.25.lo_ref.refs_1_), channel_id=1, source_target_pairs={{1,0},{2,1},{3,2},{5,4},{6,5},{7,6},{9,8},{10,9},{11,10},{13,12},{... | collective-permute-start | bytes 1179656 | tf_op jit(solution)/shard_map/ppermute | solution.py:16
  79.5 9.5 %shard_map.106 = (f32[4,8,48,512]{3,2,1,0:T(8,128)}, f32[4,48,512]{2,1,0:T(8,128)}, f32[4,48,512]{2,1,0:T(8,128)}) custom-call(f32[8]{0:T(128)} %compare_convert_fusion.north_ref.refs_0_, f32[4,8,48,512]{3,2,1,0:T(8,128)} %q_ref.1, f32[4,48,512]{2,1,0:T(8,128)} %get-tuple-element.25.lo_ref.refs_1_, f32[4,48,512]{2,1,0:T(8,128)} %get-tuple-element.26.hi_ref.refs_2_, ...), custom_call_target="tpu_custom_call" | custom-call | tf_op jit(solution)/shard_map/pallas_call | solution.py:361
  89.0 0.7 copy-done.2
  89.9 3.5 %shard_map.107 = f32[4,8,48,512]{3,2,1,0:T(8,128)} custom-call(f32[8]{0:T(128)} %compare_convert_fusion.north_ref.refs_0_, f32[4,48,512]{2,1,0:T(8,128)} %get-tuple-element.25.lo_ref.refs_1_, f32[4,48,512]{2,1,0:T(8,128)} %get-tuple-element.26.hi_ref.refs_2_, f32[4,48,512]{2,1,0:T(8,128)} %get-tuple-element.27.refs_3_, ...), custom_call_target="tpu_custom_call", output_to_operand_aliasing={{}: (16, {})} | custom-call | tf_op jit(solution)/shard_map/pallas_call | solution.py:275
  (43 shorter events, 3.3 us)
Async XLA Ops:
  0.6 6.0 %copy-start = (f32[8,8,8]{2,1,0:T(8,128)S(1)}, f32[8,8,8]{2,1,0:T(8,128)}, u32[]{:S(2)}) copy-start(f32[8,8,8]{2,1,0:T(8,128)} %param.11) | copy-start | bytes 6148
  0.6 18.9 %copy-start.9 = (s32[8,512]{1,0:T(8,128)S(1)}, s32[8,512]{1,0:T(8,128)}, u32[]{:S(2)}) copy-start(s32[8,512]{1,0:T(8,128)} %param.13) | copy-start | bytes 49156
  0.7 18.9 %copy-start.10 = (f32[4,22]{1,0:T(4,128)S(1)}, f32[4,22]{1,0:T(4,128)}, u32[]{:S(2)}) copy-start(f32[4,22]{1,0:T(4,128)} %param.14) | copy-start | bytes 1060
  1.4 7.7 %collective-permute-start = (f32[1,48,128]{2,1,0:T(8,128)S(1)}, f32[1,48,128]{2,1,0:T(8,128)S(1)}, u32[]{:S(2)}, u32[]{:S(2)}) collective-permute-start(f32[1,48,128]{2,1,0:T(8,128)S(1)} %slice.21), channel_id=1, source_target_pairs={{0,1},{1,2},{2,3},{4,5},{5,6},{6,7},{8,9},{9,10},{10,11},{12,13},{... | collective-permute-start | bytes 73736 | tf_op jit(solution)/shard_map/ppermute | solution.py:16
  9.1 0.6 copy-start.8
  11.7 16.4 %collective-permute-start.3 = (f32[25,48,128]{2,1,0:T(8,128)}, f32[25,48,128]{2,1,0:T(8,128)}, u32[]{:S(2)}, u32[]{:S(2)}) collective-permute-start(f32[25,48,128]{2,1,0:T(8,128)} %shard_map.104), channel_id=1, source_target_pairs={{0,4},{4,8},{8,12},{1,5},{5,9},{9,13},{2,6},{6,10},{10,14},{3,7},{... | collective-permute-start | bytes 1843208 | tf_op jit(solution)/shard_map/ppermute | solution.py:44
  18.2 17.3 %collective-permute-start.4 = (f32[25,48,128]{2,1,0:T(8,128)}, f32[25,48,128]{2,1,0:T(8,128)}, u32[]{:S(2)}, u32[]{:S(2)}) collective-permute-start(f32[25,48,128]{2,1,0:T(8,128)} %shard_map.104), channel_id=1, source_target_pairs={{4,0},{8,4},{12,8},{5,1},{9,5},{13,9},{6,2},{10,6},{14,10},{7,3},{... | collective-permute-start | bytes 1843208 | tf_op jit(solution)/shard_map/ppermute | solution.py:45
  20.4 19.6 %copy-start.6 = (f32[4,8,512]{2,1,0:T(8,128)S(1)}, f32[4,8,512]{2,1,0:T(8,128)}, u32[]{:S(2)}) copy-start(f32[4,8,512]{2,1,0:T(8,128)} %convolution_bitcast_fusion.3) | copy-start | bytes 196612
  20.4 19.6 %copy-start.7 = (f32[8,512,4]{1,2,0:T(4,128)S(1)}, f32[8,512,4]{1,2,0:T(4,128)}, u32[]{:S(2)}) copy-start(f32[8,512,4]{1,2,0:T(4,128)} %fusion) | copy-start | bytes 196612
  20.4 9.7 %collective-permute-start.10 = (f32[4,8,512]{2,1,0:T(8,128)}, f32[4,8,512]{2,1,0:T(8,128)S(1)}, u32[]{:S(2)}, u32[]{:S(2)}) collective-permute-start(f32[4,8,512]{2,1,0:T(8,128)} %param.10), channel_id=1, source_target_pairs={{0,2},{1,3},{2,0},{3,1},{4,6},{5,7},{6,4},{7,5},{8,10},{9,11},{10,... | collective-permute-start | bytes 196616 | tf_op jit(solution)/shard_map/ppermute | solution.py:406
  20.4 16.5 %collective-permute-start.9 = (f32[4,8,512]{2,1,0:T(8,128)}, f32[4,8,512]{2,1,0:T(8,128)S(1)}, u32[]{:S(2)}, u32[]{:S(2)}) collective-permute-start(f32[4,8,512]{2,1,0:T(8,128)} %param.10), channel_id=1, source_target_pairs={{0,1},{1,2},{2,3},{3,0},{4,5},{5,6},{6,7},{7,4},{8,9},{9,10},{10,1... | collective-permute-start | bytes 196616 | tf_op jit(solution)/shard_map/ppermute | solution.py:406
  21.1 19.0 %collective-permute-start.11 = (f32[4,8,512]{2,1,0:T(8,128)}, f32[4,8,512]{2,1,0:T(8,128)S(1)}, u32[]{:S(2)}, u32[]{:S(2)}) collective-permute-start(f32[4,8,512]{2,1,0:T(8,128)} %param.10), channel_id=1, source_target_pairs={{0,3},{1,0},{2,1},{3,2},{4,7},{5,4},{6,5},{7,6},{8,11},{9,8},{10,9... | collective-permute-start | bytes 196616 | tf_op jit(solution)/shard_map/ppermute | solution.py:406
  28.0 11.3 %collective-permute-start.5 = (f32[25,48,128]{2,1,0:T(8,128)}, f32[25,48,128]{2,1,0:T(8,128)S(1)}, u32[]{:S(2)}, u32[]{:S(2)}) collective-permute-start(f32[25,48,128]{2,1,0:T(8,128)} %collective-permute-done.3), channel_id=1, source_target_pairs={{4,8},{8,12},{5,9},{9,13},{6,10},{10,14},{7,11},{11,15},{20,24},{2... | collective-permute-start | bytes 1843208 | tf_op jit(solution)/shard_map/ppermute | solution.py:44
  30.1 39.1 %collective-permute-start.1 = (f32[4,48,512]{2,1,0:T(8,128)S(1)}, f32[4,48,512]{2,1,0:T(8,128)S(1)}, u32[]{:S(2)}, u32[]{:S(2)}) collective-permute-start(f32[4,48,512]{2,1,0:T(8,128)S(1)} %get-tuple-element.31), channel_id=1, source_target_pairs={{0,1},{1,2},{2,3},{4,5},{5,6},{6,7},{8,9},{9,10},{10,11},{12,13},{... | collective-permute-start | bytes 1179656 | tf_op jit(solution)/shard_map/ppermute | solution.py:16
  35.5 17.4 %collective-permute-start.6 = (f32[25,48,128]{2,1,0:T(8,128)}, f32[25,48,128]{2,1,0:T(8,128)S(1)}, u32[]{:S(2)}, u32[]{:S(2)}) collective-permute-start(f32[25,48,128]{2,1,0:T(8,128)} %collective-permute-done.4), channel_id=1, source_target_pairs={{4,0},{8,4},{5,1},{9,5},{6,2},{10,6},{7,3},{11,7},{20,16},{24,20},... | collective-permute-start | bytes 1843208 | tf_op jit(solution)/shard_map/ppermute | solution.py:45
  37.0 32.2 %collective-permute-start.2 = (f32[4,48,512]{2,1,0:T(8,128)S(1)}, f32[4,48,512]{2,1,0:T(8,128)S(1)}, u32[]{:S(2)}, u32[]{:S(2)}) collective-permute-start(f32[4,48,512]{2,1,0:T(8,128)S(1)} %get-tuple-element.30), channel_id=1, source_target_pairs={{1,0},{2,1},{3,2},{5,4},{6,5},{7,6},{9,8},{10,9},{11,10},{13,12},{... | collective-permute-start | bytes 1179656 | tf_op jit(solution)/shard_map/ppermute | solution.py:16
  39.3 17.2 %collective-permute-start.7 = (f32[25,48,128]{2,1,0:T(8,128)S(1)}, f32[25,48,128]{2,1,0:T(8,128)S(1)}, u32[]{:S(2)}, u32[]{:S(2)}) collective-permute-start(f32[25,48,128]{2,1,0:T(8,128)S(1)} %collective-permute-done.5), channel_id=1, source_target_pairs={{8,12},{9,13},{10,14},{11,15},{24,28},{25,29},{26,30},{27,31}} | collective-permute-start | bytes 1843208 | tf_op jit(solution)/shard_map/ppermute | solution.py:44
  52.9 16.2 %collective-permute-start.8 = (f32[25,48,128]{2,1,0:T(8,128)S(1)}, f32[25,48,128]{2,1,0:T(8,128)S(1)}, u32[]{:S(2)}, u32[]{:S(2)}) collective-permute-start(f32[25,48,128]{2,1,0:T(8,128)S(1)} %collective-permute-done.6), channel_id=1, source_target_pairs={{4,0},{5,1},{6,2},{7,3},{20,16},{21,17},{22,18},{23,19}} | collective-permute-start | bytes 1843208 | tf_op jit(solution)/shard_map/ppermute | solution.py:45
  69.1 1.7 %copy-start.1 = (f32[25,48,640]{2,1,0:T(8,128)}, f32[25,48,640]{2,1,0:T(8,128)S(1)}, u32[]{:S(2)}) copy-start(f32[25,48,640]{2,1,0:T(8,128)S(1)} %constant_dynamic-update-slice_fusion.rest_0_.rest_1_.rest_2_.rest_3_.rest_4_.rest_5_.rest_6_.rest_7_.wx_hbm.refs_7_.refs_8_.refs_9_.refs_10_.refs_11_.refs_12_.refs_13_.refs_14_) | copy-start | bytes 9216004
  69.2 1.9 %copy-start.4 = (f32[4,48,512]{2,1,0:T(8,128)}, f32[4,48,512]{2,1,0:T(8,128)S(1)}, u32[]{:S(2)}) copy-start(f32[4,48,512]{2,1,0:T(8,128)S(1)} %collective-permute-done.1.qs_ref) | copy-start | bytes 1179652
  69.2 0.8 copy-start.5
  74.4 14.6 %collective-permute-start.12 = (f32[4,48,512]{2,1,0:T(8,128)}, f32[4,48,512]{2,1,0:T(8,128)S(1)}, u32[]{:S(2)}, u32[]{:S(2)}) collective-permute-start(f32[4,48,512]{2,1,0:T(8,128)} %get-tuple-element.26.hi_ref.refs_2_), channel_id=1, source_target_pairs={{0,1},{1,2},{2,3},{4,5},{5,6},{6,7},{8,9},{9,10},{10,11},{12,13},{... | collective-permute-start | bytes 1179656 | tf_op jit(solution)/shard_map/ppermute | solution.py:16
  76.3 12.7 %collective-permute-start.13 = (f32[4,48,512]{2,1,0:T(8,128)}, f32[4,48,512]{2,1,0:T(8,128)S(1)}, u32[]{:S(2)}, u32[]{:S(2)}) collective-permute-start(f32[4,48,512]{2,1,0:T(8,128)} %get-tuple-element.25.lo_ref.refs_1_), channel_id=1, source_target_pairs={{1,0},{2,1},{3,2},{5,4},{6,5},{7,6},{9,8},{10,9},{11,10},{13,12},{... | collective-permute-start | bytes 1179656 | tf_op jit(solution)/shard_map/ppermute | solution.py:16
  89.0 0.8 copy-start.2
  89.0 0.9 copy-start.3

commit v18 on v16

--- a/solution.py
+++ b/solution.py
@@ -244,13 +244,14 @@
 def edge_step(rows, base, south, north, weather, emission, north_open):
     tracers, levels, lon = rows[0].shape
     lat_rows = emission.shape[1]
-    vmem = pl.BlockSpec(memory_space=pltpu.VMEM)
-    in_specs = [pl.BlockSpec(memory_space=pltpu.SMEM)] + [vmem] * 6
+    whole = pl.BlockSpec((tracers, levels, lon), lambda i: (0, 0, 0))
+    in_specs = [pl.BlockSpec(memory_space=pltpu.SMEM)] + [whole] * 6
     last = lat_rows - 1
     met_rows = []
     for a, below in ((0, 3 * lat_rows), (last, lat_rows + last - 1)):
         met_rows += [a, lat_rows + a, below, 2 * lat_rows + a]
-    in_specs += [pl.BlockSpec((1, levels, lon), lambda i, r=r: (r, 0, 0)) for r in met_rows] + [vmem]
+    in_specs += [pl.BlockSpec((1, levels, lon), lambda i, r=r: (r, 0, 0)) for r in met_rows]
+    in_specs += [pl.BlockSpec(emission.shape, lambda i: (0, 0, 0))]
     args = [north_open, *rows, south, north] + [weather] * len(met_rows) + [emission]
     edge = pl.BlockSpec((tracers, levels, lon), lambda i: (0, 0, 0))
     scratch = []

time: 93.4 us -> 93.4 us (level)
  no operation moved by 1% of the time
where the time goes in v18:
time: 93.4 us; the launch traced here: 92.6 us
  waiting for transfers between devices  33.7 us (36%)
  starting transfers between devices  23.7 us (25%)
  Pallas kernels  17.5 us (19%)
  local copies, waits for them, and re-layouts  12.3 us (13%)
  matrix products  3.94 us (4%)
  between operations  0.97 us (1%)
    ppermute x3, waiting for transfers between devices, relay_gather(): lax.ppermute(left, axis, [(j, j - 1) for j in range(1, count - r + 1)])  27.9 us
    ppermute x5, starting transfers between devices, passed_along(): return lax.ppermute(value, axis, pairs)  13.7 us
    pallas_call x1, Pallas kernels, fused_steps(): pl.pallas_call(fused_kernel, grid_spec=grid_spec, out_shape=[jax.ShapeDty...  8.67 us
    pallas_call x2, Pallas kernels, edge_step(): pl.pallas_call(kernel, grid_spec=grid_spec, out_shape=out_shape, input_ou...  6.84 us
    ppermute x3, waiting for transfers between devices, relay_gather(): lax.ppermute(right, axis, [(i, i + 1) for i in range(r - 1, count - 1)])  5.7 us
    ppermute x3, starting transfers between devices, relay_gather(): lax.ppermute(right, axis, [(i, i + 1) for i in range(r - 1, count - 1)])  5.41 us
    ppermute x3, starting transfers between devices, relay_gather(): lax.ppermute(left, axis, [(j, j - 1) for j in range(1, count - r + 1)])  3.84 us
    unnamed x22, local copies, waits for them, and re-layouts  3.35 us
  transfers between devices with their start and end apart: 14, of which 4 were waited for; matrix products, arithmetic and copies ran while one was open for 14% of the time, Pallas kernels for 9%

profile of v18, /device:TPU:1, one launch (start us, length us, event | category | flops | bytes accessed | tf_op | source)
XLA Modules:
  0.0 92.6 jit_solution(15321481333532520554)
XLA Ops:
  0.7 0.8 slice.21
  1.4 4.5 %collective-permute-start = (f32[1,48,128]{2,1,0:T(8,128)S(1)}, f32[1,48,128]{2,1,0:T(8,128)S(1)}, u32[]{:S(2)}, u32[]{:S(2)}) collective-permute-start(f32[1,48,128]{2,1,0:T(8,128)S(1)} %slice.21), channel_id=1, source_target_pairs={{0,1},{1,2},{2,3},{4,5},{5,6},{6,7},{8,9},{9,10},{10,11},{12,13},{... | collective-permute-start | bytes 73736 | tf_op jit(solution)/shard_map/ppermute | solution.py:16
  5.9 0.7 constant_dynamic-slice_fusion.4
  6.8 1.7 %convolution_bitcast_fusion.3 = f32[4,8,512]{2,1,0:T(8,128)} fusion(f32[8,8,1]{1,0,2:T(8,128)S(1)} %bitcast.56, f32[4,8,512]{2,1,0:T(8,128)} %param.10), kind=kOutput, calls=%fused_computation.3 | convolution fusion | flops 1572864 | bytes 131328 | tf_op jit(solution)/shard_map/jm,kmn->kjn/dot_general | solution.py:372
  9.7 2.0 %shard_map.104 = f32[25,48,128]{2,1,0:T(8,128)} custom-call(f32[8,48,128]{2,1,0:T(8,128)} %refs_0_, f32[8,48,128]{2,1,0:T(8,128)} %refs_1_, f32[8,48,128]{2,1,0:T(8,128)} %refs_2_, f32[1,48,128]{2,1,0:T(8,128)} %copy-done.8), custom_call_target="tpu_custom_call" | custom-call | tf_op jit(solution)/shard_map/pallas_call | solution.py:30
  11.7 4.0 %collective-permute-start.3 = (f32[25,48,128]{2,1,0:T(8,128)}, f32[25,48,128]{2,1,0:T(8,128)}, u32[]{:S(2)}, u32[]{:S(2)}) collective-permute-start(f32[25,48,128]{2,1,0:T(8,128)} %shard_map.104), channel_id=1, source_target_pairs={{0,4},{4,8},{8,12},{1,5},{5,9},{9,13},{2,6},{6,10},{10,14},{3,7},{... | collective-permute-start | bytes 1843208 | tf_op jit(solution)/shard_map/ppermute | solution.py:44
  15.7 2.5 %slice_bitcast_fusion.2 = (f32[4,48,512]{2,1,0:T(8,128)}, f32[4,48,512]{2,1,0:T(8,128)}, f32[4,48,512]{2,1,0:T(8,128)}, f32[4,48,512]{2,1,0:T(8,128)}) fusion(f32[4,8,48,512]{3,2,1,0:T(8,128)} %q_ref.1), kind=kLoop, calls=%fused_computation.7 | loop fusion | bytes 3145728 | tf_op jit(solution)/shard_map/squeeze | solution.py:395
  18.2 1.3 %collective-permute-start.4 = (f32[25,48,128]{2,1,0:T(8,128)}, f32[25,48,128]{2,1,0:T(8,128)}, u32[]{:S(2)}, u32[]{:S(2)}) collective-permute-start(f32[25,48,128]{2,1,0:T(8,128)} %shard_map.104), channel_id=1, source_target_pairs={{4,0},{8,4},{12,8},{5,1},{9,5},{13,9},{6,2},{10,6},{14,10},{7,3},{... | collective-permute-start | bytes 1843208 | tf_op jit(solution)/shard_map/ppermute | solution.py:45
  19.5 0.9 fusion
  21.2 1.2 %slice_bitcast_fusion = (f32[4,48,512]{2,1,0:T(8,128)S(1)}, f32[4,48,512]{2,1,0:T(8,128)S(1)}) fusion(f32[4,8,48,512]{3,2,1,0:T(8,128)} %q_ref.1), kind=kLoop, calls=%fused_computation.4 | loop fusion | bytes 1572864 | tf_op jit(solution)/shard_map/squeeze | solution.py:381
  22.3 5.7 %collective-permute-done.3 = f32[25,48,128]{2,1,0:T(8,128)} collective-permute-done((f32[25,48,128]{2,1,0:T(8,128)}, f32[25,48,128]{2,1,0:T(8,128)}, u32[]{:S(2)}, u32[]{:S(2)}) %collective-permute-start.3) | collective-permute-done | bytes 614432 | tf_op jit(solution)/shard_map/ppermute | solution.py:44
  28.0 0.7 collective-permute-start.5
  28.9 1.1 %constant_dynamic-update-slice_fusion.6 = f32[25,48,640]{2,1,0:T(8,128)S(1)} fusion(f32[25,48,640]{2,1,0:T(8,128)S(1)} %broadcast_in_dim.2, f32[25,48,128]{2,1,0:T(8,128)} %shard_map.104, s32[]{:T(128)S(6)} %select_n.70), kind=kLoop, calls=%fused_computation.25 | loop fusion | bytes 1228804 | tf_op jit(solution)/shard_map/dynamic_update_slice | solution.py:41
  30.1 1.9 %collective-permute-start.1 = (f32[4,48,512]{2,1,0:T(8,128)S(1)}, f32[4,48,512]{2,1,0:T(8,128)S(1)}, u32[]{:S(2)}, u32[]{:S(2)}) collective-permute-start(f32[4,48,512]{2,1,0:T(8,128)S(1)} %get-tuple-element.31), channel_id=1, source_target_pairs={{0,1},{1,2},{2,3},{4,5},{5,6},{6,7},{8,9},{9,10},{10,11},{12,13},{... | collective-permute-start | bytes 1179656 | tf_op jit(solution)/shard_map/ppermute | solution.py:16
  32.0 3.4 %collective-permute-done.4 = f32[25,48,128]{2,1,0:T(8,128)} collective-permute-done((f32[25,48,128]{2,1,0:T(8,128)}, f32[25,48,128]{2,1,0:T(8,128)}, u32[]{:S(2)}, u32[]{:S(2)}) %collective-permute-start.4) | collective-permute-done | bytes 614432 | tf_op jit(solution)/shard_map/ppermute | solution.py:45
  35.5 1.3 %collective-permute-start.6 = (f32[25,48,128]{2,1,0:T(8,128)}, f32[25,48,128]{2,1,0:T(8,128)S(1)}, u32[]{:S(2)}, u32[]{:S(2)}) collective-permute-start(f32[25,48,128]{2,1,0:T(8,128)} %collective-permute-done.4), channel_id=1, source_target_pairs={{4,0},{8,4},{5,1},{9,5},{6,2},{10,6},{7,3},{11,7},{20,16},{24,20},... | collective-permute-start | bytes 1843208 | tf_op jit(solution)/shard_map/ppermute | solution.py:45
  37.0 2.1 %collective-permute-start.2 = (f32[4,48,512]{2,1,0:T(8,128)S(1)}, f32[4,48,512]{2,1,0:T(8,128)S(1)}, u32[]{:S(2)}, u32[]{:S(2)}) collective-permute-start(f32[4,48,512]{2,1,0:T(8,128)S(1)} %get-tuple-element.30), channel_id=1, source_target_pairs={{1,0},{2,1},{3,2},{5,4},{6,5},{7,6},{9,8},{10,9},{11,10},{13,12},{... | collective-permute-start | bytes 1179656 | tf_op jit(solution)/shard_map/ppermute | solution.py:16
  39.3 0.7 collective-permute-start.7
  40.1 0.8 bitcast_multiply_fusion.rest_8_.src_ref.refs_15_
  40.9 12.0 %collective-permute-done.6 = f32[25,48,128]{2,1,0:T(8,128)S(1)} collective-permute-done((f32[25,48,128]{2,1,0:T(8,128)}, f32[25,48,128]{2,1,0:T(8,128)S(1)}, u32[]{:S(2)}, u32[]{:S(2)}) %collective-permute-start.6) | collective-permute-done | bytes 614432 | tf_op jit(solution)/shard_map/ppermute | solution.py:45
  52.9 1.3 %collective-permute-start.8 = (f32[25,48,128]{2,1,0:T(8,128)S(1)}, f32[25,48,128]{2,1,0:T(8,128)S(1)}, u32[]{:S(2)}, u32[]{:S(2)}) collective-permute-start(f32[25,48,128]{2,1,0:T(8,128)S(1)} %collective-permute-done.6), channel_id=1, source_target_pairs={{4,0},{5,1},{6,2},{7,3},{20,16},{21,17},{22,18},{23,19}} | collective-permute-start | bytes 1843208 | tf_op jit(solution)/shard_map/ppermute | solution.py:45
  54.2 1.1 %constant_dynamic-update-slice_fusion.5 = f32[25,48,640]{2,1,0:T(8,128)S(1)} fusion(f32[25,48,640]{2,1,0:T(8,128)S(1)} %constant_dynamic-update-slice_fusion.6, f32[25,48,128]{2,1,0:T(8,128)} %collective-permute-done.3, s32[]{:T(128)S(6)} %select_n.72), kind=kLoop, calls=%fused_computation.24 | loop fusion | bytes 1228804 | tf_op jit(solution)/shard_map/dynamic_update_slice | solution.py:47
  55.3 1.1 %constant_dynamic-update-slice_fusion.4 = f32[25,48,640]{2,1,0:T(8,128)S(1)} fusion(f32[25,48,640]{2,1,0:T(8,128)S(1)} %constant_dynamic-update-slice_fusion.5, f32[25,48,128]{2,1,0:T(8,128)} %collective-permute-done.4, s32[]{:T(128)S(6)} %select_n.74), kind=kLoop, calls=%fused_computation.23 | loop fusion | bytes 1228804 | tf_op jit(solution)/shard_map/dynamic_update_slice | solution.py:49
  56.6 12.5 %collective-permute-done.8 = f32[25,48,128]{2,1,0:T(8,128)S(1)} collective-permute-done((f32[25,48,128]{2,1,0:T(8,128)S(1)}, f32[25,48,128]{2,1,0:T(8,128)S(1)}, u32[]{:S(2)}, u32[]{:S(2)}) %collective-permute-start.8) | collective-permute-done | bytes 614432 | tf_op jit(solution)/shard_map/ppermute | solution.py:45
  69.2 0.8 copy-done.5
  70.0 0.9 copy-done.1
  71.0 3.4 %shard_map.105 = (f32[4,48,512]{2,1,0:T(8,128)}, f32[4,48,512]{2,1,0:T(8,128)}) custom-call(f32[8]{0:T(128)} %compare_convert_fusion.north_ref.refs_0_, f32[4,48,512]{2,1,0:T(8,128)} %get-tuple-element.35.lo_ref, f32[4,48,512]{2,1,0:T(8,128)} %get-tuple-element.34.hi_ref, f32[4,48,512]{2,1,0:T(8,128)} %get-tuple-element.33.lo_in_ref, ...), custom_call_target="tpu_custom_call" | custom-call | tf_op jit(solution)/shard_map/pallas_call | solution.py:274
  74.4 1.9 %collective-permute-start.12 = (f32[4,48,512]{2,1,0:T(8,128)}, f32[4,48,512]{2,1,0:T(8,128)S(1)}, u32[]{:S(2)}, u32[]{:S(2)}) collective-permute-start(f32[4,48,512]{2,1,0:T(8,128)} %get-tuple-element.26.hi_ref.refs_2_), channel_id=1, source_target_pairs={{0,1},{1,2},{2,3},{4,5},{5,6},{6,7},{8,9},{9,10},{10,11},{12,13},{... | collective-permute-start | bytes 1179656 | tf_op jit(solution)/shard_map/ppermute | solution.py:16
  76.3 3.2 %collective-permute-start.13 = (f32[4,48,512]{2,1,0:T(8,128)}, f32[4,48,512]{2,1,0:T(8,128)S(1)}, u32[]{:S(2)}, u32[]{:S(2)}) collective-permute-start(f32[4,48,512]{2,1,0:T(8,128)} %get-tuple-element.25.lo_ref.refs_1_), channel_id=1, source_target_pairs={{1,0},{2,1},{3,2},{5,4},{6,5},{7,6},{9,8},{10,9},{11,10},{13,12},{... | collective-permute-start | bytes 1179656 | tf_op jit(solution)/shard_map/ppermute | solution.py:16
  79.5 8.7 %shard_map.106 = (f32[4,8,48,512]{3,2,1,0:T(8,128)}, f32[4,48,512]{2,1,0:T(8,128)}, f32[4,48,512]{2,1,0:T(8,128)}) custom-call(f32[8]{0:T(128)} %compare_convert_fusion.north_ref.refs_0_, f32[4,8,48,512]{3,2,1,0:T(8,128)} %q_ref.1, f32[4,48,512]{2,1,0:T(8,128)} %get-tuple-element.25.lo_ref.refs_1_, f32[4,48,512]{2,1,0:T(8,128)} %get-tuple-element.26.hi_ref.refs_2_, ...), custom_call_target="tpu_custom_call" | custom-call | tf_op jit(solution)/shard_map/pallas_call | solution.py:339
  88.2 0.7 copy-done.2
  89.1 3.5 %shard_map.107 = f32[4,8,48,512]{3,2,1,0:T(8,128)} custom-call(f32[8]{0:T(128)} %compare_convert_fusion.north_ref.refs_0_, f32[4,48,512]{2,1,0:T(8,128)} %get-tuple-element.25.lo_ref.refs_1_, f32[4,48,512]{2,1,0:T(8,128)} %get-tuple-element.26.hi_ref.refs_2_, f32[4,48,512]{2,1,0:T(8,128)} %get-tuple-element.27.refs_3_, ...), custom_call_target="tpu_custom_call", output_to_operand_aliasing={{}: (16, {})} | custom-call | tf_op jit(solution)/shard_map/pallas_call | solution.py:274
  (43 shorter events, 3.3 us)
Async XLA Ops:
  0.6 6.0 %copy-start = (f32[8,8,8]{2,1,0:T(8,128)S(1)}, f32[8,8,8]{2,1,0:T(8,128)}, u32[]{:S(2)}) copy-start(f32[8,8,8]{2,1,0:T(8,128)} %param.11) | copy-start | bytes 6148
  0.6 18.9 %copy-start.9 = (s32[8,512]{1,0:T(8,128)S(1)}, s32[8,512]{1,0:T(8,128)}, u32[]{:S(2)}) copy-start(s32[8,512]{1,0:T(8,128)} %param.13) | copy-start | bytes 49156
  0.7 18.9 %copy-start.10 = (f32[4,22]{1,0:T(4,128)S(1)}, f32[4,22]{1,0:T(4,128)}, u32[]{:S(2)}) copy-start(f32[4,22]{1,0:T(4,128)} %param.14) | copy-start | bytes 1060
  1.4 7.7 %collective-permute-start = (f32[1,48,128]{2,1,0:T(8,128)S(1)}, f32[1,48,128]{2,1,0:T(8,128)S(1)}, u32[]{:S(2)}, u32[]{:S(2)}) collective-permute-start(f32[1,48,128]{2,1,0:T(8,128)S(1)} %slice.21), channel_id=1, source_target_pairs={{0,1},{1,2},{2,3},{4,5},{5,6},{6,7},{8,9},{9,10},{10,11},{12,13},{... | collective-permute-start | bytes 73736 | tf_op jit(solution)/shard_map/ppermute | solution.py:16
  9.1 0.6 copy-start.8
  11.7 16.4 %collective-permute-start.3 = (f32[25,48,128]{2,1,0:T(8,128)}, f32[25,48,128]{2,1,0:T(8,128)}, u32[]{:S(2)}, u32[]{:S(2)}) collective-permute-start(f32[25,48,128]{2,1,0:T(8,128)} %shard_map.104), channel_id=1, source_target_pairs={{0,4},{4,8},{8,12},{1,5},{5,9},{9,13},{2,6},{6,10},{10,14},{3,7},{... | collective-permute-start | bytes 1843208 | tf_op jit(solution)/shard_map/ppermute | solution.py:44
  18.2 17.3 %collective-permute-start.4 = (f32[25,48,128]{2,1,0:T(8,128)}, f32[25,48,128]{2,1,0:T(8,128)}, u32[]{:S(2)}, u32[]{:S(2)}) collective-permute-start(f32[25,48,128]{2,1,0:T(8,128)} %shard_map.104), channel_id=1, source_target_pairs={{4,0},{8,4},{12,8},{5,1},{9,5},{13,9},{6,2},{10,6},{14,10},{7,3},{... | collective-permute-start | bytes 1843208 | tf_op jit(solution)/shard_map/ppermute | solution.py:45
  20.4 19.6 %copy-start.6 = (f32[4,8,512]{2,1,0:T(8,128)S(1)}, f32[4,8,512]{2,1,0:T(8,128)}, u32[]{:S(2)}) copy-start(f32[4,8,512]{2,1,0:T(8,128)} %convolution_bitcast_fusion.3) | copy-start | bytes 196612
  20.4 19.6 %copy-start.7 = (f32[8,512,4]{1,2,0:T(4,128)S(1)}, f32[8,512,4]{1,2,0:T(4,128)}, u32[]{:S(2)}) copy-start(f32[8,512,4]{1,2,0:T(4,128)} %fusion) | copy-start | bytes 196612
  20.4 9.7 %collective-permute-start.10 = (f32[4,8,512]{2,1,0:T(8,128)}, f32[4,8,512]{2,1,0:T(8,128)S(1)}, u32[]{:S(2)}, u32[]{:S(2)}) collective-permute-start(f32[4,8,512]{2,1,0:T(8,128)} %param.10), channel_id=1, source_target_pairs={{0,2},{1,3},{2,0},{3,1},{4,6},{5,7},{6,4},{7,5},{8,10},{9,11},{10,... | collective-permute-start | bytes 196616 | tf_op jit(solution)/shard_map/ppermute | solution.py:384
  20.4 16.5 %collective-permute-start.9 = (f32[4,8,512]{2,1,0:T(8,128)}, f32[4,8,512]{2,1,0:T(8,128)S(1)}, u32[]{:S(2)}, u32[]{:S(2)}) collective-permute-start(f32[4,8,512]{2,1,0:T(8,128)} %param.10), channel_id=1, source_target_pairs={{0,1},{1,2},{2,3},{3,0},{4,5},{5,6},{6,7},{7,4},{8,9},{9,10},{10,1... | collective-permute-start | bytes 196616 | tf_op jit(solution)/shard_map/ppermute | solution.py:384
  21.1 19.0 %collective-permute-start.11 = (f32[4,8,512]{2,1,0:T(8,128)}, f32[4,8,512]{2,1,0:T(8,128)S(1)}, u32[]{:S(2)}, u32[]{:S(2)}) collective-permute-start(f32[4,8,512]{2,1,0:T(8,128)} %param.10), channel_id=1, source_target_pairs={{0,3},{1,0},{2,1},{3,2},{4,7},{5,4},{6,5},{7,6},{8,11},{9,8},{10,9... | collective-permute-start | bytes 196616 | tf_op jit(solution)/shard_map/ppermute | solution.py:384
  28.0 11.3 %collective-permute-start.5 = (f32[25,48,128]{2,1,0:T(8,128)}, f32[25,48,128]{2,1,0:T(8,128)S(1)}, u32[]{:S(2)}, u32[]{:S(2)}) collective-permute-start(f32[25,48,128]{2,1,0:T(8,128)} %collective-permute-done.3), channel_id=1, source_target_pairs={{4,8},{8,12},{5,9},{9,13},{6,10},{10,14},{7,11},{11,15},{20,24},{2... | collective-permute-start | bytes 1843208 | tf_op jit(solution)/shard_map/ppermute | solution.py:44
  30.1 39.1 %collective-permute-start.1 = (f32[4,48,512]{2,1,0:T(8,128)S(1)}, f32[4,48,512]{2,1,0:T(8,128)S(1)}, u32[]{:S(2)}, u32[]{:S(2)}) collective-permute-start(f32[4,48,512]{2,1,0:T(8,128)S(1)} %get-tuple-element.31), channel_id=1, source_target_pairs={{0,1},{1,2},{2,3},{4,5},{5,6},{6,7},{8,9},{9,10},{10,11},{12,13},{... | collective-permute-start | bytes 1179656 | tf_op jit(solution)/shard_map/ppermute | solution.py:16
  35.5 17.4 %collective-permute-start.6 = (f32[25,48,128]{2,1,0:T(8,128)}, f32[25,48,128]{2,1,0:T(8,128)S(1)}, u32[]{:S(2)}, u32[]{:S(2)}) collective-permute-start(f32[25,48,128]{2,1,0:T(8,128)} %collective-permute-done.4), channel_id=1, source_target_pairs={{4,0},{8,4},{5,1},{9,5},{6,2},{10,6},{7,3},{11,7},{20,16},{24,20},... | collective-permute-start | bytes 1843208 | tf_op jit(solution)/shard_map/ppermute | solution.py:45
  37.0 32.2 %collective-permute-start.2 = (f32[4,48,512]{2,1,0:T(8,128)S(1)}, f32[4,48,512]{2,1,0:T(8,128)S(1)}, u32[]{:S(2)}, u32[]{:S(2)}) collective-permute-start(f32[4,48,512]{2,1,0:T(8,128)S(1)} %get-tuple-element.30), channel_id=1, source_target_pairs={{1,0},{2,1},{3,2},{5,4},{6,5},{7,6},{9,8},{10,9},{11,10},{13,12},{... | collective-permute-start | bytes 1179656 | tf_op jit(solution)/shard_map/ppermute | solution.py:16
  39.3 17.2 %collective-permute-start.7 = (f32[25,48,128]{2,1,0:T(8,128)S(1)}, f32[25,48,128]{2,1,0:T(8,128)S(1)}, u32[]{:S(2)}, u32[]{:S(2)}) collective-permute-start(f32[25,48,128]{2,1,0:T(8,128)S(1)} %collective-permute-done.5), channel_id=1, source_target_pairs={{8,12},{9,13},{10,14},{11,15},{24,28},{25,29},{26,30},{27,31}} | collective-permute-start | bytes 1843208 | tf_op jit(solution)/shard_map/ppermute | solution.py:44
  52.9 16.2 %collective-permute-start.8 = (f32[25,48,128]{2,1,0:T(8,128)S(1)}, f32[25,48,128]{2,1,0:T(8,128)S(1)}, u32[]{:S(2)}, u32[]{:S(2)}) collective-permute-start(f32[25,48,128]{2,1,0:T(8,128)S(1)} %collective-permute-done.6), channel_id=1, source_target_pairs={{4,0},{5,1},{6,2},{7,3},{20,16},{21,17},{22,18},{23,19}} | collective-permute-start | bytes 1843208 | tf_op jit(solution)/shard_map/ppermute | solution.py:45
  69.1 1.7 %copy-start.1 = (f32[25,48,640]{2,1,0:T(8,128)}, f32[25,48,640]{2,1,0:T(8,128)S(1)}, u32[]{:S(2)}) copy-start(f32[25,48,640]{2,1,0:T(8,128)S(1)} %constant_dynamic-update-slice_fusion.rest_0_.rest_1_.rest_2_.rest_3_.rest_4_.rest_5_.rest_6_.rest_7_.wx_ref.refs_7_.refs_8_.refs_9_.refs_10_.refs_11_.refs_12_.refs_13_.refs_14_) | copy-start | bytes 9216004
  69.2 1.9 %copy-start.4 = (f32[4,48,512]{2,1,0:T(8,128)}, f32[4,48,512]{2,1,0:T(8,128)S(1)}, u32[]{:S(2)}) copy-start(f32[4,48,512]{2,1,0:T(8,128)S(1)} %collective-permute-done.1.qs_ref) | copy-start | bytes 1179652
  69.2 0.8 copy-start.5
  74.4 13.8 %collective-permute-start.12 = (f32[4,48,512]{2,1,0:T(8,128)}, f32[4,48,512]{2,1,0:T(8,128)S(1)}, u32[]{:S(2)}, u32[]{:S(2)}) collective-permute-start(f32[4,48,512]{2,1,0:T(8,128)} %get-tuple-element.26.hi_ref.refs_2_), channel_id=1, source_target_pairs={{0,1},{1,2},{2,3},{4,5},{5,6},{6,7},{8,9},{9,10},{10,11},{12,13},{... | collective-permute-start | bytes 1179656 | tf_op jit(solution)/shard_map/ppermute | solution.py:16
  76.3 11.9 %collective-permute-start.13 = (f32[4,48,512]{2,1,0:T(8,128)}, f32[4,48,512]{2,1,0:T(8,128)S(1)}, u32[]{:S(2)}, u32[]{:S(2)}) collective-permute-start(f32[4,48,512]{2,1,0:T(8,128)} %get-tuple-element.25.lo_ref.refs_1_), channel_id=1, source_target_pairs={{1,0},{2,1},{3,2},{5,4},{6,5},{7,6},{9,8},{10,9},{11,10},{13,12},{... | collective-permute-start | bytes 1179656 | tf_op jit(solution)/shard_map/ppermute | solution.py:16
  88.2 0.8 copy-start.2
  88.2 0.9 copy-start.3

commit v19 on v18

--- a/solution.py
+++ b/solution.py
@@ -50,13 +50,13 @@
     return buf
 
 
-def fill_coefficients(north_ref, wx_ref, coef_ref):
+def fill_coefficients(north_ref, wx_ref, coef_ref, rows=None):
     lat_rows = coef_ref.shape[1]
     levels, lon = coef_ref.shape[2], coef_ref.shape[3]
     level = lax.broadcasted_iota(jnp.int32, (levels, lon), 0)
     not_top = level < levels - 1
     not_bottom = level > 0
-    for a in range(lat_rows):
+    for a in range(lat_rows) if rows is None else rows:
         u = wx_ref[a]
         uw = pltpu.roll(u, 1, 1)
         v = wx_ref[lat_rows + a] * north_ref[a]
@@ -285,7 +285,7 @@
 
     @pl.when(pl.program_id(0) == 0)
     def _():
-        fill_coefficients(north_ref, wx_ref, coef_ref)
+        fill_coefficients(north_ref, wx_ref, coef_ref, range(1, lat_rows - 1))
 
     def stencil(a, qa, qm, qp):
         result = (

time: 93.4 us -> 93.3 us (level)
  no operation moved by 1% of the time
where the time goes in v19:
time: 93.3 us; the launch traced here: 92.5 us
  waiting for transfers between devices  33.7 us (36%)
  starting transfers between devices  23.7 us (25%)
  Pallas kernels  17.4 us (19%)
  local copies, waits for them, and re-layouts  12.3 us (13%)
  matrix products  3.94 us (4%)
  between operations  0.97 us (1%)
    ppermute x3, waiting for transfers between devices, relay_gather(): lax.ppermute(left, axis, [(j, j - 1) for j in range(1, count - r + 1)])  27.9 us
    ppermute x5, starting transfers between devices, passed_along(): return lax.ppermute(value, axis, pairs)  13.7 us
    pallas_call x1, Pallas kernels, fused_steps(): pl.pallas_call(fused_kernel, grid_spec=grid_spec, out_shape=[jax.ShapeDty...  8.61 us
    pallas_call x2, Pallas kernels, edge_step(): pl.pallas_call(kernel, grid_spec=grid_spec, out_shape=out_shape, input_ou...  6.84 us
    ppermute x3, waiting for transfers between devices, relay_gather(): lax.ppermute(right, axis, [(i, i + 1) for i in range(r - 1, count - 1)])  5.7 us
    ppermute x3, starting transfers between devices, relay_gather(): lax.ppermute(right, axis, [(i, i + 1) for i in range(r - 1, count - 1)])  5.41 us
    ppermute x3, starting transfers between devices, relay_gather(): lax.ppermute(left, axis, [(j, j - 1) for j in range(1, count - r + 1)])  3.84 us
    unnamed x22, local copies, waits for them, and re-layouts  3.35 us
  transfers between devices with their start and end apart: 14, of which 4 were waited for; matrix products, arithmetic and copies ran while one was open for 14% of the time, Pallas kernels for 9%

profile of v19, /device:TPU:1, one launch (start us, length us, event | category | flops | bytes accessed | tf_op | source)
XLA Modules:
  0.0 92.5 jit_solution(3894140733119865919)
XLA Ops:
  0.7 0.8 slice.21
  1.4 4.5 %collective-permute-start = (f32[1,48,128]{2,1,0:T(8,128)S(1)}, f32[1,48,128]{2,1,0:T(8,128)S(1)}, u32[]{:S(2)}, u32[]{:S(2)}) collective-permute-start(f32[1,48,128]{2,1,0:T(8,128)S(1)} %slice.21), channel_id=1, source_target_pairs={{0,1},{1,2},{2,3},{4,5},{5,6},{6,7},{8,9},{9,10},{10,11},{12,13},{... | collective-permute-start | bytes 73736 | tf_op jit(solution)/shard_map/ppermute | solution.py:16
  5.9 0.7 constant_dynamic-slice_fusion.4
  6.8 1.7 %convolution_bitcast_fusion.3 = f32[4,8,512]{2,1,0:T(8,128)} fusion(f32[8,8,1]{1,0,2:T(8,128)S(1)} %bitcast.56, f32[4,8,512]{2,1,0:T(8,128)} %param.10), kind=kOutput, calls=%fused_computation.3 | convolution fusion | flops 1572864 | bytes 131328 | tf_op jit(solution)/shard_map/jm,kmn->kjn/dot_general | solution.py:372
  9.7 2.0 %shard_map.104 = f32[25,48,128]{2,1,0:T(8,128)} custom-call(f32[8,48,128]{2,1,0:T(8,128)} %refs_0_, f32[8,48,128]{2,1,0:T(8,128)} %refs_1_, f32[8,48,128]{2,1,0:T(8,128)} %refs_2_, f32[1,48,128]{2,1,0:T(8,128)} %copy-done.8), custom_call_target="tpu_custom_call" | custom-call | tf_op jit(solution)/shard_map/pallas_call | solution.py:30
  11.7 4.0 %collective-permute-start.3 = (f32[25,48,128]{2,1,0:T(8,128)}, f32[25,48,128]{2,1,0:T(8,128)}, u32[]{:S(2)}, u32[]{:S(2)}) collective-permute-start(f32[25,48,128]{2,1,0:T(8,128)} %shard_map.104), channel_id=1, source_target_pairs={{0,4},{4,8},{8,12},{1,5},{5,9},{9,13},{2,6},{6,10},{10,14},{3,7},{... | collective-permute-start | bytes 1843208 | tf_op jit(solution)/shard_map/ppermute | solution.py:44
  15.7 2.5 %slice_bitcast_fusion.2 = (f32[4,48,512]{2,1,0:T(8,128)}, f32[4,48,512]{2,1,0:T(8,128)}, f32[4,48,512]{2,1,0:T(8,128)}, f32[4,48,512]{2,1,0:T(8,128)}) fusion(f32[4,8,48,512]{3,2,1,0:T(8,128)} %q_ref.1), kind=kLoop, calls=%fused_computation.7 | loop fusion | bytes 3145728 | tf_op jit(solution)/shard_map/squeeze | solution.py:395
  18.2 1.3 %collective-permute-start.4 = (f32[25,48,128]{2,1,0:T(8,128)}, f32[25,48,128]{2,1,0:T(8,128)}, u32[]{:S(2)}, u32[]{:S(2)}) collective-permute-start(f32[25,48,128]{2,1,0:T(8,128)} %shard_map.104), channel_id=1, source_target_pairs={{4,0},{8,4},{12,8},{5,1},{9,5},{13,9},{6,2},{10,6},{14,10},{7,3},{... | collective-permute-start | bytes 1843208 | tf_op jit(solution)/shard_map/ppermute | solution.py:45
  19.5 0.9 fusion
  21.2 1.2 %slice_bitcast_fusion = (f32[4,48,512]{2,1,0:T(8,128)S(1)}, f32[4,48,512]{2,1,0:T(8,128)S(1)}) fusion(f32[4,8,48,512]{3,2,1,0:T(8,128)} %q_ref.1), kind=kLoop, calls=%fused_computation.4 | loop fusion | bytes 1572864 | tf_op jit(solution)/shard_map/squeeze | solution.py:381
  22.3 5.7 %collective-permute-done.3 = f32[25,48,128]{2,1,0:T(8,128)} collective-permute-done((f32[25,48,128]{2,1,0:T(8,128)}, f32[25,48,128]{2,1,0:T(8,128)}, u32[]{:S(2)}, u32[]{:S(2)}) %collective-permute-start.3) | collective-permute-done | bytes 614432 | tf_op jit(solution)/shard_map/ppermute | solution.py:44
  28.0 0.7 collective-permute-start.5
  28.9 1.1 %constant_dynamic-update-slice_fusion.6 = f32[25,48,640]{2,1,0:T(8,128)S(1)} fusion(f32[25,48,640]{2,1,0:T(8,128)S(1)} %broadcast_in_dim.2, f32[25,48,128]{2,1,0:T(8,128)} %shard_map.104, s32[]{:T(128)S(6)} %select_n.70), kind=kLoop, calls=%fused_computation.25 | loop fusion | bytes 1228804 | tf_op jit(solution)/shard_map/dynamic_update_slice | solution.py:41
  30.1 1.9 %collective-permute-start.1 = (f32[4,48,512]{2,1,0:T(8,128)S(1)}, f32[4,48,512]{2,1,0:T(8,128)S(1)}, u32[]{:S(2)}, u32[]{:S(2)}) collective-permute-start(f32[4,48,512]{2,1,0:T(8,128)S(1)} %get-tuple-element.31), channel_id=1, source_target_pairs={{0,1},{1,2},{2,3},{4,5},{5,6},{6,7},{8,9},{9,10},{10,11},{12,13},{... | collective-permute-start | bytes 1179656 | tf_op jit(solution)/shard_map/ppermute | solution.py:16
  32.0 3.4 %collective-permute-done.4 = f32[25,48,128]{2,1,0:T(8,128)} collective-permute-done((f32[25,48,128]{2,1,0:T(8,128)}, f32[25,48,128]{2,1,0:T(8,128)}, u32[]{:S(2)}, u32[]{:S(2)}) %collective-permute-start.4) | collective-permute-done | bytes 614432 | tf_op jit(solution)/shard_map/ppermute | solution.py:45
  35.5 1.3 %collective-permute-start.6 = (f32[25,48,128]{2,1,0:T(8,128)}, f32[25,48,128]{2,1,0:T(8,128)S(1)}, u32[]{:S(2)}, u32[]{:S(2)}) collective-permute-start(f32[25,48,128]{2,1,0:T(8,128)} %collective-permute-done.4), channel_id=1, source_target_pairs={{4,0},{8,4},{5,1},{9,5},{6,2},{10,6},{7,3},{11,7},{20,16},{24,20},... | collective-permute-start | bytes 1843208 | tf_op jit(solution)/shard_map/ppermute | solution.py:45
  37.0 2.1 %collective-permute-start.2 = (f32[4,48,512]{2,1,0:T(8,128)S(1)}, f32[4,48,512]{2,1,0:T(8,128)S(1)}, u32[]{:S(2)}, u32[]{:S(2)}) collective-permute-start(f32[4,48,512]{2,1,0:T(8,128)S(1)} %get-tuple-element.30), channel_id=1, source_target_pairs={{1,0},{2,1},{3,2},{5,4},{6,5},{7,6},{9,8},{10,9},{11,10},{13,12},{... | collective-permute-start | bytes 1179656 | tf_op jit(solution)/shard_map/ppermute | solution.py:16
  39.3 0.7 collective-permute-start.7
  40.1 0.8 bitcast_multiply_fusion.rest_8_.src_ref.refs_15_
  40.9 12.0 %collective-permute-done.6 = f32[25,48,128]{2,1,0:T(8,128)S(1)} collective-permute-done((f32[25,48,128]{2,1,0:T(8,128)}, f32[25,48,128]{2,1,0:T(8,128)S(1)}, u32[]{:S(2)}, u32[]{:S(2)}) %collective-permute-start.6) | collective-permute-done | bytes 614432 | tf_op jit(solution)/shard_map/ppermute | solution.py:45
  52.9 1.3 %collective-permute-start.8 = (f32[25,48,128]{2,1,0:T(8,128)S(1)}, f32[25,48,128]{2,1,0:T(8,128)S(1)}, u32[]{:S(2)}, u32[]{:S(2)}) collective-permute-start(f32[25,48,128]{2,1,0:T(8,128)S(1)} %collective-permute-done.6), channel_id=1, source_target_pairs={{4,0},{5,1},{6,2},{7,3},{20,16},{21,17},{22,18},{23,19}} | collective-permute-start | bytes 1843208 | tf_op jit(solution)/shard_map/ppermute | solution.py:45
  54.2 1.1 %constant_dynamic-update-slice_fusion.5 = f32[25,48,640]{2,1,0:T(8,128)S(1)} fusion(f32[25,48,640]{2,1,0:T(8,128)S(1)} %constant_dynamic-update-slice_fusion.6, f32[25,48,128]{2,1,0:T(8,128)} %collective-permute-done.3, s32[]{:T(128)S(6)} %select_n.72), kind=kLoop, calls=%fused_computation.24 | loop fusion | bytes 1228804 | tf_op jit(solution)/shard_map/dynamic_update_slice | solution.py:47
  55.3 1.1 %constant_dynamic-update-slice_fusion.4 = f32[25,48,640]{2,1,0:T(8,128)S(1)} fusion(f32[25,48,640]{2,1,0:T(8,128)S(1)} %constant_dynamic-update-slice_fusion.5, f32[25,48,128]{2,1,0:T(8,128)} %collective-permute-done.4, s32[]{:T(128)S(6)} %select_n.74), kind=kLoop, calls=%fused_computation.23 | loop fusion | bytes 1228804 | tf_op jit(solution)/shard_map/dynamic_update_slice | solution.py:49
  56.6 12.5 %collective-permute-done.8 = f32[25,48,128]{2,1,0:T(8,128)S(1)} collective-permute-done((f32[25,48,128]{2,1,0:T(8,128)S(1)}, f32[25,48,128]{2,1,0:T(8,128)S(1)}, u32[]{:S(2)}, u32[]{:S(2)}) %collective-permute-start.8) | collective-permute-done | bytes 614432 | tf_op jit(solution)/shard_map/ppermute | solution.py:45
  69.2 0.8 copy-done.5
  70.0 0.9 copy-done.1
  71.0 3.4 %shard_map.105 = (f32[4,48,512]{2,1,0:T(8,128)}, f32[4,48,512]{2,1,0:T(8,128)}) custom-call(f32[8]{0:T(128)} %compare_convert_fusion.north_ref.refs_0_, f32[4,48,512]{2,1,0:T(8,128)} %get-tuple-element.35.lo_ref, f32[4,48,512]{2,1,0:T(8,128)} %get-tuple-element.34.hi_ref, f32[4,48,512]{2,1,0:T(8,128)} %get-tuple-element.33.lo_in_ref, ...), custom_call_target="tpu_custom_call" | custom-call | tf_op jit(solution)/shard_map/pallas_call | solution.py:274
  74.4 1.9 %collective-permute-start.12 = (f32[4,48,512]{2,1,0:T(8,128)}, f32[4,48,512]{2,1,0:T(8,128)S(1)}, u32[]{:S(2)}, u32[]{:S(2)}) collective-permute-start(f32[4,48,512]{2,1,0:T(8,128)} %get-tuple-element.26.hi_ref.refs_2_), channel_id=1, source_target_pairs={{0,1},{1,2},{2,3},{4,5},{5,6},{6,7},{8,9},{9,10},{10,11},{12,13},{... | collective-permute-start | bytes 1179656 | tf_op jit(solution)/shard_map/ppermute | solution.py:16
  76.3 3.2 %collective-permute-start.13 = (f32[4,48,512]{2,1,0:T(8,128)}, f32[4,48,512]{2,1,0:T(8,128)S(1)}, u32[]{:S(2)}, u32[]{:S(2)}) collective-permute-start(f32[4,48,512]{2,1,0:T(8,128)} %get-tuple-element.25.lo_ref.refs_1_), channel_id=1, source_target_pairs={{1,0},{2,1},{3,2},{5,4},{6,5},{7,6},{9,8},{10,9},{11,10},{13,12},{... | collective-permute-start | bytes 1179656 | tf_op jit(solution)/shard_map/ppermute | solution.py:16
  79.5 8.6 %shard_map.106 = (f32[4,8,48,512]{3,2,1,0:T(8,128)}, f32[4,48,512]{2,1,0:T(8,128)}, f32[4,48,512]{2,1,0:T(8,128)}) custom-call(f32[8]{0:T(128)} %compare_convert_fusion.north_ref.refs_0_, f32[4,8,48,512]{3,2,1,0:T(8,128)} %q_ref.1, f32[4,48,512]{2,1,0:T(8,128)} %get-tuple-element.25.lo_ref.refs_1_, f32[4,48,512]{2,1,0:T(8,128)} %get-tuple-element.26.hi_ref.refs_2_, ...), custom_call_target="tpu_custom_call" | custom-call | tf_op jit(solution)/shard_map/pallas_call | solution.py:339
  88.2 0.7 copy-done.2
  89.0 3.5 %shard_map.107 = f32[4,8,48,512]{3,2,1,0:T(8,128)} custom-call(f32[8]{0:T(128)} %compare_convert_fusion.north_ref.refs_0_, f32[4,48,512]{2,1,0:T(8,128)} %get-tuple-element.25.lo_ref.refs_1_, f32[4,48,512]{2,1,0:T(8,128)} %get-tuple-element.26.hi_ref.refs_2_, f32[4,48,512]{2,1,0:T(8,128)} %get-tuple-element.27.refs_3_, ...), custom_call_target="tpu_custom_call", output_to_operand_aliasing={{}: (16, {})} | custom-call | tf_op jit(solution)/shard_map/pallas_call | solution.py:274
  (43 shorter events, 3.3 us)
Async XLA Ops:
  0.6 6.0 %copy-start = (f32[8,8,8]{2,1,0:T(8,128)S(1)}, f32[8,8,8]{2,1,0:T(8,128)}, u32[]{:S(2)}) copy-start(f32[8,8,8]{2,1,0:T(8,128)} %param.11) | copy-start | bytes 6148
  0.6 18.9 %copy-start.9 = (s32[8,512]{1,0:T(8,128)S(1)}, s32[8,512]{1,0:T(8,128)}, u32[]{:S(2)}) copy-start(s32[8,512]{1,0:T(8,128)} %param.13) | copy-start | bytes 49156
  0.7 18.9 %copy-start.10 = (f32[4,22]{1,0:T(4,128)S(1)}, f32[4,22]{1,0:T(4,128)}, u32[]{:S(2)}) copy-start(f32[4,22]{1,0:T(4,128)} %param.14) | copy-start | bytes 1060
  1.4 7.7 %collective-permute-start = (f32[1,48,128]{2,1,0:T(8,128)S(1)}, f32[1,48,128]{2,1,0:T(8,128)S(1)}, u32[]{:S(2)}, u32[]{:S(2)}) collective-permute-start(f32[1,48,128]{2,1,0:T(8,128)S(1)} %slice.21), channel_id=1, source_target_pairs={{0,1},{1,2},{2,3},{4,5},{5,6},{6,7},{8,9},{9,10},{10,11},{12,13},{... | collective-permute-start | bytes 73736 | tf_op jit(solution)/shard_map/ppermute | solution.py:16
  9.1 0.6 copy-start.8
  11.7 16.4 %collective-permute-start.3 = (f32[25,48,128]{2,1,0:T(8,128)}, f32[25,48,128]{2,1,0:T(8,128)}, u32[]{:S(2)}, u32[]{:S(2)}) collective-permute-start(f32[25,48,128]{2,1,0:T(8,128)} %shard_map.104), channel_id=1, source_target_pairs={{0,4},{4,8},{8,12},{1,5},{5,9},{9,13},{2,6},{6,10},{10,14},{3,7},{... | collective-permute-start | bytes 1843208 | tf_op jit(solution)/shard_map/ppermute | solution.py:44
  18.2 17.3 %collective-permute-start.4 = (f32[25,48,128]{2,1,0:T(8,128)}, f32[25,48,128]{2,1,0:T(8,128)}, u32[]{:S(2)}, u32[]{:S(2)}) collective-permute-start(f32[25,48,128]{2,1,0:T(8,128)} %shard_map.104), channel_id=1, source_target_pairs={{4,0},{8,4},{12,8},{5,1},{9,5},{13,9},{6,2},{10,6},{14,10},{7,3},{... | collective-permute-start | bytes 1843208 | tf_op jit(solution)/shard_map/ppermute | solution.py:45
  20.4 19.6 %copy-start.6 = (f32[4,8,512]{2,1,0:T(8,128)S(1)}, f32[4,8,512]{2,1,0:T(8,128)}, u32[]{:S(2)}) copy-start(f32[4,8,512]{2,1,0:T(8,128)} %convolution_bitcast_fusion.3) | copy-start | bytes 196612
  20.4 19.6 %copy-start.7 = (f32[8,512,4]{1,2,0:T(4,128)S(1)}, f32[8,512,4]{1,2,0:T(4,128)}, u32[]{:S(2)}) copy-start(f32[8,512,4]{1,2,0:T(4,128)} %fusion) | copy-start | bytes 196612
  20.4 9.7 %collective-permute-start.10 = (f32[4,8,512]{2,1,0:T(8,128)}, f32[4,8,512]{2,1,0:T(8,128)S(1)}, u32[]{:S(2)}, u32[]{:S(2)}) collective-permute-start(f32[4,8,512]{2,1,0:T(8,128)} %param.10), channel_id=1, source_target_pairs={{0,2},{1,3},{2,0},{3,1},{4,6},{5,7},{6,4},{7,5},{8,10},{9,11},{10,... | collective-permute-start | bytes 196616 | tf_op jit(solution)/shard_map/ppermute | solution.py:384
  20.4 16.5 %collective-permute-start.9 = (f32[4,8,512]{2,1,0:T(8,128)}, f32[4,8,512]{2,1,0:T(8,128)S(1)}, u32[]{:S(2)}, u32[]{:S(2)}) collective-permute-start(f32[4,8,512]{2,1,0:T(8,128)} %param.10), channel_id=1, source_target_pairs={{0,1},{1,2},{2,3},{3,0},{4,5},{5,6},{6,7},{7,4},{8,9},{9,10},{10,1... | collective-permute-start | bytes 196616 | tf_op jit(solution)/shard_map/ppermute | solution.py:384
  21.1 19.0 %collective-permute-start.11 = (f32[4,8,512]{2,1,0:T(8,128)}, f32[4,8,512]{2,1,0:T(8,128)S(1)}, u32[]{:S(2)}, u32[]{:S(2)}) collective-permute-start(f32[4,8,512]{2,1,0:T(8,128)} %param.10), channel_id=1, source_target_pairs={{0,3},{1,0},{2,1},{3,2},{4,7},{5,4},{6,5},{7,6},{8,11},{9,8},{10,9... | collective-permute-start | bytes 196616 | tf_op jit(solution)/shard_map/ppermute | solution.py:384
  28.0 11.3 %collective-permute-start.5 = (f32[25,48,128]{2,1,0:T(8,128)}, f32[25,48,128]{2,1,0:T(8,128)S(1)}, u32[]{:S(2)}, u32[]{:S(2)}) collective-permute-start(f32[25,48,128]{2,1,0:T(8,128)} %collective-permute-done.3), channel_id=1, source_target_pairs={{4,8},{8,12},{5,9},{9,13},{6,10},{10,14},{7,11},{11,15},{20,24},{2... | collective-permute-start | bytes 1843208 | tf_op jit(solution)/shard_map/ppermute | solution.py:44
  30.1 39.1 %collective-permute-start.1 = (f32[4,48,512]{2,1,0:T(8,128)S(1)}, f32[4,48,512]{2,1,0:T(8,128)S(1)}, u32[]{:S(2)}, u32[]{:S(2)}) collective-permute-start(f32[4,48,512]{2,1,0:T(8,128)S(1)} %get-tuple-element.31), channel_id=1, source_target_pairs={{0,1},{1,2},{2,3},{4,5},{5,6},{6,7},{8,9},{9,10},{10,11},{12,13},{... | collective-permute-start | bytes 1179656 | tf_op jit(solution)/shard_map/ppermute | solution.py:16
  35.5 17.4 %collective-permute-start.6 = (f32[25,48,128]{2,1,0:T(8,128)}, f32[25,48,128]{2,1,0:T(8,128)S(1)}, u32[]{:S(2)}, u32[]{:S(2)}) collective-permute-start(f32[25,48,128]{2,1,0:T(8,128)} %collective-permute-done.4), channel_id=1, source_target_pairs={{4,0},{8,4},{5,1},{9,5},{6,2},{10,6},{7,3},{11,7},{20,16},{24,20},... | collective-permute-start | bytes 1843208 | tf_op jit(solution)/shard_map/ppermute | solution.py:45
  37.0 32.2 %collective-permute-start.2 = (f32[4,48,512]{2,1,0:T(8,128)S(1)}, f32[4,48,512]{2,1,0:T(8,128)S(1)}, u32[]{:S(2)}, u32[]{:S(2)}) collective-permute-start(f32[4,48,512]{2,1,0:T(8,128)S(1)} %get-tuple-element.30), channel_id=1, source_target_pairs={{1,0},{2,1},{3,2},{5,4},{6,5},{7,6},{9,8},{10,9},{11,10},{13,12},{... | collective-permute-start | bytes 1179656 | tf_op jit(solution)/shard_map/ppermute | solution.py:16
  39.3 17.2 %collective-permute-start.7 = (f32[25,48,128]{2,1,0:T(8,128)S(1)}, f32[25,48,128]{2,1,0:T(8,128)S(1)}, u32[]{:S(2)}, u32[]{:S(2)}) collective-permute-start(f32[25,48,128]{2,1,0:T(8,128)S(1)} %collective-permute-done.5), channel_id=1, source_target_pairs={{8,12},{9,13},{10,14},{11,15},{24,28},{25,29},{26,30},{27,31}} | collective-permute-start | bytes 1843208 | tf_op jit(solution)/shard_map/ppermute | solution.py:44
  52.9 16.2 %collective-permute-start.8 = (f32[25,48,128]{2,1,0:T(8,128)S(1)}, f32[25,48,128]{2,1,0:T(8,128)S(1)}, u32[]{:S(2)}, u32[]{:S(2)}) collective-permute-start(f32[25,48,128]{2,1,0:T(8,128)S(1)} %collective-permute-done.6), channel_id=1, source_target_pairs={{4,0},{5,1},{6,2},{7,3},{20,16},{21,17},{22,18},{23,19}} | collective-permute-start | bytes 1843208 | tf_op jit(solution)/shard_map/ppermute | solution.py:45
  69.1 1.7 %copy-start.1 = (f32[25,48,640]{2,1,0:T(8,128)}, f32[25,48,640]{2,1,0:T(8,128)S(1)}, u32[]{:S(2)}) copy-start(f32[25,48,640]{2,1,0:T(8,128)S(1)} %constant_dynamic-update-slice_fusion.rest_0_.rest_1_.rest_2_.rest_3_.rest_4_.rest_5_.rest_6_.rest_7_.wx_ref.refs_7_.refs_8_.refs_9_.refs_10_.refs_11_.refs_12_.refs_13_.refs_14_) | copy-start | bytes 9216004
  69.2 1.9 %copy-start.4 = (f32[4,48,512]{2,1,0:T(8,128)}, f32[4,48,512]{2,1,0:T(8,128)S(1)}, u32[]{:S(2)}) copy-start(f32[4,48,512]{2,1,0:T(8,128)S(1)} %collective-permute-done.1.qs_ref) | copy-start | bytes 1179652
  69.2 0.8 copy-start.5
  74.4 13.8 %collective-permute-start.12 = (f32[4,48,512]{2,1,0:T(8,128)}, f32[4,48,512]{2,1,0:T(8,128)S(1)}, u32[]{:S(2)}, u32[]{:S(2)}) collective-permute-start(f32[4,48,512]{2,1,0:T(8,128)} %get-tuple-element.26.hi_ref.refs_2_), channel_id=1, source_target_pairs={{0,1},{1,2},{2,3},{4,5},{5,6},{6,7},{8,9},{9,10},{10,11},{12,13},{... | collective-permute-start | bytes 1179656 | tf_op jit(solution)/shard_map/ppermute | solution.py:16
  76.3 11.9 %collective-permute-start.13 = (f32[4,48,512]{2,1,0:T(8,128)}, f32[4,48,512]{2,1,0:T(8,128)S(1)}, u32[]{:S(2)}, u32[]{:S(2)}) collective-permute-start(f32[4,48,512]{2,1,0:T(8,128)} %get-tuple-element.25.lo_ref.refs_1_), channel_id=1, source_target_pairs={{1,0},{2,1},{3,2},{5,4},{6,5},{7,6},{9,8},{10,9},{11,10},{13,12},{... | collective-permute-start | bytes 1179656 | tf_op jit(solution)/shard_map/ppermute | solution.py:16
  88.1 0.8 copy-start.2
  88.2 0.9 copy-start.3

commit v20 on v19

--- a/solution.py
+++ b/solution.py
@@ -241,18 +241,18 @@
             copy.wait()
 
 
-def edge_step(rows, base, south, north, weather, emission, north_open):
+def edge_step(rows, base, south, north, weather, merid_south, emission, north_open):
     tracers, levels, lon = rows[0].shape
     lat_rows = emission.shape[1]
     whole = pl.BlockSpec((tracers, levels, lon), lambda i: (0, 0, 0))
     in_specs = [pl.BlockSpec(memory_space=pltpu.SMEM)] + [whole] * 6
     last = lat_rows - 1
     met_rows = []
-    for a, below in ((0, 3 * lat_rows), (last, lat_rows + last - 1)):
-        met_rows += [a, lat_rows + a, below, 2 * lat_rows + a]
-    in_specs += [pl.BlockSpec((1, levels, lon), lambda i, r=r: (r, 0, 0)) for r in met_rows]
+    for a, below in ((0, (merid_south, 0)), (last, (weather, lat_rows + last - 1))):
+        met_rows += [(weather, a), (weather, lat_rows + a), below, (weather, 2 * lat_rows + a)]
+    in_specs += [pl.BlockSpec((1, levels, lon), lambda i, r=r: (r, 0, 0)) for _, r in met_rows]
     in_specs += [pl.BlockSpec(emission.shape, lambda i: (0, 0, 0))]
-    args = [north_open, *rows, south, north] + [weather] * len(met_rows) + [emission]
+    args = [north_open, *rows, south, north] + [m for m, _ in met_rows] + [emission]
     edge = pl.BlockSpec((tracers, levels, lon), lambda i: (0, 0, 0))
     scratch = []
     if base is None:
@@ -370,12 +370,23 @@
     row_tiles = jnp.einsum("bt,tmn->bmn", own_row, prior_tiles, precision=exact_dot)
     own_tile = lax.dynamic_index_in_dim(row_tiles, band_index, 0, keepdims=False)
     prior_field = jnp.einsum("jm,kmn->kjn", own_tile, control, precision=exact_dot)
-    south_v = passed_along(meridional_courant[-1:], "band", 1)
     parts, (north_open, row_tiles, prior_field) = lax.optimization_barrier(
-        ((zonal_courant, meridional_courant, vertical_diffusion, south_v), (north_open, row_tiles, prior_field))
+        ((zonal_courant, meridional_courant, vertical_diffusion), (north_open, row_tiles, prior_field))
     )
     pack = packed(list(parts))
     weather = relay_gather(pack, "tracer")
+    tracer_count = lax.axis_size("tracer")
+    me = lax.axis_index("tracer")
+    chunk = meridional_courant.shape[2]
+    merid_south = jnp.zeros((1,) + meridional_courant.shape[1:2] + (tracer_count * chunk,), jnp.float32)
+    for s in range(tracer_count):
+        pairs = [
+            (t * band_count + b, ((t + s) % tracer_count) * band_count + b + 1)
+            for t in range(tracer_count)
+            for b in range(band_count - 1)
+        ]
+        part = lax.ppermute(meridional_courant[-1:], ("tracer", "band"), pairs)
+        merid_south = lax.dynamic_update_slice(merid_south, part, (0, 0, ((me - s) % tracer_count) * chunk))
     held_state, held_control, _ = lax.optimization_barrier((tracer_state, control, pack))
     q_south = passed_along(held_state[:, -1], "band", 1)
     q_north = passed_along(held_state[:, 0], "band", -1)
@@ -393,12 +404,12 @@
     emission = cell_sigma * prior_field
 
     rim = (tracer_state[:, 0], tracer_state[:, lat_rows - 1], tracer_state[:, 1], tracer_state[:, lat_rows - 2])
-    bottom_row, top_row = edge_step(rim, None, q_south, q_north, weather, emission, north_open)
+    bottom_row, top_row = edge_step(rim, None, q_south, q_north, weather, merid_south, emission, north_open)
     s1_south = passed_along(top_row, "band", 1)
     s1_north = passed_along(bottom_row, "band", -1)
     inside, bottom_in, top_in = fused_steps(tracer_state, bottom_row, top_row, weather, emission, north_open)
     rim = (bottom_row, top_row, bottom_in, top_in)
-    tracer_field = edge_step(rim, inside, s1_south, s1_north, weather, emission, north_open)
+    tracer_field = edge_step(rim, inside, s1_south, s1_north, weather, merid_south, emission, north_open)
     return (tracer_field, emission)
 
 

time: 93.3 us -> 105 us (1.13)
  starting transfers between devices: 23.7 us -> 39.4 us
  waiting for transfers between devices: 33.7 us -> 27 us
  local copies, waits for them, and re-layouts: 12.3 us -> 13.9 us
  matrix products: 3.94 us -> 5.05 us
    ppermute x0 -> x4, starting transfers between devices: none -> 15.1 us  [on_device(): part = lax.ppermute(meridional_courant[-1:], ('tracer', 'band'), pairs)]
    ppermute x3, waiting for transfers between devices: 27.9 us -> 20.1 us  [relay_gather(): lax.ppermute(left, axis, [(j, j - 1) for j in range(1, count - r + 1)])]
    ppermute x0 -> x4, waiting for transfers between devices: none -> 6.88 us  [on_device(): part = lax.ppermute(meridional_courant[-1:], ('tracer', 'band'), pairs)]
    ppermute x3, waiting for transfers between devices: 5.7 us -> 0.01 us  [relay_gather(): lax.ppermute(right, axis, [(i, i + 1) for i in range(r - 1, count - 1)])]
    ppermute x5 -> x4, starting transfers between devices: 13.7 us -> 9.85 us  [passed_along(): return lax.ppermute(value, axis, pairs)]
    ppermute x3, starting transfers between devices: 0.76 us -> 4.33 us  [on_device(): part = lax.ppermute(held_control, 'band', pairs)]
    dot_general x3, matrix products: 1.2 us -> 3.57 us  [on_device(): jnp.einsum('jm,kmn->kjn', tile, part, precision=exact_dot)]
    dynamic_slice x1, local copies, waits for them, and re-layouts: 0.02 us -> 1.44 us  [on_device(): tile = lax.dynamic_index_in_dim(row_tiles, source_band, 0, keepdims=False)]
  transfers between devices with their start and end apart: 14 -> 17, of which waited for: 4 -> 5; matrix products, arithmetic and copies ran while one was open for 14% -> 14% of each run, Pallas kernels for 9% -> 8%
where the time goes in v20:
time: 105 us; the launch traced here: 104 us
  starting transfers between devices  39.4 us (38%)
  waiting for transfers between devices  27 us (26%)
  Pallas kernels  17.4 us (17%)
  local copies, waits for them, and re-layouts  13.9 us (13%)
  matrix products  5.05 us (5%)
  between operations  1.08 us (1%)
    ppermute x3, waiting for transfers between devices, relay_gather(): lax.ppermute(left, axis, [(j, j - 1) for j in range(1, count - r + 1)])  20.1 us
    ppermute x4, starting transfers between devices, on_device(): part = lax.ppermute(meridional_courant[-1:], ('tracer', 'band'), pairs)  15.1 us
    ppermute x4, starting transfers between devices, passed_along(): return lax.ppermute(value, axis, pairs)  9.85 us
    pallas_call x1, Pallas kernels, fused_steps(): pl.pallas_call(fused_kernel, grid_spec=grid_spec, out_shape=[jax.ShapeDty...  8.58 us
    ppermute x4, waiting for transfers between devices, on_device(): part = lax.ppermute(meridional_courant[-1:], ('tracer', 'band'), pairs)  6.88 us
    pallas_call x2, Pallas kernels, edge_step(): pl.pallas_call(kernel, grid_spec=grid_spec, out_shape=out_shape, input_ou...  6.87 us
    ppermute x3, starting transfers between devices, relay_gather(): lax.ppermute(right, axis, [(i, i + 1) for i in range(r - 1, count - 1)])  6.23 us
    ppermute x3, starting transfers between devices, on_device(): part = lax.ppermute(held_control, 'band', pairs)  4.33 us
  transfers between devices with their start and end apart: 17, of which 5 were waited for; matrix products, arithmetic and copies ran while one was open for 14% of the time, Pallas kernels for 8%

profile of v20, /device:TPU:1, one launch (start us, length us, event | category | flops | bytes accessed | tf_op | source)
XLA Modules:
  0.0 104.3 jit_solution(214027325501689291)
XLA Ops:
  2.2 1.0 convolution_bitcast_fusion.3
  3.3 2.0 %shard_map.104 = f32[24,48,128]{2,1,0:T(8,128)} custom-call(f32[8,48,128]{2,1,0:T(8,128)} %refs_0_, f32[8,48,128]{2,1,0:T(8,128)} %refs_1_, f32[8,48,128]{2,1,0:T(8,128)} %refs_2_), custom_call_target="tpu_custom_call" | custom-call | tf_op jit(solution)/shard_map/pallas_call | solution.py:30
  5.2 4.8 %collective-permute-start.2 = (f32[24,48,128]{2,1,0:T(8,128)}, f32[24,48,128]{2,1,0:T(8,128)}, u32[]{:S(2)}, u32[]{:S(2)}) collective-permute-start(f32[24,48,128]{2,1,0:T(8,128)} %shard_map.104), channel_id=1, source_target_pairs={{0,4},{4,8},{8,12},{1,5},{5,9},{9,13},{2,6},{6,10},{10,14},{3,7},{... | collective-permute-start | bytes 1769480 | tf_op jit(solution)/shard_map/ppermute | solution.py:44
  10.1 1.3 %collective-permute-start.3 = (f32[24,48,128]{2,1,0:T(8,128)}, f32[24,48,128]{2,1,0:T(8,128)}, u32[]{:S(2)}, u32[]{:S(2)}) collective-permute-start(f32[24,48,128]{2,1,0:T(8,128)} %shard_map.104), channel_id=1, source_target_pairs={{4,0},{8,4},{12,8},{5,1},{9,5},{13,9},{6,2},{10,6},{14,10},{7,3},{... | collective-permute-start | bytes 1769480 | tf_op jit(solution)/shard_map/ppermute | solution.py:45
  12.4 1.2 %collective-permute-start.13 = (f32[4,8,512]{2,1,0:T(8,128)}, f32[4,8,512]{2,1,0:T(8,128)}, u32[]{:S(2)}, u32[]{:S(2)}) collective-permute-start(f32[4,8,512]{2,1,0:T(8,128)} %param.10), channel_id=1, source_target_pairs={{0,2},{1,3},{2,0},{3,1},{4,6},{5,7},{6,4},{7,5},{8,10},{9,11},{10,... | collective-permute-start | bytes 196616 | tf_op jit(solution)/shard_map/ppermute | solution.py:395
  14.3 3.0 %collective-permute-start.8 = (f32[1,48,128]{2,1,0:T(8,128)S(1)}, f32[1,48,128]{2,1,0:T(8,128)S(1)}, u32[]{:S(2)}, u32[]{:S(2)}) collective-permute-start(f32[1,48,128]{2,1,0:T(8,128)S(1)} %slice.30), channel_id=1, source_target_pairs={{0,1},{1,2},{2,3},{4,5},{5,6},{6,7},{8,9},{9,10},{10,11},{12,13},{... | collective-permute-start | bytes 73736 | tf_op jit(solution)/shard_map/ppermute | solution.py:388
  17.3 2.6 %slice_bitcast_fusion.2 = (f32[4,48,512]{2,1,0:T(8,128)}, f32[4,48,512]{2,1,0:T(8,128)}, f32[4,48,512]{2,1,0:T(8,128)}, f32[4,48,512]{2,1,0:T(8,128)}) fusion(f32[4,8,48,512]{3,2,1,0:T(8,128)} %q_ref.1), kind=kLoop, calls=%fused_computation.11 | loop fusion | bytes 3145728 | tf_op jit(solution)/shard_map/squeeze | solution.py:406
  19.9 1.9 %slice_bitcast_fusion = (f32[4,48,512]{2,1,0:T(8,128)S(1)}, f32[4,48,512]{2,1,0:T(8,128)}) fusion(f32[4,8,48,512]{3,2,1,0:T(8,128)} %q_ref.1), kind=kLoop, calls=%fused_computation.8 | loop fusion | bytes 1572864 | tf_op jit(solution)/shard_map/squeeze | solution.py:392
  22.3 1.1 %constant_dynamic-update-slice_fusion.10 = f32[24,48,640]{2,1,0:T(8,128)S(1)} fusion(f32[24,48,640]{2,1,0:T(8,128)S(1)} %broadcast_in_dim.8, f32[24,48,128]{2,1,0:T(8,128)} %shard_map.104, s32[]{:T(128)S(6)} %select_n.98), kind=kLoop, calls=%fused_computation.32 | loop fusion | bytes 1179652 | tf_op jit(solution)/shard_map/dynamic_update_slice | solution.py:41
  23.5 1.4 %constant_dynamic-slice_fusion.2 = (f32[1,8,8]{2,0,1:T(1,128)}, f32[1,8,8]{2,0,1:T(1,128)}, f32[1,8,8]{2,0,1:T(1,128)}) fusion(f32[4,8,8]{2,0,1:T(4,128)} %copy-done.7, s32[]{:T(128)S(6)} %select_n.120, s32[]{:T(128)S(6)} %select_n.124, s32[]{:T(128)S(6)} %select_n.122), kind=kLoop, calls=%fused_computation.21 | loop fusion | bytes 1548 | tf_op jit(solution)/shard_map/jit(dynamic_index_in_dim)/dynamic_slice | solution.py:397
  24.9 3.7 %collective-permute-start.9 = (f32[1,48,128]{2,1,0:T(8,128)S(1)}, f32[1,48,128]{2,1,0:T(8,128)S(1)}, u32[]{:S(2)}, u32[]{:S(2)}) collective-permute-start(f32[1,48,128]{2,1,0:T(8,128)S(1)} %slice.30), channel_id=1, source_target_pairs={{0,5},{1,6},{2,7},{4,9},{5,10},{6,11},{8,13},{9,14},{10,15},{12,1}... | collective-permute-start | bytes 73736 | tf_op jit(solution)/shard_map/ppermute | solution.py:388
  28.7 3.2 %collective-permute-done.9 = f32[1,48,128]{2,1,0:T(8,128)S(1)} collective-permute-done((f32[1,48,128]{2,1,0:T(8,128)S(1)}, f32[1,48,128]{2,1,0:T(8,128)S(1)}, u32[]{:S(2)}, u32[]{:S(2)}) %collective-permute-start.9) | collective-permute-done | bytes 24608 | tf_op jit(solution)/shard_map/ppermute | solution.py:388
  31.8 3.0 %collective-permute-start.10 = (f32[1,48,128]{2,1,0:T(8,128)S(1)}, f32[1,48,128]{2,1,0:T(8,128)S(1)}, u32[]{:S(2)}, u32[]{:S(2)}) collective-permute-start(f32[1,48,128]{2,1,0:T(8,128)S(1)} %slice.30), channel_id=1, source_target_pairs={{0,9},{1,10},{2,11},{4,13},{5,14},{6,15},{8,1},{9,2},{10,3},{12,5}... | collective-permute-start | bytes 73736 | tf_op jit(solution)/shard_map/ppermute | solution.py:388
  34.9 3.5 %collective-permute-done.10 = f32[1,48,128]{2,1,0:T(8,128)S(1)} collective-permute-done((f32[1,48,128]{2,1,0:T(8,128)S(1)}, f32[1,48,128]{2,1,0:T(8,128)S(1)}, u32[]{:S(2)}, u32[]{:S(2)}) %collective-permute-start.10) | collective-permute-done | bytes 24608 | tf_op jit(solution)/shard_map/ppermute | solution.py:388
  38.4 5.4 %collective-permute-start.11 = (f32[1,48,128]{2,1,0:T(8,128)S(1)}, f32[1,48,128]{2,1,0:T(8,128)S(1)}, u32[]{:S(2)}, u32[]{:S(2)}) collective-permute-start(f32[1,48,128]{2,1,0:T(8,128)S(1)} %slice.30), channel_id=1, source_target_pairs={{0,13},{1,14},{2,15},{4,1},{5,2},{6,3},{8,5},{9,6},{10,7},{12,9},{... | collective-permute-start | bytes 73736 | tf_op jit(solution)/shard_map/ppermute | solution.py:388
  44.7 2.1 %collective-permute-start.12 = (f32[4,8,512]{2,1,0:T(8,128)}, f32[4,8,512]{2,1,0:T(8,128)S(1)}, u32[]{:S(2)}, u32[]{:S(2)}) collective-permute-start(f32[4,8,512]{2,1,0:T(8,128)} %param.10), channel_id=1, source_target_pairs={{0,1},{1,2},{2,3},{3,0},{4,5},{5,6},{6,7},{7,4},{8,9},{9,10},{10,1... | collective-permute-start | bytes 196616 | tf_op jit(solution)/shard_map/ppermute | solution.py:395
  46.8 1.9 %collective-permute-start = (f32[4,48,512]{2,1,0:T(8,128)}, f32[4,48,512]{2,1,0:T(8,128)S(1)}, u32[]{:S(2)}, u32[]{:S(2)}) collective-permute-start(f32[4,48,512]{2,1,0:T(8,128)} %get-tuple-element.29), channel_id=1, source_target_pairs={{0,1},{1,2},{2,3},{4,5},{5,6},{6,7},{8,9},{9,10},{10,11},{12,13},{... | collective-permute-start | bytes 1179656 | tf_op jit(solution)/shard_map/ppermute | solution.py:16
  48.8 1.3 %collective-permute-start.5 = (f32[24,48,128]{2,1,0:T(8,128)}, f32[24,48,128]{2,1,0:T(8,128)S(1)}, u32[]{:S(2)}, u32[]{:S(2)}) collective-permute-start(f32[24,48,128]{2,1,0:T(8,128)} %collective-permute-done.3), channel_id=1, source_target_pairs={{4,0},{8,4},{5,1},{9,5},{6,2},{10,6},{7,3},{11,7},{20,16},{24,20},... | collective-permute-start | bytes 1769480 | tf_op jit(solution)/shard_map/ppermute | solution.py:45
  50.1 1.0 convolution_bitcast_fusion
  51.1 2.4 %collective-permute-start.1 = (f32[4,48,512]{2,1,0:T(8,128)S(1)}, f32[4,48,512]{2,1,0:T(8,128)S(1)}, u32[]{:S(2)}, u32[]{:S(2)}) collective-permute-start(f32[4,48,512]{2,1,0:T(8,128)S(1)} %get-tuple-element.28), channel_id=1, source_target_pairs={{1,0},{2,1},{3,2},{5,4},{6,5},{7,6},{9,8},{10,9},{11,10},{13,12},{... | collective-permute-start | bytes 1179656 | tf_op jit(solution)/shard_map/ppermute | solution.py:16
  53.6 1.0 convolution_bitcast_fusion.1
  55.3 1.5 %fusion.3.rest_8_.src_ref.refs_15_ = f32[4,8,512]{2,1,0:T(8,128)} fusion(f32[4,8,512]{2,1,0:T(8,128)S(1)} %convolution_bitcast_fusion, f32[4,8,512]{2,1,0:T(8,128)S(1)} %convolution_bitcast_fusion.1, f32[4,8,512]{2,1,0:T(8,128)S(1)} %convolution_bitcast_fusion.3, f32[4,8,512]{2,1,0:T(8,128)S(1)} %collective-permute-done.12, f32[8,8,1]{1,0,2:T(8,128)} %bitcast.61, ...), kind=kOutput, calls=%fused_computation.6 | convolution fusion | flops 1638400 | bytes 393472 | tf_op jit(solution)/shard_map/jm,kmn->kjn/dot_general | solution.py:398
  56.8 8.4 %collective-permute-done.5 = f32[24,48,128]{2,1,0:T(8,128)S(1)} collective-permute-done((f32[24,48,128]{2,1,0:T(8,128)}, f32[24,48,128]{2,1,0:T(8,128)S(1)}, u32[]{:S(2)}, u32[]{:S(2)}) %collective-permute-start.5) | collective-permute-done | bytes 589856 | tf_op jit(solution)/shard_map/ppermute | solution.py:45
  65.3 1.3 %collective-permute-start.7 = (f32[24,48,128]{2,1,0:T(8,128)S(1)}, f32[24,48,128]{2,1,0:T(8,128)S(1)}, u32[]{:S(2)}, u32[]{:S(2)}) collective-permute-start(f32[24,48,128]{2,1,0:T(8,128)S(1)} %collective-permute-done.5), channel_id=1, source_target_pairs={{4,0},{5,1},{6,2},{7,3},{20,16},{21,17},{22,18},{23,19}} | collective-permute-start | bytes 1769480 | tf_op jit(solution)/shard_map/ppermute | solution.py:45
  66.5 1.1 %constant_dynamic-update-slice_fusion.9 = f32[24,48,640]{2,1,0:T(8,128)S(1)} fusion(f32[24,48,640]{2,1,0:T(8,128)S(1)} %constant_dynamic-update-slice_fusion.10, f32[24,48,128]{2,1,0:T(8,128)} %collective-permute-done.2, s32[]{:T(128)S(6)} %select_n.100), kind=kLoop, calls=%fused_computation.31 | loop fusion | bytes 1179652 | tf_op jit(solution)/shard_map/dynamic_update_slice | solution.py:47
  67.7 1.1 %constant_dynamic-update-slice_fusion.8 = f32[24,48,640]{2,1,0:T(8,128)S(1)} fusion(f32[24,48,640]{2,1,0:T(8,128)S(1)} %constant_dynamic-update-slice_fusion.9, f32[24,48,128]{2,1,0:T(8,128)} %collective-permute-done.3, s32[]{:T(128)S(6)} %select_n.102), kind=kLoop, calls=%fused_computation.30 | loop fusion | bytes 1179652 | tf_op jit(solution)/shard_map/dynamic_update_slice | solution.py:49
  69.0 11.6 %collective-permute-done.7 = f32[24,48,128]{2,1,0:T(8,128)S(1)} collective-permute-done((f32[24,48,128]{2,1,0:T(8,128)S(1)}, f32[24,48,128]{2,1,0:T(8,128)S(1)}, u32[]{:S(2)}, u32[]{:S(2)}) %collective-permute-start.7) | collective-permute-done | bytes 589856 | tf_op jit(solution)/shard_map/ppermute | solution.py:45
  82.5 3.4 %shard_map.105 = (f32[4,48,512]{2,1,0:T(8,128)}, f32[4,48,512]{2,1,0:T(8,128)}) custom-call(f32[8]{0:T(128)} %compare_convert_fusion.north_ref.refs_0_, f32[4,48,512]{2,1,0:T(8,128)} %get-tuple-element.33.lo_ref, f32[4,48,512]{2,1,0:T(8,128)} %get-tuple-element.32.hi_ref, f32[4,48,512]{2,1,0:T(8,128)} %get-tuple-element.31.lo_in_ref, ...), custom_call_target="tpu_custom_call" | custom-call | tf_op jit(solution)/shard_map/pallas_call | solution.py:274
  85.9 1.9 %collective-permute-start.15 = (f32[4,48,512]{2,1,0:T(8,128)}, f32[4,48,512]{2,1,0:T(8,128)S(1)}, u32[]{:S(2)}, u32[]{:S(2)}) collective-permute-start(f32[4,48,512]{2,1,0:T(8,128)} %get-tuple-element.24.hi_ref.refs_2_), channel_id=1, source_target_pairs={{0,1},{1,2},{2,3},{4,5},{5,6},{6,7},{8,9},{9,10},{10,11},{12,13},{... | collective-permute-start | bytes 1179656 | tf_op jit(solution)/shard_map/ppermute | solution.py:16
  87.8 3.6 %collective-permute-start.16 = (f32[4,48,512]{2,1,0:T(8,128)}, f32[4,48,512]{2,1,0:T(8,128)S(1)}, u32[]{:S(2)}, u32[]{:S(2)}) collective-permute-start(f32[4,48,512]{2,1,0:T(8,128)} %get-tuple-element.23.lo_ref.refs_1_), channel_id=1, source_target_pairs={{1,0},{2,1},{3,2},{5,4},{6,5},{7,6},{9,8},{10,9},{11,10},{13,12},{... | collective-permute-start | bytes 1179656 | tf_op jit(solution)/shard_map/ppermute | solution.py:16
  91.4 8.6 %shard_map.106 = (f32[4,8,48,512]{3,2,1,0:T(8,128)}, f32[4,48,512]{2,1,0:T(8,128)}, f32[4,48,512]{2,1,0:T(8,128)}) custom-call(f32[8]{0:T(128)} %compare_convert_fusion.north_ref.refs_0_, f32[4,8,48,512]{3,2,1,0:T(8,128)} %q_ref.1, f32[4,48,512]{2,1,0:T(8,128)} %get-tuple-element.23.lo_ref.refs_1_, f32[4,48,512]{2,1,0:T(8,128)} %get-tuple-element.24.hi_ref.refs_2_, ...), custom_call_target="tpu_custom_call" | custom-call | tf_op jit(solution)/shard_map/pallas_call | solution.py:339
  100.8 3.5 %shard_map.107 = f32[4,8,48,512]{3,2,1,0:T(8,128)} custom-call(f32[8]{0:T(128)} %compare_convert_fusion.north_ref.refs_0_, f32[4,48,512]{2,1,0:T(8,128)} %get-tuple-element.23.lo_ref.refs_1_, f32[4,48,512]{2,1,0:T(8,128)} %get-tuple-element.24.hi_ref.refs_2_, f32[4,48,512]{2,1,0:T(8,128)} %get-tuple-element.25.refs_3_, ...), custom_call_target="tpu_custom_call", output_to_operand_aliasing={{}: (16, {})} | custom-call | tf_op jit(solution)/shard_map/pallas_call | solution.py:274
  (52 shorter events, 8.2 us)
Async XLA Ops:
  0.6 0.8 copy-start
  1.6 0.6 copy-start.7
  3.2 18.6 %copy-start.8 = (s32[8,512]{1,0:T(8,128)S(1)}, s32[8,512]{1,0:T(8,128)}, u32[]{:S(2)}) copy-start(s32[8,512]{1,0:T(8,128)} %param.13) | copy-start | bytes 49156
  3.3 18.6 %copy-start.9 = (f32[4,22]{1,0:T(4,128)S(1)}, f32[4,22]{1,0:T(4,128)}, u32[]{:S(2)}) copy-start(f32[4,22]{1,0:T(4,128)} %param.14) | copy-start | bytes 1060
  5.2 38.6 %collective-permute-start.2 = (f32[24,48,128]{2,1,0:T(8,128)}, f32[24,48,128]{2,1,0:T(8,128)}, u32[]{:S(2)}, u32[]{:S(2)}) collective-permute-start(f32[24,48,128]{2,1,0:T(8,128)} %shard_map.104), channel_id=1, source_target_pairs={{0,4},{4,8},{8,12},{1,5},{5,9},{9,13},{2,6},{6,10},{10,14},{3,7},{... | collective-permute-start | bytes 1769480 | tf_op jit(solution)/shard_map/ppermute | solution.py:44
  10.1 38.7 %collective-permute-start.3 = (f32[24,48,128]{2,1,0:T(8,128)}, f32[24,48,128]{2,1,0:T(8,128)}, u32[]{:S(2)}, u32[]{:S(2)}) collective-permute-start(f32[24,48,128]{2,1,0:T(8,128)} %shard_map.104), channel_id=1, source_target_pairs={{4,0},{8,4},{12,8},{5,1},{9,5},{13,9},{6,2},{10,6},{14,10},{7,3},{... | collective-permute-start | bytes 1769480 | tf_op jit(solution)/shard_map/ppermute | solution.py:45
  11.4 35.5 %collective-permute-start.14 = (f32[4,8,512]{2,1,0:T(8,128)}, f32[4,8,512]{2,1,0:T(8,128)}, u32[]{:S(2)}, u32[]{:S(2)}) collective-permute-start(f32[4,8,512]{2,1,0:T(8,128)} %param.10), channel_id=1, source_target_pairs={{0,3},{1,0},{2,1},{3,2},{4,7},{5,4},{6,5},{7,6},{8,11},{9,8},{10,9... | collective-permute-start | bytes 196616 | tf_op jit(solution)/shard_map/ppermute | solution.py:395
  12.4 38.7 %collective-permute-start.13 = (f32[4,8,512]{2,1,0:T(8,128)}, f32[4,8,512]{2,1,0:T(8,128)}, u32[]{:S(2)}, u32[]{:S(2)}) collective-permute-start(f32[4,8,512]{2,1,0:T(8,128)} %param.10), channel_id=1, source_target_pairs={{0,2},{1,3},{2,0},{3,1},{4,6},{5,7},{6,4},{7,5},{8,10},{9,11},{10,... | collective-permute-start | bytes 196616 | tf_op jit(solution)/shard_map/ppermute | solution.py:395
  14.3 10.6 %collective-permute-start.8 = (f32[1,48,128]{2,1,0:T(8,128)S(1)}, f32[1,48,128]{2,1,0:T(8,128)S(1)}, u32[]{:S(2)}, u32[]{:S(2)}) collective-permute-start(f32[1,48,128]{2,1,0:T(8,128)S(1)} %slice.30), channel_id=1, source_target_pairs={{0,1},{1,2},{2,3},{4,5},{5,6},{6,7},{8,9},{9,10},{10,11},{12,13},{... | collective-permute-start | bytes 73736 | tf_op jit(solution)/shard_map/ppermute | solution.py:388
  24.9 6.9 %collective-permute-start.9 = (f32[1,48,128]{2,1,0:T(8,128)S(1)}, f32[1,48,128]{2,1,0:T(8,128)S(1)}, u32[]{:S(2)}, u32[]{:S(2)}) collective-permute-start(f32[1,48,128]{2,1,0:T(8,128)S(1)} %slice.30), channel_id=1, source_target_pairs={{0,5},{1,6},{2,7},{4,9},{5,10},{6,11},{8,13},{9,14},{10,15},{12,1}... | collective-permute-start | bytes 73736 | tf_op jit(solution)/shard_map/ppermute | solution.py:388
  31.8 6.6 %collective-permute-start.10 = (f32[1,48,128]{2,1,0:T(8,128)S(1)}, f32[1,48,128]{2,1,0:T(8,128)S(1)}, u32[]{:S(2)}, u32[]{:S(2)}) collective-permute-start(f32[1,48,128]{2,1,0:T(8,128)S(1)} %slice.30), channel_id=1, source_target_pairs={{0,9},{1,10},{2,11},{4,13},{5,14},{6,15},{8,1},{9,2},{10,3},{12,5}... | collective-permute-start | bytes 73736 | tf_op jit(solution)/shard_map/ppermute | solution.py:388
  38.4 6.3 %collective-permute-start.11 = (f32[1,48,128]{2,1,0:T(8,128)S(1)}, f32[1,48,128]{2,1,0:T(8,128)S(1)}, u32[]{:S(2)}, u32[]{:S(2)}) collective-permute-start(f32[1,48,128]{2,1,0:T(8,128)S(1)} %slice.30), channel_id=1, source_target_pairs={{0,13},{1,14},{2,15},{4,1},{5,2},{6,3},{8,5},{9,6},{10,7},{12,9},{... | collective-permute-start | bytes 73736 | tf_op jit(solution)/shard_map/ppermute | solution.py:388
  43.8 10.8 %collective-permute-start.4 = (f32[24,48,128]{2,1,0:T(8,128)}, f32[24,48,128]{2,1,0:T(8,128)S(1)}, u32[]{:S(2)}, u32[]{:S(2)}) collective-permute-start(f32[24,48,128]{2,1,0:T(8,128)} %collective-permute-done.2), channel_id=1, source_target_pairs={{4,8},{8,12},{5,9},{9,13},{6,10},{10,14},{7,11},{11,15},{20,24},{2... | collective-permute-start | bytes 1769480 | tf_op jit(solution)/shard_map/ppermute | solution.py:44
  44.7 10.6 %collective-permute-start.12 = (f32[4,8,512]{2,1,0:T(8,128)}, f32[4,8,512]{2,1,0:T(8,128)S(1)}, u32[]{:S(2)}, u32[]{:S(2)}) collective-permute-start(f32[4,8,512]{2,1,0:T(8,128)} %param.10), channel_id=1, source_target_pairs={{0,1},{1,2},{2,3},{3,0},{4,5},{5,6},{6,7},{7,4},{8,9},{9,10},{10,1... | collective-permute-start | bytes 196616 | tf_op jit(solution)/shard_map/ppermute | solution.py:395
  46.8 22.1 %copy-start.2 = (f32[1,48,512]{2,1,0:T(8,128)}, f32[1,48,512]{2,1,0:T(8,128)S(1)}, u32[]{:S(2)}) copy-start(f32[1,48,512]{2,1,0:T(8,128)S(1)} %constant_dynamic-update-slice_fusion.rest_2_.refs_9_) | copy-start | bytes 294916
  46.8 33.8 %collective-permute-start = (f32[4,48,512]{2,1,0:T(8,128)}, f32[4,48,512]{2,1,0:T(8,128)S(1)}, u32[]{:S(2)}, u32[]{:S(2)}) collective-permute-start(f32[4,48,512]{2,1,0:T(8,128)} %get-tuple-element.29), channel_id=1, source_target_pairs={{0,1},{1,2},{2,3},{4,5},{5,6},{6,7},{8,9},{9,10},{10,11},{12,13},{... | collective-permute-start | bytes 1179656 | tf_op jit(solution)/shard_map/ppermute | solution.py:16
  48.8 16.5 %collective-permute-start.5 = (f32[24,48,128]{2,1,0:T(8,128)}, f32[24,48,128]{2,1,0:T(8,128)S(1)}, u32[]{:S(2)}, u32[]{:S(2)}) collective-permute-start(f32[24,48,128]{2,1,0:T(8,128)} %collective-permute-done.3), channel_id=1, source_target_pairs={{4,0},{8,4},{5,1},{9,5},{6,2},{10,6},{7,3},{11,7},{20,16},{24,20},... | collective-permute-start | bytes 1769480 | tf_op jit(solution)/shard_map/ppermute | solution.py:45
  51.1 29.5 %collective-permute-start.1 = (f32[4,48,512]{2,1,0:T(8,128)S(1)}, f32[4,48,512]{2,1,0:T(8,128)S(1)}, u32[]{:S(2)}, u32[]{:S(2)}) collective-permute-start(f32[4,48,512]{2,1,0:T(8,128)S(1)} %get-tuple-element.28), channel_id=1, source_target_pairs={{1,0},{2,1},{3,2},{5,4},{6,5},{7,6},{9,8},{10,9},{11,10},{13,12},{... | collective-permute-start | bytes 1179656 | tf_op jit(solution)/shard_map/ppermute | solution.py:16
  54.6 14.3 %collective-permute-start.6 = (f32[24,48,128]{2,1,0:T(8,128)S(1)}, f32[24,48,128]{2,1,0:T(8,128)S(1)}, u32[]{:S(2)}, u32[]{:S(2)}) collective-permute-start(f32[24,48,128]{2,1,0:T(8,128)S(1)} %collective-permute-done.4), channel_id=1, source_target_pairs={{8,12},{9,13},{10,14},{11,15},{24,28},{25,29},{26,30},{27,31}} | collective-permute-start | bytes 1769480 | tf_op jit(solution)/shard_map/ppermute | solution.py:44
  65.3 15.3 %collective-permute-start.7 = (f32[24,48,128]{2,1,0:T(8,128)S(1)}, f32[24,48,128]{2,1,0:T(8,128)S(1)}, u32[]{:S(2)}, u32[]{:S(2)}) collective-permute-start(f32[24,48,128]{2,1,0:T(8,128)S(1)} %collective-permute-done.5), channel_id=1, source_target_pairs={{4,0},{5,1},{6,2},{7,3},{20,16},{21,17},{22,18},{23,19}} | collective-permute-start | bytes 1769480 | tf_op jit(solution)/shard_map/ppermute | solution.py:45
  80.6 1.8 %copy-start.1 = (f32[24,48,640]{2,1,0:T(8,128)}, f32[24,48,640]{2,1,0:T(8,128)S(1)}, u32[]{:S(2)}) copy-start(f32[24,48,640]{2,1,0:T(8,128)S(1)} %constant_dynamic-update-slice_fusion.4.rest_0_.rest_1_.rest_3_.rest_4_.rest_5_.rest_6_.rest_7_.wx_ref.refs_7_.refs_8_.refs_10_.refs_11_.refs_12_.refs_13_.refs_14_) | copy-start | bytes 8847364
  80.7 0.8 copy-start.5
  81.5 1.0 copy-start.6
  85.9 14.1 %collective-permute-start.15 = (f32[4,48,512]{2,1,0:T(8,128)}, f32[4,48,512]{2,1,0:T(8,128)S(1)}, u32[]{:S(2)}, u32[]{:S(2)}) collective-permute-start(f32[4,48,512]{2,1,0:T(8,128)} %get-tuple-element.24.hi_ref.refs_2_), channel_id=1, source_target_pairs={{0,1},{1,2},{2,3},{4,5},{5,6},{6,7},{8,9},{9,10},{10,11},{12,13},{... | collective-permute-start | bytes 1179656 | tf_op jit(solution)/shard_map/ppermute | solution.py:16
  87.8 12.2 %collective-permute-start.16 = (f32[4,48,512]{2,1,0:T(8,128)}, f32[4,48,512]{2,1,0:T(8,128)S(1)}, u32[]{:S(2)}, u32[]{:S(2)}) collective-permute-start(f32[4,48,512]{2,1,0:T(8,128)} %get-tuple-element.23.lo_ref.refs_1_), channel_id=1, source_target_pairs={{1,0},{2,1},{3,2},{5,4},{6,5},{7,6},{9,8},{10,9},{11,10},{13,12},{... | collective-permute-start | bytes 1179656 | tf_op jit(solution)/shard_map/ppermute | solution.py:16
  100.0 0.8 copy-start.3
  100.0 0.9 copy-start.4

commit v21 on v18

--- a/solution.py
+++ b/solution.py
@@ -282,12 +282,13 @@
 def fused_kernel(north_ref, q_ref, lo_ref, hi_ref, wx_ref, src_ref, o_ref, lo_in_ref, hi_in_ref, coef_ref, mid_ref):
     lat_rows = q_ref.shape[1]
     levels, lon = q_ref.shape[2], q_ref.shape[3]
+    group = q_ref.shape[0]
 
     @pl.when(pl.program_id(0) == 0)
     def _():
         fill_coefficients(north_ref, wx_ref, coef_ref)
 
-    def stencil(a, qa, qm, qp):
+    def stencil(t, a, qa, qm, qp):
         result = (
             coef_ref[0, a] * qa
             + coef_ref[1, a] * pltpu.roll(qa, lon - 1, 1)
@@ -297,38 +298,40 @@
             + coef_ref[5, a] * pltpu.roll(qa, levels - 1, 0)
             + coef_ref[6, a] * pltpu.roll(qa, 1, 0)
         )
-        return result, result[0:1] + src_ref[0, a : a + 1, :]
-
-    mid_ref[0] = lo_ref[0]
-    mid_ref[lat_rows - 1] = hi_ref[0]
-    for a in range(1, lat_rows - 1):
-        result, surface = stencil(a, q_ref[0, a], q_ref[0, a - 1], q_ref[0, a + 1])
-        mid_ref[a] = result
-        mid_ref[a, 0:1, :] = surface
-        if a == 1:
-            lo_in_ref[0] = mid_ref[a]
-        if a == lat_rows - 2:
-            hi_in_ref[0] = mid_ref[a]
-    for a in range(1, lat_rows - 1):
-        result, surface = stencil(a, mid_ref[a], mid_ref[a - 1], mid_ref[a + 1])
-        o_ref[0, a] = result
-        o_ref[0, a, 0:1, :] = surface
+        return result, result[0:1] + src_ref[t, a : a + 1, :]
+
+    for t in range(group):
+        mid_ref[0] = lo_ref[t]
+        mid_ref[lat_rows - 1] = hi_ref[t]
+        for a in range(1, lat_rows - 1):
+            result, surface = stencil(t, a, q_ref[t, a], q_ref[t, a - 1], q_ref[t, a + 1])
+            mid_ref[a] = result
+            mid_ref[a, 0:1, :] = surface
+            if a == 1:
+                lo_in_ref[t] = mid_ref[a]
+            if a == lat_rows - 2:
+                hi_in_ref[t] = mid_ref[a]
+        for a in range(1, lat_rows - 1):
+            result, surface = stencil(t, a, mid_ref[a], mid_ref[a - 1], mid_ref[a + 1])
+            o_ref[t, a] = result
+            o_ref[t, a, 0:1, :] = surface
 
 
 def fused_steps(state, lo, hi, weather, emission, north_open):
     tracers, lat_rows, levels, lon = state.shape
-    row = pl.BlockSpec((1, lat_rows, levels, lon), lambda k: (k, 0, 0, 0))
-    edge = pl.BlockSpec((1, levels, lon), lambda k: (k, 0, 0))
+    group = 2 if tracers % 2 == 0 else 1
+    row = pl.BlockSpec((group, lat_rows, levels, lon), lambda k: (k, 0, 0, 0))
+    edge = pl.BlockSpec((group, levels, lon), lambda k: (k, 0, 0))
     grid_spec = pltpu.PrefetchScalarGridSpec(
         num_scalar_prefetch=0,
-        grid=(tracers,),
+        grid=(tracers // group,),
         in_specs=[
             pl.BlockSpec(memory_space=pltpu.SMEM),
             row,
             edge,
             edge,
             pl.BlockSpec(weather.shape[:2] + (lon,), lambda k: (0, 0, 0)),
-            pl.BlockSpec((1, lat_rows, lon), lambda k: (k, 0, 0)),
+            pl.BlockSpec((group, lat_rows, lon), lambda k: (k, 0, 0)),
         ],
         out_specs=[row, edge, edge],
         scratch_shapes=[

time: 93.4 us -> 93.5 us (level)
  transfers between devices with their start and end apart: 14 -> 14, of which waited for: 4 -> 4; matrix products, arithmetic and copies ran while one was open for 14% -> 14% of each run, Pallas kernels for 9% -> 10%
where the time goes in v21:
time: 93.5 us; the launch traced here: 92.8 us
  waiting for transfers between devices  33.7 us (36%)
  starting transfers between devices  23.7 us (25%)
  Pallas kernels  17.6 us (19%)
  local copies, waits for them, and re-layouts  12.3 us (13%)
  matrix products  3.94 us (4%)
  between operations  0.97 us (1%)
    ppermute x3, waiting for transfers between devices, relay_gather(): lax.ppermute(left, axis, [(j, j - 1) for j in range(1, count - r + 1)])  27.9 us
    ppermute x5, starting transfers between devices, passed_along(): return lax.ppermute(value, axis, pairs)  13.7 us
    pallas_call x1, Pallas kernels, fused_steps(): pl.pallas_call(fused_kernel, grid_spec=grid_spec, out_shape=[jax.ShapeDty...  8.82 us
    pallas_call x2, Pallas kernels, edge_step(): pl.pallas_call(kernel, grid_spec=grid_spec, out_shape=out_shape, input_ou...  6.84 us
    ppermute x3, waiting for transfers between devices, relay_gather(): lax.ppermute(right, axis, [(i, i + 1) for i in range(r - 1, count - 1)])  5.7 us
    ppermute x3, starting transfers between devices, relay_gather(): lax.ppermute(right, axis, [(i, i + 1) for i in range(r - 1, count - 1)])  5.41 us
    ppermute x3, starting transfers between devices, relay_gather(): lax.ppermute(left, axis, [(j, j - 1) for j in range(1, count - r + 1)])  3.84 us
    unnamed x22, local copies, waits for them, and re-layouts  3.35 us
  transfers between devices with their start and end apart: 14, of which 4 were waited for; matrix products, arithmetic and copies ran while one was open for 14% of the time, Pallas kernels for 10%

profile of v21, /device:TPU:1, one launch (start us, length us, event | category | flops | bytes accessed | tf_op | source)
XLA Modules:
  0.0 92.8 jit_solution(8725403994799140225)
XLA Ops:
  0.7 0.8 slice.21
  1.4 4.5 %collective-permute-start = (f32[1,48,128]{2,1,0:T(8,128)S(1)}, f32[1,48,128]{2,1,0:T(8,128)S(1)}, u32[]{:S(2)}, u32[]{:S(2)}) collective-permute-start(f32[1,48,128]{2,1,0:T(8,128)S(1)} %slice.21), channel_id=1, source_target_pairs={{0,1},{1,2},{2,3},{4,5},{5,6},{6,7},{8,9},{9,10},{10,11},{12,13},{... | collective-permute-start | bytes 73736 | tf_op jit(solution)/shard_map/ppermute | solution.py:16
  5.9 0.7 constant_dynamic-slice_fusion.4
  6.8 1.7 %convolution_bitcast_fusion.3 = f32[4,8,512]{2,1,0:T(8,128)} fusion(f32[8,8,1]{1,0,2:T(8,128)S(1)} %bitcast.56, f32[4,8,512]{2,1,0:T(8,128)} %param.10), kind=kOutput, calls=%fused_computation.3 | convolution fusion | flops 1572864 | bytes 131328 | tf_op jit(solution)/shard_map/jm,kmn->kjn/dot_general | solution.py:375
  9.7 2.0 %shard_map.104 = f32[25,48,128]{2,1,0:T(8,128)} custom-call(f32[8,48,128]{2,1,0:T(8,128)} %refs_0_, f32[8,48,128]{2,1,0:T(8,128)} %refs_1_, f32[8,48,128]{2,1,0:T(8,128)} %refs_2_, f32[1,48,128]{2,1,0:T(8,128)} %copy-done.8), custom_call_target="tpu_custom_call" | custom-call | tf_op jit(solution)/shard_map/pallas_call | solution.py:30
  11.7 4.0 %collective-permute-start.3 = (f32[25,48,128]{2,1,0:T(8,128)}, f32[25,48,128]{2,1,0:T(8,128)}, u32[]{:S(2)}, u32[]{:S(2)}) collective-permute-start(f32[25,48,128]{2,1,0:T(8,128)} %shard_map.104), channel_id=1, source_target_pairs={{0,4},{4,8},{8,12},{1,5},{5,9},{9,13},{2,6},{6,10},{10,14},{3,7},{... | collective-permute-start | bytes 1843208 | tf_op jit(solution)/shard_map/ppermute | solution.py:44
  15.7 2.5 %slice_bitcast_fusion.2 = (f32[4,48,512]{2,1,0:T(8,128)}, f32[4,48,512]{2,1,0:T(8,128)}, f32[4,48,512]{2,1,0:T(8,128)}, f32[4,48,512]{2,1,0:T(8,128)}) fusion(f32[4,8,48,512]{3,2,1,0:T(8,128)} %q_ref.1), kind=kLoop, calls=%fused_computation.7 | loop fusion | bytes 3145728 | tf_op jit(solution)/shard_map/squeeze | solution.py:398
  18.2 1.3 %collective-permute-start.4 = (f32[25,48,128]{2,1,0:T(8,128)}, f32[25,48,128]{2,1,0:T(8,128)}, u32[]{:S(2)}, u32[]{:S(2)}) collective-permute-start(f32[25,48,128]{2,1,0:T(8,128)} %shard_map.104), channel_id=1, source_target_pairs={{4,0},{8,4},{12,8},{5,1},{9,5},{13,9},{6,2},{10,6},{14,10},{7,3},{... | collective-permute-start | bytes 1843208 | tf_op jit(solution)/shard_map/ppermute | solution.py:45
  19.5 0.9 fusion
  21.2 1.2 %slice_bitcast_fusion = (f32[4,48,512]{2,1,0:T(8,128)S(1)}, f32[4,48,512]{2,1,0:T(8,128)S(1)}) fusion(f32[4,8,48,512]{3,2,1,0:T(8,128)} %q_ref.1), kind=kLoop, calls=%fused_computation.4 | loop fusion | bytes 1572864 | tf_op jit(solution)/shard_map/squeeze | solution.py:384
  22.3 5.7 %collective-permute-done.3 = f32[25,48,128]{2,1,0:T(8,128)} collective-permute-done((f32[25,48,128]{2,1,0:T(8,128)}, f32[25,48,128]{2,1,0:T(8,128)}, u32[]{:S(2)}, u32[]{:S(2)}) %collective-permute-start.3) | collective-permute-done | bytes 614432 | tf_op jit(solution)/shard_map/ppermute | solution.py:44
  28.0 0.7 collective-permute-start.5
  28.9 1.1 %constant_dynamic-update-slice_fusion.6 = f32[25,48,640]{2,1,0:T(8,128)S(1)} fusion(f32[25,48,640]{2,1,0:T(8,128)S(1)} %broadcast_in_dim.2, f32[25,48,128]{2,1,0:T(8,128)} %shard_map.104, s32[]{:T(128)S(6)} %select_n.70), kind=kLoop, calls=%fused_computation.25 | loop fusion | bytes 1228804 | tf_op jit(solution)/shard_map/dynamic_update_slice | solution.py:41
  30.1 1.9 %collective-permute-start.1 = (f32[4,48,512]{2,1,0:T(8,128)S(1)}, f32[4,48,512]{2,1,0:T(8,128)S(1)}, u32[]{:S(2)}, u32[]{:S(2)}) collective-permute-start(f32[4,48,512]{2,1,0:T(8,128)S(1)} %get-tuple-element.31), channel_id=1, source_target_pairs={{0,1},{1,2},{2,3},{4,5},{5,6},{6,7},{8,9},{9,10},{10,11},{12,13},{... | collective-permute-start | bytes 1179656 | tf_op jit(solution)/shard_map/ppermute | solution.py:16
  32.0 3.4 %collective-permute-done.4 = f32[25,48,128]{2,1,0:T(8,128)} collective-permute-done((f32[25,48,128]{2,1,0:T(8,128)}, f32[25,48,128]{2,1,0:T(8,128)}, u32[]{:S(2)}, u32[]{:S(2)}) %collective-permute-start.4) | collective-permute-done | bytes 614432 | tf_op jit(solution)/shard_map/ppermute | solution.py:45
  35.5 1.3 %collective-permute-start.6 = (f32[25,48,128]{2,1,0:T(8,128)}, f32[25,48,128]{2,1,0:T(8,128)S(1)}, u32[]{:S(2)}, u32[]{:S(2)}) collective-permute-start(f32[25,48,128]{2,1,0:T(8,128)} %collective-permute-done.4), channel_id=1, source_target_pairs={{4,0},{8,4},{5,1},{9,5},{6,2},{10,6},{7,3},{11,7},{20,16},{24,20},... | collective-permute-start | bytes 1843208 | tf_op jit(solution)/shard_map/ppermute | solution.py:45
  37.0 2.1 %collective-permute-start.2 = (f32[4,48,512]{2,1,0:T(8,128)S(1)}, f32[4,48,512]{2,1,0:T(8,128)S(1)}, u32[]{:S(2)}, u32[]{:S(2)}) collective-permute-start(f32[4,48,512]{2,1,0:T(8,128)S(1)} %get-tuple-element.30), channel_id=1, source_target_pairs={{1,0},{2,1},{3,2},{5,4},{6,5},{7,6},{9,8},{10,9},{11,10},{13,12},{... | collective-permute-start | bytes 1179656 | tf_op jit(solution)/shard_map/ppermute | solution.py:16
  39.3 0.7 collective-permute-start.7
  40.1 0.8 bitcast_multiply_fusion.rest_8_.src_ref.refs_15_
  40.9 12.0 %collective-permute-done.6 = f32[25,48,128]{2,1,0:T(8,128)S(1)} collective-permute-done((f32[25,48,128]{2,1,0:T(8,128)}, f32[25,48,128]{2,1,0:T(8,128)S(1)}, u32[]{:S(2)}, u32[]{:S(2)}) %collective-permute-start.6) | collective-permute-done | bytes 614432 | tf_op jit(solution)/shard_map/ppermute | solution.py:45
  52.9 1.3 %collective-permute-start.8 = (f32[25,48,128]{2,1,0:T(8,128)S(1)}, f32[25,48,128]{2,1,0:T(8,128)S(1)}, u32[]{:S(2)}, u32[]{:S(2)}) collective-permute-start(f32[25,48,128]{2,1,0:T(8,128)S(1)} %collective-permute-done.6), channel_id=1, source_target_pairs={{4,0},{5,1},{6,2},{7,3},{20,16},{21,17},{22,18},{23,19}} | collective-permute-start | bytes 1843208 | tf_op jit(solution)/shard_map/ppermute | solution.py:45
  54.2 1.1 %constant_dynamic-update-slice_fusion.5 = f32[25,48,640]{2,1,0:T(8,128)S(1)} fusion(f32[25,48,640]{2,1,0:T(8,128)S(1)} %constant_dynamic-update-slice_fusion.6, f32[25,48,128]{2,1,0:T(8,128)} %collective-permute-done.3, s32[]{:T(128)S(6)} %select_n.72), kind=kLoop, calls=%fused_computation.24 | loop fusion | bytes 1228804 | tf_op jit(solution)/shard_map/dynamic_update_slice | solution.py:47
  55.3 1.1 %constant_dynamic-update-slice_fusion.4 = f32[25,48,640]{2,1,0:T(8,128)S(1)} fusion(f32[25,48,640]{2,1,0:T(8,128)S(1)} %constant_dynamic-update-slice_fusion.5, f32[25,48,128]{2,1,0:T(8,128)} %collective-permute-done.4, s32[]{:T(128)S(6)} %select_n.74), kind=kLoop, calls=%fused_computation.23 | loop fusion | bytes 1228804 | tf_op jit(solution)/shard_map/dynamic_update_slice | solution.py:49
  56.6 12.5 %collective-permute-done.8 = f32[25,48,128]{2,1,0:T(8,128)S(1)} collective-permute-done((f32[25,48,128]{2,1,0:T(8,128)S(1)}, f32[25,48,128]{2,1,0:T(8,128)S(1)}, u32[]{:S(2)}, u32[]{:S(2)}) %collective-permute-start.8) | collective-permute-done | bytes 614432 | tf_op jit(solution)/shard_map/ppermute | solution.py:45
  69.2 0.8 copy-done.5
  70.0 0.9 copy-done.1
  71.0 3.4 %shard_map.105 = (f32[4,48,512]{2,1,0:T(8,128)}, f32[4,48,512]{2,1,0:T(8,128)}) custom-call(f32[8]{0:T(128)} %compare_convert_fusion.north_ref.refs_0_, f32[4,48,512]{2,1,0:T(8,128)} %get-tuple-element.35.lo_ref, f32[4,48,512]{2,1,0:T(8,128)} %get-tuple-element.34.hi_ref, f32[4,48,512]{2,1,0:T(8,128)} %get-tuple-element.33.lo_in_ref, ...), custom_call_target="tpu_custom_call" | custom-call | tf_op jit(solution)/shard_map/pallas_call | solution.py:274
  74.4 1.9 %collective-permute-start.12 = (f32[4,48,512]{2,1,0:T(8,128)}, f32[4,48,512]{2,1,0:T(8,128)S(1)}, u32[]{:S(2)}, u32[]{:S(2)}) collective-permute-start(f32[4,48,512]{2,1,0:T(8,128)} %get-tuple-element.26.hi_ref.refs_2_), channel_id=1, source_target_pairs={{0,1},{1,2},{2,3},{4,5},{5,6},{6,7},{8,9},{9,10},{10,11},{12,13},{... | collective-permute-start | bytes 1179656 | tf_op jit(solution)/shard_map/ppermute | solution.py:16
  76.3 3.2 %collective-permute-start.13 = (f32[4,48,512]{2,1,0:T(8,128)}, f32[4,48,512]{2,1,0:T(8,128)S(1)}, u32[]{:S(2)}, u32[]{:S(2)}) collective-permute-start(f32[4,48,512]{2,1,0:T(8,128)} %get-tuple-element.25.lo_ref.refs_1_), channel_id=1, source_target_pairs={{1,0},{2,1},{3,2},{5,4},{6,5},{7,6},{9,8},{10,9},{11,10},{13,12},{... | collective-permute-start | bytes 1179656 | tf_op jit(solution)/shard_map/ppermute | solution.py:16
  79.5 8.8 %shard_map.106 = (f32[4,8,48,512]{3,2,1,0:T(8,128)}, f32[4,48,512]{2,1,0:T(8,128)}, f32[4,48,512]{2,1,0:T(8,128)}) custom-call(f32[8]{0:T(128)} %compare_convert_fusion.north_ref.refs_0_, f32[4,8,48,512]{3,2,1,0:T(8,128)} %q_ref.1, f32[4,48,512]{2,1,0:T(8,128)} %get-tuple-element.25.lo_ref.refs_1_, f32[4,48,512]{2,1,0:T(8,128)} %get-tuple-element.26.hi_ref.refs_2_, ...), custom_call_target="tpu_custom_call" | custom-call | tf_op jit(solution)/shard_map/pallas_call | solution.py:342
  88.4 0.7 copy-done.2
  89.3 3.5 %shard_map.107 = f32[4,8,48,512]{3,2,1,0:T(8,128)} custom-call(f32[8]{0:T(128)} %compare_convert_fusion.north_ref.refs_0_, f32[4,48,512]{2,1,0:T(8,128)} %get-tuple-element.25.lo_ref.refs_1_, f32[4,48,512]{2,1,0:T(8,128)} %get-tuple-element.26.hi_ref.refs_2_, f32[4,48,512]{2,1,0:T(8,128)} %get-tuple-element.27.refs_3_, ...), custom_call_target="tpu_custom_call", output_to_operand_aliasing={{}: (16, {})} | custom-call | tf_op jit(solution)/shard_map/pallas_call | solution.py:274
  (43 shorter events, 3.3 us)
Async XLA Ops:
  0.6 6.0 %copy-start = (f32[8,8,8]{2,1,0:T(8,128)S(1)}, f32[8,8,8]{2,1,0:T(8,128)}, u32[]{:S(2)}) copy-start(f32[8,8,8]{2,1,0:T(8,128)} %param.11) | copy-start | bytes 6148
  0.6 18.9 %copy-start.9 = (s32[8,512]{1,0:T(8,128)S(1)}, s32[8,512]{1,0:T(8,128)}, u32[]{:S(2)}) copy-start(s32[8,512]{1,0:T(8,128)} %param.13) | copy-start | bytes 49156
  0.7 18.9 %copy-start.10 = (f32[4,22]{1,0:T(4,128)S(1)}, f32[4,22]{1,0:T(4,128)}, u32[]{:S(2)}) copy-start(f32[4,22]{1,0:T(4,128)} %param.14) | copy-start | bytes 1060
  1.4 7.7 %collective-permute-start = (f32[1,48,128]{2,1,0:T(8,128)S(1)}, f32[1,48,128]{2,1,0:T(8,128)S(1)}, u32[]{:S(2)}, u32[]{:S(2)}) collective-permute-start(f32[1,48,128]{2,1,0:T(8,128)S(1)} %slice.21), channel_id=1, source_target_pairs={{0,1},{1,2},{2,3},{4,5},{5,6},{6,7},{8,9},{9,10},{10,11},{12,13},{... | collective-permute-start | bytes 73736 | tf_op jit(solution)/shard_map/ppermute | solution.py:16
  9.1 0.6 copy-start.8
  11.7 16.4 %collective-permute-start.3 = (f32[25,48,128]{2,1,0:T(8,128)}, f32[25,48,128]{2,1,0:T(8,128)}, u32[]{:S(2)}, u32[]{:S(2)}) collective-permute-start(f32[25,48,128]{2,1,0:T(8,128)} %shard_map.104), channel_id=1, source_target_pairs={{0,4},{4,8},{8,12},{1,5},{5,9},{9,13},{2,6},{6,10},{10,14},{3,7},{... | collective-permute-start | bytes 1843208 | tf_op jit(solution)/shard_map/ppermute | solution.py:44
  18.2 17.3 %collective-permute-start.4 = (f32[25,48,128]{2,1,0:T(8,128)}, f32[25,48,128]{2,1,0:T(8,128)}, u32[]{:S(2)}, u32[]{:S(2)}) collective-permute-start(f32[25,48,128]{2,1,0:T(8,128)} %shard_map.104), channel_id=1, source_target_pairs={{4,0},{8,4},{12,8},{5,1},{9,5},{13,9},{6,2},{10,6},{14,10},{7,3},{... | collective-permute-start | bytes 1843208 | tf_op jit(solution)/shard_map/ppermute | solution.py:45
  20.4 19.6 %copy-start.6 = (f32[4,8,512]{2,1,0:T(8,128)S(1)}, f32[4,8,512]{2,1,0:T(8,128)}, u32[]{:S(2)}) copy-start(f32[4,8,512]{2,1,0:T(8,128)} %convolution_bitcast_fusion.3) | copy-start | bytes 196612
  20.4 19.6 %copy-start.7 = (f32[8,512,4]{1,2,0:T(4,128)S(1)}, f32[8,512,4]{1,2,0:T(4,128)}, u32[]{:S(2)}) copy-start(f32[8,512,4]{1,2,0:T(4,128)} %fusion) | copy-start | bytes 196612
  20.4 9.7 %collective-permute-start.10 = (f32[4,8,512]{2,1,0:T(8,128)}, f32[4,8,512]{2,1,0:T(8,128)S(1)}, u32[]{:S(2)}, u32[]{:S(2)}) collective-permute-start(f32[4,8,512]{2,1,0:T(8,128)} %param.10), channel_id=1, source_target_pairs={{0,2},{1,3},{2,0},{3,1},{4,6},{5,7},{6,4},{7,5},{8,10},{9,11},{10,... | collective-permute-start | bytes 196616 | tf_op jit(solution)/shard_map/ppermute | solution.py:387
  20.4 16.5 %collective-permute-start.9 = (f32[4,8,512]{2,1,0:T(8,128)}, f32[4,8,512]{2,1,0:T(8,128)S(1)}, u32[]{:S(2)}, u32[]{:S(2)}) collective-permute-start(f32[4,8,512]{2,1,0:T(8,128)} %param.10), channel_id=1, source_target_pairs={{0,1},{1,2},{2,3},{3,0},{4,5},{5,6},{6,7},{7,4},{8,9},{9,10},{10,1... | collective-permute-start | bytes 196616 | tf_op jit(solution)/shard_map/ppermute | solution.py:387
  21.1 19.0 %collective-permute-start.11 = (f32[4,8,512]{2,1,0:T(8,128)}, f32[4,8,512]{2,1,0:T(8,128)S(1)}, u32[]{:S(2)}, u32[]{:S(2)}) collective-permute-start(f32[4,8,512]{2,1,0:T(8,128)} %param.10), channel_id=1, source_target_pairs={{0,3},{1,0},{2,1},{3,2},{4,7},{5,4},{6,5},{7,6},{8,11},{9,8},{10,9... | collective-permute-start | bytes 196616 | tf_op jit(solution)/shard_map/ppermute | solution.py:387
  28.0 11.3 %collective-permute-start.5 = (f32[25,48,128]{2,1,0:T(8,128)}, f32[25,48,128]{2,1,0:T(8,128)S(1)}, u32[]{:S(2)}, u32[]{:S(2)}) collective-permute-start(f32[25,48,128]{2,1,0:T(8,128)} %collective-permute-done.3), channel_id=1, source_target_pairs={{4,8},{8,12},{5,9},{9,13},{6,10},{10,14},{7,11},{11,15},{20,24},{2... | collective-permute-start | bytes 1843208 | tf_op jit(solution)/shard_map/ppermute | solution.py:44
  30.1 39.1 %collective-permute-start.1 = (f32[4,48,512]{2,1,0:T(8,128)S(1)}, f32[4,48,512]{2,1,0:T(8,128)S(1)}, u32[]{:S(2)}, u32[]{:S(2)}) collective-permute-start(f32[4,48,512]{2,1,0:T(8,128)S(1)} %get-tuple-element.31), channel_id=1, source_target_pairs={{0,1},{1,2},{2,3},{4,5},{5,6},{6,7},{8,9},{9,10},{10,11},{12,13},{... | collective-permute-start | bytes 1179656 | tf_op jit(solution)/shard_map/ppermute | solution.py:16
  35.5 17.4 %collective-permute-start.6 = (f32[25,48,128]{2,1,0:T(8,128)}, f32[25,48,128]{2,1,0:T(8,128)S(1)}, u32[]{:S(2)}, u32[]{:S(2)}) collective-permute-start(f32[25,48,128]{2,1,0:T(8,128)} %collective-permute-done.4), channel_id=1, source_target_pairs={{4,0},{8,4},{5,1},{9,5},{6,2},{10,6},{7,3},{11,7},{20,16},{24,20},... | collective-permute-start | bytes 1843208 | tf_op jit(solution)/shard_map/ppermute | solution.py:45
  37.0 32.2 %collective-permute-start.2 = (f32[4,48,512]{2,1,0:T(8,128)S(1)}, f32[4,48,512]{2,1,0:T(8,128)S(1)}, u32[]{:S(2)}, u32[]{:S(2)}) collective-permute-start(f32[4,48,512]{2,1,0:T(8,128)S(1)} %get-tuple-element.30), channel_id=1, source_target_pairs={{1,0},{2,1},{3,2},{5,4},{6,5},{7,6},{9,8},{10,9},{11,10},{13,12},{... | collective-permute-start | bytes 1179656 | tf_op jit(solution)/shard_map/ppermute | solution.py:16
  39.3 17.2 %collective-permute-start.7 = (f32[25,48,128]{2,1,0:T(8,128)S(1)}, f32[25,48,128]{2,1,0:T(8,128)S(1)}, u32[]{:S(2)}, u32[]{:S(2)}) collective-permute-start(f32[25,48,128]{2,1,0:T(8,128)S(1)} %collective-permute-done.5), channel_id=1, source_target_pairs={{8,12},{9,13},{10,14},{11,15},{24,28},{25,29},{26,30},{27,31}} | collective-permute-start | bytes 1843208 | tf_op jit(solution)/shard_map/ppermute | solution.py:44
  52.9 16.2 %collective-permute-start.8 = (f32[25,48,128]{2,1,0:T(8,128)S(1)}, f32[25,48,128]{2,1,0:T(8,128)S(1)}, u32[]{:S(2)}, u32[]{:S(2)}) collective-permute-start(f32[25,48,128]{2,1,0:T(8,128)S(1)} %collective-permute-done.6), channel_id=1, source_target_pairs={{4,0},{5,1},{6,2},{7,3},{20,16},{21,17},{22,18},{23,19}} | collective-permute-start | bytes 1843208 | tf_op jit(solution)/shard_map/ppermute | solution.py:45
  69.1 1.7 %copy-start.1 = (f32[25,48,640]{2,1,0:T(8,128)}, f32[25,48,640]{2,1,0:T(8,128)S(1)}, u32[]{:S(2)}) copy-start(f32[25,48,640]{2,1,0:T(8,128)S(1)} %constant_dynamic-update-slice_fusion.rest_0_.rest_1_.rest_2_.rest_3_.rest_4_.rest_5_.rest_6_.rest_7_.wx_ref.refs_7_.refs_8_.refs_9_.refs_10_.refs_11_.refs_12_.refs_13_.refs_14_) | copy-start | bytes 9216004
  69.2 1.9 %copy-start.4 = (f32[4,48,512]{2,1,0:T(8,128)}, f32[4,48,512]{2,1,0:T(8,128)S(1)}, u32[]{:S(2)}) copy-start(f32[4,48,512]{2,1,0:T(8,128)S(1)} %collective-permute-done.1.qs_ref) | copy-start | bytes 1179652
  69.2 0.8 copy-start.5
  74.4 14.0 %collective-permute-start.12 = (f32[4,48,512]{2,1,0:T(8,128)}, f32[4,48,512]{2,1,0:T(8,128)S(1)}, u32[]{:S(2)}, u32[]{:S(2)}) collective-permute-start(f32[4,48,512]{2,1,0:T(8,128)} %get-tuple-element.26.hi_ref.refs_2_), channel_id=1, source_target_pairs={{0,1},{1,2},{2,3},{4,5},{5,6},{6,7},{8,9},{9,10},{10,11},{12,13},{... | collective-permute-start | bytes 1179656 | tf_op jit(solution)/shard_map/ppermute | solution.py:16
  76.3 12.1 %collective-permute-start.13 = (f32[4,48,512]{2,1,0:T(8,128)}, f32[4,48,512]{2,1,0:T(8,128)S(1)}, u32[]{:S(2)}, u32[]{:S(2)}) collective-permute-start(f32[4,48,512]{2,1,0:T(8,128)} %get-tuple-element.25.lo_ref.refs_1_), channel_id=1, source_target_pairs={{1,0},{2,1},{3,2},{5,4},{6,5},{7,6},{9,8},{10,9},{11,10},{13,12},{... | collective-permute-start | bytes 1179656 | tf_op jit(solution)/shard_map/ppermute | solution.py:16
  88.4 0.8 copy-start.2
  88.4 0.9 copy-start.3
